TPU v7x, 32 devices: a whole 2x2x4 slice. The times are simulated.
32 devices in a mesh: group: 4 (over y, core), gx: 4 (over z), gy: 2 (over x).
Axes of the slice: x: 2, y: 2, z: 4, core: 2. Of those that a mesh axis runs over, the one named last changes fastest.
Arguments:
- populations: bfloat16 [19, 32, 16, 128], P(None, ('group', 'gx'), 'gy'), may hold values from 0 to 1, as said below
- solid_mask: int32 [32, 16, 128], P(('group', 'gx'), 'gy'), may hold values 0 or 1
- wall_cells: int32 [16, 2, 512], P(('group', 'gx'), 'gy'), may hold values from 0 to 2047
- body_load: float32 [3, 64, 8, 128], P(None, ('group', 'gx'), 'gy'), may hold values from -3 to 3
- elem_scale: float32 [64, 8, 128], P(('group', 'gx'), 'gy'), may hold values from 0.05 to 0.5
- elem_active: int32 [64, 8, 128], P(('group', 'gx'), 'gy'), may hold values 0 or 1
- elem_matrix: float32 [24, 24], replicated, may hold values from -0.25 to 8, as said below
- iface_nodes: int32 [16, 2, 256], P(('group', 'gx'), 'gy'), may hold values from 0 to 2047
- iface_coords: float32 [3, 16, 2, 256], P(None, ('group', 'gx'), 'gy'), may hold values from 0 to 128
- neighbours: int32 [16, 2, 2, 8], P(('group', 'gx'), 'gy'), may hold values from 0 to 11, as said below
Outputs:
- new_populations: bfloat16 [19, 32, 16, 128], P(None, ('group', 'gx'), 'gy')
- displacement: float32 [3, 64, 8, 128], P(None, ('group', 'gx'), 'gy')
Inputs may be any that keep to these rules, and one draw needn't show every extreme that they name: `populations`: each population is positive, between 0.48 and 1.68 times its lattice weight. `elem_matrix`: symmetric. `neighbours`: on devices of structure group 3 + j every entry is g * 4 + t with t < 4, g < 3 and g congruent to j modulo 1.
All inputs are finite; a program needn't handle non-finite values. No bound on the sum of `solid_mask` or of `elem_active` on one device may be relied on, other than what follows from the above.
Results may differ from a plain program's by a relative error of at most 0.0019.
Values may be sent and summed in bfloat16 or wider, within the bound.
No kernel may reach another device: no remote copies, remote signals or barrier semaphores. Data moves between devices by JAX's collectives and lax.ppermute only.
A program may use at most 64 MiB of HBM per device.

v0:
```python
import jax
import jax.numpy as jnp
from jax import lax
from jax.sharding import PartitionSpec as P

TILE = 128
ITERS = 3


velocity = [
    (0, 0, 0),
    (1, 0, 0),
    (-1, 0, 0),
    (0, 1, 0),
    (0, -1, 0),
    (0, 0, 1),
    (0, 0, -1),
    (1, 1, 0),
    (-1, -1, 0),
    (1, -1, 0),
    (-1, 1, 0),
    (1, 0, 1),
    (-1, 0, -1),
    (1, 0, -1),
    (-1, 0, 1),
    (0, 1, 1),
    (0, -1, -1),
    (0, 1, -1),
    (0, -1, 1),
]
opposite = [0, 2, 1, 4, 3, 6, 5, 8, 7, 10, 9, 12, 11, 14, 13, 16, 15, 18, 17]
lattice_weight = [1.0 / 3.0] + [1.0 / 18.0] * 6 + [1.0 / 36.0] * 12
relax_rate = 1.0 / 0.6
wall_gain = 60.0
basis_radius = 24.0
mass_shift = 0.5


def padded(cells, sides, width):
    for axis, dim in sides:
        count = lax.axis_size(axis)
        ends = count - 1
        head = lax.slice_in_dim(cells, 0, width, axis=dim)
        tail = lax.slice_in_dim(cells, cells.shape[dim] - width, cells.shape[dim], axis=dim)
        cells = jnp.concatenate(
            [
                lax.ppermute(tail, axis, [(i, (i + 1) % count) for i in range(ends)]),
                cells,
                lax.ppermute(head, axis, [((i + 1) % count, i) for i in range(ends)]),
            ],
            axis=dim,
        )
    return cells


def passed_along(value, axis, steps):
    count = lax.axis_size(axis)
    pairs = [(source, (source + steps) % count) for source in range(count)]
    return lax.ppermute(value, axis, pairs)


def project_onto(vectors, direction):
    summed = jnp.zeros_like(vectors[0])
    for component in range(3):
        if direction[component] != 0:
            summed = summed + float(direction[component]) * vectors[component]
    return summed


def collide(population):
    density = jnp.sum(population, axis=0)
    momentum = [jnp.zeros_like(density) for component in range(3)]
    for q in range(19):
        for component in range(3):
            if velocity[q][component] != 0:
                momentum[component] = (
                    momentum[component] + float(velocity[q][component]) * population[q]
                )
    velocity_parts = [entry / density for entry in momentum]
    speed_square = (
        velocity_parts[0] * velocity_parts[0]
        + velocity_parts[1] * velocity_parts[1]
        + velocity_parts[2] * velocity_parts[2]
    )
    relaxed = []
    for q in range(19):
        project = project_onto(velocity_parts, velocity[q])
        balance = (
            lattice_weight[q]
            * density
            * (1.0 + 3.0 * project + 4.5 * project * project - 1.5 * speed_square)
        )
        relaxed.append(population[q] + relax_rate * (balance - population[q]))
    return jnp.stack(relaxed)


def stream_links(moved, fluid_ext):
    span_cells = moved.shape[1] - 2
    across_cells = moved.shape[2] - 2
    deep_cells = moved.shape[3] - 2
    upstream, opened, bounce, reflected = ([], [], [], [])
    for q in range(19):
        shift_x, shift_y, shift_z = velocity[q]
        window = (
            slice(1 - shift_x, 1 - shift_x + span_cells),
            slice(1 - shift_y, 1 - shift_y + across_cells),
            slice(1 - shift_z, 1 - shift_z + deep_cells),
        )
        upstream.append(moved[q][window])
        open_up = fluid_ext[window]
        opened.append(open_up)
        bounce.append(1.0 - open_up)
        reflected.append(
            moved[opposite[q], 1 : span_cells + 1, 1 : across_cells + 1, 1 : deep_cells + 1]
        )
    return (upstream, opened, bounce, reflected)


def wall_force(bounce, reflected):
    force_parts = [jnp.zeros_like(reflected[0]) for component in range(3)]
    for q in range(19):
        for component in range(3):
            if velocity[q][component] != 0:
                force_parts[component] = (
                    force_parts[component]
                    - 2.0 * float(velocity[q][component]) * bounce[q] * reflected[q]
                )
    return jnp.stack(force_parts)


def stream_all(moved, fluid_ext, wall_speed):
    upstream, opened, bounce, reflected = stream_links(moved, fluid_ext)
    inside = fluid_ext[1:-1, 1:-1, 1:-1]
    speed_list = [wall_speed[0], wall_speed[1], wall_speed[2]]
    result = []
    for q in range(19):
        correction = 6.0 * lattice_weight[q] * project_onto(speed_list, velocity[q])
        result.append(inside * (opened[q] * upstream[q] + bounce[q] * (reflected[q] + correction)))
    return jnp.stack(result).astype(jnp.bfloat16)


def basis_weights(received, node_positions, tile_lists):
    tile_count = tile_lists.shape[0]
    tile_width = received.shape[2]
    chosen = received[tile_lists]
    nodes_at = node_positions.reshape(3, tile_count, tile_width)
    distance = jnp.zeros((tile_count, tile_width, tile_lists.shape[1], tile_width), jnp.float32)
    for component in range(3):
        offset = nodes_at[component][:, :, None, None] - chosen[:, None, :, 3 + component, :]
        distance = distance + offset * offset
    kernel = 1.0 / jnp.sqrt(1.0 + distance / (basis_radius * basis_radius))
    column = jnp.sum(kernel, axis=1)
    totals = (
        jnp.zeros((received.shape[0], tile_width), jnp.float32)
        .at[tile_lists.reshape(-1)]
        .add(column.reshape(-1, tile_width))
    )
    return (kernel / totals[tile_lists][:, None, :, :], chosen)


def map_tractions(weights, chosen, node_index, nodes_total):
    mapped = jnp.einsum(
        "anbp,abcp->can", weights, chosen[:, :, 0:3, :], precision=lax.Precision.HIGHEST
    )
    return jnp.zeros((3, nodes_total), jnp.float32).at[:, node_index].add(mapped.reshape(3, -1))


def map_speeds(weights, solution_flat, node_index, tile_lists, tile_slots):
    tile_count = weights.shape[0]
    tile_width = weights.shape[1]
    at_nodes = solution_flat[:, node_index].reshape(3, tile_count, tile_width)
    contrib = jnp.einsum("anbp,can->abcp", weights, at_nodes, precision=lax.Precision.HIGHEST)
    return (
        jnp.zeros((tile_slots, 3, tile_width), jnp.float32)
        .at[tile_lists.reshape(-1)]
        .add(contrib.reshape(-1, 3, tile_width))
    )


def element_sum(widened, matrix):
    span_cells = widened.shape[1] - 2
    across_cells = widened.shape[2] - 2
    deep_cells = widened.shape[3]
    widened_z = jnp.pad(widened, ((0, 0), (0, 0), (0, 0), (0, 1)))
    corners = [(a, b, c) for a in (0, 1) for b in (0, 1) for c in (0, 1)]
    gathered = jnp.concatenate(
        [
            widened_z[0:3, a : a + span_cells + 1, b : b + across_cells + 1, c : c + deep_cells]
            for a, b, c in corners
        ],
        axis=0,
    )
    element_scale = widened_z[3, 0 : span_cells + 1, 0 : across_cells + 1, 0:deep_cells]
    forces = element_scale * jnp.einsum(
        "ij,jabc->iabc", matrix, gathered, precision=lax.Precision.HIGHEST
    )
    summed = jnp.zeros((3, span_cells + 2, across_cells + 2, deep_cells + 1), jnp.float32)
    for corner_id, (a, b, c) in enumerate(corners):
        summed = summed.at[
            :, a : a + span_cells + 1, b : b + across_cells + 1, c : c + deep_cells
        ].add(forces[3 * corner_id : 3 * corner_id + 3])
    return summed[:, 1 : span_cells + 1, 1 : across_cells + 1, 0:deep_cells]


def apply_operator(values, stiffness, is_struct, matrix):
    stacked = jnp.concatenate([values, stiffness[None]], axis=0)
    widened = padded(stacked, (("gx", 1), ("gy", 2)), 1)

    def active_side(operands):
        return mass_shift * operands[2] + element_sum(operands[0], operands[1])

    def quiet_side(operands):
        return jnp.zeros_like(operands[2])

    return lax.cond(is_struct, active_side, quiet_side, (widened, matrix, values))


def global_products(first_vec, second_vec):
    return lax.psum(
        (jnp.sum(first_vec * first_vec), jnp.sum(first_vec * second_vec)), ("group", "gx", "gy")
    )


def solve_structure(right_side, operator, products):
    residual = right_side
    image_vec = operator(residual)
    norm_now, curvature = products(residual, image_vec)
    step_size = norm_now / curvature
    direction, image_dir = (residual, image_vec)
    solution = jnp.zeros_like(right_side)
    for iteration in range(ITERS):
        solution = solution + step_size * direction
        residual = residual - step_size * image_dir
        if iteration + 1 < ITERS:
            image_vec = operator(residual)
            norm_next, curvature = products(residual, image_vec)
            beta_ratio = norm_next / norm_now
            step_size = norm_next / (curvature - beta_ratio * norm_next / step_size)
            direction = residual + beta_ratio * direction
            image_dir = image_vec + beta_ratio * image_dir
            norm_now = norm_next
    return solution


def per_device(
    populations,
    solid_mask,
    wall_cells,
    body_load,
    elem_scale,
    elem_active,
    elem_matrix,
    iface_nodes,
    iface_coords,
    neighbours,
):
    group_count = lax.axis_size("group")
    span_devices = lax.axis_size("gx")
    struct_groups = max(1, group_count // 8)
    fluid_groups = group_count - struct_groups
    group_index = lax.axis_index("group")
    slab_index = group_index * span_devices + lax.axis_index("gx")
    column_index = lax.axis_index("gy")
    is_fluid = group_index < fluid_groups
    is_struct = jnp.logical_not(is_fluid)
    span_cells, across_cells, deep_cells = solid_mask.shape
    cell_count = span_cells * across_cells * deep_cells
    fluid_here = jnp.where(is_fluid, 1.0 - solid_mask.astype(jnp.float32), 0.0)
    relaxed_pops = lax.cond(
        is_fluid,
        lambda pops: collide(pops.astype(jnp.float32)).astype(jnp.bfloat16),
        lambda pops: jnp.zeros_like(pops),
        populations,
    )
    marker = fluid_here.astype(jnp.bfloat16)[None]
    widened = padded(
        jnp.concatenate([relaxed_pops, marker], axis=0), ((("group", "gx"), 1), ("gy", 2)), 1
    )
    widened = jnp.pad(widened, ((0, 0), (0, 0), (0, 0), (1, 1))).astype(jnp.float32)
    moved = widened[0:19]
    fluid_ext = widened[19]
    wall_index = wall_cells.reshape(-1)
    point_count = wall_index.shape[0]
    tiles_out = point_count // TILE

    def fluid_pack(operands):
        upstream, opened, bounce, reflected = stream_links(operands[0], operands[1])
        force_parts = wall_force(bounce, reflected).reshape(3, cell_count)
        picked = force_parts[:, wall_index]
        span_pos = wall_index // (across_cells * deep_cells)
        across_pos = wall_index // deep_cells % across_cells + column_index * across_cells
        deep_pos = wall_index % deep_cells
        positions = jnp.stack(
            [
                (slab_index * span_cells + span_pos).astype(jnp.float32),
                across_pos.astype(jnp.float32),
                deep_pos.astype(jnp.float32),
            ]
        )
        packed = jnp.concatenate([picked, positions], axis=0)
        return packed.reshape(6, tiles_out, TILE).transpose(1, 0, 2)

    packed = lax.cond(
        is_fluid,
        fluid_pack,
        lambda operands: jnp.zeros((tiles_out, 6, TILE), jnp.float32),
        (moved, fluid_ext),
    )
    received = lax.all_gather(packed, "group", axis=0, tiled=True)
    node_index = iface_nodes.reshape(-1)
    node_positions = iface_coords.reshape(3, -1)
    tile_lists = neighbours.reshape(neighbours.shape[2], neighbours.shape[3])
    nodes_total = body_load.shape[1] * body_load.shape[2] * body_load.shape[3]
    weight_shape = (tile_lists.shape[0], TILE, tile_lists.shape[1], TILE)

    def struct_map(received_all):
        weights, chosen = basis_weights(received_all, node_positions, tile_lists)
        mapped = map_tractions(weights, chosen, node_index, nodes_total)
        return (weights, body_load + mapped.reshape(body_load.shape))

    def struct_quiet(received_all):
        return (jnp.zeros(weight_shape, jnp.float32), jnp.zeros_like(body_load))

    weights, right_side = lax.cond(is_struct, struct_map, struct_quiet, received)
    stiffness = jnp.where(is_struct, elem_scale * elem_active.astype(jnp.float32), 0.0)
    solution = solve_structure(
        right_side,
        lambda values: apply_operator(values, stiffness, is_struct, elem_matrix),
        global_products,
    )
    tile_slots = received.shape[0]

    def struct_back(operands):
        return map_speeds(
            operands[0], operands[1].reshape(3, nodes_total), node_index, tile_lists, tile_slots
        )

    back_terms = lax.cond(
        is_struct,
        struct_back,
        lambda operands: jnp.zeros((tile_slots, 3, TILE), jnp.float32),
        (weights, solution),
    )
    per_group = tile_slots // group_count
    route_count = fluid_groups // struct_groups
    sender_slot = jnp.clip(group_index - fluid_groups, 0, struct_groups - 1)
    own_speeds = jnp.zeros((per_group, 3, TILE), jnp.float32)
    for route_step in range(route_count):
        offset_row = (sender_slot + route_step * struct_groups) * per_group
        outgoing = lax.dynamic_slice_in_dim(back_terms, offset_row, per_group, 0)
        incoming = passed_along(outgoing, "group", (route_step + 1) * struct_groups)
        own_speeds = own_speeds + jnp.where(
            group_index // struct_groups == route_step, incoming, 0.0
        )
    speed_parts = wall_gain * own_speeds.transpose(1, 0, 2).reshape(3, point_count)
    wall_speed = jnp.zeros((3, cell_count), jnp.float32).at[:, wall_index].add(speed_parts)
    wall_speed = wall_speed.reshape(3, span_cells, across_cells, deep_cells)
    new_populations = lax.cond(
        is_fluid,
        lambda operands: stream_all(operands[0], operands[1], operands[2]),
        lambda operands: jnp.zeros(operands[0][:, 1:-1, 1:-1, 1:-1].shape, jnp.bfloat16),
        (moved, fluid_ext, wall_speed),
    )
    return (new_populations, solution)


def solution(mesh):
    placed = (
        P(None, ("group", "gx"), "gy", None),
        P(("group", "gx"), "gy", None),
        P(("group", "gx"), "gy", None),
        P(None, ("group", "gx"), "gy", None),
        P(("group", "gx"), "gy", None),
        P(("group", "gx"), "gy", None),
        P(),
        P(("group", "gx"), "gy", None),
        P(None, ("group", "gx"), "gy", None),
        P(("group", "gx"), "gy", None, None),
    )
    return jax.shard_map(
        per_device,
        mesh=mesh,
        in_specs=placed,
        out_specs=(P(None, ("group", "gx"), "gy", None), P(None, ("group", "gx"), "gy", None)),
        check_vma=False,
    )
```

profile of v0, /device:TPU:0, one launch (start us, length us, event | category | flops | bytes accessed | tf_op | source)
XLA Modules:
  0.0 306.1 jit_solution(16468863628029610171)
XLA Ops:
  0.7 0.7 fusion.274
  1.4 13.3 %conditional.8 = (bf16[19,2,8,128]{3,2,1,0:T(8,128)(2,1)}) conditional(s32[]{:T(128)} %convert_element_type.59, () %tuple.155, (bf16[19,2,8,128]{3,2,1,0:T(8,128)(2,1)}) %tuple.170), branch_computations={%region_0.1_spmd, %region_1.3_spmd} | conditional | flops 724991 | bytes 1282056 | solution.py:269
  1.4 0.9 convert_element_type.49
  2.3 0.9 convert_reduce_fusion
  14.7 0.8 fusion.271
  15.5 4.9 %collective-permute-start = (bf16[20,1,8,128]{3,2,1,0:T(8,128)(2,1)S(1)}, bf16[20,1,8,128]{3,2,1,0:T(8,128)(2,1)S(1)}, u32[]{:S(2)}, u32[]{:S(2)}) collective-permute-start(bf16[20,1,8,128]{3,2,1,0:T(8,128)(2,1)S(1)} %get-tuple-element.547), channel_id=1, source_target_pairs={{0,2},{2,4},{4,6},{6,8},{8,10},{10,12},{12,14},{14,16},{16,18},{18... | collective-permute-start | bytes 122888 | tf_op jit(solution)/shard_map/ppermute | solution.py:47
  20.4 1.3 collective-permute-start.1
  22.1 4.2 %collective-permute-done.1 = bf16[20,1,8,128]{3,2,1,0:T(8,128)(2,1)S(1)} collective-permute-done((bf16[20,1,8,128]{3,2,1,0:T(8,128)(2,1)S(1)}, bf16[20,1,8,128]{3,2,1,0:T(8,128)(2,1)S(1)}, u32[]{:S(2)}, u32[]{:S(2)}) %collective-permute-start.1) | collective-permute-done | bytes 40992 | tf_op jit(solution)/shard_map/ppermute | solution.py:49
  26.3 1.0 pad_maximum_fusion.9
  27.4 3.4 %collective-permute-start.2 = (bf16[20,4,1,128]{3,2,1,0:T(2,128)(2,1)S(1)}, bf16[20,4,1,128]{3,2,1,0:T(2,128)(2,1)S(1)}, u32[]{:S(2)}, u32[]{:S(2)}) collective-permute-start(bf16[20,4,1,128]{3,2,1,0:T(2,128)(2,1)S(1)} %get-tuple-element.545), channel_id=1, source_target_pairs={{0,1},{2,3},{4,5},{6,7},{8,9},{10,11},{12,13},{14,15},{16,17},{18,... | collective-permute-start | bytes 61448 | tf_op jit(solution)/shard_map/ppermute | solution.py:47
  30.8 1.3 collective-permute-start.3
  32.4 4.2 %collective-permute-done.3 = bf16[20,4,1,128]{3,2,1,0:T(2,128)(2,1)S(1)} collective-permute-done((bf16[20,4,1,128]{3,2,1,0:T(2,128)(2,1)S(1)}, bf16[20,4,1,128]{3,2,1,0:T(2,128)(2,1)S(1)}, u32[]{:S(2)}, u32[]{:S(2)}) %collective-permute-start.3) | collective-permute-done | bytes 20512 | tf_op jit(solution)/shard_map/ppermute | solution.py:49
  36.7 1.5 fusion.249
  38.9 2.0 conditional.9
  39.6 1.0 gather_fusion
  40.9 5.3 %all_gather.3 = f32[16,6,128]{2,1,0:T(8,128)S(1)} all-gather(f32[4,6,128]{2,1,0:T(8,128)S(1)} %copy.69), channel_id=1, replica_groups=mesh['group'=4,'gx'=4,'gy'=2] {'group'}, dimensions={0}, use_global_device_ids=true | all-gather | bytes 61440 | tf_op jit(solution)/shard_map/all_gather | solution.py:309
  46.2 1.2 conditional.10
  46.2 1.1 broadcast.1066
  47.7 3.4 %collective-permute-start.4 = (f32[4,1,4,128]{3,0,2,1:T(4,128)S(1)}, f32[4,1,4,128]{3,0,2,1:T(4,128)S(1)}, u32[]{:S(2)}, u32[]{:S(2)}) collective-permute-start(f32[4,1,4,128]{3,0,2,1:T(4,128)S(1)} %get-tuple-element.555), channel_id=1, source_target_pairs={{0,2},{2,4},{4,6},{1,3},{3,5},{5,7},{8,10},{10,12},{12,14},{9,11},... | collective-permute-start | bytes 24584 | tf_op jit(solution)/shard_map/ppermute | solution.py:47
  51.2 1.3 collective-permute-start.5
  52.5 4.2 %collective-permute-done.5 = f32[4,1,4,128]{3,0,2,1:T(4,128)S(1)} collective-permute-done((f32[4,1,4,128]{3,0,2,1:T(4,128)S(1)}, f32[4,1,4,128]{3,0,2,1:T(4,128)S(1)}, u32[]{:S(2)}, u32[]{:S(2)}) %collective-permute-start.5) | collective-permute-done | bytes 8224 | tf_op jit(solution)/shard_map/ppermute | solution.py:49
  56.8 1.6 collective-permute-start.6
  58.4 1.3 collective-permute-start.7
  59.7 0.9 multiply_reduce_fusion
  60.5 3.4 %collective-permute-done.7 = f32[4,6,1,128]{3,0,2,1:T(4,128)S(1)} collective-permute-done((f32[4,6,1,128]{3,0,2,1:T(4,128)S(1)}, f32[4,6,1,128]{3,0,2,1:T(4,128)S(1)}, u32[]{:S(2)}, u32[]{:S(2)}) %collective-permute-start.7) | collective-permute-done | bytes 12320 | tf_op jit(solution)/shard_map/ppermute | solution.py:49
  65.0 63.7 %all-reduce.9 = (f32[]{:T(128)}, f32[]{:T(128)}) all-reduce(f32[]{:T(128)} %multiply_reduce_fusion, f32[]{:T(128)} %multiply_reduce_fusion.1), channel_id=1, replica_groups=mesh['group'=4,'gx'=4,'gy'=2] {'group','gx','gy'}, use_global_device_ids=true, to_apply=%region_11.12 | all-reduce | flops 2 | bytes 16 | tf_op jit(solution)/shard_map/psum | solution.py:219
  130.1 2.3 collective-permute-start.8
  132.4 1.3 collective-permute-start.9
  133.8 4.2 %collective-permute-done.9 = f32[4,1,4,128]{3,2,1,0:T(4,128)S(1)} collective-permute-done((f32[4,1,4,128]{3,2,1,0:T(4,128)S(1)}, f32[4,1,4,128]{3,2,1,0:T(4,128)S(1)}, u32[]{:S(2)}, u32[]{:S(2)}) %collective-permute-start.9) | collective-permute-done | bytes 8224 | tf_op jit(solution)/shard_map/ppermute | solution.py:49
  138.0 4.2 %collective-permute-start.10 = (f32[4,6,1,128]{3,2,1,0:T(1,128)S(1)}, f32[4,6,1,128]{3,2,1,0:T(1,128)S(1)}, u32[]{:S(2)}, u32[]{:S(2)}) collective-permute-start(f32[4,6,1,128]{3,2,1,0:T(1,128)S(1)} %get-tuple-element.553), channel_id=1, source_target_pairs={{0,1},{2,3},{4,5},{6,7},{8,9},{10,11},{12,13},{14,15},{16,17},{18,... | collective-permute-start | bytes 36872 | tf_op jit(solution)/shard_map/ppermute | solution.py:47
  142.2 1.3 collective-permute-start.11
  143.6 4.2 %collective-permute-done.11 = f32[4,6,1,128]{3,2,1,0:T(1,128)S(1)} collective-permute-done((f32[4,6,1,128]{3,2,1,0:T(1,128)S(1)}, f32[4,6,1,128]{3,2,1,0:T(1,128)S(1)}, u32[]{:S(2)}, u32[]{:S(2)}) %collective-permute-start.11) | collective-permute-done | bytes 12320 | tf_op jit(solution)/shard_map/ppermute | solution.py:49
  148.7 51.6 %all-reduce.8 = (f32[]{:T(128)}, f32[]{:T(128)}) all-reduce(f32[]{:T(128)} %get-tuple-element.478, f32[]{:T(128)} %get-tuple-element.477), channel_id=1, replica_groups=mesh['group'=4,'gx'=4,'gy'=2] {'group','gx','gy'}, use_global_device_ids=true, to_apply=%region_17.18 | all-reduce | flops 2 | bytes 16 | tf_op jit(solution)/shard_map/psum | solution.py:219
  204.9 2.5 collective-permute-start.12
  207.4 1.3 collective-permute-start.13
  208.7 4.2 %collective-permute-done.13 = f32[4,1,4,128]{3,2,1,0:T(4,128)S(1)} collective-permute-done((f32[4,1,4,128]{3,2,1,0:T(4,128)S(1)}, f32[4,1,4,128]{3,2,1,0:T(4,128)S(1)}, u32[]{:S(2)}, u32[]{:S(2)}) %collective-permute-start.13) | collective-permute-done | bytes 8224 | tf_op jit(solution)/shard_map/ppermute | solution.py:49
  213.0 4.2 %collective-permute-start.14 = (f32[4,6,1,128]{3,2,1,0:T(1,128)S(1)}, f32[4,6,1,128]{3,2,1,0:T(1,128)S(1)}, u32[]{:S(2)}, u32[]{:S(2)}) collective-permute-start(f32[4,6,1,128]{3,2,1,0:T(1,128)S(1)} %get-tuple-element.551), channel_id=1, source_target_pairs={{0,1},{2,3},{4,5},{6,7},{8,9},{10,11},{12,13},{14,15},{16,17},{18,... | collective-permute-start | bytes 36872 | tf_op jit(solution)/shard_map/ppermute | solution.py:47
  217.2 1.3 collective-permute-start.15
  218.5 4.2 %collective-permute-done.15 = f32[4,6,1,128]{3,2,1,0:T(1,128)S(1)} collective-permute-done((f32[4,6,1,128]{3,2,1,0:T(1,128)S(1)}, f32[4,6,1,128]{3,2,1,0:T(1,128)S(1)}, u32[]{:S(2)}, u32[]{:S(2)}) %collective-permute-start.15) | collective-permute-done | bytes 12320 | tf_op jit(solution)/shard_map/ppermute | solution.py:49
  223.4 51.6 %all-reduce.7 = (f32[]{:T(128)}, f32[]{:T(128)}) all-reduce(f32[]{:T(128)} %get-tuple-element.476, f32[]{:T(128)} %get-tuple-element.475), channel_id=1, replica_groups=mesh['group'=4,'gx'=4,'gy'=2] {'group','gx','gy'}, use_global_device_ids=true, to_apply=%region_23.24 | all-reduce | flops 2 | bytes 16 | tf_op jit(solution)/shard_map/psum | solution.py:219
  280.3 0.7 constant_dynamic-slice_fusion.2
  281.0 6.1 %collective-permute-start.17 = (f32[4,3,128]{2,1,0:T(4,128)S(1)}, f32[4,3,128]{2,1,0:T(4,128)S(1)}, u32[]{:S(2)}, u32[]{:S(2)}) collective-permute-start(f32[4,3,128]{2,1,0:T(4,128)S(1)} %get-tuple-element.559), channel_id=1, source_target_pairs={{0,16},{8,24},{16,0},{24,8},{1,17},{9,25},{17,1},{25,9},{2,18},{10... | collective-permute-start | bytes 18440 | tf_op jit(solution)/shard_map/ppermute | solution.py:59
  287.1 0.9 collective-permute-done.16
  288.0 0.7 collective-permute-done.17
  288.9 2.5 scatter_custom_fusion.3
  291.4 14.7 %conditional.15 = (bf16[19,2,8,128]{3,2,1,0:T(8,128)(2,1)}) conditional(s32[]{:T(128)} %convert_element_type.59, () %tuple.154, (f32[4,10,130]{2,1,0:T(8,128)S(1)}, f32[19,4,10,130]{3,2,1,0:T(8,128)S(1)}, f32[3,2048]{0,1:T(8,128)S(1)}) %tuple.168), branch_computations={%region_32.33_spmd, %region_33.34_spmd} | conditional | flops 356351 | bytes 1826696 | solution.py:358
  291.4 0.7 slice_bitcast_fusion
  293.2 1.4 constant_dynamic-update-slice_fusion.36
  (111 shorter events, 31.6 us)
Async XLA Ops:
  0.6 31.4 %copy-start.3 = (f32[4,4,128]{2,1,0:T(4,128)S(1)}, f32[4,4,128]{2,1,0:T(4,128)}, u32[]{:S(2)}) copy-start(f32[4,4,128]{2,1,0:T(4,128)} %param.78) | copy-start | bytes 24580
  0.6 31.4 %copy-start.4 = (s32[4,4,128]{2,1,0:T(4,128)S(1)}, s32[4,4,128]{2,1,0:T(4,128)}, u32[]{:S(2)}) copy-start(s32[4,4,128]{2,1,0:T(4,128)} %param.79) | copy-start | bytes 24580
  15.5 6.6 %collective-permute-start = (bf16[20,1,8,128]{3,2,1,0:T(8,128)(2,1)S(1)}, bf16[20,1,8,128]{3,2,1,0:T(8,128)(2,1)S(1)}, u32[]{:S(2)}, u32[]{:S(2)}) collective-permute-start(bf16[20,1,8,128]{3,2,1,0:T(8,128)(2,1)S(1)} %get-tuple-element.547), channel_id=1, source_target_pairs={{0,2},{2,4},{4,6},{6,8},{8,10},{10,12},{12,14},{14,16},{16,18},{18... | collective-permute-start | bytes 122888 | tf_op jit(solution)/shard_map/ppermute | solution.py:47
  20.4 5.9 %collective-permute-start.1 = (bf16[20,1,8,128]{3,2,1,0:T(8,128)(2,1)S(1)}, bf16[20,1,8,128]{3,2,1,0:T(8,128)(2,1)S(1)}, u32[]{:S(2)}, u32[]{:S(2)}) collective-permute-start(bf16[20,1,8,128]{3,2,1,0:T(8,128)(2,1)S(1)} %get-tuple-element.548), channel_id=1, source_target_pairs={{2,0},{4,2},{6,4},{8,6},{10,8},{12,10},{14,12},{16,14},{18,16},{20... | collective-permute-start | bytes 122888 | tf_op jit(solution)/shard_map/ppermute | solution.py:49
  27.4 5.1 %collective-permute-start.2 = (bf16[20,4,1,128]{3,2,1,0:T(2,128)(2,1)S(1)}, bf16[20,4,1,128]{3,2,1,0:T(2,128)(2,1)S(1)}, u32[]{:S(2)}, u32[]{:S(2)}) collective-permute-start(bf16[20,4,1,128]{3,2,1,0:T(2,128)(2,1)S(1)} %get-tuple-element.545), channel_id=1, source_target_pairs={{0,1},{2,3},{4,5},{6,7},{8,9},{10,11},{12,13},{14,15},{16,17},{18,... | collective-permute-start | bytes 61448 | tf_op jit(solution)/shard_map/ppermute | solution.py:47
  30.8 5.9 %collective-permute-start.3 = (bf16[20,4,1,128]{3,2,1,0:T(2,128)(2,1)S(1)}, bf16[20,4,1,128]{3,2,1,0:T(2,128)(2,1)S(1)}, u32[]{:S(2)}, u32[]{:S(2)}) collective-permute-start(bf16[20,4,1,128]{3,2,1,0:T(2,128)(2,1)S(1)} %get-tuple-element.546), channel_id=1, source_target_pairs={{1,0},{3,2},{5,4},{7,6},{9,8},{11,10},{13,12},{15,14},{17,16},{19,... | collective-permute-start | bytes 61448 | tf_op jit(solution)/shard_map/ppermute | solution.py:49
  38.2 0.7 copy-start.2
  38.3 7.8 %copy-start.1 = (f32[3,4,4,128]{3,2,1,0:T(4,128)S(1)}, f32[3,4,4,128]{3,2,1,0:T(4,128)}, u32[]{:S(2)}) copy-start(f32[3,4,4,128]{3,2,1,0:T(4,128)} %param.77) | copy-start | bytes 73732
  38.3 7.8 %copy-start.5 = (s32[1,1,256]{2,1,0:T(1,128)S(1)}, s32[1,1,256]{2,1,0:T(1,128)}, u32[]{:S(2)}) copy-start(s32[1,1,256]{2,1,0:T(1,128)} %param.81) | copy-start | bytes 3076
  38.4 7.8 %copy-start.6 = (f32[3,1,1,256]{3,2,1,0:T(1,128)S(1)}, f32[3,1,1,256]{3,2,1,0:T(1,128)}, u32[]{:S(2)}) copy-start(f32[3,1,1,256]{3,2,1,0:T(1,128)} %param.82) | copy-start | bytes 9220
  38.4 7.8 %copy-start.7 = (s32[1,1,2,8]{3,2,1,0:T(2,128)S(1)}, s32[1,1,2,8]{3,2,1,0:T(2,128)}, u32[]{:S(2)}) copy-start(s32[1,1,2,8]{3,2,1,0:T(2,128)} %param.83) | copy-start | bytes 196
  47.4 16.6 %copy-start = (f32[24,24]{1,0:T(8,128)S(1)}, f32[24,24]{1,0:T(8,128)}, u32[]{:S(2)}) copy-start(f32[24,24]{1,0:T(8,128)} %param.80) | copy-start | bytes 6916
  47.7 4.8 %collective-permute-start.4 = (f32[4,1,4,128]{3,0,2,1:T(4,128)S(1)}, f32[4,1,4,128]{3,0,2,1:T(4,128)S(1)}, u32[]{:S(2)}, u32[]{:S(2)}) collective-permute-start(f32[4,1,4,128]{3,0,2,1:T(4,128)S(1)} %get-tuple-element.555), channel_id=1, source_target_pairs={{0,2},{2,4},{4,6},{1,3},{3,5},{5,7},{8,10},{10,12},{12,14},{9,11},... | collective-permute-start | bytes 24584 | tf_op jit(solution)/shard_map/ppermute | solution.py:47
  51.2 5.5 %collective-permute-start.5 = (f32[4,1,4,128]{3,0,2,1:T(4,128)S(1)}, f32[4,1,4,128]{3,0,2,1:T(4,128)S(1)}, u32[]{:S(2)}, u32[]{:S(2)}) collective-permute-start(f32[4,1,4,128]{3,0,2,1:T(4,128)S(1)} %get-tuple-element.556), channel_id=1, source_target_pairs={{2,0},{4,2},{6,4},{3,1},{5,3},{7,5},{10,8},{12,10},{14,12},{11,9},... | collective-permute-start | bytes 24584 | tf_op jit(solution)/shard_map/ppermute | solution.py:49
  56.8 3.8 %collective-permute-start.6 = (f32[4,6,1,128]{3,0,2,1:T(4,128)S(1)}, f32[4,6,1,128]{3,0,2,1:T(4,128)S(1)}, u32[]{:S(2)}, u32[]{:S(2)}) collective-permute-start(f32[4,6,1,128]{3,0,2,1:T(4,128)S(1)} %get-tuple-element.549), channel_id=1, source_target_pairs={{0,1},{2,3},{4,5},{6,7},{8,9},{10,11},{12,13},{14,15},{16,17},{18,... | collective-permute-start | bytes 36872 | tf_op jit(solution)/shard_map/ppermute | solution.py:47
  58.4 5.6 %collective-permute-start.7 = (f32[4,6,1,128]{3,0,2,1:T(4,128)S(1)}, f32[4,6,1,128]{3,0,2,1:T(4,128)S(1)}, u32[]{:S(2)}, u32[]{:S(2)}) collective-permute-start(f32[4,6,1,128]{3,0,2,1:T(4,128)S(1)} %get-tuple-element.550), channel_id=1, source_target_pairs={{1,0},{3,2},{5,4},{7,6},{9,8},{11,10},{13,12},{15,14},{17,16},{19,... | collective-permute-start | bytes 36872 | tf_op jit(solution)/shard_map/ppermute | solution.py:49
  130.1 3.7 %collective-permute-start.8 = (f32[4,1,4,128]{3,2,1,0:T(4,128)S(1)}, f32[4,1,4,128]{3,2,1,0:T(4,128)S(1)}, u32[]{:S(2)}, u32[]{:S(2)}) collective-permute-start(f32[4,1,4,128]{3,2,1,0:T(4,128)S(1)} %get-tuple-element.562), channel_id=1, source_target_pairs={{0,2},{2,4},{4,6},{1,3},{3,5},{5,7},{8,10},{10,12},{12,14},{9,11},... | collective-permute-start | bytes 24584 | tf_op jit(solution)/shard_map/ppermute | solution.py:47
  132.4 5.5 %collective-permute-start.9 = (f32[4,1,4,128]{3,2,1,0:T(4,128)S(1)}, f32[4,1,4,128]{3,2,1,0:T(4,128)S(1)}, u32[]{:S(2)}, u32[]{:S(2)}) collective-permute-start(f32[4,1,4,128]{3,2,1,0:T(4,128)S(1)} %get-tuple-element.563), channel_id=1, source_target_pairs={{2,0},{4,2},{6,4},{3,1},{5,3},{7,5},{10,8},{12,10},{14,12},{11,9},... | collective-permute-start | bytes 24584 | tf_op jit(solution)/shard_map/ppermute | solution.py:49
  138.0 5.6 %collective-permute-start.10 = (f32[4,6,1,128]{3,2,1,0:T(1,128)S(1)}, f32[4,6,1,128]{3,2,1,0:T(1,128)S(1)}, u32[]{:S(2)}, u32[]{:S(2)}) collective-permute-start(f32[4,6,1,128]{3,2,1,0:T(1,128)S(1)} %get-tuple-element.553), channel_id=1, source_target_pairs={{0,1},{2,3},{4,5},{6,7},{8,9},{10,11},{12,13},{14,15},{16,17},{18,... | collective-permute-start | bytes 36872 | tf_op jit(solution)/shard_map/ppermute | solution.py:47
  142.2 5.6 %collective-permute-start.11 = (f32[4,6,1,128]{3,2,1,0:T(1,128)S(1)}, f32[4,6,1,128]{3,2,1,0:T(1,128)S(1)}, u32[]{:S(2)}, u32[]{:S(2)}) collective-permute-start(f32[4,6,1,128]{3,2,1,0:T(1,128)S(1)} %get-tuple-element.554), channel_id=1, source_target_pairs={{1,0},{3,2},{5,4},{7,6},{9,8},{11,10},{13,12},{15,14},{17,16},{19,... | collective-permute-start | bytes 36872 | tf_op jit(solution)/shard_map/ppermute | solution.py:49
  204.9 3.8 %collective-permute-start.12 = (f32[4,1,4,128]{3,2,1,0:T(4,128)S(1)}, f32[4,1,4,128]{3,2,1,0:T(4,128)S(1)}, u32[]{:S(2)}, u32[]{:S(2)}) collective-permute-start(f32[4,1,4,128]{3,2,1,0:T(4,128)S(1)} %get-tuple-element.560), channel_id=1, source_target_pairs={{0,2},{2,4},{4,6},{1,3},{3,5},{5,7},{8,10},{10,12},{12,14},{9,11},... | collective-permute-start | bytes 24584 | tf_op jit(solution)/shard_map/ppermute | solution.py:47
  207.4 5.5 %collective-permute-start.13 = (f32[4,1,4,128]{3,2,1,0:T(4,128)S(1)}, f32[4,1,4,128]{3,2,1,0:T(4,128)S(1)}, u32[]{:S(2)}, u32[]{:S(2)}) collective-permute-start(f32[4,1,4,128]{3,2,1,0:T(4,128)S(1)} %get-tuple-element.561), channel_id=1, source_target_pairs={{2,0},{4,2},{6,4},{3,1},{5,3},{7,5},{10,8},{12,10},{14,12},{11,9},... | collective-permute-start | bytes 24584 | tf_op jit(solution)/shard_map/ppermute | solution.py:49
  213.0 5.6 %collective-permute-start.14 = (f32[4,6,1,128]{3,2,1,0:T(1,128)S(1)}, f32[4,6,1,128]{3,2,1,0:T(1,128)S(1)}, u32[]{:S(2)}, u32[]{:S(2)}) collective-permute-start(f32[4,6,1,128]{3,2,1,0:T(1,128)S(1)} %get-tuple-element.551), channel_id=1, source_target_pairs={{0,1},{2,3},{4,5},{6,7},{8,9},{10,11},{12,13},{14,15},{16,17},{18,... | collective-permute-start | bytes 36872 | tf_op jit(solution)/shard_map/ppermute | solution.py:47
  217.2 5.6 %collective-permute-start.15 = (f32[4,6,1,128]{3,2,1,0:T(1,128)S(1)}, f32[4,6,1,128]{3,2,1,0:T(1,128)S(1)}, u32[]{:S(2)}, u32[]{:S(2)}) collective-permute-start(f32[4,6,1,128]{3,2,1,0:T(1,128)S(1)} %get-tuple-element.552), channel_id=1, source_target_pairs={{1,0},{3,2},{5,4},{7,6},{9,8},{11,10},{13,12},{15,14},{17,16},{19,... | collective-permute-start | bytes 36872 | tf_op jit(solution)/shard_map/ppermute | solution.py:49
  281.0 7.0 %collective-permute-start.16 = (f32[4,3,128]{2,1,0:T(4,128)S(1)}, f32[4,3,128]{2,1,0:T(4,128)S(1)}, u32[]{:S(2)}, u32[]{:S(2)}) collective-permute-start(f32[4,3,128]{2,1,0:T(4,128)S(1)} %get-tuple-element.557), channel_id=1, source_target_pairs={{0,8},{8,16},{16,24},{24,0},{1,9},{9,17},{17,25},{25,1},{2,10},{10... | collective-permute-start | bytes 18440 | tf_op jit(solution)/shard_map/ppermute | solution.py:59
  281.0 7.7 %collective-permute-start.17 = (f32[4,3,128]{2,1,0:T(4,128)S(1)}, f32[4,3,128]{2,1,0:T(4,128)S(1)}, u32[]{:S(2)}, u32[]{:S(2)}) collective-permute-start(f32[4,3,128]{2,1,0:T(4,128)S(1)} %get-tuple-element.559), channel_id=1, source_target_pairs={{0,16},{8,24},{16,0},{24,8},{1,17},{9,25},{17,1},{25,9},{2,18},{10... | collective-permute-start | bytes 18440 | tf_op jit(solution)/shard_map/ppermute | solution.py:59
  287.1 1.6 collective-permute-start.18
where the time goes:
time: 308 us; the launch traced here: 306 us
  blocking collectives  172 us (56%)
  starting transfers between devices  43 us (14%)
  other arithmetic  37.4 us (12%)
  waiting for transfers between devices  35.5 us (12%)
  between operations  10.9 us (4%)
  local copies, waits for them, and re-layouts  6.67 us (2%)
    psum x3, blocking collectives, global_products(): lax.psum((jnp.sum(first_vec * first_vec), jnp.sum(first_vec * second_vec)...  167 us
    ppermute x8, waiting for transfers between devices, padded(): lax.ppermute(head, axis, [((i + 1) % count, i) for i in range(ends)])  32.9 us
    ppermute x8, starting transfers between devices, padded(): lax.ppermute(tail, axis, [(i, (i + 1) % count) for i in range(ends)])  26.6 us
    cond x36, other arithmetic  23.8 us
    ppermute x8, starting transfers between devices, padded(): lax.ppermute(head, axis, [((i + 1) % count, i) for i in range(ends)])  10.3 us
  transfers between devices with their start and end apart: 19, of which 14 were waited for; matrix products, arithmetic and copies ran while one was open for 0% of the time, Pallas kernels for 0%

commit v1 on v0

--- a/solution.py
+++ b/solution.py
@@ -2,6 +2,8 @@
 import jax.numpy as jnp
 from jax import lax
 from jax.sharding import PartitionSpec as P
+from jax.experimental import pallas as pl
+from jax.experimental.pallas import tpu as pltpu
 
 TILE = 128
 ITERS = 3
@@ -202,23 +204,79 @@
     return summed[:, 1 : span_cells + 1, 1 : across_cells + 1, 0:deep_cells]
 
 
-def apply_operator(values, stiffness, is_struct, matrix):
-    stacked = jnp.concatenate([values, stiffness[None]], axis=0)
-    widened = padded(stacked, (("gx", 1), ("gy", 2)), 1)
-
-    def active_side(operands):
-        return mass_shift * operands[2] + element_sum(operands[0], operands[1])
-
-    def quiet_side(operands):
-        return jnp.zeros_like(operands[2])
-
-    return lax.cond(is_struct, active_side, quiet_side, (widened, matrix, values))
-
-
-def global_products(first_vec, second_vec):
-    return lax.psum(
-        (jnp.sum(first_vec * first_vec), jnp.sum(first_vec * second_vec)), ("group", "gx", "gy")
-    )
+def operator_kernel(matrix_ref, values_ref, stiff_ref, out_ref):
+    span_cells, across_cells, deep_cells = stiff_ref.shape
+    across_at = lax.broadcasted_iota(jnp.int32, (across_cells, deep_cells), 0)
+    deep_at = lax.broadcasted_iota(jnp.int32, (across_cells, deep_cells), 1)
+    corners = [(a, b, c) for a in (0, 1) for b in (0, 1) for c in (0, 1)]
+    for component in range(3):
+        out_ref[component, 0:span_cells] = mass_shift * values_ref[component, 0:span_cells]
+        out_ref[component, span_cells] = jnp.zeros((across_cells, deep_cells), jnp.float32)
+
+    def ahead(value, across, deep):
+        if across:
+            value = jnp.where(
+                across_at < across_cells - 1, pltpu.roll(value, across_cells - 1, 0), 0.0
+            )
+        if deep:
+            value = jnp.where(deep_at < deep_cells - 1, pltpu.roll(value, deep_cells - 1, 1), 0.0)
+        return value
+
+    def behind(value, across, deep):
+        if across:
+            value = jnp.where(across_at >= 1, pltpu.roll(value, 1, 0), 0.0)
+        if deep:
+            value = jnp.where(deep_at >= 1, pltpu.roll(value, 1, 1), 0.0)
+        return value
+
+    def element_row(row, carry):
+        gathered = []
+        for a, b, c in corners:
+            for component in range(3):
+                gathered.append(ahead(values_ref[component, row + a], b, c))
+        scale = stiff_ref[row]
+        for corner_id, (a, b, c) in enumerate(corners):
+            for component in range(3):
+                line = 3 * corner_id + component
+                force = matrix_ref[line * 24] * gathered[0]
+                for other in range(1, 24):
+                    force = force + matrix_ref[line * 24 + other] * gathered[other]
+                out_ref[component, row + a] += behind(scale * force, b, c)
+        return carry
+
+    lax.fori_loop(0, span_cells, element_row, 0)
+
+
+def partition_operator(values, stiffness, matrix):
+    span_cells, across_cells, deep_cells = stiffness.shape
+    widened = jnp.pad(values, ((0, 0), (0, 1), (0, 0), (0, 0)))
+    cells = span_cells * across_cells * deep_cells
+    summed = pl.pallas_call(
+        operator_kernel,
+        out_shape=jax.ShapeDtypeStruct(widened.shape, jnp.float32),
+        in_specs=[
+            pl.BlockSpec(memory_space=pltpu.SMEM),
+            pl.BlockSpec(memory_space=pltpu.VMEM),
+            pl.BlockSpec(memory_space=pltpu.VMEM),
+        ],
+        out_specs=pl.BlockSpec(memory_space=pltpu.VMEM),
+        cost_estimate=pl.CostEstimate(
+            flops=2 * 24 * 24 * cells, transcendentals=0, bytes_accessed=28 * cells
+        ),
+    )(matrix.reshape(-1), widened, stiffness)
+    return summed[:, :span_cells]
+
+
+def whole_partition(block):
+    lead = block.shape[:-3]
+    count = len(lead)
+    every = lax.all_gather(block, "gy", axis=count + 1, tiled=True)
+    return lax.all_gather(every, "gx", axis=count, tiled=True)
+
+
+def own_part(whole, rows, cols):
+    start = (0, lax.axis_index("gx") * rows, lax.axis_index("gy") * cols, 0)
+    return lax.dynamic_slice(whole, start, (whole.shape[0], rows, cols, whole.shape[3]))
 
 
 def solve_structure(right_side, operator, products):
@@ -322,12 +380,34 @@
         return (jnp.zeros(weight_shape, jnp.float32), jnp.zeros_like(body_load))
 
     weights, right_side = lax.cond(is_struct, struct_map, struct_quiet, received)
-    stiffness = jnp.where(is_struct, elem_scale * elem_active.astype(jnp.float32), 0.0)
-    solution = solve_structure(
-        right_side,
-        lambda values: apply_operator(values, stiffness, is_struct, elem_matrix),
-        global_products,
-    )
+    stiffness = elem_scale * elem_active.astype(jnp.float32)
+    joined = whole_partition(jnp.concatenate([right_side, stiffness[None]], axis=0))
+    whole_side = joined[0:3]
+    stiffness = joined[3]
+    rows, cols = body_load.shape[1], body_load.shape[2]
+
+    def partition_products(first_vec, second_vec):
+        pair = (jnp.sum(first_vec * first_vec), jnp.sum(first_vec * second_vec))
+        if struct_groups > 1:
+            pair = lax.psum(tuple(jnp.where(is_struct, x, 0.0) for x in pair), "group")
+        return pair
+
+    def partition_solve(operands):
+        side, stiff, matrix = operands
+        return solve_structure(
+            side, lambda values: partition_operator(values, stiff, matrix), partition_products
+        )
+
+    if struct_groups > 1:
+        whole_solution = partition_solve((whole_side, stiffness, elem_matrix))
+    else:
+        whole_solution = lax.cond(
+            is_struct,
+            partition_solve,
+            lambda operands: jnp.zeros_like(operands[0]),
+            (whole_side, stiffness, elem_matrix),
+        )
+    solution = jnp.where(is_struct, own_part(whole_solution, rows, cols), 0.0)
     tile_slots = received.shape[0]
 
     def struct_back(operands):

time: 308 us -> 144 us (0.47)
  blocking collectives: 172 us -> 24 us
  waiting for transfers between devices: 35.5 us -> 10.8 us
  starting transfers between devices: 43 us -> 65.7 us
  between operations: 10.9 us -> 0.87 us
    psum x3 -> x0, blocking collectives: 167 us -> none  [global_products(): lax.psum((jnp.sum(first_vec * first_vec), jnp.sum(first_vec * second_vec)...]
    ppermute x3, starting transfers between devices: 6.08 us -> 54.8 us  [passed_along(): return lax.ppermute(value, axis, pairs)]
    ppermute x8 -> x2, waiting for transfers between devices: 32.9 us -> 8.48 us  [padded(): lax.ppermute(head, axis, [((i + 1) % count, i) for i in range(ends)])]
    all_gather x0 -> x2, blocking collectives: none -> 18.7 us  [the longest x1 14.1 us: whole_partition(): return lax.all_gather(every, 'gx', axis=count, tiled=True)]
    ppermute x8 -> x2, starting transfers between devices: 26.6 us -> 8.33 us  [padded(): lax.ppermute(tail, axis, [(i, (i + 1) % count) for i in range(ends)])]
    ppermute x8 -> x2, starting transfers between devices: 10.3 us -> 2.58 us  [padded(): lax.ppermute(head, axis, [((i + 1) % count, i) for i in range(ends)])]
  transfers between devices with their start and end apart: 19 -> 7, of which waited for: 14 -> 6; matrix products, arithmetic and copies ran while one was open for 0% -> 0% of each run, Pallas kernels for 0% -> 0%
where the time goes in v1:
time: 144 us; the launch traced here: 142 us
  starting transfers between devices  65.7 us (46%)
  other arithmetic  34.5 us (24%)
  blocking collectives  24 us (17%)
  waiting for transfers between devices  10.8 us (8%)
  local copies, waits for them, and re-layouts  5.92 us (4%)
    ppermute x3, starting transfers between devices, passed_along(): return lax.ppermute(value, axis, pairs)  54.8 us
    cond x36, other arithmetic  23.8 us
    all_gather x1, blocking collectives, whole_partition(): return lax.all_gather(every, 'gx', axis=count, tiled=True)  14.1 us
    ppermute x2, waiting for transfers between devices, padded(): lax.ppermute(head, axis, [((i + 1) % count, i) for i in range(ends)])  8.48 us
    ppermute x2, starting transfers between devices, padded(): lax.ppermute(tail, axis, [(i, (i + 1) % count) for i in range(ends)])  8.33 us
    all_gather x1, blocking collectives, per_device(): received = lax.all_gather(packed, 'group', axis=0, tiled=True)  5.28 us
    all_gather x1, blocking collectives, whole_partition(): every = lax.all_gather(block, 'gy', axis=count + 1, tiled=True)  4.59 us
  transfers between devices with their start and end apart: 7, of which 6 were waited for; matrix products, arithmetic and copies ran while one was open for 0% of the time, Pallas kernels for 0%

profile of v1, /device:TPU:0, one launch (start us, length us, event | category | flops | bytes accessed | tf_op | source)
XLA Modules:
  0.0 141.9 jit_solution(15658858337666743631)
XLA Ops:
  0.7 0.7 fusion.247
  1.4 13.3 %conditional.6 = (bf16[19,2,8,128]{3,2,1,0:T(8,128)(2,1)}) conditional(s32[]{:T(128)} %convert_element_type.57, () %tuple.47, (bf16[19,2,8,128]{3,2,1,0:T(8,128)(2,1)}) %tuple.58), branch_computations={%region_0.1_spmd, %region_1.3_spmd} | conditional | flops 724991 | bytes 1282056 | solution.py:327
  1.4 0.9 convert_element_type.47
  2.3 0.9 convert_reduce_fusion
  3.2 0.6 constant_dynamic-update-slice_fusion.18
  14.7 0.8 fusion.245
  15.5 4.9 %collective-permute-start = (bf16[20,1,8,128]{3,2,1,0:T(8,128)(2,1)S(1)}, bf16[20,1,8,128]{3,2,1,0:T(8,128)(2,1)S(1)}, u32[]{:S(2)}, u32[]{:S(2)}) collective-permute-start(bf16[20,1,8,128]{3,2,1,0:T(8,128)(2,1)S(1)} %get-tuple-element.198), channel_id=1, source_target_pairs={{0,2},{2,4},{4,6},{6,8},{8,10},{10,12},{12,14},{14,16},{16,18},{18... | collective-permute-start | bytes 122888 | tf_op jit(solution)/shard_map/ppermute | solution.py:49
  20.4 1.3 collective-permute-start.1
  22.1 4.2 %collective-permute-done.1 = bf16[20,1,8,128]{3,2,1,0:T(8,128)(2,1)S(1)} collective-permute-done((bf16[20,1,8,128]{3,2,1,0:T(8,128)(2,1)S(1)}, bf16[20,1,8,128]{3,2,1,0:T(8,128)(2,1)S(1)}, u32[]{:S(2)}, u32[]{:S(2)}) %collective-permute-start.1) | collective-permute-done | bytes 40992 | tf_op jit(solution)/shard_map/ppermute | solution.py:51
  26.3 1.0 pad_maximum_fusion.4
  27.4 3.4 %collective-permute-start.2 = (bf16[20,4,1,128]{3,2,1,0:T(2,128)(2,1)S(1)}, bf16[20,4,1,128]{3,2,1,0:T(2,128)(2,1)S(1)}, u32[]{:S(2)}, u32[]{:S(2)}) collective-permute-start(bf16[20,4,1,128]{3,2,1,0:T(2,128)(2,1)S(1)} %get-tuple-element.196), channel_id=1, source_target_pairs={{0,1},{2,3},{4,5},{6,7},{8,9},{10,11},{12,13},{14,15},{16,17},{18,... | collective-permute-start | bytes 61448 | tf_op jit(solution)/shard_map/ppermute | solution.py:49
  30.8 1.3 collective-permute-start.3
  32.4 4.2 %collective-permute-done.3 = bf16[20,4,1,128]{3,2,1,0:T(2,128)(2,1)S(1)} collective-permute-done((bf16[20,4,1,128]{3,2,1,0:T(2,128)(2,1)S(1)}, bf16[20,4,1,128]{3,2,1,0:T(2,128)(2,1)S(1)}, u32[]{:S(2)}, u32[]{:S(2)}) %collective-permute-start.3) | collective-permute-done | bytes 20512 | tf_op jit(solution)/shard_map/ppermute | solution.py:51
  36.7 1.5 %fusion.235 = f32[20,4,10,130]{3,2,1,0:T(8,128)S(1)} fusion(bf16[20,4,1,128]{3,2,1,0:T(2,128)(2,1)S(1)} %collective-permute-done.3, bf16[20,4,1,128]{3,2,1,0:T(2,128)(2,1)S(1)} %collective-permute-done.2, bf16[20,1,8,128]{3,2,1,0:T(8,128)(2,1)S(1)} %collective-permute-done.1, bf16[20,1,8,128]{3,2,1,0:T(8,128)(2,1)S(1)} %collective-permute-done, ...), kind=kLoop, calls=%fused_computation.436 | loop fusion | flops 2184000 | bytes 620800 | tf_op jit(solution)/shard_map/convert_element_type | solution.py:337
  38.9 2.0 %conditional.7 = (f32[4,6,128]{2,0,1:T(4,128)S(1)}) conditional(s32[]{:T(128)} %convert_element_type.57, () %tuple.51, (f32[4,10,130]{2,1,0:T(8,128)S(1)}, f32[19,4,10,130]{3,2,1,0:T(8,128)S(1)}, s32[1,1,512]{2,1,0:T(1,128)S(1)}, s32[]{:T(128)}, s32[]{:T(128)}, /*index=5*/s32[]{:T(128)}) %tuple.125), branch_computations={%region_3.4_spmd, %region_4.5_spmd} | conditional | flops 292868 | bytes 684096 | solution.py:361
  39.6 1.0 gather_fusion
  40.9 5.3 %all_gather.9 = f32[16,6,128]{2,1,0:T(8,128)S(1)} all-gather(f32[4,6,128]{2,1,0:T(8,128)S(1)} %copy.53), channel_id=1, replica_groups=mesh['group'=4,'gx'=4,'gy'=2] {'group'}, dimensions={0}, use_global_device_ids=true | all-gather | bytes 61440 | tf_op jit(solution)/shard_map/all_gather | solution.py:367
  46.2 1.1 conditional.8
  46.2 1.1 broadcast.687
  47.3 4.6 %all_gather.10 = f32[4,4,8,128]{3,1,0,2:T(4,128)S(1)} all-gather(f32[4,4,4,128]{3,1,0,2:T(4,128)S(1)} %pad_maximum_fusion.6), channel_id=1, replica_groups=mesh['group'=4,'gx'=4,'gy'=2] {'gy'}, dimensions={2}, use_global_device_ids=true | all-gather | bytes 98304 | tf_op jit(solution)/shard_map/all_gather | solution.py:273
  51.9 14.1 %all_gather.11 = f32[4,16,8,128]{3,2,0,1:T(8,128)S(1)} all-gather(f32[4,4,8,128]{3,2,0,1:T(8,128)S(1)} %copy.58), channel_id=1, replica_groups=mesh['group'=4,'gx'=4,'gy'=2] {'gx'}, dimensions={1}, use_global_device_ids=true | all-gather | bytes 327680 | tf_op jit(solution)/shard_map/all_gather | solution.py:274
  66.1 0.6 dynamic-slice_select_fusion
  67.3 0.7 constant_dynamic-slice_fusion.2
  68.1 54.8 %collective-permute-start.5 = (f32[4,3,128]{2,1,0:T(4,128)S(1)}, f32[4,3,128]{2,1,0:T(4,128)S(1)}, u32[]{:S(2)}, u32[]{:S(2)}) collective-permute-start(f32[4,3,128]{2,1,0:T(4,128)S(1)} %get-tuple-element.202), channel_id=1, source_target_pairs={{0,16},{8,24},{16,0},{24,8},{1,17},{9,25},{17,1},{25,9},{2,18},{10... | collective-permute-start | bytes 18440 | tf_op jit(solution)/shard_map/ppermute | solution.py:61
  122.9 0.9 collective-permute-done.4
  123.8 0.7 collective-permute-done.5
  124.7 2.5 %scatter_custom_fusion.3 = f32[3,2048]{0,1:T(8,128)S(1)} fusion(s32[512]{0:T(512)S(1)} %bitcast.589, f32[512,3]{1,0:T(8,128)S(1)} %copy.61, f32[]{:T(128)} %constant.188.clone.1), kind=kCustom, calls=%fused_computation.445 | custom fusion | flops 1536 | bytes 24580 | tf_op jit(solution)/shard_map/scatter-add | solution.py:436
  127.2 14.7 %conditional.11 = (bf16[19,2,8,128]{3,2,1,0:T(8,128)(2,1)}) conditional(s32[]{:T(128)} %convert_element_type.57, () %tuple.46, (f32[4,10,130]{2,1,0:T(8,128)S(1)}, f32[19,4,10,130]{3,2,1,0:T(8,128)S(1)}, f32[3,2048]{0,1:T(8,128)S(1)}) %tuple.56), branch_computations={%region_22.23_spmd, %region_23.24_spmd} | conditional | flops 356351 | bytes 1826696 | solution.py:438
  127.2 0.8 slice_bitcast_fusion.1
  128.0 0.7 constant_dynamic-update-slice_fusion.37
  129.0 1.4 %constant_dynamic-update-slice_fusion.36 = bf16[19,2,8,128]{3,2,1,0:T(8,128)(2,1)} fusion(bf16[19,2,8,128]{3,2,1,0:T(8,128)(2,1)} %constant_dynamic-update-slice_fusion.37, f32[2,8,128]{2,1,0:T(8,128)S(1)} %bitcast.554, f32[19,4,10,130]{3,2,1,0:T(8,128)S(1)} %get-tuple-element.85, f32[4,10,130]{2,1,0:T(8,128)} %get-tuple-element.182, ...), kind=kLoop, calls=%fused_computation.213 | loop fusion | flops 16384 | bytes 45056 | tf_op jit(solution)/shard_map/cond
  130.5 0.7 constant_dynamic-update-slice_fusion.35
  131.1 0.7 constant_dynamic-update-slice_fusion.34
  131.8 0.7 constant_dynamic-update-slice_fusion.33
  132.5 0.7 constant_dynamic-update-slice_fusion.32
  133.2 0.7 constant_dynamic-update-slice_fusion.31
  133.8 0.7 constant_dynamic-update-slice_fusion.30
  134.5 0.7 constant_dynamic-update-slice_fusion.29
  135.2 0.7 constant_dynamic-update-slice_fusion.28
  135.8 0.7 constant_dynamic-update-slice_fusion.27
  136.5 0.7 constant_dynamic-update-slice_fusion.26
  137.2 0.7 constant_dynamic-update-slice_fusion.25
  137.9 0.7 constant_dynamic-update-slice_fusion.24
  138.5 0.7 constant_dynamic-update-slice_fusion.23
  139.2 0.7 constant_dynamic-update-slice_fusion.22
  139.9 0.7 constant_dynamic-update-slice_fusion.21
  140.5 0.7 constant_dynamic-update-slice_fusion.20
  141.2 0.7 constant_dynamic-update-slice_fusion.19
  (67 shorter events, 14.9 us)
Async XLA Ops:
  0.6 31.4 %copy-start.4 = (f32[4,4,128]{2,1,0:T(4,128)S(1)}, f32[4,4,128]{2,1,0:T(4,128)}, u32[]{:S(2)}) copy-start(f32[4,4,128]{2,1,0:T(4,128)} %param.26) | copy-start | bytes 24580
  0.6 31.4 %copy-start.5 = (s32[4,4,128]{2,1,0:T(4,128)S(1)}, s32[4,4,128]{2,1,0:T(4,128)}, u32[]{:S(2)}) copy-start(s32[4,4,128]{2,1,0:T(4,128)} %param.27) | copy-start | bytes 24580
  15.5 6.6 %collective-permute-start = (bf16[20,1,8,128]{3,2,1,0:T(8,128)(2,1)S(1)}, bf16[20,1,8,128]{3,2,1,0:T(8,128)(2,1)S(1)}, u32[]{:S(2)}, u32[]{:S(2)}) collective-permute-start(bf16[20,1,8,128]{3,2,1,0:T(8,128)(2,1)S(1)} %get-tuple-element.198), channel_id=1, source_target_pairs={{0,2},{2,4},{4,6},{6,8},{8,10},{10,12},{12,14},{14,16},{16,18},{18... | collective-permute-start | bytes 122888 | tf_op jit(solution)/shard_map/ppermute | solution.py:49
  20.4 5.9 %collective-permute-start.1 = (bf16[20,1,8,128]{3,2,1,0:T(8,128)(2,1)S(1)}, bf16[20,1,8,128]{3,2,1,0:T(8,128)(2,1)S(1)}, u32[]{:S(2)}, u32[]{:S(2)}) collective-permute-start(bf16[20,1,8,128]{3,2,1,0:T(8,128)(2,1)S(1)} %get-tuple-element.199), channel_id=1, source_target_pairs={{2,0},{4,2},{6,4},{8,6},{10,8},{12,10},{14,12},{16,14},{18,16},{20... | collective-permute-start | bytes 122888 | tf_op jit(solution)/shard_map/ppermute | solution.py:51
  27.4 5.1 %collective-permute-start.2 = (bf16[20,4,1,128]{3,2,1,0:T(2,128)(2,1)S(1)}, bf16[20,4,1,128]{3,2,1,0:T(2,128)(2,1)S(1)}, u32[]{:S(2)}, u32[]{:S(2)}) collective-permute-start(bf16[20,4,1,128]{3,2,1,0:T(2,128)(2,1)S(1)} %get-tuple-element.196), channel_id=1, source_target_pairs={{0,1},{2,3},{4,5},{6,7},{8,9},{10,11},{12,13},{14,15},{16,17},{18,... | collective-permute-start | bytes 61448 | tf_op jit(solution)/shard_map/ppermute | solution.py:49
  30.8 5.9 %collective-permute-start.3 = (bf16[20,4,1,128]{3,2,1,0:T(2,128)(2,1)S(1)}, bf16[20,4,1,128]{3,2,1,0:T(2,128)(2,1)S(1)}, u32[]{:S(2)}, u32[]{:S(2)}) collective-permute-start(bf16[20,4,1,128]{3,2,1,0:T(2,128)(2,1)S(1)} %get-tuple-element.197), channel_id=1, source_target_pairs={{1,0},{3,2},{5,4},{7,6},{9,8},{11,10},{13,12},{15,14},{17,16},{19,... | collective-permute-start | bytes 61448 | tf_op jit(solution)/shard_map/ppermute | solution.py:51
  38.2 0.7 copy-start.2
  38.3 7.8 %copy-start.1 = (f32[3,4,4,128]{3,2,1,0:T(4,128)S(1)}, f32[3,4,4,128]{3,2,1,0:T(4,128)}, u32[]{:S(2)}) copy-start(f32[3,4,4,128]{3,2,1,0:T(4,128)} %param.25) | copy-start | bytes 73732
  38.3 7.8 %copy-start.6 = (s32[1,1,256]{2,1,0:T(1,128)S(1)}, s32[1,1,256]{2,1,0:T(1,128)}, u32[]{:S(2)}) copy-start(s32[1,1,256]{2,1,0:T(1,128)} %param.29) | copy-start | bytes 3076
  38.4 7.8 %copy-start.7 = (f32[3,1,1,256]{3,2,1,0:T(1,128)S(1)}, f32[3,1,1,256]{3,2,1,0:T(1,128)}, u32[]{:S(2)}) copy-start(f32[3,1,1,256]{3,2,1,0:T(1,128)} %param.30) | copy-start | bytes 9220
  38.4 7.8 %copy-start.8 = (s32[1,1,2,8]{3,2,1,0:T(2,128)S(1)}, s32[1,1,2,8]{3,2,1,0:T(2,128)}, u32[]{:S(2)}) copy-start(s32[1,1,2,8]{3,2,1,0:T(2,128)} %param.31) | copy-start | bytes 196
  46.2 19.9 %copy-start.3 = (f32[24,24]{1,0:T(8,128)S(1)}, f32[24,24]{1,0:T(8,128)}, u32[]{:S(2)}) copy-start(f32[24,24]{1,0:T(8,128)} %param.28) | copy-start | bytes 6916
  66.0 0.7 copy-start.9
  68.1 55.8 %collective-permute-start.4 = (f32[4,3,128]{2,1,0:T(4,128)S(1)}, f32[4,3,128]{2,1,0:T(4,128)S(1)}, u32[]{:S(2)}, u32[]{:S(2)}) collective-permute-start(f32[4,3,128]{2,1,0:T(4,128)S(1)} %get-tuple-element.200), channel_id=1, source_target_pairs={{0,8},{8,16},{16,24},{24,0},{1,9},{9,17},{17,25},{25,1},{2,10},{10... | collective-permute-start | bytes 18440 | tf_op jit(solution)/shard_map/ppermute | solution.py:61
  68.1 56.4 %collective-permute-start.5 = (f32[4,3,128]{2,1,0:T(4,128)S(1)}, f32[4,3,128]{2,1,0:T(4,128)S(1)}, u32[]{:S(2)}, u32[]{:S(2)}) collective-permute-start(f32[4,3,128]{2,1,0:T(4,128)S(1)} %get-tuple-element.202), channel_id=1, source_target_pairs={{0,16},{8,24},{16,0},{24,8},{1,17},{9,25},{17,1},{25,9},{2,18},{10... | collective-permute-start | bytes 18440 | tf_op jit(solution)/shard_map/ppermute | solution.py:61
  122.9 1.6 %collective-permute-start.6 = (f32[4,3,128]{2,1,0:T(4,128)S(1)}, f32[4,3,128]{2,1,0:T(4,128)S(1)}, u32[]{:S(2)}, u32[]{:S(2)}) collective-permute-start(f32[4,3,128]{2,1,0:T(4,128)S(1)} %get-tuple-element.201), channel_id=1, source_target_pairs={{0,24},{8,0},{16,8},{24,16},{1,25},{9,1},{17,9},{25,17},{2,26},{10... | collective-permute-start | bytes 18440 | tf_op jit(solution)/shard_map/ppermute | solution.py:61

commit v2 on v1

--- a/solution.py
+++ b/solution.py
@@ -1,5 +1,6 @@
 import jax
 import jax.numpy as jnp
+import numpy as np
 from jax import lax
 from jax.sharding import PartitionSpec as P
 from jax.experimental import pallas as pl
@@ -38,21 +39,30 @@
 mass_shift = 0.5
 
 
-def padded(cells, sides, width):
-    for axis, dim in sides:
-        count = lax.axis_size(axis)
-        ends = count - 1
-        head = lax.slice_in_dim(cells, 0, width, axis=dim)
-        tail = lax.slice_in_dim(cells, cells.shape[dim] - width, cells.shape[dim], axis=dim)
-        cells = jnp.concatenate(
-            [
-                lax.ppermute(tail, axis, [(i, (i + 1) % count) for i in range(ends)]),
-                cells,
-                lax.ppermute(head, axis, [((i + 1) % count, i) for i in range(ends)]),
-            ],
-            axis=dim,
-        )
-    return cells
+def halo_exchange(cells):
+    span_devices = lax.axis_size(("group", "gx"))
+    columns = lax.axis_size("gy")
+    rows, cols = cells.shape[1], cells.shape[2]
+    row_pick = {1: slice(rows - 1, rows), 0: slice(0, rows), -1: slice(0, 1)}
+    col_pick = {1: slice(cols - 1, cols), 0: slice(0, cols), -1: slice(0, 1)}
+    received = {}
+    for dr in (-1, 0, 1):
+        for dc in (-1, 0, 1):
+            if dr == 0 and dc == 0:
+                received[(dr, dc)] = cells
+                continue
+            pairs = [
+                (r * columns + c, (r + dr) * columns + c + dc)
+                for r in range(span_devices)
+                for c in range(columns)
+                if 0 <= r + dr < span_devices and 0 <= c + dc < columns
+            ]
+            piece = cells[:, row_pick[dr], col_pick[dc]]
+            received[(dr, dc)] = lax.ppermute(piece, ("group", "gx", "gy"), pairs)
+    bands = [
+        jnp.concatenate([received[(dr, dc)] for dc in (1, 0, -1)], axis=2) for dr in (1, 0, -1)
+    ]
+    return jnp.concatenate(bands, axis=1)
 
 
 def passed_along(value, axis, steps):
@@ -69,76 +79,76 @@
     return summed
 
 
+def per_direction(values):
+    return jnp.asarray(np.array(values, np.float32).reshape(19, 1, 1, 1))
+
+
 def collide(population):
     density = jnp.sum(population, axis=0)
-    momentum = [jnp.zeros_like(density) for component in range(3)]
-    for q in range(19):
-        for component in range(3):
-            if velocity[q][component] != 0:
-                momentum[component] = (
-                    momentum[component] + float(velocity[q][component]) * population[q]
-                )
-    velocity_parts = [entry / density for entry in momentum]
+    velocity_parts = [
+        jnp.sum(per_direction([c[component] for c in velocity]) * population, axis=0) / density
+        for component in range(3)
+    ]
     speed_square = (
         velocity_parts[0] * velocity_parts[0]
         + velocity_parts[1] * velocity_parts[1]
         + velocity_parts[2] * velocity_parts[2]
     )
-    relaxed = []
-    for q in range(19):
-        project = project_onto(velocity_parts, velocity[q])
-        balance = (
-            lattice_weight[q]
-            * density
-            * (1.0 + 3.0 * project + 4.5 * project * project - 1.5 * speed_square)
-        )
-        relaxed.append(population[q] + relax_rate * (balance - population[q]))
-    return jnp.stack(relaxed)
+    project = project_all(velocity_parts)
+    balance = (
+        per_direction(lattice_weight)
+        * density
+        * (1.0 + 3.0 * project + 4.5 * project * project - 1.5 * speed_square)
+    )
+    return population + relax_rate * (balance - population)
+
+
+def project_all(vectors):
+    summed = per_direction([c[0] for c in velocity]) * vectors[0]
+    for component in (1, 2):
+        summed = summed + per_direction([c[component] for c in velocity]) * vectors[component]
+    return summed
+
+
+def upstream_of(values, inner):
+    for axis in range(3):
+        shift = per_direction([c[axis] for c in velocity])
+        pick = {
+            s: lax.slice_in_dim(values, 1 - s, 1 - s + inner[axis], axis=axis + 1)
+            for s in (-1, 0, 1)
+        }
+        values = jnp.where(shift > 0.5, pick[1], jnp.where(shift < -0.5, pick[-1], pick[0]))
+    return values
 
 
 def stream_links(moved, fluid_ext):
-    span_cells = moved.shape[1] - 2
-    across_cells = moved.shape[2] - 2
-    deep_cells = moved.shape[3] - 2
-    upstream, opened, bounce, reflected = ([], [], [], [])
-    for q in range(19):
-        shift_x, shift_y, shift_z = velocity[q]
-        window = (
-            slice(1 - shift_x, 1 - shift_x + span_cells),
-            slice(1 - shift_y, 1 - shift_y + across_cells),
-            slice(1 - shift_z, 1 - shift_z + deep_cells),
-        )
-        upstream.append(moved[q][window])
-        open_up = fluid_ext[window]
-        opened.append(open_up)
-        bounce.append(1.0 - open_up)
-        reflected.append(
-            moved[opposite[q], 1 : span_cells + 1, 1 : across_cells + 1, 1 : deep_cells + 1]
-        )
+    inner = tuple(size - 2 for size in fluid_ext.shape)
+    upstream = upstream_of(moved, inner)
+    opened = upstream_of(jnp.broadcast_to(fluid_ext[None], (19,) + fluid_ext.shape), inner)
+    bounce = 1.0 - opened
+    centre = moved[:, 1 : inner[0] + 1, 1 : inner[1] + 1, 1 : inner[2] + 1]
+    paired = centre[1:].reshape((9, 2) + inner)[:, ::-1].reshape((18,) + inner)
+    reflected = jnp.concatenate([centre[0:1], paired], axis=0)
     return (upstream, opened, bounce, reflected)
 
 
 def wall_force(bounce, reflected):
-    force_parts = [jnp.zeros_like(reflected[0]) for component in range(3)]
-    for q in range(19):
-        for component in range(3):
-            if velocity[q][component] != 0:
-                force_parts[component] = (
-                    force_parts[component]
-                    - 2.0 * float(velocity[q][component]) * bounce[q] * reflected[q]
-                )
-    return jnp.stack(force_parts)
+    carried = bounce * reflected
+    return jnp.stack(
+        [
+            jnp.sum(per_direction([-2.0 * c[component] for c in velocity]) * carried, axis=0)
+            for component in range(3)
+        ]
+    )
 
 
 def stream_all(moved, fluid_ext, wall_speed):
     upstream, opened, bounce, reflected = stream_links(moved, fluid_ext)
     inside = fluid_ext[1:-1, 1:-1, 1:-1]
     speed_list = [wall_speed[0], wall_speed[1], wall_speed[2]]
-    result = []
-    for q in range(19):
-        correction = 6.0 * lattice_weight[q] * project_onto(speed_list, velocity[q])
-        result.append(inside * (opened[q] * upstream[q] + bounce[q] * (reflected[q] + correction)))
-    return jnp.stack(result).astype(jnp.bfloat16)
+    correction = per_direction([6.0 * w for w in lattice_weight]) * project_all(speed_list)
+    result = inside * (opened * upstream + bounce * (reflected + correction))
+    return result.astype(jnp.bfloat16)
 
 
 def basis_weights(received, node_positions, tile_lists):
@@ -324,16 +334,11 @@
     span_cells, across_cells, deep_cells = solid_mask.shape
     cell_count = span_cells * across_cells * deep_cells
     fluid_here = jnp.where(is_fluid, 1.0 - solid_mask.astype(jnp.float32), 0.0)
-    relaxed_pops = lax.cond(
-        is_fluid,
-        lambda pops: collide(pops.astype(jnp.float32)).astype(jnp.bfloat16),
-        lambda pops: jnp.zeros_like(pops),
-        populations,
-    )
+    relaxed_pops = jnp.where(
+        is_fluid, collide(populations.astype(jnp.float32)), 0.0
+    ).astype(jnp.bfloat16)
     marker = fluid_here.astype(jnp.bfloat16)[None]
-    widened = padded(
-        jnp.concatenate([relaxed_pops, marker], axis=0), ((("group", "gx"), 1), ("gy", 2)), 1
-    )
+    widened = halo_exchange(jnp.concatenate([relaxed_pops, marker], axis=0))
     widened = jnp.pad(widened, ((0, 0), (0, 0), (0, 0), (1, 1))).astype(jnp.float32)
     moved = widened[0:19]
     fluid_ext = widened[19]

time: 144 us -> 133 us (0.924)
  other arithmetic: 34.5 us -> 9.1 us
  starting transfers between devices: 65.7 us -> 76.5 us
  blocking collectives: 24 us -> 31.6 us
  waiting for transfers between devices: 10.8 us -> 6.71 us
    cond x36 -> x0, other arithmetic: 23.8 us -> none
    ppermute x4 -> x8, starting transfers between devices: 10.9 us -> 21.4 us  [halo_exchange(): received[dr, dc] = lax.ppermute(piece, ('group', 'gx', 'gy'), pairs)]
    all_gather x1, blocking collectives: 5.28 us -> 13.1 us  [per_device(): received = lax.all_gather(packed, 'group', axis=0, tiled=True)]
    ppermute x4 -> x8, waiting for transfers between devices: 9.13 us -> 3.66 us  [halo_exchange(): received[dr, dc] = lax.ppermute(piece, ('group', 'gx', 'gy'), pairs)]
  transfers between devices with their start and end apart: 7 -> 11, of which waited for: 6 -> 4; matrix products, arithmetic and copies ran while one was open for 0% -> 1% of each run, Pallas kernels for 0% -> 0%
where the time goes in v2:
time: 133 us; the launch traced here: 132 us
  starting transfers between devices  76.5 us (58%)
  blocking collectives  31.6 us (24%)
  other arithmetic  9.1 us (7%)
  waiting for transfers between devices  6.71 us (5%)
  local copies, waits for them, and re-layouts  6.47 us (5%)
    ppermute x3, starting transfers between devices, passed_along(): return lax.ppermute(value, axis, pairs)  55.1 us
    ppermute x8, starting transfers between devices, halo_exchange(): received[dr, dc] = lax.ppermute(piece, ('group', 'gx', 'gy'), pairs)  21.4 us
    all_gather x1, blocking collectives, whole_partition(): return lax.all_gather(every, 'gx', axis=count, tiled=True)  13.9 us
    all_gather x1, blocking collectives, per_device(): received = lax.all_gather(packed, 'group', axis=0, tiled=True)  13.1 us
    all_gather x1, blocking collectives, whole_partition(): every = lax.all_gather(block, 'gy', axis=count + 1, tiled=True)  4.59 us
    ppermute x8, waiting for transfers between devices, halo_exchange(): received[dr, dc] = lax.ppermute(piece, ('group', 'gx', 'gy'), pairs)  3.66 us
    ppermute x3, waiting for transfers between devices, passed_along(): return lax.ppermute(value, axis, pairs)  3.05 us
  transfers between devices with their start and end apart: 11, of which 4 were waited for; matrix products, arithmetic and copies ran while one was open for 1% of the time, Pallas kernels for 0%

profile of v2, /device:TPU:0, one launch (start us, length us, event | category | flops | bytes accessed | tf_op | source)
XLA Modules:
  0.0 131.6 jit_solution(540502713605189117)
XLA Ops:
  0.6 0.7 fusion.57
  1.3 1.0 fusion.43
  2.4 1.1 fusion.48
  3.6 5.9 %collective-permute-start = (bf16[20,1,1,128]{3,2,1,0:T(2,128)(2,1)S(1)}, bf16[20,1,1,128]{3,2,1,0:T(2,128)(2,1)S(1)}, u32[]{:S(2)}, u32[]{:S(2)}) collective-permute-start(bf16[20,1,1,128]{3,2,1,0:T(2,128)(2,1)S(1)} %get-tuple-element.345), channel_id=1, source_target_pairs={{0,3},{2,5},{4,7},{6,9},{8,11},{10,13},{12,15},{14,17},{16,19},{18... | collective-permute-start | bytes 15368 | tf_op jit(solution)/shard_map/ppermute | solution.py:61
  9.4 0.7 collective-permute-start.2
  10.1 0.7 collective-permute-start.5
  10.8 1.3 collective-permute-start.7
  12.1 8.9 %collective-permute-start.1 = (bf16[20,1,8,128]{3,2,1,0:T(8,128)(2,1)S(1)}, bf16[20,1,8,128]{3,2,1,0:T(8,128)(2,1)S(1)}, u32[]{:S(2)}, u32[]{:S(2)}) collective-permute-start(bf16[20,1,8,128]{3,2,1,0:T(8,128)(2,1)S(1)} %get-tuple-element.349), channel_id=1, source_target_pairs={{0,2},{1,3},{2,4},{3,5},{4,6},{5,7},{6,8},{7,9},{8,10},{9,11},{10,... | collective-permute-start | bytes 122888 | tf_op jit(solution)/shard_map/ppermute | solution.py:61
  21.1 1.3 collective-permute-start.6
  22.4 1.4 %collective-permute-start.3 = (bf16[20,2,1,128]{3,2,1,0:T(2,128)(2,1)S(1)}, bf16[20,2,1,128]{3,2,1,0:T(2,128)(2,1)S(1)}, u32[]{:S(2)}, u32[]{:S(2)}) collective-permute-start(bf16[20,2,1,128]{3,2,1,0:T(2,128)(2,1)S(1)} %get-tuple-element.351), channel_id=1, source_target_pairs={{0,1},{2,3},{4,5},{6,7},{8,9},{10,11},{12,13},{14,15},{16,17},{18,... | collective-permute-start | bytes 30728 | tf_op jit(solution)/shard_map/ppermute | solution.py:61
  23.8 1.3 collective-permute-start.4
  25.1 0.7 fusion.56
  25.8 3.6 %collective-permute-done.4 = bf16[20,2,1,128]{3,2,1,0:T(2,128)(2,1)S(1)} collective-permute-done((bf16[20,2,1,128]{3,2,1,0:T(2,128)(2,1)S(1)}, bf16[20,2,1,128]{3,2,1,0:T(2,128)(2,1)S(1)}, u32[]{:S(2)}, u32[]{:S(2)}) %collective-permute-start.4) | collective-permute-done | bytes 10272 | tf_op jit(solution)/shard_map/ppermute | solution.py:61
  29.5 0.6 fusion.33
  30.2 0.1 slice.314
  30.3 0.5 copy-done.3
  30.9 2.6 %conditional.5 = (f32[4,6,128]{2,0,1:T(4,128)S(1)}) conditional(s32[]{:T(128)} %convert_element_type.60, () %tuple.44, (f32[19,1,1,1]{0,3,2,1:T(1,128)S(1)}, f32[19,1,1,1]{0,3,2,1:T(1,128)S(1)}, f32[19,1,1,1]{0,3,2,1:T(1,128)S(1)}, f32[1,4,10,130]{3,2,1,0:T(8,128)S(1)}, f32[19,4,10,130]{3,2,1,0:T(8,128)S(1)}, ...), branch_computations={%region_4.5_spmd, %region_5.9_spmd.clone} | conditional | flops 646950 | bytes 2346576 | solution.py:366
  30.9 0.1 select_select_fusion.2
  31.1 0.1 fusion.10
  31.5 0.1 copy-done.15
  31.6 0.2 multiply_reduce_fusion.7
  31.9 0.4 copy.79
  32.3 1.0 gather_fusion
  33.3 0.1 copy.80
  33.5 13.1 %all_gather.9 = f32[16,6,128]{2,1,0:T(8,128)S(1)} all-gather(f32[4,6,128]{2,1,0:T(8,128)S(1)} %copy.83), channel_id=1, replica_groups=mesh['group'=4,'gx'=4,'gy'=2] {'group'}, dimensions={0}, use_global_device_ids=true | all-gather | bytes 61440 | tf_op jit(solution)/shard_map/all_gather | solution.py:372
  46.6 1.1 conditional.6
  46.6 1.1 broadcast.282
  47.7 4.6 %all_gather.10 = f32[4,4,8,128]{3,1,0,2:T(4,128)S(1)} all-gather(f32[4,4,4,128]{3,1,0,2:T(4,128)S(1)} %pad_maximum_fusion.1), channel_id=1, replica_groups=mesh['group'=4,'gx'=4,'gy'=2] {'gy'}, dimensions={2}, use_global_device_ids=true | all-gather | bytes 98304 | tf_op jit(solution)/shard_map/all_gather | solution.py:283
  52.4 13.9 %all_gather.11 = f32[4,16,8,128]{3,2,0,1:T(8,128)S(1)} all-gather(f32[4,4,8,128]{3,2,0,1:T(8,128)S(1)} %copy.88), channel_id=1, replica_groups=mesh['group'=4,'gx'=4,'gy'=2] {'gx'}, dimensions={1}, use_global_device_ids=true | all-gather | bytes 327680 | tf_op jit(solution)/shard_map/all_gather | solution.py:284
  66.3 0.6 dynamic-slice_select_fusion
  66.9 0.6 conditional.8
  66.9 0.6 broadcast.301
  67.6 0.7 constant_dynamic-slice_fusion.2
  68.3 54.5 %collective-permute-start.10 = (f32[4,3,128]{2,1,0:T(4,128)S(1)}, f32[4,3,128]{2,1,0:T(4,128)S(1)}, u32[]{:S(2)}, u32[]{:S(2)}) collective-permute-start(f32[4,3,128]{2,1,0:T(4,128)S(1)} %get-tuple-element.354), channel_id=1, source_target_pairs={{0,24},{8,0},{16,8},{24,16},{1,25},{9,1},{17,9},{25,17},{2,26},{10... | collective-permute-start | bytes 18440 | tf_op jit(solution)/shard_map/ppermute | solution.py:71
  122.8 0.6 collective-permute-start.9
  123.4 0.7 collective-permute-done.10
  124.2 1.7 %collective-permute-done.8 = f32[4,3,128]{2,1,0:T(4,128)S(1)} collective-permute-done((f32[4,3,128]{2,1,0:T(4,128)S(1)}, f32[4,3,128]{2,1,0:T(4,128)S(1)}, u32[]{:S(2)}, u32[]{:S(2)}) %collective-permute-start.8) | collective-permute-done | bytes 6176 | tf_op jit(solution)/shard_map/ppermute | solution.py:71
  125.9 0.6 collective-permute-done.9
  126.5 0.1 copy.91
  126.7 2.5 %scatter_custom_fusion.3 = f32[3,2048]{0,1:T(8,128)S(1)} fusion(s32[512]{0:T(512)S(1)} %bitcast.168, f32[512,3]{1,0:T(8,128)S(1)} %copy.91, f32[]{:T(128)} %constant.172.clone.1), kind=kCustom, calls=%fused_computation.127 | custom fusion | flops 1536 | bytes 24580 | tf_op jit(solution)/shard_map/scatter-add | solution.py:441
  129.2 1.8 %conditional.9 = (bf16[19,2,8,128]{3,2,1,0:T(8,128)(2,1)S(1)}) conditional(s32[]{:T(128)} %convert_element_type.60, () %tuple.40, (f32[1,4,10,130]{3,2,1,0:T(8,128)S(1)}, f32[19,1,1,1]{0,3,2,1:T(1,128)S(1)}, f32[19,1,1,1]{0,3,2,1:T(1,128)S(1)}, f32[19,1,1,1]{0,3,2,1:T(1,128)S(1)}, f32[19,1,1,1]{0,3,2,1:T(1,128)S(1)}, ...), branch_computations={%region_26.27_spmd, %region_27.28_spmd.clone} | conditional | flops 1056324 | bytes 4268820 | solution.py:443
  129.2 0.1 select_select_fusion.1
  129.4 0.1 fusion.2
  129.6 0.2 select_select_fusion
  129.7 0.1 fusion.1
  130.0 0.3 copy.92
  130.5 0.4 fusion.7
  131.0 0.6 copy-done.1
  (72 shorter events, 1.0 us)
Async XLA Ops:
  3.6 17.5 %collective-permute-start = (bf16[20,1,1,128]{3,2,1,0:T(2,128)(2,1)S(1)}, bf16[20,1,1,128]{3,2,1,0:T(2,128)(2,1)S(1)}, u32[]{:S(2)}, u32[]{:S(2)}) collective-permute-start(bf16[20,1,1,128]{3,2,1,0:T(2,128)(2,1)S(1)} %get-tuple-element.345), channel_id=1, source_target_pairs={{0,3},{2,5},{4,7},{6,9},{8,11},{10,13},{12,15},{14,17},{16,19},{18... | collective-permute-start | bytes 15368 | tf_op jit(solution)/shard_map/ppermute | solution.py:61
  9.4 12.9 %collective-permute-start.2 = (bf16[20,1,1,128]{3,2,1,0:T(2,128)(2,1)S(1)}, bf16[20,1,1,128]{3,2,1,0:T(2,128)(2,1)S(1)}, u32[]{:S(2)}, u32[]{:S(2)}) collective-permute-start(bf16[20,1,1,128]{3,2,1,0:T(2,128)(2,1)S(1)} %get-tuple-element.346), channel_id=1, source_target_pairs={{1,2},{3,4},{5,6},{7,8},{9,10},{11,12},{13,14},{15,16},{17,18},{19... | collective-permute-start | bytes 15368 | tf_op jit(solution)/shard_map/ppermute | solution.py:61
  10.1 13.7 %collective-permute-start.5 = (bf16[20,1,1,128]{3,2,1,0:T(2,128)(2,1)S(1)}, bf16[20,1,1,128]{3,2,1,0:T(2,128)(2,1)S(1)}, u32[]{:S(2)}, u32[]{:S(2)}) collective-permute-start(bf16[20,1,1,128]{3,2,1,0:T(2,128)(2,1)S(1)} %get-tuple-element.347), channel_id=1, source_target_pairs={{2,1},{4,3},{6,5},{8,7},{10,9},{12,11},{14,13},{16,15},{18,17},{20... | collective-permute-start | bytes 15368 | tf_op jit(solution)/shard_map/ppermute | solution.py:61
  10.8 15.0 %collective-permute-start.7 = (bf16[20,1,1,128]{3,2,1,0:T(2,128)(2,1)S(1)}, bf16[20,1,1,128]{3,2,1,0:T(2,128)(2,1)S(1)}, u32[]{:S(2)}, u32[]{:S(2)}) collective-permute-start(bf16[20,1,1,128]{3,2,1,0:T(2,128)(2,1)S(1)} %get-tuple-element.348), channel_id=1, source_target_pairs={{3,0},{5,2},{7,4},{9,6},{11,8},{13,10},{15,12},{17,14},{19,16},{21... | collective-permute-start | bytes 15368 | tf_op jit(solution)/shard_map/ppermute | solution.py:61
  12.1 17.4 %collective-permute-start.1 = (bf16[20,1,8,128]{3,2,1,0:T(8,128)(2,1)S(1)}, bf16[20,1,8,128]{3,2,1,0:T(8,128)(2,1)S(1)}, u32[]{:S(2)}, u32[]{:S(2)}) collective-permute-start(bf16[20,1,8,128]{3,2,1,0:T(8,128)(2,1)S(1)} %get-tuple-element.349), channel_id=1, source_target_pairs={{0,2},{1,3},{2,4},{3,5},{4,6},{5,7},{6,8},{7,9},{8,10},{9,11},{10,... | collective-permute-start | bytes 122888 | tf_op jit(solution)/shard_map/ppermute | solution.py:61
  21.1 8.4 %collective-permute-start.6 = (bf16[20,1,8,128]{3,2,1,0:T(8,128)(2,1)S(1)}, bf16[20,1,8,128]{3,2,1,0:T(8,128)(2,1)S(1)}, u32[]{:S(2)}, u32[]{:S(2)}) collective-permute-start(bf16[20,1,8,128]{3,2,1,0:T(8,128)(2,1)S(1)} %get-tuple-element.350), channel_id=1, source_target_pairs={{2,0},{3,1},{4,2},{5,3},{6,4},{7,5},{8,6},{9,7},{10,8},{11,9},{12,... | collective-permute-start | bytes 122888 | tf_op jit(solution)/shard_map/ppermute | solution.py:61
  22.4 3.5 %collective-permute-start.3 = (bf16[20,2,1,128]{3,2,1,0:T(2,128)(2,1)S(1)}, bf16[20,2,1,128]{3,2,1,0:T(2,128)(2,1)S(1)}, u32[]{:S(2)}, u32[]{:S(2)}) collective-permute-start(bf16[20,2,1,128]{3,2,1,0:T(2,128)(2,1)S(1)} %get-tuple-element.351), channel_id=1, source_target_pairs={{0,1},{2,3},{4,5},{6,7},{8,9},{10,11},{12,13},{14,15},{16,17},{18,... | collective-permute-start | bytes 30728 | tf_op jit(solution)/shard_map/ppermute | solution.py:61
  23.8 5.7 %collective-permute-start.4 = (bf16[20,2,1,128]{3,2,1,0:T(2,128)(2,1)S(1)}, bf16[20,2,1,128]{3,2,1,0:T(2,128)(2,1)S(1)}, u32[]{:S(2)}, u32[]{:S(2)}) collective-permute-start(bf16[20,2,1,128]{3,2,1,0:T(2,128)(2,1)S(1)} %get-tuple-element.352), channel_id=1, source_target_pairs={{1,0},{3,2},{5,4},{7,6},{9,8},{11,10},{13,12},{15,14},{17,16},{19,... | collective-permute-start | bytes 30728 | tf_op jit(solution)/shard_map/ppermute | solution.py:61
  30.1 0.7 copy-start.3
  30.1 0.7 copy-start.5
  30.1 0.7 copy-start.6
  30.2 0.7 copy-start.7
  30.8 15.8 %copy-start.2 = (f32[3,4,4,128]{3,2,1,0:T(4,128)S(1)}, f32[3,4,4,128]{3,2,1,0:T(4,128)}, u32[]{:S(2)}) copy-start(f32[3,4,4,128]{3,2,1,0:T(4,128)} %param.46) | copy-start | bytes 73732
  30.8 15.8 %copy-start.9 = (s32[1,1,256]{2,1,0:T(1,128)S(1)}, s32[1,1,256]{2,1,0:T(1,128)}, u32[]{:S(2)}) copy-start(s32[1,1,256]{2,1,0:T(1,128)} %param.50) | copy-start | bytes 3076
  30.8 15.8 %copy-start.11 = (f32[3,1,1,256]{3,2,1,0:T(1,128)S(1)}, f32[3,1,1,256]{3,2,1,0:T(1,128)}, u32[]{:S(2)}) copy-start(f32[3,1,1,256]{3,2,1,0:T(1,128)} %param.51) | copy-start | bytes 9220
  30.8 15.8 %copy-start.12 = (s32[1,1,2,8]{3,2,1,0:T(2,128)S(1)}, s32[1,1,2,8]{3,2,1,0:T(2,128)}, u32[]{:S(2)}) copy-start(s32[1,1,2,8]{3,2,1,0:T(2,128)} %param.52) | copy-start | bytes 196
  30.9 0.7 copy-start.15
  30.9 0.7 copy-start.16
  30.9 0.7 copy-start.17
  46.6 19.6 %copy-start.4 = (f32[24,24]{1,0:T(8,128)S(1)}, f32[24,24]{1,0:T(8,128)}, u32[]{:S(2)}) copy-start(f32[24,24]{1,0:T(8,128)} %param.49) | copy-start | bytes 6916
  66.2 0.7 copy-start.10
  66.2 0.7 copy-start.13
  67.6 61.6 %copy-start.8 = (f32[19,1,1,1]{0,3,2,1:T(1,128)S(1)}, f32[19,1,1,1]{0,3,2,1:T(1,128)}, u32[]{:S(2)}) copy-start(f32[19,1,1,1]{0,3,2,1:T(1,128)} %constant.191.clone) | copy-start | bytes 232
  68.3 55.9 %collective-permute-start.10 = (f32[4,3,128]{2,1,0:T(4,128)S(1)}, f32[4,3,128]{2,1,0:T(4,128)S(1)}, u32[]{:S(2)}, u32[]{:S(2)}) collective-permute-start(f32[4,3,128]{2,1,0:T(4,128)S(1)} %get-tuple-element.354), channel_id=1, source_target_pairs={{0,24},{8,0},{16,8},{24,16},{1,25},{9,1},{17,9},{25,17},{2,26},{10... | collective-permute-start | bytes 18440 | tf_op jit(solution)/shard_map/ppermute | solution.py:71
  122.8 3.1 %collective-permute-start.8 = (f32[4,3,128]{2,1,0:T(4,128)S(1)}, f32[4,3,128]{2,1,0:T(4,128)S(1)}, u32[]{:S(2)}, u32[]{:S(2)}) collective-permute-start(f32[4,3,128]{2,1,0:T(4,128)S(1)} %get-tuple-element.353), channel_id=1, source_target_pairs={{0,8},{8,16},{16,24},{24,0},{1,9},{9,17},{17,25},{25,1},{2,10},{10... | collective-permute-start | bytes 18440 | tf_op jit(solution)/shard_map/ppermute | solution.py:71
  122.8 3.7 %collective-permute-start.9 = (f32[4,3,128]{2,1,0:T(4,128)S(1)}, f32[4,3,128]{2,1,0:T(4,128)S(1)}, u32[]{:S(2)}, u32[]{:S(2)}) collective-permute-start(f32[4,3,128]{2,1,0:T(4,128)S(1)} %get-tuple-element.355), channel_id=1, source_target_pairs={{0,16},{8,24},{16,0},{24,8},{1,17},{9,25},{17,1},{25,9},{2,18},{10... | collective-permute-start | bytes 18440 | tf_op jit(solution)/shard_map/ppermute | solution.py:71
  129.7 0.8 copy-start.14
  130.9 0.6 copy-start.1

commit v3 on v2

--- a/solution.py
+++ b/solution.py
@@ -214,10 +214,12 @@
     return summed[:, 1 : span_cells + 1, 1 : across_cells + 1, 0:deep_cells]
 
 
-def operator_kernel(matrix_ref, values_ref, stiff_ref, out_ref):
+def apply_rows(matrix_ref, values_ref, stiff_ref, out_ref):
     span_cells, across_cells, deep_cells = stiff_ref.shape
-    across_at = lax.broadcasted_iota(jnp.int32, (across_cells, deep_cells), 0)
-    deep_at = lax.broadcasted_iota(jnp.int32, (across_cells, deep_cells), 1)
+    step = 2 if span_cells % 2 == 0 else 1
+    shape = (step, across_cells, deep_cells)
+    across_at = lax.broadcasted_iota(jnp.int32, shape, 1)
+    deep_at = lax.broadcasted_iota(jnp.int32, shape, 2)
     corners = [(a, b, c) for a in (0, 1) for b in (0, 1) for c in (0, 1)]
     for component in range(3):
         out_ref[component, 0:span_cells] = mass_shift * values_ref[component, 0:span_cells]
@@ -226,35 +228,99 @@
     def ahead(value, across, deep):
         if across:
             value = jnp.where(
-                across_at < across_cells - 1, pltpu.roll(value, across_cells - 1, 0), 0.0
+                across_at < across_cells - 1, pltpu.roll(value, across_cells - 1, 1), 0.0
             )
         if deep:
-            value = jnp.where(deep_at < deep_cells - 1, pltpu.roll(value, deep_cells - 1, 1), 0.0)
+            value = jnp.where(deep_at < deep_cells - 1, pltpu.roll(value, deep_cells - 1, 2), 0.0)
         return value
 
     def behind(value, across, deep):
         if across:
-            value = jnp.where(across_at >= 1, pltpu.roll(value, 1, 0), 0.0)
+            value = jnp.where(across_at >= 1, pltpu.roll(value, 1, 1), 0.0)
         if deep:
-            value = jnp.where(deep_at >= 1, pltpu.roll(value, 1, 1), 0.0)
+            value = jnp.where(deep_at >= 1, pltpu.roll(value, 1, 2), 0.0)
         return value
 
-    def element_row(row, carry):
+    def element_rows(block, carry):
+        row = block * step
         gathered = []
         for a, b, c in corners:
             for component in range(3):
-                gathered.append(ahead(values_ref[component, row + a], b, c))
-        scale = stiff_ref[row]
+                gathered.append(ahead(values_ref[component, pl.ds(row + a, step)], b, c))
+        scale = stiff_ref[pl.ds(row, step)]
         for corner_id, (a, b, c) in enumerate(corners):
             for component in range(3):
                 line = 3 * corner_id + component
                 force = matrix_ref[line * 24] * gathered[0]
                 for other in range(1, 24):
                     force = force + matrix_ref[line * 24 + other] * gathered[other]
-                out_ref[component, row + a] += behind(scale * force, b, c)
+                out_ref[component, pl.ds(row + a, step)] += behind(scale * force, b, c)
         return carry
 
-    lax.fori_loop(0, span_cells, element_row, 0)
+    lax.fori_loop(0, span_cells // step, element_rows, 0)
+
+
+def operator_kernel(matrix_ref, values_ref, stiff_ref, out_ref):
+    apply_rows(matrix_ref, values_ref, stiff_ref, out_ref)
+
+
+def whole_sum(value):
+    value = jnp.sum(value, axis=(0, 1))
+    value = jnp.sum(value, axis=0, keepdims=True)
+    return jnp.sum(value, axis=1, keepdims=True)
+
+
+def solve_kernel(matrix_ref, side_ref, stiff_ref, out_ref, ahead_ref, image_ref, dir_ref, img_ref):
+    span_cells = stiff_ref.shape[0]
+    residual = side_ref[...]
+    ahead_ref[:, 0:span_cells] = residual
+    ahead_ref[:, span_cells : span_cells + 1] = jnp.zeros_like(residual[:, 0:1])
+    apply_rows(matrix_ref, ahead_ref, stiff_ref, image_ref)
+    image_vec = image_ref[:, 0:span_cells]
+    norm_now = whole_sum(residual * residual)
+    step_size = norm_now / whole_sum(residual * image_vec)
+    dir_ref[...] = residual
+    img_ref[...] = image_vec
+    out_ref[...] = jnp.zeros_like(residual)
+    for iteration in range(ITERS):
+        out_ref[...] = out_ref[...] + step_size * dir_ref[...]
+        residual = residual - step_size * img_ref[...]
+        if iteration + 1 < ITERS:
+            ahead_ref[:, 0:span_cells] = residual
+            apply_rows(matrix_ref, ahead_ref, stiff_ref, image_ref)
+            image_vec = image_ref[:, 0:span_cells]
+            norm_next = whole_sum(residual * residual)
+            curvature = whole_sum(residual * image_vec)
+            beta_ratio = norm_next / norm_now
+            step_size = norm_next / (curvature - beta_ratio * norm_next / step_size)
+            dir_ref[...] = residual + beta_ratio * dir_ref[...]
+            img_ref[...] = image_vec + beta_ratio * img_ref[...]
+            norm_now = norm_next
+
+
+def partition_solve_kernel(side, stiffness, matrix):
+    span_cells, across_cells, deep_cells = stiffness.shape
+    cells = span_cells * across_cells * deep_cells
+    wide = (3, span_cells + 1, across_cells, deep_cells)
+    return pl.pallas_call(
+        solve_kernel,
+        out_shape=jax.ShapeDtypeStruct(side.shape, jnp.float32),
+        in_specs=[
+            pl.BlockSpec(memory_space=pltpu.SMEM),
+            pl.BlockSpec(memory_space=pltpu.VMEM),
+            pl.BlockSpec(memory_space=pltpu.VMEM),
+        ],
+        out_specs=pl.BlockSpec(memory_space=pltpu.VMEM),
+        scratch_shapes=[
+            pltpu.VMEM(wide, jnp.float32),
+            pltpu.VMEM(wide, jnp.float32),
+            pltpu.VMEM(side.shape, jnp.float32),
+            pltpu.VMEM(side.shape, jnp.float32),
+        ],
+        cost_estimate=pl.CostEstimate(
+            flops=ITERS * 2 * 24 * 24 * cells, transcendentals=0, bytes_accessed=28 * cells
+        ),
+    )(matrix.reshape(-1), side, stiffness)
 
 
 def partition_operator(values, stiffness, matrix):
@@ -408,7 +474,7 @@
     else:
         whole_solution = lax.cond(
             is_struct,
-            partition_solve,
+            lambda operands: partition_solve_kernel(*operands),
             lambda operands: jnp.zeros_like(operands[0]),
             (whole_side, stiffness, elem_matrix),
         )

time: 133 us -> 109 us (0.82)
  starting transfers between devices: 76.5 us -> 53.3 us
    ppermute x3, starting transfers between devices: 55.1 us -> 32 us  [passed_along(): return lax.ppermute(value, axis, pairs)]
where the time goes in v3:
time: 109 us; the launch traced here: 108 us
  starting transfers between devices  53.3 us (49%)
  blocking collectives  31.6 us (29%)
  other arithmetic  9.1 us (8%)
  waiting for transfers between devices  6.71 us (6%)
  local copies, waits for them, and re-layouts  6.47 us (6%)
    ppermute x3, starting transfers between devices, passed_along(): return lax.ppermute(value, axis, pairs)  32 us
    ppermute x8, starting transfers between devices, halo_exchange(): received[dr, dc] = lax.ppermute(piece, ('group', 'gx', 'gy'), pairs)  21.4 us
    all_gather x1, blocking collectives, whole_partition(): return lax.all_gather(every, 'gx', axis=count, tiled=True)  13.9 us
    all_gather x1, blocking collectives, per_device(): received = lax.all_gather(packed, 'group', axis=0, tiled=True)  13.1 us
    all_gather x1, blocking collectives, whole_partition(): every = lax.all_gather(block, 'gy', axis=count + 1, tiled=True)  4.59 us
    ppermute x8, waiting for transfers between devices, halo_exchange(): received[dr, dc] = lax.ppermute(piece, ('group', 'gx', 'gy'), pairs)  3.66 us
    ppermute x3, waiting for transfers between devices, passed_along(): return lax.ppermute(value, axis, pairs)  3.05 us
    scatter-add x1, other arithmetic, per_device(): jnp.zeros((3, cell_count), jnp.float32).at[:, wall_index].add(speed_parts)  2.51 us
  transfers between devices with their start and end apart: 11, of which 4 were waited for; matrix products, arithmetic and copies ran while one was open for 1% of the time, Pallas kernels for 0%

profile of v3, /device:TPU:0, one launch (start us, length us, event | category | flops | bytes accessed | tf_op | source)
XLA Modules:
  0.0 108.4 jit_solution(8529262098042819326)
XLA Ops:
  0.6 0.7 fusion.56
  1.3 1.0 fusion.42
  2.4 1.1 %fusion.47 = bf16[19,2,8,128]{3,2,1,0:T(8,128)(2,1)S(1)} fusion(bf16[19,2,8,128]{3,2,1,0:T(8,128)(2,1)} %param.43, f32[2,8,128]{2,1,0:T(8,128)S(1)} %get-tuple-element.295, f32[2,8,128]{2,1,0:T(8,128)S(1)} %get-tuple-element.298, f32[19]{0:T(128)} %constant.207, f32[2,8,128]{2,1,0:T(8,128)S(1)} %get-tuple-element.297, f32[19]{0:T(128)} %constant.206, ...), kind=kLoop, calls=%fused_computation.141 | loop fusion | flops 739328 | bytes 196913 | tf_op jit(solution)/shard_map/convert_element_type | solution.py:405
  3.6 5.9 %collective-permute-start = (bf16[20,1,1,128]{3,2,1,0:T(2,128)(2,1)S(1)}, bf16[20,1,1,128]{3,2,1,0:T(2,128)(2,1)S(1)}, u32[]{:S(2)}, u32[]{:S(2)}) collective-permute-start(bf16[20,1,1,128]{3,2,1,0:T(2,128)(2,1)S(1)} %get-tuple-element.343), channel_id=1, source_target_pairs={{0,3},{2,5},{4,7},{6,9},{8,11},{10,13},{12,15},{14,17},{16,19},{18... | collective-permute-start | bytes 15368 | tf_op jit(solution)/shard_map/ppermute | solution.py:61
  9.4 0.7 collective-permute-start.2
  10.1 0.7 collective-permute-start.5
  10.8 1.3 %collective-permute-start.7 = (bf16[20,1,1,128]{3,2,1,0:T(2,128)(2,1)S(1)}, bf16[20,1,1,128]{3,2,1,0:T(2,128)(2,1)S(1)}, u32[]{:S(2)}, u32[]{:S(2)}) collective-permute-start(bf16[20,1,1,128]{3,2,1,0:T(2,128)(2,1)S(1)} %get-tuple-element.346), channel_id=1, source_target_pairs={{3,0},{5,2},{7,4},{9,6},{11,8},{13,10},{15,12},{17,14},{19,16},{21... | collective-permute-start | bytes 15368 | tf_op jit(solution)/shard_map/ppermute | solution.py:61
  12.1 8.9 %collective-permute-start.1 = (bf16[20,1,8,128]{3,2,1,0:T(8,128)(2,1)S(1)}, bf16[20,1,8,128]{3,2,1,0:T(8,128)(2,1)S(1)}, u32[]{:S(2)}, u32[]{:S(2)}) collective-permute-start(bf16[20,1,8,128]{3,2,1,0:T(8,128)(2,1)S(1)} %get-tuple-element.347), channel_id=1, source_target_pairs={{0,2},{1,3},{2,4},{3,5},{4,6},{5,7},{6,8},{7,9},{8,10},{9,11},{10,... | collective-permute-start | bytes 122888 | tf_op jit(solution)/shard_map/ppermute | solution.py:61
  21.1 1.3 %collective-permute-start.6 = (bf16[20,1,8,128]{3,2,1,0:T(8,128)(2,1)S(1)}, bf16[20,1,8,128]{3,2,1,0:T(8,128)(2,1)S(1)}, u32[]{:S(2)}, u32[]{:S(2)}) collective-permute-start(bf16[20,1,8,128]{3,2,1,0:T(8,128)(2,1)S(1)} %get-tuple-element.348), channel_id=1, source_target_pairs={{2,0},{3,1},{4,2},{5,3},{6,4},{7,5},{8,6},{9,7},{10,8},{11,9},{12,... | collective-permute-start | bytes 122888 | tf_op jit(solution)/shard_map/ppermute | solution.py:61
  22.4 1.4 %collective-permute-start.3 = (bf16[20,2,1,128]{3,2,1,0:T(2,128)(2,1)S(1)}, bf16[20,2,1,128]{3,2,1,0:T(2,128)(2,1)S(1)}, u32[]{:S(2)}, u32[]{:S(2)}) collective-permute-start(bf16[20,2,1,128]{3,2,1,0:T(2,128)(2,1)S(1)} %get-tuple-element.349), channel_id=1, source_target_pairs={{0,1},{2,3},{4,5},{6,7},{8,9},{10,11},{12,13},{14,15},{16,17},{18,... | collective-permute-start | bytes 30728 | tf_op jit(solution)/shard_map/ppermute | solution.py:61
  23.8 1.3 %collective-permute-start.4 = (bf16[20,2,1,128]{3,2,1,0:T(2,128)(2,1)S(1)}, bf16[20,2,1,128]{3,2,1,0:T(2,128)(2,1)S(1)}, u32[]{:S(2)}, u32[]{:S(2)}) collective-permute-start(bf16[20,2,1,128]{3,2,1,0:T(2,128)(2,1)S(1)} %get-tuple-element.350), channel_id=1, source_target_pairs={{1,0},{3,2},{5,4},{7,6},{9,8},{11,10},{13,12},{15,14},{17,16},{19,... | collective-permute-start | bytes 30728 | tf_op jit(solution)/shard_map/ppermute | solution.py:61
  25.1 0.7 fusion.55
  25.8 3.6 %collective-permute-done.4 = bf16[20,2,1,128]{3,2,1,0:T(2,128)(2,1)S(1)} collective-permute-done((bf16[20,2,1,128]{3,2,1,0:T(2,128)(2,1)S(1)}, bf16[20,2,1,128]{3,2,1,0:T(2,128)(2,1)S(1)}, u32[]{:S(2)}, u32[]{:S(2)}) %collective-permute-start.4) | collective-permute-done | bytes 10272 | tf_op jit(solution)/shard_map/ppermute | solution.py:61
  29.5 0.6 fusion.32
  30.2 0.1 slice.304
  30.3 0.5 copy-done.2
  30.9 2.6 %conditional.5 = (f32[4,6,128]{2,0,1:T(4,128)S(1)}) conditional(s32[]{:T(128)} %convert_element_type.56, () %tuple.44, (f32[19,1,1,1]{0,3,2,1:T(1,128)S(1)}, f32[19,1,1,1]{0,3,2,1:T(1,128)S(1)}, f32[19,1,1,1]{0,3,2,1:T(1,128)S(1)}, f32[1,4,10,130]{3,2,1,0:T(8,128)S(1)}, f32[19,4,10,130]{3,2,1,0:T(8,128)S(1)}, ...), branch_computations={%region_4.5_spmd, %region_5.9_spmd.clone} | conditional | flops 646950 | bytes 2346576 | solution.py:432
  30.9 0.1 select_select_fusion.2
  31.1 0.1 fusion.9
  31.5 0.1 copy-done.14
  31.6 0.2 multiply_reduce_fusion.2
  31.9 0.4 copy.80
  32.3 1.0 gather_fusion
  33.3 0.1 copy.81
  33.5 13.1 %all_gather.9 = f32[16,6,128]{2,1,0:T(8,128)S(1)} all-gather(f32[4,6,128]{2,1,0:T(8,128)S(1)} %copy.84), channel_id=1, replica_groups=mesh['group'=4,'gx'=4,'gy'=2] {'group'}, dimensions={0}, use_global_device_ids=true | all-gather | bytes 61440 | tf_op jit(solution)/shard_map/all_gather | solution.py:438
  46.6 1.1 %conditional.6 = (f32[2,128,8,128]{3,1,2,0:T(8,128)}, f32[3,4,4,128]{3,1,0,2:T(4,128)S(1)}) conditional(s32[]{:T(128)} %convert_element_type.62, () %tuple.43, (f32[3,1,1,256]{3,2,1,0:T(1,128)S(1)}, s32[1,1,2,8]{3,2,1,0:T(2,128)S(1)}, f32[16,6,128]{2,1,0:T(8,128)S(1)}, s32[256]{0:T(256)S(1)}, f32[3,4,4,128]{3,2,1,0:T(4,128)S(1)}) %tuple.148), branch_computations={%region_9.10_spmd, %region_10.14_spmd} | conditional | flops 15213152 | bytes 2600664 | solution.py:453
  46.6 1.1 %broadcast.282 = f32[2,128,8,128]{3,1,2,0:T(8,128)} broadcast(f32[]{:T(128)} %constant.149.clone), dimensions={} | broadcast | bytes 1048580 | tf_op jit(solution)/shard_map/broadcast.21
  47.8 4.6 %all_gather.10 = f32[4,4,8,128]{3,1,0,2:T(4,128)S(1)} all-gather(f32[4,4,4,128]{3,1,0,2:T(4,128)S(1)} %pad_maximum_fusion.1), channel_id=1, replica_groups=mesh['group'=4,'gx'=4,'gy'=2] {'gy'}, dimensions={2}, use_global_device_ids=true | all-gather | bytes 98304 | tf_op jit(solution)/shard_map/all_gather | solution.py:349
  52.4 13.9 %all_gather.11 = f32[4,16,8,128]{3,2,0,1:T(8,128)S(1)} all-gather(f32[4,4,8,128]{3,2,0,1:T(8,128)S(1)} %copy.89), channel_id=1, replica_groups=mesh['group'=4,'gx'=4,'gy'=2] {'gx'}, dimensions={1}, use_global_device_ids=true | all-gather | bytes 327680 | tf_op jit(solution)/shard_map/all_gather | solution.py:350
  66.3 0.6 dynamic-slice_select_fusion
  66.9 0.6 conditional.8
  66.9 0.6 broadcast.295
  67.6 0.7 constant_dynamic-slice_fusion.2
  68.3 31.4 %collective-permute-start.10 = (f32[4,3,128]{2,1,0:T(4,128)S(1)}, f32[4,3,128]{2,1,0:T(4,128)S(1)}, u32[]{:S(2)}, u32[]{:S(2)}) collective-permute-start(f32[4,3,128]{2,1,0:T(4,128)S(1)} %get-tuple-element.352), channel_id=1, source_target_pairs={{0,24},{8,0},{16,8},{24,16},{1,25},{9,1},{17,9},{25,17},{2,26},{10... | collective-permute-start | bytes 18440 | tf_op jit(solution)/shard_map/ppermute | solution.py:71
  99.7 0.6 collective-permute-start.9
  100.3 0.7 collective-permute-done.10
  101.0 1.7 %collective-permute-done.8 = f32[4,3,128]{2,1,0:T(4,128)S(1)} collective-permute-done((f32[4,3,128]{2,1,0:T(4,128)S(1)}, f32[4,3,128]{2,1,0:T(4,128)S(1)}, u32[]{:S(2)}, u32[]{:S(2)}) %collective-permute-start.8) | collective-permute-done | bytes 6176 | tf_op jit(solution)/shard_map/ppermute | solution.py:71
  102.8 0.6 collective-permute-done.9
  103.4 0.1 copy.93
  103.5 2.5 %scatter_custom_fusion.3 = f32[3,2048]{0,1:T(8,128)S(1)} fusion(s32[512]{0:T(512)S(1)} %bitcast.168, f32[512,3]{1,0:T(8,128)S(1)} %copy.93, f32[]{:T(128)} %constant.168.clone.1), kind=kCustom, calls=%fused_computation.117 | custom fusion | flops 1536 | bytes 24580 | tf_op jit(solution)/shard_map/scatter-add | solution.py:507
  106.0 1.8 %conditional.9 = (bf16[19,2,8,128]{3,2,1,0:T(8,128)(2,1)S(1)}) conditional(s32[]{:T(128)} %convert_element_type.56, () %tuple.40, (f32[1,4,10,130]{3,2,1,0:T(8,128)S(1)}, f32[19,1,1,1]{0,3,2,1:T(1,128)S(1)}, f32[19,1,1,1]{0,3,2,1:T(1,128)S(1)}, f32[19,1,1,1]{0,3,2,1:T(1,128)S(1)}, f32[19,1,1,1]{0,3,2,1:T(1,128)S(1)}, ...), branch_computations={%region_20.21_spmd, %region_21.22_spmd.clone} | conditional | flops 1056324 | bytes 4268820 | solution.py:509
  106.1 0.1 select_select_fusion.1
  106.3 0.1 fusion.1
  106.4 0.2 select_select_fusion
  106.6 0.1 fusion
  106.9 0.3 copy.94
  107.4 0.4 fusion.6
  107.8 0.6 copy-done
  (72 shorter events, 1.0 us)
Async XLA Ops:
  3.6 17.5 %collective-permute-start = (bf16[20,1,1,128]{3,2,1,0:T(2,128)(2,1)S(1)}, bf16[20,1,1,128]{3,2,1,0:T(2,128)(2,1)S(1)}, u32[]{:S(2)}, u32[]{:S(2)}) collective-permute-start(bf16[20,1,1,128]{3,2,1,0:T(2,128)(2,1)S(1)} %get-tuple-element.343), channel_id=1, source_target_pairs={{0,3},{2,5},{4,7},{6,9},{8,11},{10,13},{12,15},{14,17},{16,19},{18... | collective-permute-start | bytes 15368 | tf_op jit(solution)/shard_map/ppermute | solution.py:61
  9.4 12.9 %collective-permute-start.2 = (bf16[20,1,1,128]{3,2,1,0:T(2,128)(2,1)S(1)}, bf16[20,1,1,128]{3,2,1,0:T(2,128)(2,1)S(1)}, u32[]{:S(2)}, u32[]{:S(2)}) collective-permute-start(bf16[20,1,1,128]{3,2,1,0:T(2,128)(2,1)S(1)} %get-tuple-element.344), channel_id=1, source_target_pairs={{1,2},{3,4},{5,6},{7,8},{9,10},{11,12},{13,14},{15,16},{17,18},{19... | collective-permute-start | bytes 15368 | tf_op jit(solution)/shard_map/ppermute | solution.py:61
  10.1 13.7 %collective-permute-start.5 = (bf16[20,1,1,128]{3,2,1,0:T(2,128)(2,1)S(1)}, bf16[20,1,1,128]{3,2,1,0:T(2,128)(2,1)S(1)}, u32[]{:S(2)}, u32[]{:S(2)}) collective-permute-start(bf16[20,1,1,128]{3,2,1,0:T(2,128)(2,1)S(1)} %get-tuple-element.345), channel_id=1, source_target_pairs={{2,1},{4,3},{6,5},{8,7},{10,9},{12,11},{14,13},{16,15},{18,17},{20... | collective-permute-start | bytes 15368 | tf_op jit(solution)/shard_map/ppermute | solution.py:61
  10.8 15.0 %collective-permute-start.7 = (bf16[20,1,1,128]{3,2,1,0:T(2,128)(2,1)S(1)}, bf16[20,1,1,128]{3,2,1,0:T(2,128)(2,1)S(1)}, u32[]{:S(2)}, u32[]{:S(2)}) collective-permute-start(bf16[20,1,1,128]{3,2,1,0:T(2,128)(2,1)S(1)} %get-tuple-element.346), channel_id=1, source_target_pairs={{3,0},{5,2},{7,4},{9,6},{11,8},{13,10},{15,12},{17,14},{19,16},{21... | collective-permute-start | bytes 15368 | tf_op jit(solution)/shard_map/ppermute | solution.py:61
  12.1 17.4 %collective-permute-start.1 = (bf16[20,1,8,128]{3,2,1,0:T(8,128)(2,1)S(1)}, bf16[20,1,8,128]{3,2,1,0:T(8,128)(2,1)S(1)}, u32[]{:S(2)}, u32[]{:S(2)}) collective-permute-start(bf16[20,1,8,128]{3,2,1,0:T(8,128)(2,1)S(1)} %get-tuple-element.347), channel_id=1, source_target_pairs={{0,2},{1,3},{2,4},{3,5},{4,6},{5,7},{6,8},{7,9},{8,10},{9,11},{10,... | collective-permute-start | bytes 122888 | tf_op jit(solution)/shard_map/ppermute | solution.py:61
  21.1 8.4 %collective-permute-start.6 = (bf16[20,1,8,128]{3,2,1,0:T(8,128)(2,1)S(1)}, bf16[20,1,8,128]{3,2,1,0:T(8,128)(2,1)S(1)}, u32[]{:S(2)}, u32[]{:S(2)}) collective-permute-start(bf16[20,1,8,128]{3,2,1,0:T(8,128)(2,1)S(1)} %get-tuple-element.348), channel_id=1, source_target_pairs={{2,0},{3,1},{4,2},{5,3},{6,4},{7,5},{8,6},{9,7},{10,8},{11,9},{12,... | collective-permute-start | bytes 122888 | tf_op jit(solution)/shard_map/ppermute | solution.py:61
  22.4 3.5 %collective-permute-start.3 = (bf16[20,2,1,128]{3,2,1,0:T(2,128)(2,1)S(1)}, bf16[20,2,1,128]{3,2,1,0:T(2,128)(2,1)S(1)}, u32[]{:S(2)}, u32[]{:S(2)}) collective-permute-start(bf16[20,2,1,128]{3,2,1,0:T(2,128)(2,1)S(1)} %get-tuple-element.349), channel_id=1, source_target_pairs={{0,1},{2,3},{4,5},{6,7},{8,9},{10,11},{12,13},{14,15},{16,17},{18,... | collective-permute-start | bytes 30728 | tf_op jit(solution)/shard_map/ppermute | solution.py:61
  23.8 5.7 %collective-permute-start.4 = (bf16[20,2,1,128]{3,2,1,0:T(2,128)(2,1)S(1)}, bf16[20,2,1,128]{3,2,1,0:T(2,128)(2,1)S(1)}, u32[]{:S(2)}, u32[]{:S(2)}) collective-permute-start(bf16[20,2,1,128]{3,2,1,0:T(2,128)(2,1)S(1)} %get-tuple-element.350), channel_id=1, source_target_pairs={{1,0},{3,2},{5,4},{7,6},{9,8},{11,10},{13,12},{15,14},{17,16},{19,... | collective-permute-start | bytes 30728 | tf_op jit(solution)/shard_map/ppermute | solution.py:61
  30.1 0.7 copy-start.2
  30.1 0.7 copy-start.4
  30.1 0.7 copy-start.5
  30.2 0.7 copy-start.6
  30.8 15.8 %copy-start.1 = (f32[3,4,4,128]{3,2,1,0:T(4,128)S(1)}, f32[3,4,4,128]{3,2,1,0:T(4,128)}, u32[]{:S(2)}) copy-start(f32[3,4,4,128]{3,2,1,0:T(4,128)} %param.46) | copy-start | bytes 73732
  30.8 15.8 %copy-start.8 = (s32[1,1,256]{2,1,0:T(1,128)S(1)}, s32[1,1,256]{2,1,0:T(1,128)}, u32[]{:S(2)}) copy-start(s32[1,1,256]{2,1,0:T(1,128)} %param.50) | copy-start | bytes 3076
  30.8 15.8 %copy-start.10 = (f32[3,1,1,256]{3,2,1,0:T(1,128)S(1)}, f32[3,1,1,256]{3,2,1,0:T(1,128)}, u32[]{:S(2)}) copy-start(f32[3,1,1,256]{3,2,1,0:T(1,128)} %param.51) | copy-start | bytes 9220
  30.8 15.8 %copy-start.11 = (s32[1,1,2,8]{3,2,1,0:T(2,128)S(1)}, s32[1,1,2,8]{3,2,1,0:T(2,128)}, u32[]{:S(2)}) copy-start(s32[1,1,2,8]{3,2,1,0:T(2,128)} %param.52) | copy-start | bytes 196
  30.9 0.7 copy-start.14
  30.9 0.7 copy-start.15
  30.9 0.7 copy-start.16
  46.6 19.7 %copy-start.3 = (f32[24,24]{1,0:T(8,128)S(1)}, f32[24,24]{1,0:T(8,128)}, u32[]{:S(2)}) copy-start(f32[24,24]{1,0:T(8,128)} %param.49) | copy-start | bytes 6916
  47.8 19.2 %copy-start.9 = (s32[1,1,256]{2,1,0:T(1,128)S(1)}, s32[1,1,256]{2,1,0:T(1,128)}, u32[]{:S(2)}) copy-start(s32[1,1,256]{2,1,0:T(1,128)} %param.50) | copy-start | bytes 3076
  47.8 19.2 %copy-start.12 = (s32[1,1,2,8]{3,2,1,0:T(2,128)S(1)}, s32[1,1,2,8]{3,2,1,0:T(2,128)}, u32[]{:S(2)}) copy-start(s32[1,1,2,8]{3,2,1,0:T(2,128)} %param.52) | copy-start | bytes 196
  67.6 38.5 %copy-start.7 = (f32[19,1,1,1]{0,3,2,1:T(1,128)S(1)}, f32[19,1,1,1]{0,3,2,1:T(1,128)}, u32[]{:S(2)}) copy-start(f32[19,1,1,1]{0,3,2,1:T(1,128)} %constant.187.clone) | copy-start | bytes 232
  68.3 32.7 %collective-permute-start.10 = (f32[4,3,128]{2,1,0:T(4,128)S(1)}, f32[4,3,128]{2,1,0:T(4,128)S(1)}, u32[]{:S(2)}, u32[]{:S(2)}) collective-permute-start(f32[4,3,128]{2,1,0:T(4,128)S(1)} %get-tuple-element.352), channel_id=1, source_target_pairs={{0,24},{8,0},{16,8},{24,16},{1,25},{9,1},{17,9},{25,17},{2,26},{10... | collective-permute-start | bytes 18440 | tf_op jit(solution)/shard_map/ppermute | solution.py:71
  99.7 3.1 %collective-permute-start.8 = (f32[4,3,128]{2,1,0:T(4,128)S(1)}, f32[4,3,128]{2,1,0:T(4,128)S(1)}, u32[]{:S(2)}, u32[]{:S(2)}) collective-permute-start(f32[4,3,128]{2,1,0:T(4,128)S(1)} %get-tuple-element.351), channel_id=1, source_target_pairs={{0,8},{8,16},{16,24},{24,0},{1,9},{9,17},{17,25},{25,1},{2,10},{10... | collective-permute-start | bytes 18440 | tf_op jit(solution)/shard_map/ppermute | solution.py:71
  99.7 3.7 %collective-permute-start.9 = (f32[4,3,128]{2,1,0:T(4,128)S(1)}, f32[4,3,128]{2,1,0:T(4,128)S(1)}, u32[]{:S(2)}, u32[]{:S(2)}) collective-permute-start(f32[4,3,128]{2,1,0:T(4,128)S(1)} %get-tuple-element.353), channel_id=1, source_target_pairs={{0,16},{8,24},{16,0},{24,8},{1,17},{9,25},{17,1},{25,9},{2,18},{10... | collective-permute-start | bytes 18440 | tf_op jit(solution)/shard_map/ppermute | solution.py:71
  106.6 0.8 copy-start.13
  107.8 0.6 copy-start

commit v4 on v3

--- a/solution.py
+++ b/solution.py
@@ -39,8 +39,7 @@
 mass_shift = 0.5
 
 
-def halo_exchange(cells):
-    span_devices = lax.axis_size(("group", "gx"))
+def halo_exchange(cells, span_devices):
     columns = lax.axis_size("gy")
     rows, cols = cells.shape[1], cells.shape[2]
     row_pick = {1: slice(rows - 1, rows), 0: slice(0, rows), -1: slice(0, 1)}
@@ -130,6 +129,14 @@
     paired = centre[1:].reshape((9, 2) + inner)[:, ::-1].reshape((18,) + inner)
     reflected = jnp.concatenate([centre[0:1], paired], axis=0)
     return (upstream, opened, bounce, reflected)
+
+
+def local_force(relaxed, fluid_ext):
+    inner = relaxed.shape[1:]
+    opened = upstream_of(jnp.broadcast_to(fluid_ext[None], (19,) + fluid_ext.shape), inner)
+    paired = relaxed[1:].reshape((9, 2) + inner)[:, ::-1].reshape((18,) + inner)
+    reflected = jnp.concatenate([relaxed[0:1], paired], axis=0)
+    return wall_force(1.0 - opened, reflected)
 
 
 def wall_force(bounce, reflected):
@@ -403,18 +410,16 @@
     relaxed_pops = jnp.where(
         is_fluid, collide(populations.astype(jnp.float32)), 0.0
     ).astype(jnp.bfloat16)
+    fluid_slabs = fluid_groups * span_devices
     marker = fluid_here.astype(jnp.bfloat16)[None]
-    widened = halo_exchange(jnp.concatenate([relaxed_pops, marker], axis=0))
-    widened = jnp.pad(widened, ((0, 0), (0, 0), (0, 0), (1, 1))).astype(jnp.float32)
-    moved = widened[0:19]
-    fluid_ext = widened[19]
+    fluid_ext = halo_exchange(marker, fluid_slabs)[0]
+    fluid_ext = jnp.pad(fluid_ext, ((0, 0), (0, 0), (1, 1))).astype(jnp.float32)
     wall_index = wall_cells.reshape(-1)
     point_count = wall_index.shape[0]
     tiles_out = point_count // TILE
 
     def fluid_pack(operands):
-        upstream, opened, bounce, reflected = stream_links(operands[0], operands[1])
-        force_parts = wall_force(bounce, reflected).reshape(3, cell_count)
+        force_parts = local_force(operands[0], operands[1]).reshape(3, cell_count)
         picked = force_parts[:, wall_index]
         span_pos = wall_index // (across_cells * deep_cells)
         across_pos = wall_index // deep_cells % across_cells + column_index * across_cells
@@ -433,9 +438,12 @@
         is_fluid,
         fluid_pack,
         lambda operands: jnp.zeros((tiles_out, 6, TILE), jnp.float32),
-        (moved, fluid_ext),
+        (relaxed_pops.astype(jnp.float32), fluid_ext),
     )
     received = lax.all_gather(packed, "group", axis=0, tiled=True)
+    relaxed_pops, received = lax.optimization_barrier((relaxed_pops, received))
+    moved = halo_exchange(relaxed_pops, fluid_slabs)
+    moved = jnp.pad(moved, ((0, 0), (0, 0), (0, 0), (1, 1))).astype(jnp.float32)
     node_index = iface_nodes.reshape(-1)
     node_positions = iface_coords.reshape(3, -1)
     tile_lists = neighbours.reshape(neighbours.shape[2], neighbours.shape[3])
@@ -492,6 +500,7 @@
         lambda operands: jnp.zeros((tile_slots, 3, TILE), jnp.float32),
         (weights, solution),
     )
+    back_terms, moved = lax.optimization_barrier((back_terms, moved))
     per_group = tile_slots // group_count
     route_count = fluid_groups // struct_groups
     sender_slot = jnp.clip(group_index - fluid_groups, 0, struct_groups - 1)

time: 109 us -> 110 us (level)
  blocking collectives: 31.6 us -> 33.5 us
  waiting for transfers between devices: 6.71 us -> 4.88 us
  other arithmetic: 9.1 us -> 10.4 us
    ppermute x8 -> x16, starting transfers between devices: 21.4 us -> 39.3 us  [halo_exchange(): received[dr, dc] = lax.ppermute(piece, ('group', 'gx', 'gy'), pairs)]
    ppermute x3, starting transfers between devices: 32 us -> 14.3 us  [passed_along(): return lax.ppermute(value, axis, pairs)]
    all_gather x1, blocking collectives: 13.1 us -> 6.7 us  [per_device(): received = lax.all_gather(packed, 'group', axis=0, tiled=True)]
    all_gather x1, blocking collectives: 13.9 us -> 19 us  [whole_partition(): return lax.all_gather(every, 'gx', axis=count, tiled=True)]
    all_gather x1, blocking collectives: 4.59 us -> 7.81 us  [whole_partition(): every = lax.all_gather(block, 'gy', axis=count + 1, tiled=True)]
    ppermute x8 -> x16, waiting for transfers between devices: 3.66 us -> 1.41 us  [halo_exchange(): received[dr, dc] = lax.ppermute(piece, ('group', 'gx', 'gy'), pairs)]
    slice x2 -> x8, local copies, waits for them, and re-layouts: 0.13 us -> 1.3 us  [the longest x6 1.29 us: halo_exchange(): piece = cells[:, row_pick[dr], col_pick[dc]]]
  transfers between devices with their start and end apart: 11 -> 19, of which waited for: 4 -> 4; matrix products, arithmetic and copies ran while one was open for 1% -> 4% of each run, Pallas kernels for 0% -> 0%
where the time goes in v4:
time: 110 us
  starting transfers between devices  53.6 us (49%)
  blocking collectives  33.5 us (30%)
  other arithmetic  10.4 us (9%)
  local copies, waits for them, and re-layouts  5.87 us (5%)
  waiting for transfers between devices  4.88 us (4%)
  between operations  1.1 us (1%)
    ppermute x16, starting transfers between devices, halo_exchange(): received[dr, dc] = lax.ppermute(piece, ('group', 'gx', 'gy'), pairs)  39.3 us
    all_gather x1, blocking collectives, whole_partition(): return lax.all_gather(every, 'gx', axis=count, tiled=True)  19 us
    ppermute x3, starting transfers between devices, passed_along(): return lax.ppermute(value, axis, pairs)  14.3 us
    all_gather x1, blocking collectives, whole_partition(): every = lax.all_gather(block, 'gy', axis=count + 1, tiled=True)  7.81 us
    all_gather x1, blocking collectives, per_device(): received = lax.all_gather(packed, 'group', axis=0, tiled=True)  6.7 us
    ppermute x3, waiting for transfers between devices, passed_along(): return lax.ppermute(value, axis, pairs)  3.47 us
    scatter-add x1, other arithmetic, per_device(): jnp.zeros((3, cell_count), jnp.float32).at[:, wall_index].add(speed_parts)  2.51 us
  transfers between devices with their start and end apart: 19, of which 4 were waited for; matrix products, arithmetic and copies ran while one was open for 4% of the time, Pallas kernels for 0%

profile of v4, /device:TPU:0, one launch (start us, length us, event | category | flops | bytes accessed | tf_op | source)
XLA Modules:
  0.0 109.8 jit_solution(14273868737831666477)
XLA Ops:
  0.6 0.7 fusion.49
  1.4 1.3 %collective-permute-start.7 = (bf16[1,1,1,128]{3,2,1,0:T(2,128)(2,1)S(1)}, bf16[1,1,1,128]{3,2,1,0:T(2,128)(2,1)S(1)}, u32[]{:S(2)}, u32[]{:S(2)}) collective-permute-start(bf16[1,1,1,128]{3,2,1,0:T(2,128)(2,1)S(1)} %get-tuple-element.363), channel_id=1, source_target_pairs={{3,0},{5,2},{7,4},{9,6},{11,8},{13,10},{15,12},{17,14},{19,16},{21... | collective-permute-start | bytes 776 | tf_op jit(solution)/shard_map/ppermute | solution.py:60
  2.7 1.3 %collective-permute-start.6 = (bf16[1,1,8,128]{3,2,1,0:T(8,128)(2,1)S(1)}, bf16[1,1,8,128]{3,2,1,0:T(8,128)(2,1)S(1)}, u32[]{:S(2)}, u32[]{:S(2)}) collective-permute-start(bf16[1,1,8,128]{3,2,1,0:T(8,128)(2,1)S(1)} %get-tuple-element.367), channel_id=1, source_target_pairs={{2,0},{3,1},{4,2},{5,3},{6,4},{7,5},{8,6},{9,7},{10,8},{11,9},{12,... | collective-permute-start | bytes 6152 | tf_op jit(solution)/shard_map/ppermute | solution.py:60
  4.0 0.7 collective-permute-start.5
  4.6 0.7 collective-permute-start.2
  5.3 7.5 %collective-permute-start.1 = (bf16[1,1,8,128]{3,2,1,0:T(8,128)(2,1)S(1)}, bf16[1,1,8,128]{3,2,1,0:T(8,128)(2,1)S(1)}, u32[]{:S(2)}, u32[]{:S(2)}) collective-permute-start(bf16[1,1,8,128]{3,2,1,0:T(8,128)(2,1)S(1)} %get-tuple-element.366), channel_id=1, source_target_pairs={{0,2},{1,3},{2,4},{3,5},{4,6},{5,7},{6,8},{7,9},{8,10},{9,11},{10,... | collective-permute-start | bytes 6152 | tf_op jit(solution)/shard_map/ppermute | solution.py:60
  12.9 0.7 fusion.48
  13.6 1.0 fusion.42
  14.7 1.1 %fusion.50 = (f32[19,2,8,128]{3,2,1,0:T(8,128)S(1)}, bf16[19,2,8,128]{3,2,1,0:T(8,128)(2,1)S(1)}) fusion(f32[2,8,128]{2,1,0:T(8,128)S(1)} %get-tuple-element.303, f32[2,8,128]{2,1,0:T(8,128)S(1)} %get-tuple-element.306, f32[19]{0:T(128)} %constant.209, f32[2,8,128]{2,1,0:T(8,128)S(1)} %get-tuple-element.305, f32[19]{0:T(128)} %constant.208, ...), kind=kLoop, calls=%fused_computation.143 | loop fusion | flops 778240 | bytes 352561 | tf_op jit(solution)/shard_map/convert_element_type | solution.py:441
  15.8 1.3 %collective-permute-start.4 = (bf16[1,2,1,128]{3,2,1,0:T(2,128)(2,1)S(1)}, bf16[1,2,1,128]{3,2,1,0:T(2,128)(2,1)S(1)}, u32[]{:S(2)}, u32[]{:S(2)}) collective-permute-start(bf16[1,2,1,128]{3,2,1,0:T(2,128)(2,1)S(1)} %get-tuple-element.369), channel_id=1, source_target_pairs={{1,0},{3,2},{5,4},{7,6},{9,8},{11,10},{13,12},{15,14},{17,16},{19,... | collective-permute-start | bytes 1544 | tf_op jit(solution)/shard_map/ppermute | solution.py:60
  17.1 6.8 %collective-permute-start.3 = (bf16[1,2,1,128]{3,2,1,0:T(2,128)(2,1)S(1)}, bf16[1,2,1,128]{3,2,1,0:T(2,128)(2,1)S(1)}, u32[]{:S(2)}, u32[]{:S(2)}) collective-permute-start(bf16[1,2,1,128]{3,2,1,0:T(2,128)(2,1)S(1)} %get-tuple-element.368), channel_id=1, source_target_pairs={{0,1},{2,3},{4,5},{6,7},{8,9},{10,11},{12,13},{14,15},{16,17},{18,... | collective-permute-start | bytes 1544 | tf_op jit(solution)/shard_map/ppermute | solution.py:60
  24.0 3.3 %collective-permute-start = (bf16[1,1,1,128]{3,2,1,0:T(2,128)(2,1)S(1)}, bf16[1,1,1,128]{3,2,1,0:T(2,128)(2,1)S(1)}, u32[]{:S(2)}, u32[]{:S(2)}) collective-permute-start(bf16[1,1,1,128]{3,2,1,0:T(2,128)(2,1)S(1)} %get-tuple-element.362), channel_id=1, source_target_pairs={{0,3},{2,5},{4,7},{6,9},{8,11},{10,13},{12,15},{14,17},{16,19},{18... | collective-permute-start | bytes 776 | tf_op jit(solution)/shard_map/ppermute | solution.py:60
  27.3 1.3 %collective-permute-done = bf16[1,1,1,128]{3,2,1,0:T(2,128)(2,1)S(1)} collective-permute-done((bf16[1,1,1,128]{3,2,1,0:T(2,128)(2,1)S(1)}, bf16[1,1,1,128]{3,2,1,0:T(2,128)(2,1)S(1)}, u32[]{:S(2)}, u32[]{:S(2)}) %collective-permute-start) | collective-permute-done | bytes 288 | tf_op jit(solution)/shard_map/ppermute | solution.py:60
  28.8 3.8 %conditional.5 = (f32[4,6,128]{2,0,1:T(4,128)S(1)}) conditional(s32[]{:T(128)} %convert_element_type.64, () %tuple.46, (f32[19,1,1,1]{0,3,2,1:T(1,128)}, f32[19,1,1,1]{0,3,2,1:T(1,128)}, f32[19,1,1,1]{0,3,2,1:T(1,128)}, f32[4,10,130]{2,1,0:T(8,128)S(1)}, f32[19,2,8,128]{3,2,1,0:T(8,128)S(1)}, /*index=5*/s32[1,1,512]{2,1,0:T(1,128)}, s32[]{:T(128)}, ...), branch_computations={%region_4.5_spmd, %region_5.9_spmd.clone} | conditional | flops 646950 | bytes 2355128 | solution.py:437
  28.8 0.7 fusion.15
  29.6 0.7 compare_bitcast_fusion.15
  30.7 0.3 multiply_reduce_fusion.2
  31.0 0.4 copy.80
  31.4 1.0 gather_fusion
  32.5 6.7 %all_gather.9 = f32[16,6,128]{2,1,0:T(8,128)S(1)} all-gather(f32[4,6,128]{2,1,0:T(8,128)S(1)} %copy.84), channel_id=1, replica_groups=mesh['group'=4,'gx'=4,'gy'=2] {'group'}, dimensions={0}, use_global_device_ids=true | all-gather | bytes 61440 | tf_op jit(solution)/shard_map/all_gather | solution.py:443
  39.2 0.6 fusion.57
  39.9 0.6 fusion.59
  40.7 7.8 %all_gather.10 = f32[4,4,8,128]{3,1,0,2:T(4,128)S(1)} all-gather(f32[4,4,4,128]{3,1,0,2:T(4,128)S(1)} %pad_maximum_fusion.1), channel_id=1, replica_groups=mesh['group'=4,'gx'=4,'gy'=2] {'gy'}, dimensions={2}, use_global_device_ids=true | all-gather | bytes 98304 | tf_op jit(solution)/shard_map/all_gather | solution.py:356
  48.6 1.3 %collective-permute-start.15 = (bf16[19,1,1,128]{3,2,1,0:T(2,128)(2,1)}, bf16[19,1,1,128]{3,2,1,0:T(2,128)(2,1)S(1)}, u32[]{:S(2)}, u32[]{:S(2)}) collective-permute-start(bf16[19,1,1,128]{3,2,1,0:T(2,128)(2,1)} %get-tuple-element.352), channel_id=1, source_target_pairs={{3,0},{5,2},{7,4},{9,6},{11,8},{13,10},{15,12},{17,14},{19,16},{21... | collective-permute-start | bytes 14600 | tf_op jit(solution)/shard_map/ppermute | solution.py:60
  49.9 0.7 collective-permute-start.13
  50.5 0.7 collective-permute-start.10
  51.2 19.0 %all_gather.11 = f32[4,16,8,128]{3,2,0,1:T(8,128)S(1)} all-gather(f32[4,4,8,128]{3,2,0,1:T(8,128)S(1)} %copy.89), channel_id=1, replica_groups=mesh['group'=4,'gx'=4,'gy'=2] {'gx'}, dimensions={1}, use_global_device_ids=true | all-gather | bytes 327680 | tf_op jit(solution)/shard_map/all_gather | solution.py:357
  70.2 1.3 %collective-permute-start.14 = (bf16[19,1,8,128]{3,2,1,0:T(8,128)(2,1)S(1)}, bf16[19,1,8,128]{3,2,1,0:T(8,128)(2,1)S(1)}, u32[]{:S(2)}, u32[]{:S(2)}) collective-permute-start(bf16[19,1,8,128]{3,2,1,0:T(8,128)(2,1)S(1)} %get-tuple-element.356), channel_id=1, source_target_pairs={{2,0},{3,1},{4,2},{5,3},{6,4},{7,5},{8,6},{9,7},{10,8},{11,9},{12,... | collective-permute-start | bytes 116744 | tf_op jit(solution)/shard_map/ppermute | solution.py:60
  71.5 1.3 %collective-permute-start.12 = (bf16[19,2,1,128]{3,2,1,0:T(2,128)(2,1)}, bf16[19,2,1,128]{3,2,1,0:T(2,128)(2,1)S(1)}, u32[]{:S(2)}, u32[]{:S(2)}) collective-permute-start(bf16[19,2,1,128]{3,2,1,0:T(2,128)(2,1)} %get-tuple-element.358), channel_id=1, source_target_pairs={{1,0},{3,2},{5,4},{7,6},{9,8},{11,10},{13,12},{15,14},{17,16},{19,... | collective-permute-start | bytes 29192 | tf_op jit(solution)/shard_map/ppermute | solution.py:60
  72.8 4.5 %collective-permute-start.11 = (bf16[19,2,1,128]{3,2,1,0:T(2,128)(2,1)S(1)}, bf16[19,2,1,128]{3,2,1,0:T(2,128)(2,1)S(1)}, u32[]{:S(2)}, u32[]{:S(2)}) collective-permute-start(bf16[19,2,1,128]{3,2,1,0:T(2,128)(2,1)S(1)} %get-tuple-element.357), channel_id=1, source_target_pairs={{0,1},{2,3},{4,5},{6,7},{8,9},{10,11},{12,13},{14,15},{16,17},{18,... | collective-permute-start | bytes 29192 | tf_op jit(solution)/shard_map/ppermute | solution.py:60
  77.4 4.5 %collective-permute-start.9 = (bf16[19,1,8,128]{3,2,1,0:T(8,128)(2,1)S(1)}, bf16[19,1,8,128]{3,2,1,0:T(8,128)(2,1)S(1)}, u32[]{:S(2)}, u32[]{:S(2)}) collective-permute-start(bf16[19,1,8,128]{3,2,1,0:T(8,128)(2,1)S(1)} %get-tuple-element.355), channel_id=1, source_target_pairs={{0,2},{1,3},{2,4},{3,5},{4,6},{5,7},{6,8},{7,9},{8,10},{9,11},{10,... | collective-permute-start | bytes 116744 | tf_op jit(solution)/shard_map/ppermute | solution.py:60
  81.9 2.2 %collective-permute-start.8 = (bf16[19,1,1,128]{3,2,1,0:T(2,128)(2,1)S(1)}, bf16[19,1,1,128]{3,2,1,0:T(2,128)(2,1)S(1)}, u32[]{:S(2)}, u32[]{:S(2)}) collective-permute-start(bf16[19,1,1,128]{3,2,1,0:T(2,128)(2,1)S(1)} %copy-done.6), channel_id=1, source_target_pairs={{0,3},{2,5},{4,7},{6,9},{8,11},{10,13},{12,15},{14,17},{16,19},{18... | collective-permute-start | bytes 14600 | tf_op jit(solution)/shard_map/ppermute | solution.py:60
  84.1 0.6 dynamic-slice_select_fusion
  84.7 0.6 conditional.8
  84.7 0.6 broadcast.297
  85.5 0.6 fusion.32
  86.1 0.7 constant_dynamic-slice_fusion.2
  86.8 14.1 %collective-permute-start.18 = (f32[4,3,128]{2,1,0:T(4,128)S(1)}, f32[4,3,128]{2,1,0:T(4,128)S(1)}, u32[]{:S(2)}, u32[]{:S(2)}) collective-permute-start(f32[4,3,128]{2,1,0:T(4,128)S(1)} %get-tuple-element.360), channel_id=1, source_target_pairs={{0,24},{8,0},{16,8},{24,16},{1,25},{9,1},{17,9},{25,17},{2,26},{10... | collective-permute-start | bytes 18440 | tf_op jit(solution)/shard_map/ppermute | solution.py:70
  101.0 0.2 collective-permute-start.16
  101.1 1.2 %collective-permute-done.18 = f32[4,3,128]{2,1,0:T(4,128)S(1)} collective-permute-done((f32[4,3,128]{2,1,0:T(4,128)S(1)}, f32[4,3,128]{2,1,0:T(4,128)S(1)}, u32[]{:S(2)}, u32[]{:S(2)}) %collective-permute-start.18) | collective-permute-done | bytes 6176 | tf_op jit(solution)/shard_map/ppermute | solution.py:70
  102.3 2.3 %collective-permute-done.17 = f32[4,3,128]{2,1,0:T(4,128)S(1)} collective-permute-done((f32[4,3,128]{2,1,0:T(4,128)S(1)}, f32[4,3,128]{2,1,0:T(4,128)S(1)}, u32[]{:S(2)}, u32[]{:S(2)}) %collective-permute-start.17) | collective-permute-done | bytes 6176 | tf_op jit(solution)/shard_map/ppermute | solution.py:70
  104.6 0.1 copy.93
  104.8 2.5 %scatter_custom_fusion.3 = f32[3,2048]{0,1:T(8,128)S(1)} fusion(s32[512]{0:T(512)S(1)} %bitcast.156, f32[512,3]{1,0:T(8,128)S(1)} %copy.93, f32[]{:T(128)} %constant.168.clone.1), kind=kCustom, calls=%fused_computation.110 | custom fusion | flops 1536 | bytes 24580 | tf_op jit(solution)/shard_map/scatter-add | solution.py:516
  107.3 1.8 %conditional.9 = (bf16[19,2,8,128]{3,2,1,0:T(8,128)(2,1)S(1)}) conditional(s32[]{:T(128)} %convert_element_type.64, () %tuple.42, (f32[4,10,130]{2,1,0:T(8,128)S(1)}, f32[19,1,1,1]{0,3,2,1:T(1,128)S(1)}, f32[19,1,1,1]{0,3,2,1:T(1,128)S(1)}, f32[19,1,1,1]{0,3,2,1:T(1,128)S(1)}, f32[19,1,1,1]{0,3,2,1:T(1,128)S(1)}, ...), branch_computations={%region_20.21_spmd, %region_21.22_spmd.clone} | conditional | flops 1056324 | bytes 4268820 | solution.py:518
  107.4 0.2 select_select_fusion
  108.2 0.3 copy.94
  108.7 0.4 fusion.6
  109.1 0.6 copy-done.2
  (93 shorter events, 2.0 us)
Async XLA Ops:
  1.4 14.5 %collective-permute-start.7 = (bf16[1,1,1,128]{3,2,1,0:T(2,128)(2,1)S(1)}, bf16[1,1,1,128]{3,2,1,0:T(2,128)(2,1)S(1)}, u32[]{:S(2)}, u32[]{:S(2)}) collective-permute-start(bf16[1,1,1,128]{3,2,1,0:T(2,128)(2,1)S(1)} %get-tuple-element.363), channel_id=1, source_target_pairs={{3,0},{5,2},{7,4},{9,6},{11,8},{13,10},{15,12},{17,14},{19,16},{21... | collective-permute-start | bytes 776 | tf_op jit(solution)/shard_map/ppermute | solution.py:60
  2.7 26.0 %collective-permute-start.6 = (bf16[1,1,8,128]{3,2,1,0:T(8,128)(2,1)S(1)}, bf16[1,1,8,128]{3,2,1,0:T(8,128)(2,1)S(1)}, u32[]{:S(2)}, u32[]{:S(2)}) collective-permute-start(bf16[1,1,8,128]{3,2,1,0:T(8,128)(2,1)S(1)} %get-tuple-element.367), channel_id=1, source_target_pairs={{2,0},{3,1},{4,2},{5,3},{6,4},{7,5},{8,6},{9,7},{10,8},{11,9},{12,... | collective-permute-start | bytes 6152 | tf_op jit(solution)/shard_map/ppermute | solution.py:60
  4.0 13.2 %collective-permute-start.5 = (bf16[1,1,1,128]{3,2,1,0:T(2,128)(2,1)S(1)}, bf16[1,1,1,128]{3,2,1,0:T(2,128)(2,1)S(1)}, u32[]{:S(2)}, u32[]{:S(2)}) collective-permute-start(bf16[1,1,1,128]{3,2,1,0:T(2,128)(2,1)S(1)} %get-tuple-element.364), channel_id=1, source_target_pairs={{2,1},{4,3},{6,5},{8,7},{10,9},{12,11},{14,13},{16,15},{18,17},{20... | collective-permute-start | bytes 776 | tf_op jit(solution)/shard_map/ppermute | solution.py:60
  4.6 19.3 %collective-permute-start.2 = (bf16[1,1,1,128]{3,2,1,0:T(2,128)(2,1)S(1)}, bf16[1,1,1,128]{3,2,1,0:T(2,128)(2,1)S(1)}, u32[]{:S(2)}, u32[]{:S(2)}) collective-permute-start(bf16[1,1,1,128]{3,2,1,0:T(2,128)(2,1)S(1)} %get-tuple-element.365), channel_id=1, source_target_pairs={{1,2},{3,4},{5,6},{7,8},{9,10},{11,12},{13,14},{15,16},{17,18},{19... | collective-permute-start | bytes 776 | tf_op jit(solution)/shard_map/ppermute | solution.py:60
  5.3 23.3 %collective-permute-start.1 = (bf16[1,1,8,128]{3,2,1,0:T(8,128)(2,1)S(1)}, bf16[1,1,8,128]{3,2,1,0:T(8,128)(2,1)S(1)}, u32[]{:S(2)}, u32[]{:S(2)}) collective-permute-start(bf16[1,1,8,128]{3,2,1,0:T(8,128)(2,1)S(1)} %get-tuple-element.366), channel_id=1, source_target_pairs={{0,2},{1,3},{2,4},{3,5},{4,6},{5,7},{6,8},{7,9},{8,10},{9,11},{10,... | collective-permute-start | bytes 6152 | tf_op jit(solution)/shard_map/ppermute | solution.py:60
  15.8 12.8 %collective-permute-start.4 = (bf16[1,2,1,128]{3,2,1,0:T(2,128)(2,1)S(1)}, bf16[1,2,1,128]{3,2,1,0:T(2,128)(2,1)S(1)}, u32[]{:S(2)}, u32[]{:S(2)}) collective-permute-start(bf16[1,2,1,128]{3,2,1,0:T(2,128)(2,1)S(1)} %get-tuple-element.369), channel_id=1, source_target_pairs={{1,0},{3,2},{5,4},{7,6},{9,8},{11,10},{13,12},{15,14},{17,16},{19,... | collective-permute-start | bytes 1544 | tf_op jit(solution)/shard_map/ppermute | solution.py:60
  17.1 11.5 %collective-permute-start.3 = (bf16[1,2,1,128]{3,2,1,0:T(2,128)(2,1)S(1)}, bf16[1,2,1,128]{3,2,1,0:T(2,128)(2,1)S(1)}, u32[]{:S(2)}, u32[]{:S(2)}) collective-permute-start(bf16[1,2,1,128]{3,2,1,0:T(2,128)(2,1)S(1)} %get-tuple-element.368), channel_id=1, source_target_pairs={{0,1},{2,3},{4,5},{6,7},{8,9},{10,11},{12,13},{14,15},{16,17},{18,... | collective-permute-start | bytes 1544 | tf_op jit(solution)/shard_map/ppermute | solution.py:60
  24.0 4.6 %collective-permute-start = (bf16[1,1,1,128]{3,2,1,0:T(2,128)(2,1)S(1)}, bf16[1,1,1,128]{3,2,1,0:T(2,128)(2,1)S(1)}, u32[]{:S(2)}, u32[]{:S(2)}) collective-permute-start(bf16[1,1,1,128]{3,2,1,0:T(2,128)(2,1)S(1)} %get-tuple-element.362), channel_id=1, source_target_pairs={{0,3},{2,5},{4,7},{6,9},{8,11},{10,13},{12,15},{14,17},{16,19},{18... | collective-permute-start | bytes 776 | tf_op jit(solution)/shard_map/ppermute | solution.py:60
  28.7 11.8 %copy-start.3 = (f32[3,4,4,128]{3,2,1,0:T(4,128)S(1)}, f32[3,4,4,128]{3,2,1,0:T(4,128)}, u32[]{:S(2)}) copy-start(f32[3,4,4,128]{3,2,1,0:T(4,128)} %param.46) | copy-start | bytes 73732
  28.7 11.8 %copy-start.11 = (s32[1,1,256]{2,1,0:T(1,128)S(1)}, s32[1,1,256]{2,1,0:T(1,128)}, u32[]{:S(2)}) copy-start(s32[1,1,256]{2,1,0:T(1,128)} %param.50) | copy-start | bytes 3076
  28.7 11.8 %copy-start.13 = (f32[3,1,1,256]{3,2,1,0:T(1,128)S(1)}, f32[3,1,1,256]{3,2,1,0:T(1,128)}, u32[]{:S(2)}) copy-start(f32[3,1,1,256]{3,2,1,0:T(1,128)} %param.51) | copy-start | bytes 9220
  28.8 11.8 %copy-start.14 = (s32[1,1,2,8]{3,2,1,0:T(2,128)S(1)}, s32[1,1,2,8]{3,2,1,0:T(2,128)}, u32[]{:S(2)}) copy-start(s32[1,1,2,8]{3,2,1,0:T(2,128)} %param.52) | copy-start | bytes 196
  29.5 1.1 copy-start.10
  29.5 1.1 %copy-start.17 = (f32[19]{0:T(128)S(1)}, f32[19]{0:T(128)}, u32[]{:S(2)}) copy-start(f32[19]{0:T(128)} %constant.211) | copy-start | bytes 232 | tf_op jit(solution)/shard_map/cond
  29.5 1.1 %copy-start.18 = (f32[19]{0:T(128)S(1)}, f32[19]{0:T(128)}, u32[]{:S(2)}) copy-start(f32[19]{0:T(128)} %constant.213) | copy-start | bytes 232 | tf_op jit(solution)/shard_map/cond
  29.6 1.1 %copy-start.19 = (f32[19]{0:T(128)S(1)}, f32[19]{0:T(128)}, u32[]{:S(2)}) copy-start(f32[19]{0:T(128)} %constant.212) | copy-start | bytes 232 | tf_op jit(solution)/shard_map/cond
  30.5 0.9 copy-start.5
  40.7 41.3 %copy-start.6 = (bf16[19,1,1,128]{3,2,1,0:T(2,128)(2,1)S(1)}, bf16[19,1,1,128]{3,2,1,0:T(2,128)(2,1)}, u32[]{:S(2)}) copy-start(bf16[19,1,1,128]{3,2,1,0:T(2,128)(2,1)} %get-tuple-element.351) | copy-start | bytes 14596
  40.7 44.0 %copy-start.12 = (s32[1,1,256]{2,1,0:T(1,128)S(1)}, s32[1,1,256]{2,1,0:T(1,128)}, u32[]{:S(2)}) copy-start(s32[1,1,256]{2,1,0:T(1,128)} %param.50) | copy-start | bytes 3076
  40.7 44.0 %copy-start.15 = (s32[1,1,2,8]{3,2,1,0:T(2,128)S(1)}, s32[1,1,2,8]{3,2,1,0:T(2,128)}, u32[]{:S(2)}) copy-start(s32[1,1,2,8]{3,2,1,0:T(2,128)} %param.52) | copy-start | bytes 196
  48.6 24.2 %collective-permute-start.15 = (bf16[19,1,1,128]{3,2,1,0:T(2,128)(2,1)}, bf16[19,1,1,128]{3,2,1,0:T(2,128)(2,1)S(1)}, u32[]{:S(2)}, u32[]{:S(2)}) collective-permute-start(bf16[19,1,1,128]{3,2,1,0:T(2,128)(2,1)} %get-tuple-element.352), channel_id=1, source_target_pairs={{3,0},{5,2},{7,4},{9,6},{11,8},{13,10},{15,12},{17,14},{19,16},{21... | collective-permute-start | bytes 14600 | tf_op jit(solution)/shard_map/ppermute | solution.py:60
  49.9 27.5 %collective-permute-start.13 = (bf16[19,1,1,128]{3,2,1,0:T(2,128)(2,1)}, bf16[19,1,1,128]{3,2,1,0:T(2,128)(2,1)S(1)}, u32[]{:S(2)}, u32[]{:S(2)}) collective-permute-start(bf16[19,1,1,128]{3,2,1,0:T(2,128)(2,1)} %get-tuple-element.353), channel_id=1, source_target_pairs={{2,1},{4,3},{6,5},{8,7},{10,9},{12,11},{14,13},{16,15},{18,17},{20... | collective-permute-start | bytes 14600 | tf_op jit(solution)/shard_map/ppermute | solution.py:60
  50.5 31.4 %collective-permute-start.10 = (bf16[19,1,1,128]{3,2,1,0:T(2,128)(2,1)}, bf16[19,1,1,128]{3,2,1,0:T(2,128)(2,1)S(1)}, u32[]{:S(2)}, u32[]{:S(2)}) collective-permute-start(bf16[19,1,1,128]{3,2,1,0:T(2,128)(2,1)} %get-tuple-element.354), channel_id=1, source_target_pairs={{1,2},{3,4},{5,6},{7,8},{9,10},{11,12},{13,14},{15,16},{17,18},{19... | collective-permute-start | bytes 14600 | tf_op jit(solution)/shard_map/ppermute | solution.py:60
  70.2 15.3 %collective-permute-start.14 = (bf16[19,1,8,128]{3,2,1,0:T(8,128)(2,1)S(1)}, bf16[19,1,8,128]{3,2,1,0:T(8,128)(2,1)S(1)}, u32[]{:S(2)}, u32[]{:S(2)}) collective-permute-start(bf16[19,1,8,128]{3,2,1,0:T(8,128)(2,1)S(1)} %get-tuple-element.356), channel_id=1, source_target_pairs={{2,0},{3,1},{4,2},{5,3},{6,4},{7,5},{8,6},{9,7},{10,8},{11,9},{12,... | collective-permute-start | bytes 116744 | tf_op jit(solution)/shard_map/ppermute | solution.py:60
  71.5 14.0 %collective-permute-start.12 = (bf16[19,2,1,128]{3,2,1,0:T(2,128)(2,1)}, bf16[19,2,1,128]{3,2,1,0:T(2,128)(2,1)S(1)}, u32[]{:S(2)}, u32[]{:S(2)}) collective-permute-start(bf16[19,2,1,128]{3,2,1,0:T(2,128)(2,1)} %get-tuple-element.358), channel_id=1, source_target_pairs={{1,0},{3,2},{5,4},{7,6},{9,8},{11,10},{13,12},{15,14},{17,16},{19,... | collective-permute-start | bytes 29192 | tf_op jit(solution)/shard_map/ppermute | solution.py:60
  72.8 12.7 %collective-permute-start.11 = (bf16[19,2,1,128]{3,2,1,0:T(2,128)(2,1)S(1)}, bf16[19,2,1,128]{3,2,1,0:T(2,128)(2,1)S(1)}, u32[]{:S(2)}, u32[]{:S(2)}) collective-permute-start(bf16[19,2,1,128]{3,2,1,0:T(2,128)(2,1)S(1)} %get-tuple-element.357), channel_id=1, source_target_pairs={{0,1},{2,3},{4,5},{6,7},{8,9},{10,11},{12,13},{14,15},{16,17},{18,... | collective-permute-start | bytes 29192 | tf_op jit(solution)/shard_map/ppermute | solution.py:60
  77.4 8.1 %collective-permute-start.9 = (bf16[19,1,8,128]{3,2,1,0:T(8,128)(2,1)S(1)}, bf16[19,1,8,128]{3,2,1,0:T(8,128)(2,1)S(1)}, u32[]{:S(2)}, u32[]{:S(2)}) collective-permute-start(bf16[19,1,8,128]{3,2,1,0:T(8,128)(2,1)S(1)} %get-tuple-element.355), channel_id=1, source_target_pairs={{0,2},{1,3},{2,4},{3,5},{4,6},{5,7},{6,8},{7,9},{8,10},{9,11},{10,... | collective-permute-start | bytes 116744 | tf_op jit(solution)/shard_map/ppermute | solution.py:60
  81.9 3.5 %collective-permute-start.8 = (bf16[19,1,1,128]{3,2,1,0:T(2,128)(2,1)S(1)}, bf16[19,1,1,128]{3,2,1,0:T(2,128)(2,1)S(1)}, u32[]{:S(2)}, u32[]{:S(2)}) collective-permute-start(bf16[19,1,1,128]{3,2,1,0:T(2,128)(2,1)S(1)} %copy-done.6), channel_id=1, source_target_pairs={{0,3},{2,5},{4,7},{6,9},{8,11},{10,13},{12,15},{14,17},{16,19},{18... | collective-permute-start | bytes 14600 | tf_op jit(solution)/shard_map/ppermute | solution.py:60
  85.4 15.8 %copy-start.4 = (s32[1,1,512]{2,1,0:T(1,128)S(1)}, s32[1,1,512]{2,1,0:T(1,128)}, u32[]{:S(2)}) copy-start(s32[1,1,512]{2,1,0:T(1,128)} %param.45) | copy-start | bytes 6148
  85.4 21.9 %copy-start.7 = (f32[19,1,1,1]{0,3,2,1:T(1,128)S(1)}, f32[19,1,1,1]{0,3,2,1:T(1,128)}, u32[]{:S(2)}) copy-start(f32[19,1,1,1]{0,3,2,1:T(1,128)} %constant.186.clone) | copy-start | bytes 232
  85.4 21.9 %copy-start.8 = (f32[19,1,1,1]{0,3,2,1:T(1,128)S(1)}, f32[19,1,1,1]{0,3,2,1:T(1,128)}, u32[]{:S(2)}) copy-start(f32[19,1,1,1]{0,3,2,1:T(1,128)} %constant.185.clone) | copy-start | bytes 232
  85.4 21.9 %copy-start.9 = (f32[19,1,1,1]{0,3,2,1:T(1,128)S(1)}, f32[19,1,1,1]{0,3,2,1:T(1,128)}, u32[]{:S(2)}) copy-start(f32[19,1,1,1]{0,3,2,1:T(1,128)} %constant.187.clone) | copy-start | bytes 232
  86.8 15.5 %collective-permute-start.18 = (f32[4,3,128]{2,1,0:T(4,128)S(1)}, f32[4,3,128]{2,1,0:T(4,128)S(1)}, u32[]{:S(2)}, u32[]{:S(2)}) collective-permute-start(f32[4,3,128]{2,1,0:T(4,128)S(1)} %get-tuple-element.360), channel_id=1, source_target_pairs={{0,24},{8,0},{16,8},{24,16},{1,25},{9,1},{17,9},{25,17},{2,26},{10... | collective-permute-start | bytes 18440 | tf_op jit(solution)/shard_map/ppermute | solution.py:70
  101.0 3.7 %collective-permute-start.17 = (f32[4,3,128]{2,1,0:T(4,128)S(1)}, f32[4,3,128]{2,1,0:T(4,128)S(1)}, u32[]{:S(2)}, u32[]{:S(2)}) collective-permute-start(f32[4,3,128]{2,1,0:T(4,128)S(1)} %get-tuple-element.361), channel_id=1, source_target_pairs={{0,16},{8,24},{16,0},{24,8},{1,17},{9,25},{17,1},{25,9},{2,18},{10... | collective-permute-start | bytes 18440 | tf_op jit(solution)/shard_map/ppermute | solution.py:70
  101.0 3.7 %collective-permute-start.16 = (f32[4,3,128]{2,1,0:T(4,128)S(1)}, f32[4,3,128]{2,1,0:T(4,128)S(1)}, u32[]{:S(2)}, u32[]{:S(2)}) collective-permute-start(f32[4,3,128]{2,1,0:T(4,128)S(1)} %get-tuple-element.359), channel_id=1, source_target_pairs={{0,8},{8,16},{16,24},{24,0},{1,9},{9,17},{17,25},{25,1},{2,10},{10... | collective-permute-start | bytes 18440 | tf_op jit(solution)/shard_map/ppermute | solution.py:70
  108.1 0.7 copy-start.16
  109.1 0.6 copy-start.2

commit v5 on v3

--- a/solution.py
+++ b/solution.py
@@ -39,30 +39,27 @@
 mass_shift = 0.5
 
 
-def halo_exchange(cells):
-    span_devices = lax.axis_size(("group", "gx"))
+def halo_exchange(cells, span_devices):
     columns = lax.axis_size("gy")
-    rows, cols = cells.shape[1], cells.shape[2]
-    row_pick = {1: slice(rows - 1, rows), 0: slice(0, rows), -1: slice(0, 1)}
-    col_pick = {1: slice(cols - 1, cols), 0: slice(0, cols), -1: slice(0, 1)}
-    received = {}
-    for dr in (-1, 0, 1):
-        for dc in (-1, 0, 1):
-            if dr == 0 and dc == 0:
-                received[(dr, dc)] = cells
-                continue
-            pairs = [
-                (r * columns + c, (r + dr) * columns + c + dc)
-                for r in range(span_devices)
-                for c in range(columns)
-                if 0 <= r + dr < span_devices and 0 <= c + dc < columns
-            ]
-            piece = cells[:, row_pick[dr], col_pick[dc]]
-            received[(dr, dc)] = lax.ppermute(piece, ("group", "gx", "gy"), pairs)
-    bands = [
-        jnp.concatenate([received[(dr, dc)] for dc in (1, 0, -1)], axis=2) for dr in (1, 0, -1)
-    ]
-    return jnp.concatenate(bands, axis=1)
+    axes = ("group", "gx", "gy")
+
+    def shifted(piece, dr, dc):
+        pairs = [
+            (r * columns + c, (r + dr) * columns + c + dc)
+            for r in range(span_devices)
+            for c in range(columns)
+            if 0 <= r + dr < span_devices and 0 <= c + dc < columns
+        ]
+        return lax.ppermute(piece, axes, pairs)
+
+    cols = cells.shape[2]
+    cells = jnp.concatenate(
+        [shifted(cells[:, :, cols - 1 :], 0, 1), cells, shifted(cells[:, :, :1], 0, -1)], axis=2
+    )
+    rows = cells.shape[1]
+    return jnp.concatenate(
+        [shifted(cells[:, rows - 1 :], 1, 0), cells, shifted(cells[:, :1], -1, 0)], axis=1
+    )
 
 
 def passed_along(value, axis, steps):
@@ -404,7 +401,9 @@
         is_fluid, collide(populations.astype(jnp.float32)), 0.0
     ).astype(jnp.bfloat16)
     marker = fluid_here.astype(jnp.bfloat16)[None]
-    widened = halo_exchange(jnp.concatenate([relaxed_pops, marker], axis=0))
+    widened = halo_exchange(
+        jnp.concatenate([relaxed_pops, marker], axis=0), fluid_groups * span_devices
+    )
     widened = jnp.pad(widened, ((0, 0), (0, 0), (0, 0), (1, 1))).astype(jnp.float32)
     moved = widened[0:19]
     fluid_ext = widened[19]

time: 109 us -> 95.1 us (0.87)
  starting transfers between devices: 53.3 us -> 42.8 us
  blocking collectives: 31.6 us -> 24 us
  waiting for transfers between devices: 6.71 us -> 10.3 us
    ppermute x8 -> x4, starting transfers between devices: 21.4 us -> 10.9 us  [shifted(): return lax.ppermute(piece, axes, pairs)]
    all_gather x1, blocking collectives: 13.1 us -> 5.25 us  [per_device(): received = lax.all_gather(packed, 'group', axis=0, tiled=True)]
    ppermute x8 -> x4, waiting for transfers between devices: 3.66 us -> 8.69 us  [shifted(): return lax.ppermute(piece, axes, pairs)]
    ppermute x3, waiting for transfers between devices: 3.05 us -> 1.62 us  [passed_along(): return lax.ppermute(value, axis, pairs)]
  transfers between devices with their start and end apart: 11 -> 7, of which waited for: 4 -> 5; matrix products, arithmetic and copies ran while one was open for 1% -> 1% of each run, Pallas kernels for 0% -> 0%
where the time goes in v5:
time: 95.1 us; the launch traced here: 93.7 us
  starting transfers between devices  42.8 us (45%)
  blocking collectives  24 us (25%)
  waiting for transfers between devices  10.3 us (11%)
  other arithmetic  8.96 us (9%)
  local copies, waits for them, and re-layouts  6.47 us (7%)
    ppermute x3, starting transfers between devices, passed_along(): return lax.ppermute(value, axis, pairs)  31.9 us
    all_gather x1, blocking collectives, whole_partition(): return lax.all_gather(every, 'gx', axis=count, tiled=True)  14.1 us
    ppermute x4, starting transfers between devices, shifted(): return lax.ppermute(piece, axes, pairs)  10.9 us
    ppermute x4, waiting for transfers between devices, shifted(): return lax.ppermute(piece, axes, pairs)  8.69 us
    all_gather x1, blocking collectives, per_device(): received = lax.all_gather(packed, 'group', axis=0, tiled=True)  5.25 us
    all_gather x1, blocking collectives, whole_partition(): every = lax.all_gather(block, 'gy', axis=count + 1, tiled=True)  4.59 us
    scatter-add x1, other arithmetic, per_device(): jnp.zeros((3, cell_count), jnp.float32).at[:, wall_index].add(speed_parts)  2.51 us
    another operation x5, local copies, waits for them, and re-layouts  2.06 us
  transfers between devices with their start and end apart: 7, of which 5 were waited for; matrix products, arithmetic and copies ran while one was open for 1% of the time, Pallas kernels for 0%

profile of v5, /device:TPU:0, one launch (start us, length us, event | category | flops | bytes accessed | tf_op | source)
XLA Modules:
  0.0 93.7 jit_solution(3791665565791457196)
XLA Ops:
  0.6 0.7 fusion.51
  1.3 1.0 %fusion.44 = (f32[2,8,128]{2,1,0:T(8,128)S(1)}, f32[2,8,128]{2,1,0:T(8,128)S(1)}, f32[2,8,128]{2,1,0:T(8,128)S(1)}, f32[2,8,128]{2,1,0:T(8,128)S(1)}) fusion(bf16[19,2,8,128]{3,2,1,0:T(8,128)(2,1)} %param.43, f32[19]{0:T(128)} %constant.205, f32[19]{0:T(128)} %constant.206, f32[19]{0:T(128)} %constant.207), kind=kLoop, calls=%fused_computation.128 | loop fusion | flops 303104 | bytes 110820 | tf_op jit(solution)/shard_map/reduce_sum | solution.py:86
  2.4 1.1 %fusion.49 = bf16[19,2,8,128]{3,2,1,0:T(8,128)(2,1)S(1)} fusion(bf16[19,2,8,128]{3,2,1,0:T(8,128)(2,1)} %param.43, f32[2,8,128]{2,1,0:T(8,128)S(1)} %get-tuple-element.295, f32[2,8,128]{2,1,0:T(8,128)S(1)} %get-tuple-element.298, f32[19]{0:T(128)} %constant.207, f32[2,8,128]{2,1,0:T(8,128)S(1)} %get-tuple-element.297, f32[19]{0:T(128)} %constant.206, ...), kind=kLoop, calls=%fused_computation.133 | loop fusion | flops 739328 | bytes 196913 | tf_op jit(solution)/shard_map/convert_element_type | solution.py:402
  3.6 4.8 %collective-permute-start = (bf16[20,2,1,128]{3,2,1,0:T(2,128)(2,1)S(1)}, bf16[20,2,1,128]{3,2,1,0:T(2,128)(2,1)S(1)}, u32[]{:S(2)}, u32[]{:S(2)}) collective-permute-start(bf16[20,2,1,128]{3,2,1,0:T(2,128)(2,1)S(1)} %get-tuple-element.345), channel_id=1, source_target_pairs={{0,1},{2,3},{4,5},{6,7},{8,9},{10,11},{12,13},{14,15},{16,17},{18,... | collective-permute-start | bytes 30728 | tf_op jit(solution)/shard_map/ppermute | solution.py:53
  8.4 1.3 %collective-permute-start.1 = (bf16[20,2,1,128]{3,2,1,0:T(2,128)(2,1)S(1)}, bf16[20,2,1,128]{3,2,1,0:T(2,128)(2,1)S(1)}, u32[]{:S(2)}, u32[]{:S(2)}) collective-permute-start(bf16[20,2,1,128]{3,2,1,0:T(2,128)(2,1)S(1)} %get-tuple-element.346), channel_id=1, source_target_pairs={{1,0},{3,2},{5,4},{7,6},{9,8},{11,10},{13,12},{15,14},{17,16},{19,... | collective-permute-start | bytes 30728 | tf_op jit(solution)/shard_map/ppermute | solution.py:53
  9.7 0.2 collective-permute-done
  9.9 4.2 %collective-permute-done.1 = bf16[20,2,1,128]{3,2,1,0:T(2,128)(2,1)S(1)} collective-permute-done((bf16[20,2,1,128]{3,2,1,0:T(2,128)(2,1)S(1)}, bf16[20,2,1,128]{3,2,1,0:T(2,128)(2,1)S(1)}, u32[]{:S(2)}, u32[]{:S(2)}) %collective-permute-start.1) | collective-permute-done | bytes 10272 | tf_op jit(solution)/shard_map/ppermute | solution.py:53
  14.1 0.1 pad_maximum_fusion.1
  14.2 3.5 %collective-permute-start.2 = (bf16[20,1,10,128]{3,2,1,0:T(8,128)(2,1)S(1)}, bf16[20,1,10,128]{3,2,1,0:T(8,128)(2,1)S(1)}, u32[]{:S(2)}, u32[]{:S(2)}) collective-permute-start(bf16[20,1,10,128]{3,2,1,0:T(8,128)(2,1)S(1)} %get-tuple-element.343), channel_id=1, source_target_pairs={{0,2},{1,3},{2,4},{3,5},{4,6},{5,7},{6,8},{7,9},{8,10},{9,11},{10,... | collective-permute-start | bytes 153608 | tf_op jit(solution)/shard_map/ppermute | solution.py:53
  17.7 1.3 %collective-permute-start.3 = (bf16[20,1,10,128]{3,2,1,0:T(8,128)(2,1)S(1)}, bf16[20,1,10,128]{3,2,1,0:T(8,128)(2,1)S(1)}, u32[]{:S(2)}, u32[]{:S(2)}) collective-permute-start(bf16[20,1,10,128]{3,2,1,0:T(8,128)(2,1)S(1)} %get-tuple-element.344), channel_id=1, source_target_pairs={{2,0},{3,1},{4,2},{5,3},{6,4},{7,5},{8,6},{9,7},{10,8},{11,9},{12,... | collective-permute-start | bytes 153608 | tf_op jit(solution)/shard_map/ppermute | solution.py:53
  19.0 0.7 fusion.50
  19.7 4.3 %collective-permute-done.3 = bf16[20,1,10,128]{3,2,1,0:T(8,128)(2,1)S(1)} collective-permute-done((bf16[20,1,10,128]{3,2,1,0:T(8,128)(2,1)S(1)}, bf16[20,1,10,128]{3,2,1,0:T(8,128)(2,1)S(1)}, u32[]{:S(2)}, u32[]{:S(2)}) %collective-permute-start.3) | collective-permute-done | bytes 51232 | tf_op jit(solution)/shard_map/ppermute | solution.py:53
  24.0 0.5 fusion.31
  24.6 0.1 slice.276
  24.7 0.5 copy-done.2
  25.3 2.6 %conditional.5 = (f32[4,6,128]{2,0,1:T(4,128)S(1)}) conditional(s32[]{:T(128)} %convert_element_type.56, () %tuple.44, (f32[19,1,1,1]{0,3,2,1:T(1,128)S(1)}, f32[19,1,1,1]{0,3,2,1:T(1,128)S(1)}, f32[19,1,1,1]{0,3,2,1:T(1,128)S(1)}, f32[1,4,10,130]{3,2,1,0:T(8,128)S(1)}, f32[19,4,10,130]{3,2,1,0:T(8,128)S(1)}, ...), branch_computations={%region_4.5_spmd, %region_5.9_spmd.clone} | conditional | flops 646950 | bytes 2346576 | solution.py:431
  25.3 0.1 select_select_fusion.2
  25.5 0.1 fusion.9
  25.6 0.1 slice.209
  25.8 0.1 slice.208
  25.9 0.1 copy-done.14
  26.0 0.2 multiply_reduce_fusion.2
  26.3 0.4 copy.80
  26.7 1.0 %gather_fusion = f32[512,3]{1,0:T(8,128)S(1)} fusion(f32[3,2048]{0,1:T(8,128)S(1)} %copy.80, s32[1024]{0:T(1024)S(1)} %pad_clamp_fusion), kind=kCustom, calls=%fused_computation.3 | custom fusion | bytes 14336 | tf_op jit(solution)/shard_map/cond/branch_1_fun/gather | solution.py:417
  27.7 0.1 copy.81
  27.9 5.2 %all_gather.9 = f32[16,6,128]{2,1,0:T(8,128)S(1)} all-gather(f32[4,6,128]{2,1,0:T(8,128)S(1)} %copy.84), channel_id=1, replica_groups=mesh['group'=4,'gx'=4,'gy'=2] {'group'}, dimensions={0}, use_global_device_ids=true | all-gather | bytes 61440 | tf_op jit(solution)/shard_map/all_gather | solution.py:437
  33.2 1.1 %conditional.6 = (f32[2,128,8,128]{3,1,2,0:T(8,128)}, f32[3,4,4,128]{3,1,0,2:T(4,128)S(1)}) conditional(s32[]{:T(128)} %convert_element_type.62, () %tuple.43, (f32[3,1,1,256]{3,2,1,0:T(1,128)S(1)}, s32[1,1,2,8]{3,2,1,0:T(2,128)S(1)}, f32[16,6,128]{2,1,0:T(8,128)S(1)}, s32[256]{0:T(256)S(1)}, f32[3,4,4,128]{3,2,1,0:T(4,128)S(1)}) %tuple.145), branch_computations={%region_9.10_spmd, %region_10.14_spmd} | conditional | flops 15213152 | bytes 2600664 | solution.py:452
  33.2 1.1 %broadcast.282 = f32[2,128,8,128]{3,1,2,0:T(8,128)} broadcast(f32[]{:T(128)} %constant.149.clone), dimensions={} | broadcast | bytes 1048580 | tf_op jit(solution)/shard_map/broadcast.21
  34.3 4.6 %all_gather.10 = f32[4,4,8,128]{3,1,0,2:T(4,128)S(1)} all-gather(f32[4,4,4,128]{3,1,0,2:T(4,128)S(1)} %pad_maximum_fusion.2), channel_id=1, replica_groups=mesh['group'=4,'gx'=4,'gy'=2] {'gy'}, dimensions={2}, use_global_device_ids=true | all-gather | bytes 98304 | tf_op jit(solution)/shard_map/all_gather | solution.py:346
  38.9 14.1 %all_gather.11 = f32[4,16,8,128]{3,2,0,1:T(8,128)S(1)} all-gather(f32[4,4,8,128]{3,2,0,1:T(8,128)S(1)} %copy.89), channel_id=1, replica_groups=mesh['group'=4,'gx'=4,'gy'=2] {'gx'}, dimensions={1}, use_global_device_ids=true | all-gather | bytes 327680 | tf_op jit(solution)/shard_map/all_gather | solution.py:347
  53.1 0.6 dynamic-slice_select_fusion
  53.7 0.6 conditional.8
  53.7 0.6 broadcast.295
  54.3 0.7 constant_dynamic-slice_fusion.2
  55.1 31.9 %collective-permute-start.5 = (f32[4,3,128]{2,1,0:T(4,128)S(1)}, f32[4,3,128]{2,1,0:T(4,128)S(1)}, u32[]{:S(2)}, u32[]{:S(2)}) collective-permute-start(f32[4,3,128]{2,1,0:T(4,128)S(1)} %get-tuple-element.349), channel_id=1, source_target_pairs={{0,16},{8,24},{16,0},{24,8},{1,17},{9,25},{17,1},{25,9},{2,18},{10... | collective-permute-start | bytes 18440 | tf_op jit(solution)/shard_map/ppermute | solution.py:68
  87.0 0.9 collective-permute-done.4
  87.9 0.7 collective-permute-done.5
  88.6 0.1 copy.93
  88.8 2.5 %scatter_custom_fusion.3 = f32[3,2048]{0,1:T(8,128)S(1)} fusion(s32[512]{0:T(512)S(1)} %bitcast.168, f32[512,3]{1,0:T(8,128)S(1)} %copy.93, f32[]{:T(128)} %constant.168.clone.1), kind=kCustom, calls=%fused_computation.115 | custom fusion | flops 1536 | bytes 24580 | tf_op jit(solution)/shard_map/scatter-add | solution.py:506
  91.3 1.8 %conditional.9 = (bf16[19,2,8,128]{3,2,1,0:T(8,128)(2,1)S(1)}) conditional(s32[]{:T(128)} %convert_element_type.56, () %tuple.40, (f32[1,4,10,130]{3,2,1,0:T(8,128)S(1)}, f32[19,1,1,1]{0,3,2,1:T(1,128)S(1)}, f32[19,1,1,1]{0,3,2,1:T(1,128)S(1)}, f32[19,1,1,1]{0,3,2,1:T(1,128)S(1)}, f32[19,1,1,1]{0,3,2,1:T(1,128)S(1)}, ...), branch_computations={%region_20.21_spmd, %region_21.22_spmd.clone} | conditional | flops 1056324 | bytes 4268820 | solution.py:508
  91.3 0.1 select_select_fusion.1
  91.5 0.1 fusion.1
  91.7 0.2 select_select_fusion
  91.9 0.1 fusion
  92.0 0.1 slice.233
  92.1 0.3 copy.94
  92.7 0.4 fusion.6
  93.1 0.6 copy-done
  (64 shorter events, 0.6 us)
Async XLA Ops:
  3.6 6.3 %collective-permute-start = (bf16[20,2,1,128]{3,2,1,0:T(2,128)(2,1)S(1)}, bf16[20,2,1,128]{3,2,1,0:T(2,128)(2,1)S(1)}, u32[]{:S(2)}, u32[]{:S(2)}) collective-permute-start(bf16[20,2,1,128]{3,2,1,0:T(2,128)(2,1)S(1)} %get-tuple-element.345), channel_id=1, source_target_pairs={{0,1},{2,3},{4,5},{6,7},{8,9},{10,11},{12,13},{14,15},{16,17},{18,... | collective-permute-start | bytes 30728 | tf_op jit(solution)/shard_map/ppermute | solution.py:53
  8.4 5.7 %collective-permute-start.1 = (bf16[20,2,1,128]{3,2,1,0:T(2,128)(2,1)S(1)}, bf16[20,2,1,128]{3,2,1,0:T(2,128)(2,1)S(1)}, u32[]{:S(2)}, u32[]{:S(2)}) collective-permute-start(bf16[20,2,1,128]{3,2,1,0:T(2,128)(2,1)S(1)} %get-tuple-element.346), channel_id=1, source_target_pairs={{1,0},{3,2},{5,4},{7,6},{9,8},{11,10},{13,12},{15,14},{17,16},{19,... | collective-permute-start | bytes 30728 | tf_op jit(solution)/shard_map/ppermute | solution.py:53
  14.2 5.5 %collective-permute-start.2 = (bf16[20,1,10,128]{3,2,1,0:T(8,128)(2,1)S(1)}, bf16[20,1,10,128]{3,2,1,0:T(8,128)(2,1)S(1)}, u32[]{:S(2)}, u32[]{:S(2)}) collective-permute-start(bf16[20,1,10,128]{3,2,1,0:T(8,128)(2,1)S(1)} %get-tuple-element.343), channel_id=1, source_target_pairs={{0,2},{1,3},{2,4},{3,5},{4,6},{5,7},{6,8},{7,9},{8,10},{9,11},{10,... | collective-permute-start | bytes 153608 | tf_op jit(solution)/shard_map/ppermute | solution.py:53
  17.7 6.3 %collective-permute-start.3 = (bf16[20,1,10,128]{3,2,1,0:T(8,128)(2,1)S(1)}, bf16[20,1,10,128]{3,2,1,0:T(8,128)(2,1)S(1)}, u32[]{:S(2)}, u32[]{:S(2)}) collective-permute-start(bf16[20,1,10,128]{3,2,1,0:T(8,128)(2,1)S(1)} %get-tuple-element.344), channel_id=1, source_target_pairs={{2,0},{3,1},{4,2},{5,3},{6,4},{7,5},{8,6},{9,7},{10,8},{11,9},{12,... | collective-permute-start | bytes 153608 | tf_op jit(solution)/shard_map/ppermute | solution.py:53
  24.5 0.7 copy-start.2
  24.5 0.7 copy-start.4
  24.5 0.7 copy-start.5
  24.6 0.7 copy-start.6
  25.2 7.9 %copy-start.1 = (f32[3,4,4,128]{3,2,1,0:T(4,128)S(1)}, f32[3,4,4,128]{3,2,1,0:T(4,128)}, u32[]{:S(2)}) copy-start(f32[3,4,4,128]{3,2,1,0:T(4,128)} %param.46) | copy-start | bytes 73732
  25.2 7.9 %copy-start.8 = (s32[1,1,256]{2,1,0:T(1,128)S(1)}, s32[1,1,256]{2,1,0:T(1,128)}, u32[]{:S(2)}) copy-start(s32[1,1,256]{2,1,0:T(1,128)} %param.50) | copy-start | bytes 3076
  25.2 7.9 %copy-start.10 = (f32[3,1,1,256]{3,2,1,0:T(1,128)S(1)}, f32[3,1,1,256]{3,2,1,0:T(1,128)}, u32[]{:S(2)}) copy-start(f32[3,1,1,256]{3,2,1,0:T(1,128)} %param.51) | copy-start | bytes 9220
  25.2 7.9 %copy-start.11 = (s32[1,1,2,8]{3,2,1,0:T(2,128)S(1)}, s32[1,1,2,8]{3,2,1,0:T(2,128)}, u32[]{:S(2)}) copy-start(s32[1,1,2,8]{3,2,1,0:T(2,128)} %param.52) | copy-start | bytes 196
  25.3 0.7 copy-start.14
  25.3 0.7 copy-start.15
  25.3 0.7 copy-start.16
  33.2 19.9 %copy-start.3 = (f32[24,24]{1,0:T(8,128)S(1)}, f32[24,24]{1,0:T(8,128)}, u32[]{:S(2)}) copy-start(f32[24,24]{1,0:T(8,128)} %param.49) | copy-start | bytes 6916
  34.3 19.4 %copy-start.9 = (s32[1,1,256]{2,1,0:T(1,128)S(1)}, s32[1,1,256]{2,1,0:T(1,128)}, u32[]{:S(2)}) copy-start(s32[1,1,256]{2,1,0:T(1,128)} %param.50) | copy-start | bytes 3076
  34.3 19.4 %copy-start.12 = (s32[1,1,2,8]{3,2,1,0:T(2,128)S(1)}, s32[1,1,2,8]{3,2,1,0:T(2,128)}, u32[]{:S(2)}) copy-start(s32[1,1,2,8]{3,2,1,0:T(2,128)} %param.52) | copy-start | bytes 196
  54.3 37.0 %copy-start.7 = (f32[19,1,1,1]{0,3,2,1:T(1,128)S(1)}, f32[19,1,1,1]{0,3,2,1:T(1,128)}, u32[]{:S(2)}) copy-start(f32[19,1,1,1]{0,3,2,1:T(1,128)} %constant.187.clone) | copy-start | bytes 232
  55.1 32.8 %collective-permute-start.4 = (f32[4,3,128]{2,1,0:T(4,128)S(1)}, f32[4,3,128]{2,1,0:T(4,128)S(1)}, u32[]{:S(2)}, u32[]{:S(2)}) collective-permute-start(f32[4,3,128]{2,1,0:T(4,128)S(1)} %get-tuple-element.347), channel_id=1, source_target_pairs={{0,8},{8,16},{16,24},{24,0},{1,9},{9,17},{17,25},{25,1},{2,10},{10... | collective-permute-start | bytes 18440 | tf_op jit(solution)/shard_map/ppermute | solution.py:68
  55.1 33.5 %collective-permute-start.5 = (f32[4,3,128]{2,1,0:T(4,128)S(1)}, f32[4,3,128]{2,1,0:T(4,128)S(1)}, u32[]{:S(2)}, u32[]{:S(2)}) collective-permute-start(f32[4,3,128]{2,1,0:T(4,128)S(1)} %get-tuple-element.349), channel_id=1, source_target_pairs={{0,16},{8,24},{16,0},{24,8},{1,17},{9,25},{17,1},{25,9},{2,18},{10... | collective-permute-start | bytes 18440 | tf_op jit(solution)/shard_map/ppermute | solution.py:68
  87.0 1.6 %collective-permute-start.6 = (f32[4,3,128]{2,1,0:T(4,128)S(1)}, f32[4,3,128]{2,1,0:T(4,128)S(1)}, u32[]{:S(2)}, u32[]{:S(2)}) collective-permute-start(f32[4,3,128]{2,1,0:T(4,128)S(1)} %get-tuple-element.348), channel_id=1, source_target_pairs={{0,24},{8,0},{16,8},{24,16},{1,25},{9,1},{17,9},{25,17},{2,26},{10... | collective-permute-start | bytes 18440 | tf_op jit(solution)/shard_map/ppermute | solution.py:68
  91.8 0.8 copy-start.13
  93.1 0.6 copy-start

commit v6 on v5

--- a/solution.py
+++ b/solution.py
@@ -53,8 +53,18 @@
         return lax.ppermute(piece, axes, pairs)
 
     cols = cells.shape[2]
+    column = lax.axis_index("gy")
+    edges = jnp.concatenate([cells[:, :, :1], cells[:, :, cols - 1 :]], axis=2)
+    every = lax.all_gather(edges, "gy", axis=0)
+    from_left = lax.dynamic_index_in_dim(every, jnp.maximum(column - 1, 0), 0, False)
+    from_right = lax.dynamic_index_in_dim(every, jnp.minimum(column + 1, columns - 1), 0, False)
     cells = jnp.concatenate(
-        [shifted(cells[:, :, cols - 1 :], 0, 1), cells, shifted(cells[:, :, :1], 0, -1)], axis=2
+        [
+            jnp.where(column > 0, from_left[:, :, 1:], 0.0).astype(cells.dtype),
+            cells,
+            jnp.where(column < columns - 1, from_right[:, :, :1], 0.0).astype(cells.dtype),
+        ],
+        axis=2,
     )
     rows = cells.shape[1]
     return jnp.concatenate(

time: 95.1 us -> 90.6 us (0.953)
  starting transfers between devices: 42.8 us -> 37.2 us
  blocking collectives: 24 us -> 29.2 us
  waiting for transfers between devices: 10.3 us -> 6.67 us
    ppermute x4 -> x2, starting transfers between devices: 10.9 us -> 5.33 us  [shifted(): return lax.ppermute(piece, axes, pairs)]
    all_gather x0 -> x1, blocking collectives: none -> 5.35 us  [halo_exchange(): every = lax.all_gather(edges, 'gy', axis=0)]
    ppermute x4 -> x2, waiting for transfers between devices: 8.69 us -> 5.05 us  [shifted(): return lax.ppermute(piece, axes, pairs)]
  transfers between devices with their start and end apart: 7 -> 5, of which waited for: 5 -> 4; matrix products, arithmetic and copies ran while one was open for 1% -> 0% of each run, Pallas kernels for 0% -> 0%
where the time goes in v6:
time: 90.6 us; the launch traced here: 89.2 us
  starting transfers between devices  37.2 us (41%)
  blocking collectives  29.2 us (32%)
  other arithmetic  8.31 us (9%)
  waiting for transfers between devices  6.67 us (7%)
  local copies, waits for them, and re-layouts  6.51 us (7%)
  between operations  0.96 us (1%)
    ppermute x3, starting transfers between devices, passed_along(): return lax.ppermute(value, axis, pairs)  31.9 us
    all_gather x1, blocking collectives, whole_partition(): return lax.all_gather(every, 'gx', axis=count, tiled=True)  14.1 us
    all_gather x1, blocking collectives, halo_exchange(): every = lax.all_gather(edges, 'gy', axis=0)  5.35 us
    ppermute x2, starting transfers between devices, shifted(): return lax.ppermute(piece, axes, pairs)  5.33 us
    all_gather x1, blocking collectives, per_device(): received = lax.all_gather(packed, 'group', axis=0, tiled=True)  5.25 us
    ppermute x2, waiting for transfers between devices, shifted(): return lax.ppermute(piece, axes, pairs)  5.05 us
    all_gather x1, blocking collectives, whole_partition(): every = lax.all_gather(block, 'gy', axis=count + 1, tiled=True)  4.59 us
    scatter-add x1, other arithmetic, per_device(): jnp.zeros((3, cell_count), jnp.float32).at[:, wall_index].add(speed_parts)  2.51 us
  transfers between devices with their start and end apart: 5, of which 4 were waited for; matrix products, arithmetic and copies ran while one was open for 0% of the time, Pallas kernels for 0%

profile of v6, /device:TPU:0, one launch (start us, length us, event | category | flops | bytes accessed | tf_op | source)
XLA Modules:
  0.0 89.2 jit_solution(3552876389127035898)
XLA Ops:
  0.7 0.7 fusion.58
  1.4 1.0 %fusion.44 = (f32[2,8,128]{2,1,0:T(8,128)S(1)}, f32[2,8,128]{2,1,0:T(8,128)S(1)}, f32[2,8,128]{2,1,0:T(8,128)S(1)}, f32[2,8,128]{2,1,0:T(8,128)S(1)}) fusion(bf16[19,2,8,128]{3,2,1,0:T(8,128)(2,1)} %param.43, f32[19]{0:T(128)} %constant.215, f32[19]{0:T(128)} %constant.216, f32[19]{0:T(128)} %constant.217), kind=kLoop, calls=%fused_computation.128 | loop fusion | flops 303104 | bytes 110820 | tf_op jit(solution)/shard_map/reduce_sum | solution.py:96
  2.4 1.1 %fusion.49 = bf16[19,2,8,128]{3,2,1,0:T(8,128)(2,1)S(1)} fusion(bf16[19,2,8,128]{3,2,1,0:T(8,128)(2,1)} %param.43, f32[2,8,128]{2,1,0:T(8,128)S(1)} %get-tuple-element.295, f32[2,8,128]{2,1,0:T(8,128)S(1)} %get-tuple-element.298, f32[19]{0:T(128)} %constant.217, f32[2,8,128]{2,1,0:T(8,128)S(1)} %get-tuple-element.297, f32[19]{0:T(128)} %constant.216, ...), kind=kLoop, calls=%fused_computation.133 | loop fusion | flops 739328 | bytes 196913 | tf_op jit(solution)/shard_map/convert_element_type | solution.py:412
  3.6 5.3 %all-gather = bf16[40,2,2,128]{3,2,1,0:T(2,128)(2,1)S(1)} all-gather(bf16[20,2,2,128]{3,2,1,0:T(2,128)(2,1)S(1)} %fusion.55), channel_id=2, replica_groups=mesh['group'=4,'gx'=4,'gy'=2] {'gy'}, dimensions={0}, use_global_device_ids=true | all-gather | bytes 61440 | tf_op jit(solution)/shard_map/all_gather | solution.py:58
  9.0 0.1 broadcast_select_fusion
  9.0 0.1 pad_maximum_fusion.1
  9.2 4.0 %collective-permute-start = (bf16[20,1,10,128]{3,2,1,0:T(8,128)(2,1)S(1)}, bf16[20,1,10,128]{3,2,1,0:T(8,128)(2,1)S(1)}, u32[]{:S(2)}, u32[]{:S(2)}) collective-permute-start(bf16[20,1,10,128]{3,2,1,0:T(8,128)(2,1)S(1)} %get-tuple-element.343), channel_id=1, source_target_pairs={{0,2},{1,3},{2,4},{3,5},{4,6},{5,7},{6,8},{7,9},{8,10},{9,11},{10,... | collective-permute-start | bytes 153608 | tf_op jit(solution)/shard_map/ppermute | solution.py:53
  13.2 1.3 %collective-permute-start.1 = (bf16[20,1,10,128]{3,2,1,0:T(8,128)(2,1)S(1)}, bf16[20,1,10,128]{3,2,1,0:T(8,128)(2,1)S(1)}, u32[]{:S(2)}, u32[]{:S(2)}) collective-permute-start(bf16[20,1,10,128]{3,2,1,0:T(8,128)(2,1)S(1)} %get-tuple-element.344), channel_id=1, source_target_pairs={{2,0},{3,1},{4,2},{5,3},{6,4},{7,5},{8,6},{9,7},{10,8},{11,9},{12,... | collective-permute-start | bytes 153608 | tf_op jit(solution)/shard_map/ppermute | solution.py:53
  14.6 0.7 collective-permute-done
  15.3 4.4 %collective-permute-done.1 = bf16[20,1,10,128]{3,2,1,0:T(8,128)(2,1)S(1)} collective-permute-done((bf16[20,1,10,128]{3,2,1,0:T(8,128)(2,1)S(1)}, bf16[20,1,10,128]{3,2,1,0:T(8,128)(2,1)S(1)}, u32[]{:S(2)}, u32[]{:S(2)}) %collective-permute-start.1) | collective-permute-done | bytes 51232 | tf_op jit(solution)/shard_map/ppermute | solution.py:53
  19.6 0.5 fusion.31
  20.1 0.1 slice.286
  20.3 0.5 copy-done.2
  20.8 2.6 %conditional.5 = (f32[4,6,128]{2,0,1:T(4,128)S(1)}) conditional(s32[]{:T(128)} %convert_element_type.59, () %tuple.44, (f32[19,1,1,1]{0,3,2,1:T(1,128)S(1)}, f32[19,1,1,1]{0,3,2,1:T(1,128)S(1)}, f32[19,1,1,1]{0,3,2,1:T(1,128)S(1)}, f32[1,4,10,130]{3,2,1,0:T(8,128)S(1)}, f32[19,4,10,130]{3,2,1,0:T(8,128)S(1)}, ...), branch_computations={%region_4.5_spmd, %region_5.9_spmd.clone} | conditional | flops 646950 | bytes 2346576 | solution.py:441
  20.9 0.1 select_select_fusion.2
  21.1 0.1 fusion.9
  21.2 0.1 slice.217
  21.4 0.1 slice.216
  21.4 0.1 copy-done.16
  21.6 0.2 multiply_reduce_fusion.2
  21.9 0.4 copy.80
  22.3 1.0 %gather_fusion = f32[512,3]{1,0:T(8,128)S(1)} fusion(f32[3,2048]{0,1:T(8,128)S(1)} %copy.80, s32[1024]{0:T(1024)S(1)} %pad_clamp_fusion), kind=kCustom, calls=%fused_computation.3 | custom fusion | bytes 14336 | tf_op jit(solution)/shard_map/cond/branch_1_fun/gather | solution.py:427
  23.3 0.1 copy.81
  23.5 5.2 %all_gather.17 = f32[16,6,128]{2,1,0:T(8,128)S(1)} all-gather(f32[4,6,128]{2,1,0:T(8,128)S(1)} %copy.84), channel_id=1, replica_groups=mesh['group'=4,'gx'=4,'gy'=2] {'group'}, dimensions={0}, use_global_device_ids=true | all-gather | bytes 61440 | tf_op jit(solution)/shard_map/all_gather | solution.py:447
  28.7 1.1 %conditional.6 = (f32[2,128,8,128]{3,1,2,0:T(8,128)}, f32[3,4,4,128]{3,1,0,2:T(4,128)S(1)}) conditional(s32[]{:T(128)} %convert_element_type.65, () %tuple.43, (f32[3,1,1,256]{3,2,1,0:T(1,128)S(1)}, s32[1,1,2,8]{3,2,1,0:T(2,128)S(1)}, f32[16,6,128]{2,1,0:T(8,128)S(1)}, s32[256]{0:T(256)S(1)}, f32[3,4,4,128]{3,2,1,0:T(4,128)S(1)}) %tuple.146), branch_computations={%region_9.10_spmd, %region_10.14_spmd} | conditional | flops 15213152 | bytes 2600664 | solution.py:462
  28.8 1.1 %broadcast.282 = f32[2,128,8,128]{3,1,2,0:T(8,128)} broadcast(f32[]{:T(128)} %constant.158.clone), dimensions={} | broadcast | bytes 1048580 | tf_op jit(solution)/shard_map/broadcast.21
  29.9 4.6 %all_gather.18 = f32[4,4,8,128]{3,1,0,2:T(4,128)S(1)} all-gather(f32[4,4,4,128]{3,1,0,2:T(4,128)S(1)} %pad_maximum_fusion.2), channel_id=1, replica_groups=mesh['group'=4,'gx'=4,'gy'=2] {'gy'}, dimensions={2}, use_global_device_ids=true | all-gather | bytes 98304 | tf_op jit(solution)/shard_map/all_gather | solution.py:356
  34.5 14.1 %all_gather.19 = f32[4,16,8,128]{3,2,0,1:T(8,128)S(1)} all-gather(f32[4,4,8,128]{3,2,0,1:T(8,128)S(1)} %copy.89), channel_id=1, replica_groups=mesh['group'=4,'gx'=4,'gy'=2] {'gx'}, dimensions={1}, use_global_device_ids=true | all-gather | bytes 327680 | tf_op jit(solution)/shard_map/all_gather | solution.py:357
  48.6 0.6 dynamic-slice_select_fusion
  49.2 0.6 conditional.8
  49.2 0.6 broadcast.295
  49.8 0.7 constant_dynamic-slice_fusion.2
  50.6 31.9 %collective-permute-start.3 = (f32[4,3,128]{2,1,0:T(4,128)S(1)}, f32[4,3,128]{2,1,0:T(4,128)S(1)}, u32[]{:S(2)}, u32[]{:S(2)}) collective-permute-start(f32[4,3,128]{2,1,0:T(4,128)S(1)} %get-tuple-element.349), channel_id=1, source_target_pairs={{0,16},{8,24},{16,0},{24,8},{1,17},{9,25},{17,1},{25,9},{2,18},{10... | collective-permute-start | bytes 18440 | tf_op jit(solution)/shard_map/ppermute | solution.py:78
  82.5 0.9 %collective-permute-done.2 = f32[4,3,128]{2,1,0:T(4,128)S(1)} collective-permute-done((f32[4,3,128]{2,1,0:T(4,128)S(1)}, f32[4,3,128]{2,1,0:T(4,128)S(1)}, u32[]{:S(2)}, u32[]{:S(2)}) %collective-permute-start.2) | collective-permute-done | bytes 6176 | tf_op jit(solution)/shard_map/ppermute | solution.py:78
  83.4 0.7 collective-permute-done.3
  84.1 0.1 copy.93
  84.3 2.5 %scatter_custom_fusion.3 = f32[3,2048]{0,1:T(8,128)S(1)} fusion(s32[512]{0:T(512)S(1)} %bitcast.174, f32[512,3]{1,0:T(8,128)S(1)} %copy.93, f32[]{:T(128)} %constant.179.clone.1), kind=kCustom, calls=%fused_computation.115 | custom fusion | flops 1536 | bytes 24580 | tf_op jit(solution)/shard_map/scatter-add | solution.py:516
  86.8 1.8 %conditional.9 = (bf16[19,2,8,128]{3,2,1,0:T(8,128)(2,1)S(1)}) conditional(s32[]{:T(128)} %convert_element_type.59, () %tuple.40, (f32[1,4,10,130]{3,2,1,0:T(8,128)S(1)}, f32[19,1,1,1]{0,3,2,1:T(1,128)S(1)}, f32[19,1,1,1]{0,3,2,1:T(1,128)S(1)}, f32[19,1,1,1]{0,3,2,1:T(1,128)S(1)}, f32[19,1,1,1]{0,3,2,1:T(1,128)S(1)}, ...), branch_computations={%region_20.21_spmd, %region_21.22_spmd.clone} | conditional | flops 1056324 | bytes 4268820 | solution.py:518
  86.9 0.1 select_select_fusion.1
  87.0 0.1 fusion.1
  87.2 0.2 select_select_fusion
  87.4 0.1 fusion
  87.5 0.1 slice.241
  87.7 0.3 copy.94
  88.0 0.1 slice.240
  88.1 0.1 slice.255
  88.2 0.4 fusion.6
  88.6 0.6 copy-done
  (67 shorter events, 0.5 us)
Async XLA Ops:
  0.6 13.9 %copy-start.6 = (f32[4,4,128]{2,1,0:T(4,128)S(1)}, f32[4,4,128]{2,1,0:T(4,128)}, u32[]{:S(2)}) copy-start(f32[4,4,128]{2,1,0:T(4,128)} %param.47) | copy-start | bytes 24580
  0.6 13.9 %copy-start.7 = (s32[4,4,128]{2,1,0:T(4,128)S(1)}, s32[4,4,128]{2,1,0:T(4,128)}, u32[]{:S(2)}) copy-start(s32[4,4,128]{2,1,0:T(4,128)} %param.48) | copy-start | bytes 24580
  9.2 6.1 %collective-permute-start = (bf16[20,1,10,128]{3,2,1,0:T(8,128)(2,1)S(1)}, bf16[20,1,10,128]{3,2,1,0:T(8,128)(2,1)S(1)}, u32[]{:S(2)}, u32[]{:S(2)}) collective-permute-start(bf16[20,1,10,128]{3,2,1,0:T(8,128)(2,1)S(1)} %get-tuple-element.343), channel_id=1, source_target_pairs={{0,2},{1,3},{2,4},{3,5},{4,6},{5,7},{6,8},{7,9},{8,10},{9,11},{10,... | collective-permute-start | bytes 153608 | tf_op jit(solution)/shard_map/ppermute | solution.py:53
  13.2 6.4 %collective-permute-start.1 = (bf16[20,1,10,128]{3,2,1,0:T(8,128)(2,1)S(1)}, bf16[20,1,10,128]{3,2,1,0:T(8,128)(2,1)S(1)}, u32[]{:S(2)}, u32[]{:S(2)}) collective-permute-start(bf16[20,1,10,128]{3,2,1,0:T(8,128)(2,1)S(1)} %get-tuple-element.344), channel_id=1, source_target_pairs={{2,0},{3,1},{4,2},{5,3},{6,4},{7,5},{8,6},{9,7},{10,8},{11,9},{12,... | collective-permute-start | bytes 153608 | tf_op jit(solution)/shard_map/ppermute | solution.py:53
  20.1 0.7 copy-start.2
  20.1 0.7 copy-start.4
  20.1 0.7 copy-start.5
  20.1 0.7 copy-start.8
  20.8 7.9 %copy-start.1 = (f32[3,4,4,128]{3,2,1,0:T(4,128)S(1)}, f32[3,4,4,128]{3,2,1,0:T(4,128)}, u32[]{:S(2)}) copy-start(f32[3,4,4,128]{3,2,1,0:T(4,128)} %param.46) | copy-start | bytes 73732
  20.8 7.9 %copy-start.10 = (s32[1,1,256]{2,1,0:T(1,128)S(1)}, s32[1,1,256]{2,1,0:T(1,128)}, u32[]{:S(2)}) copy-start(s32[1,1,256]{2,1,0:T(1,128)} %param.50) | copy-start | bytes 3076
  20.8 7.9 %copy-start.12 = (f32[3,1,1,256]{3,2,1,0:T(1,128)S(1)}, f32[3,1,1,256]{3,2,1,0:T(1,128)}, u32[]{:S(2)}) copy-start(f32[3,1,1,256]{3,2,1,0:T(1,128)} %param.51) | copy-start | bytes 9220
  20.8 7.9 %copy-start.13 = (s32[1,1,2,8]{3,2,1,0:T(2,128)S(1)}, s32[1,1,2,8]{3,2,1,0:T(2,128)}, u32[]{:S(2)}) copy-start(s32[1,1,2,8]{3,2,1,0:T(2,128)} %param.52) | copy-start | bytes 196
  20.9 0.7 copy-start.16
  20.9 0.7 copy-start.17
  20.9 0.7 copy-start.18
  28.7 19.8 %copy-start.3 = (f32[24,24]{1,0:T(8,128)S(1)}, f32[24,24]{1,0:T(8,128)}, u32[]{:S(2)}) copy-start(f32[24,24]{1,0:T(8,128)} %param.49) | copy-start | bytes 6916
  29.9 19.4 %copy-start.11 = (s32[1,1,256]{2,1,0:T(1,128)S(1)}, s32[1,1,256]{2,1,0:T(1,128)}, u32[]{:S(2)}) copy-start(s32[1,1,256]{2,1,0:T(1,128)} %param.50) | copy-start | bytes 3076
  29.9 19.4 %copy-start.14 = (s32[1,1,2,8]{3,2,1,0:T(2,128)S(1)}, s32[1,1,2,8]{3,2,1,0:T(2,128)}, u32[]{:S(2)}) copy-start(s32[1,1,2,8]{3,2,1,0:T(2,128)} %param.52) | copy-start | bytes 196
  49.8 37.0 %copy-start.9 = (f32[19,1,1,1]{0,3,2,1:T(1,128)S(1)}, f32[19,1,1,1]{0,3,2,1:T(1,128)}, u32[]{:S(2)}) copy-start(f32[19,1,1,1]{0,3,2,1:T(1,128)} %constant.197.clone) | copy-start | bytes 232
  50.6 32.8 %collective-permute-start.2 = (f32[4,3,128]{2,1,0:T(4,128)S(1)}, f32[4,3,128]{2,1,0:T(4,128)S(1)}, u32[]{:S(2)}, u32[]{:S(2)}) collective-permute-start(f32[4,3,128]{2,1,0:T(4,128)S(1)} %get-tuple-element.347), channel_id=1, source_target_pairs={{0,8},{8,16},{16,24},{24,0},{1,9},{9,17},{17,25},{25,1},{2,10},{10... | collective-permute-start | bytes 18440 | tf_op jit(solution)/shard_map/ppermute | solution.py:78
  50.6 33.5 %collective-permute-start.3 = (f32[4,3,128]{2,1,0:T(4,128)S(1)}, f32[4,3,128]{2,1,0:T(4,128)S(1)}, u32[]{:S(2)}, u32[]{:S(2)}) collective-permute-start(f32[4,3,128]{2,1,0:T(4,128)S(1)} %get-tuple-element.349), channel_id=1, source_target_pairs={{0,16},{8,24},{16,0},{24,8},{1,17},{9,25},{17,1},{25,9},{2,18},{10... | collective-permute-start | bytes 18440 | tf_op jit(solution)/shard_map/ppermute | solution.py:78
  82.5 1.6 %collective-permute-start.4 = (f32[4,3,128]{2,1,0:T(4,128)S(1)}, f32[4,3,128]{2,1,0:T(4,128)S(1)}, u32[]{:S(2)}, u32[]{:S(2)}) collective-permute-start(f32[4,3,128]{2,1,0:T(4,128)S(1)} %get-tuple-element.348), channel_id=1, source_target_pairs={{0,24},{8,0},{16,8},{24,16},{1,25},{9,1},{17,9},{25,17},{2,26},{10... | collective-permute-start | bytes 18440 | tf_op jit(solution)/shard_map/ppermute | solution.py:78
  87.4 0.8 copy-start.15
  88.6 0.6 copy-start

commit v7 on v6

--- a/solution.py
+++ b/solution.py
@@ -158,6 +158,11 @@
     return result.astype(jnp.bfloat16)
 
 
+def slot_table(tile_lists, tile_slots):
+    slots = lax.broadcasted_iota(jnp.int32, (tile_slots, tile_lists.size), 0)
+    return (slots == tile_lists.reshape(1, -1)).astype(jnp.float32)
+
+
 def basis_weights(received, node_positions, tile_lists):
     tile_count = tile_lists.shape[0]
     tile_width = received.shape[2]
@@ -168,20 +173,20 @@
         offset = nodes_at[component][:, :, None, None] - chosen[:, None, :, 3 + component, :]
         distance = distance + offset * offset
     kernel = 1.0 / jnp.sqrt(1.0 + distance / (basis_radius * basis_radius))
-    column = jnp.sum(kernel, axis=1)
-    totals = (
-        jnp.zeros((received.shape[0], tile_width), jnp.float32)
-        .at[tile_lists.reshape(-1)]
-        .add(column.reshape(-1, tile_width))
-    )
-    return (kernel / totals[tile_lists][:, None, :, :], chosen)
-
-
-def map_tractions(weights, chosen, node_index, nodes_total):
+    column = jnp.sum(kernel, axis=1).reshape(-1, tile_width)
+    table = slot_table(tile_lists, received.shape[0])
+    exact = lax.Precision.HIGHEST
+    totals = jnp.einsum("tk,kp->tp", table, column, precision=exact)
+    listed = jnp.einsum("tk,tp->kp", table, totals, precision=exact)
+    listed = listed.reshape(tile_count, tile_lists.shape[1], tile_width)
+    return (kernel / listed[:, None, :, :], chosen)
+
+
+def map_tractions(weights, chosen, node_index, base):
     mapped = jnp.einsum(
         "anbp,abcp->can", weights, chosen[:, :, 0:3, :], precision=lax.Precision.HIGHEST
     )
-    return jnp.zeros((3, nodes_total), jnp.float32).at[:, node_index].add(mapped.reshape(3, -1))
+    return base.at[0:3, node_index].add(mapped.reshape(3, -1))
 
 
 def map_speeds(weights, solution_flat, node_index, tile_lists, tile_slots):
@@ -189,36 +194,12 @@
     tile_width = weights.shape[1]
     at_nodes = solution_flat[:, node_index].reshape(3, tile_count, tile_width)
     contrib = jnp.einsum("anbp,can->abcp", weights, at_nodes, precision=lax.Precision.HIGHEST)
-    return (
-        jnp.zeros((tile_slots, 3, tile_width), jnp.float32)
-        .at[tile_lists.reshape(-1)]
-        .add(contrib.reshape(-1, 3, tile_width))
-    )
-
-
-def element_sum(widened, matrix):
-    span_cells = widened.shape[1] - 2
-    across_cells = widened.shape[2] - 2
-    deep_cells = widened.shape[3]
-    widened_z = jnp.pad(widened, ((0, 0), (0, 0), (0, 0), (0, 1)))
-    corners = [(a, b, c) for a in (0, 1) for b in (0, 1) for c in (0, 1)]
-    gathered = jnp.concatenate(
-        [
-            widened_z[0:3, a : a + span_cells + 1, b : b + across_cells + 1, c : c + deep_cells]
-            for a, b, c in corners
-        ],
-        axis=0,
-    )
-    element_scale = widened_z[3, 0 : span_cells + 1, 0 : across_cells + 1, 0:deep_cells]
-    forces = element_scale * jnp.einsum(
-        "ij,jabc->iabc", matrix, gathered, precision=lax.Precision.HIGHEST
-    )
-    summed = jnp.zeros((3, span_cells + 2, across_cells + 2, deep_cells + 1), jnp.float32)
-    for corner_id, (a, b, c) in enumerate(corners):
-        summed = summed.at[
-            :, a : a + span_cells + 1, b : b + across_cells + 1, c : c + deep_cells
-        ].add(forces[3 * corner_id : 3 * corner_id + 3])
-    return summed[:, 1 : span_cells + 1, 1 : across_cells + 1, 0:deep_cells]
+    return jnp.einsum(
+        "tk,kcp->tcp",
+        slot_table(tile_lists, tile_slots),
+        contrib.reshape(-1, 3, tile_width),
+        precision=lax.Precision.HIGHEST,
+    )
 
 
 def apply_rows(matrix_ref, values_ref, stiff_ref, out_ref):
@@ -451,17 +432,19 @@
     nodes_total = body_load.shape[1] * body_load.shape[2] * body_load.shape[3]
     weight_shape = (tile_lists.shape[0], TILE, tile_lists.shape[1], TILE)
 
-    def struct_map(received_all):
+    stiffness = elem_scale * elem_active.astype(jnp.float32)
+    base = jnp.concatenate([body_load, stiffness[None]], axis=0).reshape(4, nodes_total)
+
+    def struct_map(operands):
+        received_all, flat = operands
         weights, chosen = basis_weights(received_all, node_positions, tile_lists)
-        mapped = map_tractions(weights, chosen, node_index, nodes_total)
-        return (weights, body_load + mapped.reshape(body_load.shape))
-
-    def struct_quiet(received_all):
-        return (jnp.zeros(weight_shape, jnp.float32), jnp.zeros_like(body_load))
-
-    weights, right_side = lax.cond(is_struct, struct_map, struct_quiet, received)
-    stiffness = elem_scale * elem_active.astype(jnp.float32)
-    joined = whole_partition(jnp.concatenate([right_side, stiffness[None]], axis=0))
+        return (weights, map_tractions(weights, chosen, node_index, flat))
+
+    def struct_quiet(operands):
+        return (jnp.zeros(weight_shape, jnp.float32), operands[1])
+
+    weights, joined = lax.cond(is_struct, struct_map, struct_quiet, (received, base))
+    joined = whole_partition(joined.reshape((4,) + body_load.shape[1:]))
     whole_side = joined[0:3]
     stiffness = joined[3]
     rows, cols = body_load.shape[1], body_load.shape[2]

time: 90.6 us -> 2130 us (23.51); the launches traced: 89.2 us -> 2090 us
  starting transfers between devices: 37.2 us -> 2040 us
    ppermute x3, starting transfers between devices: 31.9 us -> 2040 us  [passed_along(): return lax.ppermute(value, axis, pairs)]
where the time goes in v7:
time: 2130 us; the launch traced here: 2090 us
  starting transfers between devices  2040 us (96%)
  blocking collectives  29.3 us (1%)
    ppermute x3, starting transfers between devices, passed_along(): return lax.ppermute(value, axis, pairs)  2040 us
  transfers between devices with their start and end apart: 5, of which 4 were waited for; matrix products, arithmetic and copies ran while one was open for 0% of the time, Pallas kernels for 0%

profile of v7, /device:TPU:0, one launch (start us, length us, event | category | flops | bytes accessed | tf_op | source)
XLA Modules:
  0.0 2093.9 jit_solution(13889657833379127204)
XLA Ops:
  0.7 0.7 fusion.59
  1.4 1.0 fusion.46
  2.4 1.1 fusion.51
  3.6 5.3 all-gather
  9.0 0.1 broadcast_select_fusion.1
  9.1 0.1 pad_maximum_fusion.1
  9.2 4.0 collective-permute-start
  13.2 1.3 collective-permute-start.1
  14.6 0.6 collective-permute-done
  15.3 4.4 collective-permute-done.1
  19.6 0.5 fusion.33
  20.2 0.1 slice.296
  20.3 0.5 copy-done.2
  20.8 2.6 conditional.5
  20.9 0.1 select_select_fusion.2
  21.1 0.1 fusion.14
  21.2 0.1 slice.217
  21.4 0.1 slice.216
  21.4 0.1 copy-done.14
  21.6 0.2 multiply_reduce_fusion.2
  21.9 0.4 copy.99
  22.3 1.0 gather_fusion
  23.3 0.1 copy.100
  23.5 5.2 all_gather.17
  28.7 2.4 conditional.6
  28.7 1.3 copy.120
  30.1 1.1 broadcast.236
  31.2 1.6 copy.106
  32.7 4.6 all_gather.18
  37.4 14.1 all_gather.19
  51.5 0.6 dynamic-slice_select_fusion
  52.1 0.1 collective-permute-start.2
  52.2 2035.0 %collective-permute-start.3 = (f32[4,3,128]{2,0,1:T(4,128)S(1)}, f32[4,3,128]{2,0,1:T(4,128)S(1)}, u32[]{:S(2)}, u32[]{:S(2)}) collective-permute-start(f32[4,3,128]{2,0,1:T(4,128)S(1)} %get-tuple-element.396), channel_id=1, source_target_pairs={{0,16},{8,24},{16,0},{24,8},{1,17},{9,25},{17,1},{25,9},{2,18},{10... | collective-permute-start | bytes 18440 | tf_op jit(solution)/shard_map/ppermute | solution.py:78
  2087.2 0.9 collective-permute-done.2
  2088.1 0.7 collective-permute-done.3
  2088.8 0.1 copy.119
  2088.9 2.5 scatter_custom_fusion
  2091.5 1.8 conditional.9
  2091.5 0.1 select_select_fusion.1
  2091.7 0.1 fusion.1
  2091.8 0.2 select_select_fusion
  2092.0 0.1 fusion
  2092.2 0.1 slice.241
  2092.3 0.3 copy.112
  2092.7 0.1 slice.240
  2092.7 0.1 slice.265
  2092.8 0.4 fusion.6
  2093.2 0.6 copy-done
  (63 shorter events, 0.5 us)
Async XLA Ops:
  0.6 13.9 copy-start.1
  0.6 13.9 copy-start.7
  0.7 13.9 copy-start.8
  9.2 6.1 collective-permute-start
  13.2 6.4 collective-permute-start.1
  20.1 0.7 copy-start.2
  20.1 0.7 copy-start.5
  20.1 0.7 copy-start.6
  20.1 0.7 copy-start.9
  20.8 7.9 copy-start.10
  20.8 7.9 copy-start.11
  20.8 7.9 copy-start.12
  20.9 0.7 copy-start.14
  20.9 0.7 copy-start.15
  20.9 0.7 copy-start.16
  31.2 20.3 copy-start.4
  52.1 2036.0 %collective-permute-start.2 = (f32[4,3,128]{2,0,1:T(4,128)S(1)}, f32[4,3,128]{2,0,1:T(4,128)S(1)}, u32[]{:S(2)}, u32[]{:S(2)}) collective-permute-start(f32[4,3,128]{2,0,1:T(4,128)S(1)} %get-tuple-element.394), channel_id=1, source_target_pairs={{0,8},{8,16},{16,24},{24,0},{1,9},{9,17},{17,25},{25,1},{2,10},{10... | collective-permute-start | bytes 18440 | tf_op jit(solution)/shard_map/ppermute | solution.py:78
  52.2 2036.6 %collective-permute-start.3 = (f32[4,3,128]{2,0,1:T(4,128)S(1)}, f32[4,3,128]{2,0,1:T(4,128)S(1)}, u32[]{:S(2)}, u32[]{:S(2)}) collective-permute-start(f32[4,3,128]{2,0,1:T(4,128)S(1)} %get-tuple-element.396), channel_id=1, source_target_pairs={{0,16},{8,24},{16,0},{24,8},{1,17},{9,25},{17,1},{25,9},{2,18},{10... | collective-permute-start | bytes 18440 | tf_op jit(solution)/shard_map/ppermute | solution.py:78
  2087.2 1.6 collective-permute-start.4
  2092.0 0.8 copy-start.13
  2093.2 0.6 copy-start

commit v8 on v7

--- a/solution.py
+++ b/solution.py
@@ -186,7 +186,7 @@
     mapped = jnp.einsum(
         "anbp,abcp->can", weights, chosen[:, :, 0:3, :], precision=lax.Precision.HIGHEST
     )
-    return base.at[0:3, node_index].add(mapped.reshape(3, -1))
+    return base.at[:, node_index].add(mapped.reshape(3, -1))
 
 
 def map_speeds(weights, solution_flat, node_index, tile_lists, tile_slots):
@@ -433,7 +433,6 @@
     weight_shape = (tile_lists.shape[0], TILE, tile_lists.shape[1], TILE)
 
     stiffness = elem_scale * elem_active.astype(jnp.float32)
-    base = jnp.concatenate([body_load, stiffness[None]], axis=0).reshape(4, nodes_total)
 
     def struct_map(operands):
         received_all, flat = operands
@@ -443,8 +442,11 @@
     def struct_quiet(operands):
         return (jnp.zeros(weight_shape, jnp.float32), operands[1])
 
-    weights, joined = lax.cond(is_struct, struct_map, struct_quiet, (received, base))
-    joined = whole_partition(joined.reshape((4,) + body_load.shape[1:]))
+    weights, right_side = lax.cond(
+        is_struct, struct_map, struct_quiet, (received, body_load.reshape(3, nodes_total))
+    )
+    right_side = right_side.reshape(body_load.shape)
+    joined = whole_partition(jnp.concatenate([right_side, stiffness[None]], axis=0))
     whole_side = joined[0:3]
     stiffness = joined[3]
     rows, cols = body_load.shape[1], body_load.shape[2]

time: 2130 us -> 86.8 us (0.04); the launches traced: 2090 us -> 85.5 us
  starting transfers between devices: 2040 us -> 33 us
    ppermute x3, starting transfers between devices: 2040 us -> 27.7 us  [passed_along(): return lax.ppermute(value, axis, pairs)]
where the time goes in v8:
time: 86.8 us; the launch traced here: 85.5 us
  starting transfers between devices  33 us (38%)
  blocking collectives  29.3 us (34%)
  other arithmetic  8.32 us (10%)
  local copies, waits for them, and re-layouts  7.39 us (9%)
  waiting for transfers between devices  6.27 us (7%)
  between operations  0.97 us (1%)
    ppermute x3, starting transfers between devices, passed_along(): return lax.ppermute(value, axis, pairs)  27.7 us
    all_gather x1, blocking collectives, whole_partition(): return lax.all_gather(every, 'gx', axis=count, tiled=True)  14.1 us
    all_gather x1, blocking collectives, halo_exchange(): every = lax.all_gather(edges, 'gy', axis=0)  5.35 us
    ppermute x2, starting transfers between devices, shifted(): return lax.ppermute(piece, axes, pairs)  5.33 us
    all_gather x1, blocking collectives, per_device(): received = lax.all_gather(packed, 'group', axis=0, tiled=True)  5.25 us
    ppermute x2, waiting for transfers between devices, shifted(): return lax.ppermute(piece, axes, pairs)  4.67 us
    all_gather x1, blocking collectives, whole_partition(): every = lax.all_gather(block, 'gy', axis=count + 1, tiled=True)  4.59 us
    scatter-add x1, other arithmetic, per_device(): jnp.zeros((3, cell_count), jnp.float32).at[:, wall_index].add(speed_parts)  2.51 us
  transfers between devices with their start and end apart: 5, of which 4 were waited for; matrix products, arithmetic and copies ran while one was open for 0% of the time, Pallas kernels for 0%

profile of v8, /device:TPU:0, one launch (start us, length us, event | category | flops | bytes accessed | tf_op | source)
XLA Modules:
  0.0 85.5 jit_solution(1910108471453370541)
XLA Ops:
  0.7 0.7 fusion.59
  1.4 1.0 %fusion.46 = (f32[2,8,128]{2,1,0:T(8,128)S(1)}, f32[2,8,128]{2,1,0:T(8,128)S(1)}, f32[2,8,128]{2,1,0:T(8,128)S(1)}, f32[2,8,128]{2,1,0:T(8,128)S(1)}) fusion(bf16[19,2,8,128]{3,2,1,0:T(8,128)(2,1)} %param.43, f32[19]{0:T(128)} %constant.205, f32[19]{0:T(128)} %constant.206, f32[19]{0:T(128)} %constant.207), kind=kLoop, calls=%fused_computation.127 | loop fusion | flops 303104 | bytes 110820 | tf_op jit(solution)/shard_map/reduce_sum | solution.py:96
  2.4 1.1 %fusion.51 = bf16[19,2,8,128]{3,2,1,0:T(8,128)(2,1)S(1)} fusion(bf16[19,2,8,128]{3,2,1,0:T(8,128)(2,1)} %param.43, f32[2,8,128]{2,1,0:T(8,128)S(1)} %get-tuple-element.292, f32[2,8,128]{2,1,0:T(8,128)S(1)} %get-tuple-element.295, f32[19]{0:T(128)} %constant.207, f32[2,8,128]{2,1,0:T(8,128)S(1)} %get-tuple-element.294, f32[19]{0:T(128)} %constant.206, ...), kind=kLoop, calls=%fused_computation.132 | loop fusion | flops 739328 | bytes 196913 | tf_op jit(solution)/shard_map/convert_element_type | solution.py:393
  3.6 5.3 %all-gather = bf16[40,2,2,128]{3,2,1,0:T(2,128)(2,1)S(1)} all-gather(bf16[20,2,2,128]{3,2,1,0:T(2,128)(2,1)S(1)} %fusion.57), channel_id=2, replica_groups=mesh['group'=4,'gx'=4,'gy'=2] {'gy'}, dimensions={0}, use_global_device_ids=true | all-gather | bytes 61440 | tf_op jit(solution)/shard_map/all_gather | solution.py:58
  9.0 0.1 broadcast_select_fusion
  9.1 0.1 pad_maximum_fusion.1
  9.2 4.0 %collective-permute-start = (bf16[20,1,10,128]{3,2,1,0:T(8,128)(2,1)S(1)}, bf16[20,1,10,128]{3,2,1,0:T(8,128)(2,1)S(1)}, u32[]{:S(2)}, u32[]{:S(2)}) collective-permute-start(bf16[20,1,10,128]{3,2,1,0:T(8,128)(2,1)S(1)} %get-tuple-element.340), channel_id=1, source_target_pairs={{0,2},{1,3},{2,4},{3,5},{4,6},{5,7},{6,8},{7,9},{8,10},{9,11},{10,... | collective-permute-start | bytes 153608 | tf_op jit(solution)/shard_map/ppermute | solution.py:53
  13.2 1.3 %collective-permute-start.1 = (bf16[20,1,10,128]{3,2,1,0:T(8,128)(2,1)S(1)}, bf16[20,1,10,128]{3,2,1,0:T(8,128)(2,1)S(1)}, u32[]{:S(2)}, u32[]{:S(2)}) collective-permute-start(bf16[20,1,10,128]{3,2,1,0:T(8,128)(2,1)S(1)} %get-tuple-element.341), channel_id=1, source_target_pairs={{2,0},{3,1},{4,2},{5,3},{6,4},{7,5},{8,6},{9,7},{10,8},{11,9},{12,... | collective-permute-start | bytes 153608 | tf_op jit(solution)/shard_map/ppermute | solution.py:53
  14.6 0.4 copy.101
  15.0 0.3 collective-permute-done
  15.3 4.4 %collective-permute-done.1 = bf16[20,1,10,128]{3,2,1,0:T(8,128)(2,1)S(1)} collective-permute-done((bf16[20,1,10,128]{3,2,1,0:T(8,128)(2,1)S(1)}, bf16[20,1,10,128]{3,2,1,0:T(8,128)(2,1)S(1)}, u32[]{:S(2)}, u32[]{:S(2)}) %collective-permute-start.1) | collective-permute-done | bytes 51232 | tf_op jit(solution)/shard_map/ppermute | solution.py:53
  19.6 0.5 fusion.33
  20.2 0.1 slice.284
  20.3 0.5 copy-done.2
  20.8 4.2 %conditional.5 = (f32[4,6,128]{2,0,1:T(4,128)S(1)}) conditional(s32[]{:T(128)} %convert_element_type.61, () %tuple.43, (f32[19,1,1,1]{0,3,2,1:T(1,128)S(1)}, f32[19,1,1,1]{0,3,2,1:T(1,128)S(1)}, f32[19,1,1,1]{0,3,2,1:T(1,128)S(1)}, f32[1,4,10,130]{3,2,1,0:T(8,128)S(1)}, f32[19,4,10,130]{3,2,1,0:T(8,128)S(1)}, ...), branch_computations={%region_4.5_spmd, %region_5.9_spmd.clone} | conditional | flops 646950 | bytes 2346576 | solution.py:422
  20.9 0.1 select_select_fusion.2
  21.1 0.1 fusion.14
  21.2 0.1 slice.217
  21.4 0.1 slice.216
  21.4 0.1 copy-done.13
  21.6 0.2 multiply_reduce_fusion.2
  21.9 0.4 copy.98
  22.3 1.6 %gather_fusion = f32[512,3]{1,0:T(8,128)} fusion(f32[3,2048]{0,1:T(8,128)S(1)} %copy.98, s32[1024]{0:T(1024)S(1)} %pad_clamp_fusion.1), kind=kCustom, calls=%fused_computation.2 | custom fusion | bytes 14336 | tf_op jit(solution)/shard_map/cond/branch_1_fun/gather | solution.py:408
  23.9 1.1 %copy.99 = f32[3,4,128]{2,1,0:T(4,128)S(1)} copy(f32[3,4,128]{0,2,1:T(8,128)} %bitcast.147) | data formatting | bytes 12288 | tf_op jit(solution)/shard_map/cond/branch_1_fun/concatenate | solution.py:419
  25.0 5.2 %all_gather.17 = f32[16,6,128]{2,1,0:T(8,128)S(1)} all-gather(f32[4,6,128]{2,1,0:T(8,128)S(1)} %copy.102), channel_id=1, replica_groups=mesh['group'=4,'gx'=4,'gy'=2] {'group'}, dimensions={0}, use_global_device_ids=true | all-gather | bytes 61440 | tf_op jit(solution)/shard_map/all_gather | solution.py:428
  30.3 1.1 %conditional.6 = (f32[2,128,8,128]{3,1,2,0:T(8,128)}, f32[3,2048]{0,1:T(8,128)S(1)}) conditional(s32[]{:T(128)} %convert_element_type.67, f32[3,2048]{0,1:T(8,128)S(1)} %bitcast.136, (f32[3,1,1,256]{3,2,1,0:T(1,128)S(1)}, s32[1,1,2,8]{3,2,1,0:T(2,128)S(1)}, f32[16,6,128]{2,1,0:T(8,128)S(1)}, s32[256]{0:T(256)S(1)}, f32[3,2048]{0,1:T(8,128)S(1)}) %tuple.142), branch_computations={%region_9.10_spmd, %region_10.13_spmd} | conditional | flops 15991856 | bytes 2414224 | solution.py:445
  30.3 1.1 %broadcast.235 = f32[2,128,8,128]{3,1,2,0:T(8,128)} broadcast(f32[]{:T(128)} %constant.150.clone), dimensions={} | broadcast | bytes 1048580 | tf_op jit(solution)/shard_map/broadcast.18
  31.4 0.3 copy.115
  31.7 4.6 %all_gather.18 = f32[4,4,8,128]{3,1,0,2:T(4,128)S(1)} all-gather(f32[4,4,4,128]{3,1,0,2:T(4,128)S(1)} %copy.104), channel_id=1, replica_groups=mesh['group'=4,'gx'=4,'gy'=2] {'gy'}, dimensions={2}, use_global_device_ids=true | all-gather | bytes 98304 | tf_op jit(solution)/shard_map/all_gather | solution.py:337
  36.4 14.1 %all_gather.19 = f32[4,16,8,128]{3,2,0,1:T(8,128)S(1)} all-gather(f32[4,4,8,128]{3,2,0,1:T(8,128)S(1)} %copy.105), channel_id=1, replica_groups=mesh['group'=4,'gx'=4,'gy'=2] {'gx'}, dimensions={1}, use_global_device_ids=true | all-gather | bytes 327680 | tf_op jit(solution)/shard_map/all_gather | solution.py:338
  50.5 0.6 dynamic-slice_select_fusion
  51.1 0.1 collective-permute-start.2
  51.2 27.6 %collective-permute-start.3 = (f32[4,3,128]{2,0,1:T(4,128)S(1)}, f32[4,3,128]{2,0,1:T(4,128)S(1)}, u32[]{:S(2)}, u32[]{:S(2)}) collective-permute-start(f32[4,3,128]{2,0,1:T(4,128)S(1)} %get-tuple-element.346), channel_id=1, source_target_pairs={{0,16},{8,24},{16,0},{24,8},{1,17},{9,25},{17,1},{25,9},{2,18},{10... | collective-permute-start | bytes 18440 | tf_op jit(solution)/shard_map/ppermute | solution.py:78
  78.8 0.9 %collective-permute-done.2 = f32[4,3,128]{2,0,1:T(4,128)S(1)} collective-permute-done((f32[4,3,128]{2,0,1:T(4,128)S(1)}, f32[4,3,128]{2,0,1:T(4,128)S(1)}, u32[]{:S(2)}, u32[]{:S(2)}) %collective-permute-start.2) | collective-permute-done | bytes 6176 | tf_op jit(solution)/shard_map/ppermute | solution.py:78
  79.7 0.7 collective-permute-done.3
  80.4 0.1 copy.116
  80.6 2.5 %scatter_custom_fusion.1 = f32[3,2048]{0,1:T(8,128)S(1)} fusion(s32[512]{0:T(512)S(1)} %bitcast.177, f32[512,3]{1,0:T(8,128)S(1)} %bitcast.148, f32[]{:T(128)} %constant.169.clone.1), kind=kCustom, calls=%fused_computation.114 | custom fusion | flops 1536 | bytes 24580 | tf_op jit(solution)/shard_map/scatter-add | solution.py:501
  83.1 1.8 %conditional.9 = (bf16[19,2,8,128]{3,2,1,0:T(8,128)(2,1)S(1)}) conditional(s32[]{:T(128)} %convert_element_type.61, () %tuple.40, (f32[1,4,10,130]{3,2,1,0:T(8,128)S(1)}, f32[19,1,1,1]{0,3,2,1:T(1,128)S(1)}, f32[19,1,1,1]{0,3,2,1:T(1,128)S(1)}, f32[19,1,1,1]{0,3,2,1:T(1,128)S(1)}, f32[19,1,1,1]{0,3,2,1:T(1,128)S(1)}, ...), branch_computations={%region_18.19_spmd, %region_19.20_spmd.clone} | conditional | flops 1056324 | bytes 4268820 | solution.py:503
  83.2 0.1 select_select_fusion.1
  83.3 0.1 fusion.1
  83.5 0.2 select_select_fusion
  83.7 0.1 fusion
  83.8 0.1 slice.241
  83.9 0.3 copy.110
  84.3 0.1 slice.240
  84.4 0.1 slice.253
  84.5 0.4 fusion.6
  84.9 0.6 copy-done
  (63 shorter events, 0.5 us)
Async XLA Ops:
  0.6 13.9 %copy-start.6 = (f32[4,4,128]{2,1,0:T(4,128)S(1)}, f32[4,4,128]{2,1,0:T(4,128)}, u32[]{:S(2)}) copy-start(f32[4,4,128]{2,1,0:T(4,128)} %param.47) | copy-start | bytes 24580
  0.6 13.9 %copy-start.7 = (s32[4,4,128]{2,1,0:T(4,128)S(1)}, s32[4,4,128]{2,1,0:T(4,128)}, u32[]{:S(2)}) copy-start(s32[4,4,128]{2,1,0:T(4,128)} %param.48) | copy-start | bytes 24580
  0.7 13.9 %copy-start.1 = (f32[3,4,4,128]{3,2,1,0:T(4,128)S(1)}, f32[3,4,4,128]{3,2,1,0:T(4,128)}, u32[]{:S(2)}) copy-start(f32[3,4,4,128]{3,2,1,0:T(4,128)} %param.46) | copy-start | bytes 73732
  9.2 6.1 %collective-permute-start = (bf16[20,1,10,128]{3,2,1,0:T(8,128)(2,1)S(1)}, bf16[20,1,10,128]{3,2,1,0:T(8,128)(2,1)S(1)}, u32[]{:S(2)}, u32[]{:S(2)}) collective-permute-start(bf16[20,1,10,128]{3,2,1,0:T(8,128)(2,1)S(1)} %get-tuple-element.340), channel_id=1, source_target_pairs={{0,2},{1,3},{2,4},{3,5},{4,6},{5,7},{6,8},{7,9},{8,10},{9,11},{10,... | collective-permute-start | bytes 153608 | tf_op jit(solution)/shard_map/ppermute | solution.py:53
  13.2 6.4 %collective-permute-start.1 = (bf16[20,1,10,128]{3,2,1,0:T(8,128)(2,1)S(1)}, bf16[20,1,10,128]{3,2,1,0:T(8,128)(2,1)S(1)}, u32[]{:S(2)}, u32[]{:S(2)}) collective-permute-start(bf16[20,1,10,128]{3,2,1,0:T(8,128)(2,1)S(1)} %get-tuple-element.341), channel_id=1, source_target_pairs={{2,0},{3,1},{4,2},{5,3},{6,4},{7,5},{8,6},{9,7},{10,8},{11,9},{12,... | collective-permute-start | bytes 153608 | tf_op jit(solution)/shard_map/ppermute | solution.py:53
  20.1 0.7 copy-start.2
  20.1 0.7 copy-start.4
  20.1 0.7 copy-start.5
  20.2 0.7 copy-start.8
  20.8 9.5 %copy-start.9 = (s32[1,1,256]{2,1,0:T(1,128)S(1)}, s32[1,1,256]{2,1,0:T(1,128)}, u32[]{:S(2)}) copy-start(s32[1,1,256]{2,1,0:T(1,128)} %param.50) | copy-start | bytes 3076
  20.8 9.5 %copy-start.10 = (f32[3,1,1,256]{3,2,1,0:T(1,128)S(1)}, f32[3,1,1,256]{3,2,1,0:T(1,128)}, u32[]{:S(2)}) copy-start(f32[3,1,1,256]{3,2,1,0:T(1,128)} %param.51) | copy-start | bytes 9220
  20.8 9.5 %copy-start.11 = (s32[1,1,2,8]{3,2,1,0:T(2,128)S(1)}, s32[1,1,2,8]{3,2,1,0:T(2,128)}, u32[]{:S(2)}) copy-start(s32[1,1,2,8]{3,2,1,0:T(2,128)} %param.52) | copy-start | bytes 196
  20.9 0.7 copy-start.13
  20.9 0.7 copy-start.14
  20.9 0.7 copy-start.15
  31.4 19.1 %copy-start.3 = (f32[24,24]{1,0:T(8,128)S(1)}, f32[24,24]{1,0:T(8,128)}, u32[]{:S(2)}) copy-start(f32[24,24]{1,0:T(8,128)} %param.49) | copy-start | bytes 6916
  51.1 28.6 %collective-permute-start.2 = (f32[4,3,128]{2,0,1:T(4,128)S(1)}, f32[4,3,128]{2,0,1:T(4,128)S(1)}, u32[]{:S(2)}, u32[]{:S(2)}) collective-permute-start(f32[4,3,128]{2,0,1:T(4,128)S(1)} %get-tuple-element.344), channel_id=1, source_target_pairs={{0,8},{8,16},{16,24},{24,0},{1,9},{9,17},{17,25},{25,1},{2,10},{10... | collective-permute-start | bytes 18440 | tf_op jit(solution)/shard_map/ppermute | solution.py:78
  51.2 29.3 %collective-permute-start.3 = (f32[4,3,128]{2,0,1:T(4,128)S(1)}, f32[4,3,128]{2,0,1:T(4,128)S(1)}, u32[]{:S(2)}, u32[]{:S(2)}) collective-permute-start(f32[4,3,128]{2,0,1:T(4,128)S(1)} %get-tuple-element.346), channel_id=1, source_target_pairs={{0,16},{8,24},{16,0},{24,8},{1,17},{9,25},{17,1},{25,9},{2,18},{10... | collective-permute-start | bytes 18440 | tf_op jit(solution)/shard_map/ppermute | solution.py:78
  78.8 1.6 %collective-permute-start.4 = (f32[4,3,128]{2,0,1:T(4,128)S(1)}, f32[4,3,128]{2,0,1:T(4,128)S(1)}, u32[]{:S(2)}, u32[]{:S(2)}) collective-permute-start(f32[4,3,128]{2,0,1:T(4,128)S(1)} %get-tuple-element.345), channel_id=1, source_target_pairs={{0,24},{8,0},{16,8},{24,16},{1,25},{9,1},{17,9},{25,17},{2,26},{10... | collective-permute-start | bytes 18440 | tf_op jit(solution)/shard_map/ppermute | solution.py:78
  83.7 0.8 copy-start.12
  84.9 0.6 copy-start

commit v9 on v8

--- a/solution.py
+++ b/solution.py
@@ -189,10 +189,14 @@
     return base.at[:, node_index].add(mapped.reshape(3, -1))
 
 
-def map_speeds(weights, solution_flat, node_index, tile_lists, tile_slots):
+def map_speeds(weights, solution_block, node_index, tile_lists, tile_slots):
     tile_count = weights.shape[0]
     tile_width = weights.shape[1]
-    at_nodes = solution_flat[:, node_index].reshape(3, tile_count, tile_width)
+    rows, cols, deep = solution_block.shape[1:]
+    at_nodes = solution_block[
+        :, node_index // (cols * deep), node_index // deep % cols, node_index % deep
+    ]
+    at_nodes = at_nodes.reshape(3, tile_count, tile_width)
     contrib = jnp.einsum("anbp,can->abcp", weights, at_nodes, precision=lax.Precision.HIGHEST)
     return jnp.einsum(
         "tk,kcp->tcp",
@@ -239,9 +243,9 @@
         for corner_id, (a, b, c) in enumerate(corners):
             for component in range(3):
                 line = 3 * corner_id + component
-                force = matrix_ref[line * 24] * gathered[0]
+                force = matrix_ref[line, 0] * gathered[0]
                 for other in range(1, 24):
-                    force = force + matrix_ref[line * 24 + other] * gathered[other]
+                    force = force + matrix_ref[line, other] * gathered[other]
                 out_ref[component, pl.ds(row + a, step)] += behind(scale * force, b, c)
         return carry
 
@@ -258,9 +262,10 @@
     return jnp.sum(value, axis=1, keepdims=True)
 
 
-def solve_kernel(matrix_ref, side_ref, stiff_ref, out_ref, ahead_ref, image_ref, dir_ref, img_ref):
+def solve_kernel(matrix_ref, joined_ref, out_ref, ahead_ref, image_ref, dir_ref, img_ref):
+    stiff_ref = joined_ref.at[3]
     span_cells = stiff_ref.shape[0]
-    residual = side_ref[...]
+    residual = joined_ref[0:3]
     ahead_ref[:, 0:span_cells] = residual
     ahead_ref[:, span_cells : span_cells + 1] = jnp.zeros_like(residual[:, 0:1])
     apply_rows(matrix_ref, ahead_ref, stiff_ref, image_ref)
@@ -286,29 +291,29 @@
             norm_now = norm_next
 
 
-def partition_solve_kernel(side, stiffness, matrix):
-    span_cells, across_cells, deep_cells = stiffness.shape
+def partition_solve_kernel(joined, matrix):
+    span_cells, across_cells, deep_cells = joined.shape[1:]
     cells = span_cells * across_cells * deep_cells
     wide = (3, span_cells + 1, across_cells, deep_cells)
+    side = (3, span_cells, across_cells, deep_cells)
     return pl.pallas_call(
         solve_kernel,
-        out_shape=jax.ShapeDtypeStruct(side.shape, jnp.float32),
+        out_shape=jax.ShapeDtypeStruct(side, jnp.float32),
         in_specs=[
             pl.BlockSpec(memory_space=pltpu.SMEM),
-            pl.BlockSpec(memory_space=pltpu.VMEM),
             pl.BlockSpec(memory_space=pltpu.VMEM),
         ],
         out_specs=pl.BlockSpec(memory_space=pltpu.VMEM),
         scratch_shapes=[
             pltpu.VMEM(wide, jnp.float32),
             pltpu.VMEM(wide, jnp.float32),
-            pltpu.VMEM(side.shape, jnp.float32),
-            pltpu.VMEM(side.shape, jnp.float32),
+            pltpu.VMEM(side, jnp.float32),
+            pltpu.VMEM(side, jnp.float32),
         ],
         cost_estimate=pl.CostEstimate(
             flops=ITERS * 2 * 24 * 24 * cells, transcendentals=0, bytes_accessed=28 * cells
         ),
-    )(matrix.reshape(-1), side, stiffness)
+    )(matrix, joined)
 
 
 def partition_operator(values, stiffness, matrix):
@@ -327,7 +332,7 @@
         cost_estimate=pl.CostEstimate(
             flops=2 * 24 * 24 * cells, transcendentals=0, bytes_accessed=28 * cells
         ),
-    )(matrix.reshape(-1), widened, stiffness)
+    )(matrix, widened, stiffness)
     return summed[:, :span_cells]
 
 
@@ -469,15 +474,15 @@
         whole_solution = lax.cond(
             is_struct,
             lambda operands: partition_solve_kernel(*operands),
-            lambda operands: jnp.zeros_like(operands[0]),
-            (whole_side, stiffness, elem_matrix),
+            lambda operands: jnp.zeros_like(operands[0][0:3]),
+            (joined, elem_matrix),
         )
     solution = jnp.where(is_struct, own_part(whole_solution, rows, cols), 0.0)
     tile_slots = received.shape[0]
 
     def struct_back(operands):
         return map_speeds(
-            operands[0], operands[1].reshape(3, nodes_total), node_index, tile_lists, tile_slots
+            operands[0], operands[1], node_index, tile_lists, tile_slots
         )
 
     back_terms = lax.cond(

time: 86.8 us -> 87.2 us (level)
  no operation moved by 1% of the time
where the time goes in v9:
time: 87.2 us; the launch traced here: 85.9 us
  starting transfers between devices  33.4 us (38%)
  blocking collectives  29.3 us (34%)
  other arithmetic  8.32 us (10%)
  local copies, waits for them, and re-layouts  7.39 us (8%)
  waiting for transfers between devices  6.27 us (7%)
  between operations  0.97 us (1%)
    ppermute x3, starting transfers between devices, passed_along(): return lax.ppermute(value, axis, pairs)  28.1 us
    all_gather x1, blocking collectives, whole_partition(): return lax.all_gather(every, 'gx', axis=count, tiled=True)  14.1 us
    all_gather x1, blocking collectives, halo_exchange(): every = lax.all_gather(edges, 'gy', axis=0)  5.35 us
    ppermute x2, starting transfers between devices, shifted(): return lax.ppermute(piece, axes, pairs)  5.33 us
    all_gather x1, blocking collectives, per_device(): received = lax.all_gather(packed, 'group', axis=0, tiled=True)  5.25 us
    ppermute x2, waiting for transfers between devices, shifted(): return lax.ppermute(piece, axes, pairs)  4.67 us
    all_gather x1, blocking collectives, whole_partition(): every = lax.all_gather(block, 'gy', axis=count + 1, tiled=True)  4.59 us
    scatter-add x1, other arithmetic, per_device(): jnp.zeros((3, cell_count), jnp.float32).at[:, wall_index].add(speed_parts)  2.51 us
  transfers between devices with their start and end apart: 5, of which 4 were waited for; matrix products, arithmetic and copies ran while one was open for 0% of the time, Pallas kernels for 0%

profile of v9, /device:TPU:0, one launch (start us, length us, event | category | flops | bytes accessed | tf_op | source)
XLA Modules:
  0.0 85.9 jit_solution(4256660861999057813)
XLA Ops:
  0.7 0.7 fusion.66
  1.4 1.0 %fusion.53 = (f32[2,8,128]{2,1,0:T(8,128)S(1)}, f32[2,8,128]{2,1,0:T(8,128)S(1)}, f32[2,8,128]{2,1,0:T(8,128)S(1)}, f32[2,8,128]{2,1,0:T(8,128)S(1)}) fusion(bf16[19,2,8,128]{3,2,1,0:T(8,128)(2,1)} %param.43, f32[19]{0:T(128)} %constant.254, f32[19]{0:T(128)} %constant.255, f32[19]{0:T(128)} %constant.256), kind=kLoop, calls=%fused_computation.145 | loop fusion | flops 303104 | bytes 110820 | tf_op jit(solution)/shard_map/reduce_sum | solution.py:96
  2.4 1.1 %fusion.58 = bf16[19,2,8,128]{3,2,1,0:T(8,128)(2,1)S(1)} fusion(bf16[19,2,8,128]{3,2,1,0:T(8,128)(2,1)} %param.43, f32[2,8,128]{2,1,0:T(8,128)S(1)} %get-tuple-element.283, f32[2,8,128]{2,1,0:T(8,128)S(1)} %get-tuple-element.286, f32[19]{0:T(128)} %constant.256, f32[2,8,128]{2,1,0:T(8,128)S(1)} %get-tuple-element.285, f32[19]{0:T(128)} %constant.255, ...), kind=kLoop, calls=%fused_computation.150 | loop fusion | flops 739328 | bytes 196913 | tf_op jit(solution)/shard_map/convert_element_type | solution.py:398
  3.6 5.3 %all-gather = bf16[40,2,2,128]{3,2,1,0:T(2,128)(2,1)S(1)} all-gather(bf16[20,2,2,128]{3,2,1,0:T(2,128)(2,1)S(1)} %fusion.64), channel_id=2, replica_groups=mesh['group'=4,'gx'=4,'gy'=2] {'gy'}, dimensions={0}, use_global_device_ids=true | all-gather | bytes 61440 | tf_op jit(solution)/shard_map/all_gather | solution.py:58
  9.0 0.1 broadcast_select_fusion
  9.1 0.1 pad_maximum_fusion.1
  9.2 4.0 %collective-permute-start = (bf16[20,1,10,128]{3,2,1,0:T(8,128)(2,1)S(1)}, bf16[20,1,10,128]{3,2,1,0:T(8,128)(2,1)S(1)}, u32[]{:S(2)}, u32[]{:S(2)}) collective-permute-start(bf16[20,1,10,128]{3,2,1,0:T(8,128)(2,1)S(1)} %get-tuple-element.331), channel_id=1, source_target_pairs={{0,2},{1,3},{2,4},{3,5},{4,6},{5,7},{6,8},{7,9},{8,10},{9,11},{10,... | collective-permute-start | bytes 153608 | tf_op jit(solution)/shard_map/ppermute | solution.py:53
  13.2 1.3 %collective-permute-start.1 = (bf16[20,1,10,128]{3,2,1,0:T(8,128)(2,1)S(1)}, bf16[20,1,10,128]{3,2,1,0:T(8,128)(2,1)S(1)}, u32[]{:S(2)}, u32[]{:S(2)}) collective-permute-start(bf16[20,1,10,128]{3,2,1,0:T(8,128)(2,1)S(1)} %get-tuple-element.332), channel_id=1, source_target_pairs={{2,0},{3,1},{4,2},{5,3},{6,4},{7,5},{8,6},{9,7},{10,8},{11,9},{12,... | collective-permute-start | bytes 153608 | tf_op jit(solution)/shard_map/ppermute | solution.py:53
  14.6 0.4 copy.99
  15.0 0.3 collective-permute-done
  15.3 4.4 %collective-permute-done.1 = bf16[20,1,10,128]{3,2,1,0:T(8,128)(2,1)S(1)} collective-permute-done((bf16[20,1,10,128]{3,2,1,0:T(8,128)(2,1)S(1)}, bf16[20,1,10,128]{3,2,1,0:T(8,128)(2,1)S(1)}, u32[]{:S(2)}, u32[]{:S(2)}) %collective-permute-start.1) | collective-permute-done | bytes 51232 | tf_op jit(solution)/shard_map/ppermute | solution.py:53
  19.6 0.5 fusion.40
  20.2 0.1 slice.273
  20.3 0.5 copy-done.2
  20.8 4.2 %conditional.5 = (f32[4,6,128]{2,0,1:T(4,128)S(1)}) conditional(s32[]{:T(128)} %convert_element_type.61, () %tuple.43, (f32[19,1,1,1]{0,3,2,1:T(1,128)S(1)}, f32[19,1,1,1]{0,3,2,1:T(1,128)S(1)}, f32[19,1,1,1]{0,3,2,1:T(1,128)S(1)}, f32[1,4,10,130]{3,2,1,0:T(8,128)S(1)}, f32[19,4,10,130]{3,2,1,0:T(8,128)S(1)}, ...), branch_computations={%region_4.5_spmd, %region_5.9_spmd.clone} | conditional | flops 646950 | bytes 2346576 | solution.py:427
  20.9 0.1 select_select_fusion.2
  21.1 0.1 fusion.21
  21.2 0.1 slice.207
  21.4 0.1 slice.206
  21.4 0.1 copy-done.13
  21.6 0.2 multiply_reduce_fusion.2
  21.9 0.4 copy.96
  22.3 1.6 %gather_fusion = f32[512,3]{1,0:T(8,128)} fusion(f32[3,2048]{0,1:T(8,128)S(1)} %copy.96, s32[1024]{0:T(1024)S(1)} %pad_clamp_fusion), kind=kCustom, calls=%fused_computation.2 | custom fusion | bytes 14336 | tf_op jit(solution)/shard_map/cond/branch_1_fun/gather | solution.py:413
  23.9 1.1 %copy.97 = f32[3,4,128]{2,1,0:T(4,128)S(1)} copy(f32[3,4,128]{0,2,1:T(8,128)} %bitcast.143) | data formatting | bytes 12288 | tf_op jit(solution)/shard_map/cond/branch_1_fun/concatenate | solution.py:424
  25.0 5.2 %all_gather.17 = f32[16,6,128]{2,1,0:T(8,128)S(1)} all-gather(f32[4,6,128]{2,1,0:T(8,128)S(1)} %copy.100), channel_id=1, replica_groups=mesh['group'=4,'gx'=4,'gy'=2] {'group'}, dimensions={0}, use_global_device_ids=true | all-gather | bytes 61440 | tf_op jit(solution)/shard_map/all_gather | solution.py:433
  30.3 1.1 %conditional.6 = (f32[2,128,8,128]{3,1,2,0:T(8,128)}, f32[3,2048]{0,1:T(8,128)S(1)}) conditional(s32[]{:T(128)} %convert_element_type.67, f32[3,2048]{0,1:T(8,128)S(1)} %bitcast.133, (f32[3,1,1,256]{3,2,1,0:T(1,128)S(1)}, s32[1,1,2,8]{3,2,1,0:T(2,128)S(1)}, f32[16,6,128]{2,1,0:T(8,128)S(1)}, s32[256]{0:T(256)S(1)}, f32[3,2048]{0,1:T(8,128)S(1)}) %tuple.142), branch_computations={%region_9.10_spmd, %region_10.13_spmd} | conditional | flops 15991856 | bytes 2414224 | solution.py:450
  30.3 1.1 %broadcast.253 = f32[2,128,8,128]{3,1,2,0:T(8,128)} broadcast(f32[]{:T(128)} %constant.191.clone), dimensions={} | broadcast | bytes 1048580 | tf_op jit(solution)/shard_map/broadcast.18
  31.4 0.3 copy.112
  31.7 4.6 %all_gather.18 = f32[4,4,8,128]{3,1,0,2:T(4,128)S(1)} all-gather(f32[4,4,4,128]{3,1,0,2:T(4,128)S(1)} %copy.102), channel_id=1, replica_groups=mesh['group'=4,'gx'=4,'gy'=2] {'gy'}, dimensions={2}, use_global_device_ids=true | all-gather | bytes 98304 | tf_op jit(solution)/shard_map/all_gather | solution.py:342
  36.4 14.1 %all_gather.19 = f32[4,16,8,128]{3,2,0,1:T(8,128)S(1)} all-gather(f32[4,4,8,128]{3,2,0,1:T(8,128)S(1)} %copy.103), channel_id=1, replica_groups=mesh['group'=4,'gx'=4,'gy'=2] {'gx'}, dimensions={1}, use_global_device_ids=true | all-gather | bytes 327680 | tf_op jit(solution)/shard_map/all_gather | solution.py:343
  50.5 0.6 dynamic-slice_select_fusion
  51.1 0.1 collective-permute-start.2
  51.2 28.0 %collective-permute-start.3 = (f32[4,3,128]{2,0,1:T(4,128)S(1)}, f32[4,3,128]{2,0,1:T(4,128)S(1)}, u32[]{:S(2)}, u32[]{:S(2)}) collective-permute-start(f32[4,3,128]{2,0,1:T(4,128)S(1)} %get-tuple-element.337), channel_id=1, source_target_pairs={{0,16},{8,24},{16,0},{24,8},{1,17},{9,25},{17,1},{25,9},{2,18},{10... | collective-permute-start | bytes 18440 | tf_op jit(solution)/shard_map/ppermute | solution.py:78
  79.2 0.9 %collective-permute-done.2 = f32[4,3,128]{2,0,1:T(4,128)S(1)} collective-permute-done((f32[4,3,128]{2,0,1:T(4,128)S(1)}, f32[4,3,128]{2,0,1:T(4,128)S(1)}, u32[]{:S(2)}, u32[]{:S(2)}) %collective-permute-start.2) | collective-permute-done | bytes 6176 | tf_op jit(solution)/shard_map/ppermute | solution.py:78
  80.1 0.7 collective-permute-done.3
  80.8 0.1 copy.113
  81.0 2.5 %scatter_custom_fusion.1 = f32[3,2048]{0,1:T(8,128)S(1)} fusion(s32[512]{0:T(512)S(1)} %bitcast.173, f32[512,3]{1,0:T(8,128)S(1)} %bitcast.144, f32[]{:T(128)} %constant.218.clone.1), kind=kCustom, calls=%fused_computation.132 | custom fusion | flops 1536 | bytes 24580 | tf_op jit(solution)/shard_map/scatter-add | solution.py:506
  83.5 1.8 %conditional.9 = (bf16[19,2,8,128]{3,2,1,0:T(8,128)(2,1)S(1)}) conditional(s32[]{:T(128)} %convert_element_type.61, () %tuple.40, (f32[1,4,10,130]{3,2,1,0:T(8,128)S(1)}, f32[19,1,1,1]{0,3,2,1:T(1,128)S(1)}, f32[19,1,1,1]{0,3,2,1:T(1,128)S(1)}, f32[19,1,1,1]{0,3,2,1:T(1,128)S(1)}, f32[19,1,1,1]{0,3,2,1:T(1,128)S(1)}, ...), branch_computations={%region_18.19_spmd, %region_19.20_spmd.clone} | conditional | flops 1056324 | bytes 4268820 | solution.py:508
  83.6 0.1 select_select_fusion.1
  83.7 0.1 fusion.1
  83.9 0.2 select_select_fusion
  84.1 0.1 fusion
  84.2 0.1 slice.231
  84.3 0.3 copy.107
  84.7 0.1 slice.230
  84.8 0.1 slice.242
  84.9 0.4 fusion.6
  85.3 0.6 copy-done
  (63 shorter events, 0.5 us)
Async XLA Ops:
  0.6 13.9 %copy-start.6 = (f32[4,4,128]{2,1,0:T(4,128)S(1)}, f32[4,4,128]{2,1,0:T(4,128)}, u32[]{:S(2)}) copy-start(f32[4,4,128]{2,1,0:T(4,128)} %param.47) | copy-start | bytes 24580
  0.6 13.9 %copy-start.7 = (s32[4,4,128]{2,1,0:T(4,128)S(1)}, s32[4,4,128]{2,1,0:T(4,128)}, u32[]{:S(2)}) copy-start(s32[4,4,128]{2,1,0:T(4,128)} %param.48) | copy-start | bytes 24580
  0.7 13.9 %copy-start.1 = (f32[3,4,4,128]{3,2,1,0:T(4,128)S(1)}, f32[3,4,4,128]{3,2,1,0:T(4,128)}, u32[]{:S(2)}) copy-start(f32[3,4,4,128]{3,2,1,0:T(4,128)} %param.46) | copy-start | bytes 73732
  9.2 6.1 %collective-permute-start = (bf16[20,1,10,128]{3,2,1,0:T(8,128)(2,1)S(1)}, bf16[20,1,10,128]{3,2,1,0:T(8,128)(2,1)S(1)}, u32[]{:S(2)}, u32[]{:S(2)}) collective-permute-start(bf16[20,1,10,128]{3,2,1,0:T(8,128)(2,1)S(1)} %get-tuple-element.331), channel_id=1, source_target_pairs={{0,2},{1,3},{2,4},{3,5},{4,6},{5,7},{6,8},{7,9},{8,10},{9,11},{10,... | collective-permute-start | bytes 153608 | tf_op jit(solution)/shard_map/ppermute | solution.py:53
  13.2 6.4 %collective-permute-start.1 = (bf16[20,1,10,128]{3,2,1,0:T(8,128)(2,1)S(1)}, bf16[20,1,10,128]{3,2,1,0:T(8,128)(2,1)S(1)}, u32[]{:S(2)}, u32[]{:S(2)}) collective-permute-start(bf16[20,1,10,128]{3,2,1,0:T(8,128)(2,1)S(1)} %get-tuple-element.332), channel_id=1, source_target_pairs={{2,0},{3,1},{4,2},{5,3},{6,4},{7,5},{8,6},{9,7},{10,8},{11,9},{12,... | collective-permute-start | bytes 153608 | tf_op jit(solution)/shard_map/ppermute | solution.py:53
  20.1 0.7 copy-start.2
  20.1 0.7 copy-start.4
  20.1 0.7 copy-start.5
  20.2 0.7 copy-start.8
  20.8 9.5 %copy-start.9 = (s32[1,1,256]{2,1,0:T(1,128)S(1)}, s32[1,1,256]{2,1,0:T(1,128)}, u32[]{:S(2)}) copy-start(s32[1,1,256]{2,1,0:T(1,128)} %param.50) | copy-start | bytes 3076
  20.8 9.5 %copy-start.10 = (f32[3,1,1,256]{3,2,1,0:T(1,128)S(1)}, f32[3,1,1,256]{3,2,1,0:T(1,128)}, u32[]{:S(2)}) copy-start(f32[3,1,1,256]{3,2,1,0:T(1,128)} %param.51) | copy-start | bytes 9220
  20.8 9.5 %copy-start.11 = (s32[1,1,2,8]{3,2,1,0:T(2,128)S(1)}, s32[1,1,2,8]{3,2,1,0:T(2,128)}, u32[]{:S(2)}) copy-start(s32[1,1,2,8]{3,2,1,0:T(2,128)} %param.52) | copy-start | bytes 196
  20.9 0.7 copy-start.13
  20.9 0.7 copy-start.14
  20.9 0.7 copy-start.15
  31.4 19.1 %copy-start.3 = (f32[24,24]{1,0:T(8,128)S(1)}, f32[24,24]{1,0:T(8,128)}, u32[]{:S(2)}) copy-start(f32[24,24]{1,0:T(8,128)} %param.49) | copy-start | bytes 6916
  51.1 29.0 %collective-permute-start.2 = (f32[4,3,128]{2,0,1:T(4,128)S(1)}, f32[4,3,128]{2,0,1:T(4,128)S(1)}, u32[]{:S(2)}, u32[]{:S(2)}) collective-permute-start(f32[4,3,128]{2,0,1:T(4,128)S(1)} %get-tuple-element.335), channel_id=1, source_target_pairs={{0,8},{8,16},{16,24},{24,0},{1,9},{9,17},{17,25},{25,1},{2,10},{10... | collective-permute-start | bytes 18440 | tf_op jit(solution)/shard_map/ppermute | solution.py:78
  51.2 29.7 %collective-permute-start.3 = (f32[4,3,128]{2,0,1:T(4,128)S(1)}, f32[4,3,128]{2,0,1:T(4,128)S(1)}, u32[]{:S(2)}, u32[]{:S(2)}) collective-permute-start(f32[4,3,128]{2,0,1:T(4,128)S(1)} %get-tuple-element.337), channel_id=1, source_target_pairs={{0,16},{8,24},{16,0},{24,8},{1,17},{9,25},{17,1},{25,9},{2,18},{10... | collective-permute-start | bytes 18440 | tf_op jit(solution)/shard_map/ppermute | solution.py:78
  79.2 1.6 %collective-permute-start.4 = (f32[4,3,128]{2,0,1:T(4,128)S(1)}, f32[4,3,128]{2,0,1:T(4,128)S(1)}, u32[]{:S(2)}, u32[]{:S(2)}) collective-permute-start(f32[4,3,128]{2,0,1:T(4,128)S(1)} %get-tuple-element.336), channel_id=1, source_target_pairs={{0,24},{8,0},{16,8},{24,16},{1,25},{9,1},{17,9},{25,17},{2,26},{10... | collective-permute-start | bytes 18440 | tf_op jit(solution)/shard_map/ppermute | solution.py:78
  84.1 0.8 copy-start.12
  85.3 0.6 copy-start

commit v10 on v9

--- a/solution.py
+++ b/solution.py
@@ -192,11 +192,8 @@
 def map_speeds(weights, solution_block, node_index, tile_lists, tile_slots):
     tile_count = weights.shape[0]
     tile_width = weights.shape[1]
-    rows, cols, deep = solution_block.shape[1:]
-    at_nodes = solution_block[
-        :, node_index // (cols * deep), node_index // deep % cols, node_index % deep
-    ]
-    at_nodes = at_nodes.reshape(3, tile_count, tile_width)
+    flat = solution_block.reshape(3, -1)
+    at_nodes = flat[:, node_index].reshape(3, tile_count, tile_width)
     contrib = jnp.einsum("anbp,can->abcp", weights, at_nodes, precision=lax.Precision.HIGHEST)
     return jnp.einsum(
         "tk,kcp->tcp",
@@ -208,7 +205,7 @@
 
 def apply_rows(matrix_ref, values_ref, stiff_ref, out_ref):
     span_cells, across_cells, deep_cells = stiff_ref.shape
-    step = 2 if span_cells % 2 == 0 else 1
+    step = 4 if span_cells % 4 == 0 else 1
     shape = (step, across_cells, deep_cells)
     across_at = lax.broadcasted_iota(jnp.int32, shape, 1)
     deep_at = lax.broadcasted_iota(jnp.int32, shape, 2)

time: 87.2 us -> 81.2 us (0.931)
  starting transfers between devices: 33.4 us -> 27.5 us
    ppermute x3, starting transfers between devices: 28.1 us -> 22.1 us  [passed_along(): return lax.ppermute(value, axis, pairs)]
where the time goes in v10:
time: 81.2 us; the launch traced here: 79.9 us
  blocking collectives  29.3 us (36%)
  starting transfers between devices  27.5 us (34%)
  other arithmetic  8.32 us (10%)
  local copies, waits for them, and re-layouts  7.39 us (9%)
  waiting for transfers between devices  6.27 us (8%)
  between operations  0.97 us (1%)
    ppermute x3, starting transfers between devices, passed_along(): return lax.ppermute(value, axis, pairs)  22.1 us
    all_gather x1, blocking collectives, whole_partition(): return lax.all_gather(every, 'gx', axis=count, tiled=True)  14.1 us
    all_gather x1, blocking collectives, halo_exchange(): every = lax.all_gather(edges, 'gy', axis=0)  5.35 us
    ppermute x2, starting transfers between devices, shifted(): return lax.ppermute(piece, axes, pairs)  5.33 us
    all_gather x1, blocking collectives, per_device(): received = lax.all_gather(packed, 'group', axis=0, tiled=True)  5.25 us
    ppermute x2, waiting for transfers between devices, shifted(): return lax.ppermute(piece, axes, pairs)  4.67 us
    all_gather x1, blocking collectives, whole_partition(): every = lax.all_gather(block, 'gy', axis=count + 1, tiled=True)  4.59 us
    scatter-add x1, other arithmetic, per_device(): jnp.zeros((3, cell_count), jnp.float32).at[:, wall_index].add(speed_parts)  2.51 us
  transfers between devices with their start and end apart: 5, of which 4 were waited for; matrix products, arithmetic and copies ran while one was open for 0% of the time, Pallas kernels for 0%

profile of v10, /device:TPU:0, one launch (start us, length us, event | category | flops | bytes accessed | tf_op | source)
XLA Modules:
  0.0 79.9 jit_solution(3056642027459715420)
XLA Ops:
  0.7 0.7 fusion.59
  1.4 1.0 %fusion.46 = (f32[2,8,128]{2,1,0:T(8,128)S(1)}, f32[2,8,128]{2,1,0:T(8,128)S(1)}, f32[2,8,128]{2,1,0:T(8,128)S(1)}, f32[2,8,128]{2,1,0:T(8,128)S(1)}) fusion(bf16[19,2,8,128]{3,2,1,0:T(8,128)(2,1)} %param.43, f32[19]{0:T(128)} %constant.205, f32[19]{0:T(128)} %constant.206, f32[19]{0:T(128)} %constant.207), kind=kLoop, calls=%fused_computation.126 | loop fusion | flops 303104 | bytes 110820 | tf_op jit(solution)/shard_map/reduce_sum | solution.py:96
  2.4 1.1 %fusion.51 = bf16[19,2,8,128]{3,2,1,0:T(8,128)(2,1)S(1)} fusion(bf16[19,2,8,128]{3,2,1,0:T(8,128)(2,1)} %param.43, f32[2,8,128]{2,1,0:T(8,128)S(1)} %get-tuple-element.283, f32[2,8,128]{2,1,0:T(8,128)S(1)} %get-tuple-element.286, f32[19]{0:T(128)} %constant.207, f32[2,8,128]{2,1,0:T(8,128)S(1)} %get-tuple-element.285, f32[19]{0:T(128)} %constant.206, ...), kind=kLoop, calls=%fused_computation.131 | loop fusion | flops 739328 | bytes 196913 | tf_op jit(solution)/shard_map/convert_element_type | solution.py:395
  3.6 5.3 %all-gather = bf16[40,2,2,128]{3,2,1,0:T(2,128)(2,1)S(1)} all-gather(bf16[20,2,2,128]{3,2,1,0:T(2,128)(2,1)S(1)} %fusion.57), channel_id=2, replica_groups=mesh['group'=4,'gx'=4,'gy'=2] {'gy'}, dimensions={0}, use_global_device_ids=true | all-gather | bytes 61440 | tf_op jit(solution)/shard_map/all_gather | solution.py:58
  9.0 0.1 broadcast_select_fusion
  9.1 0.1 pad_maximum_fusion.1
  9.2 4.0 %collective-permute-start = (bf16[20,1,10,128]{3,2,1,0:T(8,128)(2,1)S(1)}, bf16[20,1,10,128]{3,2,1,0:T(8,128)(2,1)S(1)}, u32[]{:S(2)}, u32[]{:S(2)}) collective-permute-start(bf16[20,1,10,128]{3,2,1,0:T(8,128)(2,1)S(1)} %get-tuple-element.331), channel_id=1, source_target_pairs={{0,2},{1,3},{2,4},{3,5},{4,6},{5,7},{6,8},{7,9},{8,10},{9,11},{10,... | collective-permute-start | bytes 153608 | tf_op jit(solution)/shard_map/ppermute | solution.py:53
  13.2 1.3 %collective-permute-start.1 = (bf16[20,1,10,128]{3,2,1,0:T(8,128)(2,1)S(1)}, bf16[20,1,10,128]{3,2,1,0:T(8,128)(2,1)S(1)}, u32[]{:S(2)}, u32[]{:S(2)}) collective-permute-start(bf16[20,1,10,128]{3,2,1,0:T(8,128)(2,1)S(1)} %get-tuple-element.332), channel_id=1, source_target_pairs={{2,0},{3,1},{4,2},{5,3},{6,4},{7,5},{8,6},{9,7},{10,8},{11,9},{12,... | collective-permute-start | bytes 153608 | tf_op jit(solution)/shard_map/ppermute | solution.py:53
  14.6 0.4 copy.99
  15.0 0.3 collective-permute-done
  15.3 4.4 %collective-permute-done.1 = bf16[20,1,10,128]{3,2,1,0:T(8,128)(2,1)S(1)} collective-permute-done((bf16[20,1,10,128]{3,2,1,0:T(8,128)(2,1)S(1)}, bf16[20,1,10,128]{3,2,1,0:T(8,128)(2,1)S(1)}, u32[]{:S(2)}, u32[]{:S(2)}) %collective-permute-start.1) | collective-permute-done | bytes 51232 | tf_op jit(solution)/shard_map/ppermute | solution.py:53
  19.6 0.5 fusion.33
  20.2 0.1 slice.272
  20.3 0.5 copy-done.2
  20.8 4.2 %conditional.5 = (f32[4,6,128]{2,0,1:T(4,128)S(1)}) conditional(s32[]{:T(128)} %convert_element_type.61, () %tuple.43, (f32[19,1,1,1]{0,3,2,1:T(1,128)S(1)}, f32[19,1,1,1]{0,3,2,1:T(1,128)S(1)}, f32[19,1,1,1]{0,3,2,1:T(1,128)S(1)}, f32[1,4,10,130]{3,2,1,0:T(8,128)S(1)}, f32[19,4,10,130]{3,2,1,0:T(8,128)S(1)}, ...), branch_computations={%region_4.5_spmd, %region_5.9_spmd.clone} | conditional | flops 646950 | bytes 2346576 | solution.py:424
  20.9 0.1 select_select_fusion.2
  21.1 0.1 fusion.14
  21.2 0.1 slice.207
  21.4 0.1 slice.206
  21.4 0.1 copy-done.13
  21.6 0.2 multiply_reduce_fusion.2
  21.9 0.4 copy.96
  22.3 1.6 %gather_fusion = f32[512,3]{1,0:T(8,128)} fusion(f32[3,2048]{0,1:T(8,128)S(1)} %copy.96, s32[1024]{0:T(1024)S(1)} %pad_clamp_fusion.1), kind=kCustom, calls=%fused_computation.2 | custom fusion | bytes 14336 | tf_op jit(solution)/shard_map/cond/branch_1_fun/gather | solution.py:410
  23.9 1.1 %copy.97 = f32[3,4,128]{2,1,0:T(4,128)S(1)} copy(f32[3,4,128]{0,2,1:T(8,128)} %bitcast.145) | data formatting | bytes 12288 | tf_op jit(solution)/shard_map/cond/branch_1_fun/concatenate | solution.py:421
  25.0 5.2 %all_gather.17 = f32[16,6,128]{2,1,0:T(8,128)S(1)} all-gather(f32[4,6,128]{2,1,0:T(8,128)S(1)} %copy.100), channel_id=1, replica_groups=mesh['group'=4,'gx'=4,'gy'=2] {'group'}, dimensions={0}, use_global_device_ids=true | all-gather | bytes 61440 | tf_op jit(solution)/shard_map/all_gather | solution.py:430
  30.3 1.1 %conditional.6 = (f32[2,128,8,128]{3,1,2,0:T(8,128)}, f32[3,2048]{0,1:T(8,128)S(1)}) conditional(s32[]{:T(128)} %convert_element_type.67, f32[3,2048]{0,1:T(8,128)S(1)} %bitcast.134, (f32[3,1,1,256]{3,2,1,0:T(1,128)S(1)}, s32[1,1,2,8]{3,2,1,0:T(2,128)S(1)}, f32[16,6,128]{2,1,0:T(8,128)S(1)}, s32[256]{0:T(256)S(1)}, f32[3,2048]{0,1:T(8,128)S(1)}) %tuple.142), branch_computations={%region_9.10_spmd, %region_10.13_spmd} | conditional | flops 15991856 | bytes 2414224 | solution.py:447
  30.3 1.1 %broadcast.235 = f32[2,128,8,128]{3,1,2,0:T(8,128)} broadcast(f32[]{:T(128)} %constant.150.clone), dimensions={} | broadcast | bytes 1048580 | tf_op jit(solution)/shard_map/broadcast.18
  31.4 0.3 copy.112
  31.7 4.6 %all_gather.18 = f32[4,4,8,128]{3,1,0,2:T(4,128)S(1)} all-gather(f32[4,4,4,128]{3,1,0,2:T(4,128)S(1)} %copy.102), channel_id=1, replica_groups=mesh['group'=4,'gx'=4,'gy'=2] {'gy'}, dimensions={2}, use_global_device_ids=true | all-gather | bytes 98304 | tf_op jit(solution)/shard_map/all_gather | solution.py:339
  36.4 14.1 %all_gather.19 = f32[4,16,8,128]{3,2,0,1:T(8,128)S(1)} all-gather(f32[4,4,8,128]{3,2,0,1:T(8,128)S(1)} %copy.103), channel_id=1, replica_groups=mesh['group'=4,'gx'=4,'gy'=2] {'gx'}, dimensions={1}, use_global_device_ids=true | all-gather | bytes 327680 | tf_op jit(solution)/shard_map/all_gather | solution.py:340
  50.5 0.6 dynamic-slice_select_fusion
  51.1 0.1 collective-permute-start.2
  51.2 22.1 %collective-permute-start.3 = (f32[4,3,128]{2,0,1:T(4,128)S(1)}, f32[4,3,128]{2,0,1:T(4,128)S(1)}, u32[]{:S(2)}, u32[]{:S(2)}) collective-permute-start(f32[4,3,128]{2,0,1:T(4,128)S(1)} %get-tuple-element.337), channel_id=1, source_target_pairs={{0,16},{8,24},{16,0},{24,8},{1,17},{9,25},{17,1},{25,9},{2,18},{10... | collective-permute-start | bytes 18440 | tf_op jit(solution)/shard_map/ppermute | solution.py:78
  73.2 0.9 %collective-permute-done.2 = f32[4,3,128]{2,0,1:T(4,128)S(1)} collective-permute-done((f32[4,3,128]{2,0,1:T(4,128)S(1)}, f32[4,3,128]{2,0,1:T(4,128)S(1)}, u32[]{:S(2)}, u32[]{:S(2)}) %collective-permute-start.2) | collective-permute-done | bytes 6176 | tf_op jit(solution)/shard_map/ppermute | solution.py:78
  74.2 0.7 collective-permute-done.3
  74.9 0.1 copy.113
  75.0 2.5 %scatter_custom_fusion.1 = f32[3,2048]{0,1:T(8,128)S(1)} fusion(s32[512]{0:T(512)S(1)} %bitcast.175, f32[512,3]{1,0:T(8,128)S(1)} %bitcast.146, f32[]{:T(128)} %constant.169.clone.1), kind=kCustom, calls=%fused_computation.113 | custom fusion | flops 1536 | bytes 24580 | tf_op jit(solution)/shard_map/scatter-add | solution.py:503
  77.5 1.8 %conditional.9 = (bf16[19,2,8,128]{3,2,1,0:T(8,128)(2,1)S(1)}) conditional(s32[]{:T(128)} %convert_element_type.61, () %tuple.40, (f32[1,4,10,130]{3,2,1,0:T(8,128)S(1)}, f32[19,1,1,1]{0,3,2,1:T(1,128)S(1)}, f32[19,1,1,1]{0,3,2,1:T(1,128)S(1)}, f32[19,1,1,1]{0,3,2,1:T(1,128)S(1)}, f32[19,1,1,1]{0,3,2,1:T(1,128)S(1)}, ...), branch_computations={%region_18.19_spmd, %region_19.20_spmd.clone} | conditional | flops 1056324 | bytes 4268820 | solution.py:505
  77.6 0.1 select_select_fusion.1
  77.7 0.1 fusion.1
  77.9 0.2 select_select_fusion
  78.1 0.1 fusion
  78.2 0.1 slice.231
  78.4 0.3 copy.107
  78.7 0.1 slice.230
  78.8 0.1 slice.241
  78.9 0.4 fusion.6
  79.3 0.6 copy-done
  (63 shorter events, 0.5 us)
Async XLA Ops:
  0.6 13.9 %copy-start.6 = (f32[4,4,128]{2,1,0:T(4,128)S(1)}, f32[4,4,128]{2,1,0:T(4,128)}, u32[]{:S(2)}) copy-start(f32[4,4,128]{2,1,0:T(4,128)} %param.47) | copy-start | bytes 24580
  0.6 13.9 %copy-start.7 = (s32[4,4,128]{2,1,0:T(4,128)S(1)}, s32[4,4,128]{2,1,0:T(4,128)}, u32[]{:S(2)}) copy-start(s32[4,4,128]{2,1,0:T(4,128)} %param.48) | copy-start | bytes 24580
  0.7 13.9 %copy-start.1 = (f32[3,4,4,128]{3,2,1,0:T(4,128)S(1)}, f32[3,4,4,128]{3,2,1,0:T(4,128)}, u32[]{:S(2)}) copy-start(f32[3,4,4,128]{3,2,1,0:T(4,128)} %param.46) | copy-start | bytes 73732
  9.2 6.1 %collective-permute-start = (bf16[20,1,10,128]{3,2,1,0:T(8,128)(2,1)S(1)}, bf16[20,1,10,128]{3,2,1,0:T(8,128)(2,1)S(1)}, u32[]{:S(2)}, u32[]{:S(2)}) collective-permute-start(bf16[20,1,10,128]{3,2,1,0:T(8,128)(2,1)S(1)} %get-tuple-element.331), channel_id=1, source_target_pairs={{0,2},{1,3},{2,4},{3,5},{4,6},{5,7},{6,8},{7,9},{8,10},{9,11},{10,... | collective-permute-start | bytes 153608 | tf_op jit(solution)/shard_map/ppermute | solution.py:53
  13.2 6.4 %collective-permute-start.1 = (bf16[20,1,10,128]{3,2,1,0:T(8,128)(2,1)S(1)}, bf16[20,1,10,128]{3,2,1,0:T(8,128)(2,1)S(1)}, u32[]{:S(2)}, u32[]{:S(2)}) collective-permute-start(bf16[20,1,10,128]{3,2,1,0:T(8,128)(2,1)S(1)} %get-tuple-element.332), channel_id=1, source_target_pairs={{2,0},{3,1},{4,2},{5,3},{6,4},{7,5},{8,6},{9,7},{10,8},{11,9},{12,... | collective-permute-start | bytes 153608 | tf_op jit(solution)/shard_map/ppermute | solution.py:53
  20.1 0.7 copy-start.2
  20.1 0.7 copy-start.4
  20.1 0.7 copy-start.5
  20.2 0.7 copy-start.8
  20.8 9.5 %copy-start.9 = (s32[1,1,256]{2,1,0:T(1,128)S(1)}, s32[1,1,256]{2,1,0:T(1,128)}, u32[]{:S(2)}) copy-start(s32[1,1,256]{2,1,0:T(1,128)} %param.50) | copy-start | bytes 3076
  20.8 9.5 %copy-start.10 = (f32[3,1,1,256]{3,2,1,0:T(1,128)S(1)}, f32[3,1,1,256]{3,2,1,0:T(1,128)}, u32[]{:S(2)}) copy-start(f32[3,1,1,256]{3,2,1,0:T(1,128)} %param.51) | copy-start | bytes 9220
  20.8 9.5 %copy-start.11 = (s32[1,1,2,8]{3,2,1,0:T(2,128)S(1)}, s32[1,1,2,8]{3,2,1,0:T(2,128)}, u32[]{:S(2)}) copy-start(s32[1,1,2,8]{3,2,1,0:T(2,128)} %param.52) | copy-start | bytes 196
  20.9 0.7 copy-start.13
  20.9 0.7 copy-start.14
  20.9 0.7 copy-start.15
  31.4 19.1 %copy-start.3 = (f32[24,24]{1,0:T(8,128)S(1)}, f32[24,24]{1,0:T(8,128)}, u32[]{:S(2)}) copy-start(f32[24,24]{1,0:T(8,128)} %param.49) | copy-start | bytes 6916
  51.1 23.1 %collective-permute-start.2 = (f32[4,3,128]{2,0,1:T(4,128)S(1)}, f32[4,3,128]{2,0,1:T(4,128)S(1)}, u32[]{:S(2)}, u32[]{:S(2)}) collective-permute-start(f32[4,3,128]{2,0,1:T(4,128)S(1)} %get-tuple-element.335), channel_id=1, source_target_pairs={{0,8},{8,16},{16,24},{24,0},{1,9},{9,17},{17,25},{25,1},{2,10},{10... | collective-permute-start | bytes 18440 | tf_op jit(solution)/shard_map/ppermute | solution.py:78
  51.2 23.7 %collective-permute-start.3 = (f32[4,3,128]{2,0,1:T(4,128)S(1)}, f32[4,3,128]{2,0,1:T(4,128)S(1)}, u32[]{:S(2)}, u32[]{:S(2)}) collective-permute-start(f32[4,3,128]{2,0,1:T(4,128)S(1)} %get-tuple-element.337), channel_id=1, source_target_pairs={{0,16},{8,24},{16,0},{24,8},{1,17},{9,25},{17,1},{25,9},{2,18},{10... | collective-permute-start | bytes 18440 | tf_op jit(solution)/shard_map/ppermute | solution.py:78
  73.2 1.6 %collective-permute-start.4 = (f32[4,3,128]{2,0,1:T(4,128)S(1)}, f32[4,3,128]{2,0,1:T(4,128)S(1)}, u32[]{:S(2)}, u32[]{:S(2)}) collective-permute-start(f32[4,3,128]{2,0,1:T(4,128)S(1)} %get-tuple-element.336), channel_id=1, source_target_pairs={{0,24},{8,0},{16,8},{24,16},{1,25},{9,1},{17,9},{25,17},{2,26},{10... | collective-permute-start | bytes 18440 | tf_op jit(solution)/shard_map/ppermute | solution.py:78
  78.1 0.8 %copy-start.12 = (f32[19]{0:T(128)S(1)}, f32[19]{0:T(128)}, u32[]{:S(2)}) copy-start(f32[19]{0:T(128)} %constant.208) | copy-start | bytes 232 | tf_op jit(solution)/shard_map/cond
  79.3 0.6 copy-start

commit v11 on v10

--- a/solution.py
+++ b/solution.py
@@ -205,7 +205,7 @@
 
 def apply_rows(matrix_ref, values_ref, stiff_ref, out_ref):
     span_cells, across_cells, deep_cells = stiff_ref.shape
-    step = 4 if span_cells % 4 == 0 else 1
+    step = next(size for size in (8, 4, 2, 1) if span_cells % size == 0)
     shape = (step, across_cells, deep_cells)
     across_at = lax.broadcasted_iota(jnp.int32, shape, 1)
     deep_at = lax.broadcasted_iota(jnp.int32, shape, 2)

time: 81.2 us -> 80.9 us (level)
  no operation moved by 1% of the time
where the time goes in v11:
time: 80.9 us; the launch traced here: 79.6 us
  blocking collectives  29.3 us (36%)
  starting transfers between devices  27 us (33%)
  other arithmetic  8.32 us (10%)
  local copies, waits for them, and re-layouts  7.39 us (9%)
  waiting for transfers between devices  6.27 us (8%)
  between operations  0.97 us (1%)
    ppermute x3, starting transfers between devices, passed_along(): return lax.ppermute(value, axis, pairs)  21.7 us
    all_gather x1, blocking collectives, whole_partition(): return lax.all_gather(every, 'gx', axis=count, tiled=True)  14.1 us
    all_gather x1, blocking collectives, halo_exchange(): every = lax.all_gather(edges, 'gy', axis=0)  5.35 us
    ppermute x2, starting transfers between devices, shifted(): return lax.ppermute(piece, axes, pairs)  5.33 us
    all_gather x1, blocking collectives, per_device(): received = lax.all_gather(packed, 'group', axis=0, tiled=True)  5.25 us
    ppermute x2, waiting for transfers between devices, shifted(): return lax.ppermute(piece, axes, pairs)  4.67 us
    all_gather x1, blocking collectives, whole_partition(): every = lax.all_gather(block, 'gy', axis=count + 1, tiled=True)  4.59 us
    scatter-add x1, other arithmetic, per_device(): jnp.zeros((3, cell_count), jnp.float32).at[:, wall_index].add(speed_parts)  2.51 us
  transfers between devices with their start and end apart: 5, of which 4 were waited for; matrix products, arithmetic and copies ran while one was open for 0% of the time, Pallas kernels for 0%

profile of v11, /device:TPU:0, one launch (start us, length us, event | category | flops | bytes accessed | tf_op | source)
XLA Modules:
  0.0 79.6 jit_solution(1200607578823148994)
XLA Ops:
  0.7 0.7 fusion.59
  1.4 1.0 %fusion.46 = (f32[2,8,128]{2,1,0:T(8,128)S(1)}, f32[2,8,128]{2,1,0:T(8,128)S(1)}, f32[2,8,128]{2,1,0:T(8,128)S(1)}, f32[2,8,128]{2,1,0:T(8,128)S(1)}) fusion(bf16[19,2,8,128]{3,2,1,0:T(8,128)(2,1)} %param.43, f32[19]{0:T(128)} %constant.205, f32[19]{0:T(128)} %constant.206, f32[19]{0:T(128)} %constant.207), kind=kLoop, calls=%fused_computation.126 | loop fusion | flops 303104 | bytes 110820 | tf_op jit(solution)/shard_map/reduce_sum | solution.py:96
  2.4 1.1 %fusion.51 = bf16[19,2,8,128]{3,2,1,0:T(8,128)(2,1)S(1)} fusion(bf16[19,2,8,128]{3,2,1,0:T(8,128)(2,1)} %param.43, f32[2,8,128]{2,1,0:T(8,128)S(1)} %get-tuple-element.283, f32[2,8,128]{2,1,0:T(8,128)S(1)} %get-tuple-element.286, f32[19]{0:T(128)} %constant.207, f32[2,8,128]{2,1,0:T(8,128)S(1)} %get-tuple-element.285, f32[19]{0:T(128)} %constant.206, ...), kind=kLoop, calls=%fused_computation.131 | loop fusion | flops 739328 | bytes 196913 | tf_op jit(solution)/shard_map/convert_element_type | solution.py:395
  3.6 5.3 %all-gather = bf16[40,2,2,128]{3,2,1,0:T(2,128)(2,1)S(1)} all-gather(bf16[20,2,2,128]{3,2,1,0:T(2,128)(2,1)S(1)} %fusion.57), channel_id=2, replica_groups=mesh['group'=4,'gx'=4,'gy'=2] {'gy'}, dimensions={0}, use_global_device_ids=true | all-gather | bytes 61440 | tf_op jit(solution)/shard_map/all_gather | solution.py:58
  9.1 0.1 pad_maximum_fusion.1
  9.2 4.0 %collective-permute-start = (bf16[20,1,10,128]{3,2,1,0:T(8,128)(2,1)S(1)}, bf16[20,1,10,128]{3,2,1,0:T(8,128)(2,1)S(1)}, u32[]{:S(2)}, u32[]{:S(2)}) collective-permute-start(bf16[20,1,10,128]{3,2,1,0:T(8,128)(2,1)S(1)} %get-tuple-element.331), channel_id=1, source_target_pairs={{0,2},{1,3},{2,4},{3,5},{4,6},{5,7},{6,8},{7,9},{8,10},{9,11},{10,... | collective-permute-start | bytes 153608 | tf_op jit(solution)/shard_map/ppermute | solution.py:53
  13.2 1.3 %collective-permute-start.1 = (bf16[20,1,10,128]{3,2,1,0:T(8,128)(2,1)S(1)}, bf16[20,1,10,128]{3,2,1,0:T(8,128)(2,1)S(1)}, u32[]{:S(2)}, u32[]{:S(2)}) collective-permute-start(bf16[20,1,10,128]{3,2,1,0:T(8,128)(2,1)S(1)} %get-tuple-element.332), channel_id=1, source_target_pairs={{2,0},{3,1},{4,2},{5,3},{6,4},{7,5},{8,6},{9,7},{10,8},{11,9},{12,... | collective-permute-start | bytes 153608 | tf_op jit(solution)/shard_map/ppermute | solution.py:53
  14.6 0.4 copy.99
  15.0 0.3 collective-permute-done
  15.3 4.4 %collective-permute-done.1 = bf16[20,1,10,128]{3,2,1,0:T(8,128)(2,1)S(1)} collective-permute-done((bf16[20,1,10,128]{3,2,1,0:T(8,128)(2,1)S(1)}, bf16[20,1,10,128]{3,2,1,0:T(8,128)(2,1)S(1)}, u32[]{:S(2)}, u32[]{:S(2)}) %collective-permute-start.1) | collective-permute-done | bytes 51232 | tf_op jit(solution)/shard_map/ppermute | solution.py:53
  19.6 0.5 fusion.33
  20.2 0.1 slice.272
  20.3 0.5 copy-done.2
  20.8 4.2 %conditional.5 = (f32[4,6,128]{2,0,1:T(4,128)S(1)}) conditional(s32[]{:T(128)} %convert_element_type.61, () %tuple.43, (f32[19,1,1,1]{0,3,2,1:T(1,128)S(1)}, f32[19,1,1,1]{0,3,2,1:T(1,128)S(1)}, f32[19,1,1,1]{0,3,2,1:T(1,128)S(1)}, f32[1,4,10,130]{3,2,1,0:T(8,128)S(1)}, f32[19,4,10,130]{3,2,1,0:T(8,128)S(1)}, ...), branch_computations={%region_4.5_spmd, %region_5.9_spmd.clone} | conditional | flops 646950 | bytes 2346576 | solution.py:424
  20.9 0.1 select_select_fusion.2
  21.1 0.1 fusion.14
  21.2 0.1 slice.207
  21.4 0.1 slice.206
  21.4 0.1 copy-done.13
  21.6 0.2 multiply_reduce_fusion.2
  21.9 0.4 copy.96
  22.3 1.6 %gather_fusion = f32[512,3]{1,0:T(8,128)} fusion(f32[3,2048]{0,1:T(8,128)S(1)} %copy.96, s32[1024]{0:T(1024)S(1)} %pad_clamp_fusion.1), kind=kCustom, calls=%fused_computation.2 | custom fusion | bytes 14336 | tf_op jit(solution)/shard_map/cond/branch_1_fun/gather | solution.py:410
  23.9 1.1 %copy.97 = f32[3,4,128]{2,1,0:T(4,128)S(1)} copy(f32[3,4,128]{0,2,1:T(8,128)} %bitcast.145) | data formatting | bytes 12288 | tf_op jit(solution)/shard_map/cond/branch_1_fun/concatenate | solution.py:421
  25.0 5.2 %all_gather.17 = f32[16,6,128]{2,1,0:T(8,128)S(1)} all-gather(f32[4,6,128]{2,1,0:T(8,128)S(1)} %copy.100), channel_id=1, replica_groups=mesh['group'=4,'gx'=4,'gy'=2] {'group'}, dimensions={0}, use_global_device_ids=true | all-gather | bytes 61440 | tf_op jit(solution)/shard_map/all_gather | solution.py:430
  30.3 1.1 %conditional.6 = (f32[2,128,8,128]{3,1,2,0:T(8,128)}, f32[3,2048]{0,1:T(8,128)S(1)}) conditional(s32[]{:T(128)} %convert_element_type.67, f32[3,2048]{0,1:T(8,128)S(1)} %bitcast.134, (f32[3,1,1,256]{3,2,1,0:T(1,128)S(1)}, s32[1,1,2,8]{3,2,1,0:T(2,128)S(1)}, f32[16,6,128]{2,1,0:T(8,128)S(1)}, s32[256]{0:T(256)S(1)}, f32[3,2048]{0,1:T(8,128)S(1)}) %tuple.142), branch_computations={%region_9.10_spmd, %region_10.13_spmd} | conditional | flops 15991856 | bytes 2414224 | solution.py:447
  30.3 1.1 %broadcast.235 = f32[2,128,8,128]{3,1,2,0:T(8,128)} broadcast(f32[]{:T(128)} %constant.150.clone), dimensions={} | broadcast | bytes 1048580 | tf_op jit(solution)/shard_map/broadcast.18
  31.4 0.3 copy.112
  31.7 4.6 %all_gather.18 = f32[4,4,8,128]{3,1,0,2:T(4,128)S(1)} all-gather(f32[4,4,4,128]{3,1,0,2:T(4,128)S(1)} %copy.102), channel_id=1, replica_groups=mesh['group'=4,'gx'=4,'gy'=2] {'gy'}, dimensions={2}, use_global_device_ids=true | all-gather | bytes 98304 | tf_op jit(solution)/shard_map/all_gather | solution.py:339
  36.4 14.1 %all_gather.19 = f32[4,16,8,128]{3,2,0,1:T(8,128)S(1)} all-gather(f32[4,4,8,128]{3,2,0,1:T(8,128)S(1)} %copy.103), channel_id=1, replica_groups=mesh['group'=4,'gx'=4,'gy'=2] {'gx'}, dimensions={1}, use_global_device_ids=true | all-gather | bytes 327680 | tf_op jit(solution)/shard_map/all_gather | solution.py:340
  50.4 0.2 conditional.7
  50.6 0.6 dynamic-slice_select_fusion
  51.3 0.1 collective-permute-start.2
  51.3 21.6 %collective-permute-start.3 = (f32[4,3,128]{2,0,1:T(4,128)S(1)}, f32[4,3,128]{2,0,1:T(4,128)S(1)}, u32[]{:S(2)}, u32[]{:S(2)}) collective-permute-start(f32[4,3,128]{2,0,1:T(4,128)S(1)} %get-tuple-element.337), channel_id=1, source_target_pairs={{0,16},{8,24},{16,0},{24,8},{1,17},{9,25},{17,1},{25,9},{2,18},{10... | collective-permute-start | bytes 18440 | tf_op jit(solution)/shard_map/ppermute | solution.py:78
  73.0 0.9 %collective-permute-done.2 = f32[4,3,128]{2,0,1:T(4,128)S(1)} collective-permute-done((f32[4,3,128]{2,0,1:T(4,128)S(1)}, f32[4,3,128]{2,0,1:T(4,128)S(1)}, u32[]{:S(2)}, u32[]{:S(2)}) %collective-permute-start.2) | collective-permute-done | bytes 6176 | tf_op jit(solution)/shard_map/ppermute | solution.py:78
  73.9 0.7 collective-permute-done.3
  74.6 0.1 copy.113
  74.7 2.5 %scatter_custom_fusion.1 = f32[3,2048]{0,1:T(8,128)S(1)} fusion(s32[512]{0:T(512)S(1)} %bitcast.175, f32[512,3]{1,0:T(8,128)S(1)} %bitcast.146, f32[]{:T(128)} %constant.169.clone.1), kind=kCustom, calls=%fused_computation.113 | custom fusion | flops 1536 | bytes 24580 | tf_op jit(solution)/shard_map/scatter-add | solution.py:503
  77.2 1.8 %conditional.9 = (bf16[19,2,8,128]{3,2,1,0:T(8,128)(2,1)S(1)}) conditional(s32[]{:T(128)} %convert_element_type.61, () %tuple.40, (f32[1,4,10,130]{3,2,1,0:T(8,128)S(1)}, f32[19,1,1,1]{0,3,2,1:T(1,128)S(1)}, f32[19,1,1,1]{0,3,2,1:T(1,128)S(1)}, f32[19,1,1,1]{0,3,2,1:T(1,128)S(1)}, f32[19,1,1,1]{0,3,2,1:T(1,128)S(1)}, ...), branch_computations={%region_18.19_spmd, %region_19.20_spmd.clone} | conditional | flops 1056324 | bytes 4268820 | solution.py:505
  77.3 0.1 select_select_fusion.1
  77.5 0.1 fusion.1
  77.6 0.2 select_select_fusion
  77.8 0.1 fusion
  78.0 0.1 slice.231
  78.1 0.3 copy.107
  78.4 0.1 slice.230
  78.5 0.1 slice.241
  78.6 0.4 fusion.6
  79.0 0.6 copy-done
  (63 shorter events, 0.6 us)
Async XLA Ops:
  0.6 13.9 %copy-start.6 = (f32[4,4,128]{2,1,0:T(4,128)S(1)}, f32[4,4,128]{2,1,0:T(4,128)}, u32[]{:S(2)}) copy-start(f32[4,4,128]{2,1,0:T(4,128)} %param.47) | copy-start | bytes 24580
  0.6 13.9 %copy-start.7 = (s32[4,4,128]{2,1,0:T(4,128)S(1)}, s32[4,4,128]{2,1,0:T(4,128)}, u32[]{:S(2)}) copy-start(s32[4,4,128]{2,1,0:T(4,128)} %param.48) | copy-start | bytes 24580
  0.7 13.9 %copy-start.1 = (f32[3,4,4,128]{3,2,1,0:T(4,128)S(1)}, f32[3,4,4,128]{3,2,1,0:T(4,128)}, u32[]{:S(2)}) copy-start(f32[3,4,4,128]{3,2,1,0:T(4,128)} %param.46) | copy-start | bytes 73732
  9.2 6.1 %collective-permute-start = (bf16[20,1,10,128]{3,2,1,0:T(8,128)(2,1)S(1)}, bf16[20,1,10,128]{3,2,1,0:T(8,128)(2,1)S(1)}, u32[]{:S(2)}, u32[]{:S(2)}) collective-permute-start(bf16[20,1,10,128]{3,2,1,0:T(8,128)(2,1)S(1)} %get-tuple-element.331), channel_id=1, source_target_pairs={{0,2},{1,3},{2,4},{3,5},{4,6},{5,7},{6,8},{7,9},{8,10},{9,11},{10,... | collective-permute-start | bytes 153608 | tf_op jit(solution)/shard_map/ppermute | solution.py:53
  13.2 6.4 %collective-permute-start.1 = (bf16[20,1,10,128]{3,2,1,0:T(8,128)(2,1)S(1)}, bf16[20,1,10,128]{3,2,1,0:T(8,128)(2,1)S(1)}, u32[]{:S(2)}, u32[]{:S(2)}) collective-permute-start(bf16[20,1,10,128]{3,2,1,0:T(8,128)(2,1)S(1)} %get-tuple-element.332), channel_id=1, source_target_pairs={{2,0},{3,1},{4,2},{5,3},{6,4},{7,5},{8,6},{9,7},{10,8},{11,9},{12,... | collective-permute-start | bytes 153608 | tf_op jit(solution)/shard_map/ppermute | solution.py:53
  20.1 0.7 copy-start.2
  20.1 0.7 copy-start.4
  20.1 0.7 copy-start.5
  20.2 0.7 copy-start.8
  20.8 9.5 %copy-start.9 = (s32[1,1,256]{2,1,0:T(1,128)S(1)}, s32[1,1,256]{2,1,0:T(1,128)}, u32[]{:S(2)}) copy-start(s32[1,1,256]{2,1,0:T(1,128)} %param.50) | copy-start | bytes 3076
  20.8 9.5 %copy-start.10 = (f32[3,1,1,256]{3,2,1,0:T(1,128)S(1)}, f32[3,1,1,256]{3,2,1,0:T(1,128)}, u32[]{:S(2)}) copy-start(f32[3,1,1,256]{3,2,1,0:T(1,128)} %param.51) | copy-start | bytes 9220
  20.8 9.5 %copy-start.11 = (s32[1,1,2,8]{3,2,1,0:T(2,128)S(1)}, s32[1,1,2,8]{3,2,1,0:T(2,128)}, u32[]{:S(2)}) copy-start(s32[1,1,2,8]{3,2,1,0:T(2,128)} %param.52) | copy-start | bytes 196
  20.9 0.7 copy-start.13
  20.9 0.7 copy-start.14
  20.9 0.7 copy-start.15
  31.4 19.1 %copy-start.3 = (f32[24,24]{1,0:T(8,128)S(1)}, f32[24,24]{1,0:T(8,128)}, u32[]{:S(2)}) copy-start(f32[24,24]{1,0:T(8,128)} %param.49) | copy-start | bytes 6916
  51.3 22.6 %collective-permute-start.2 = (f32[4,3,128]{2,0,1:T(4,128)S(1)}, f32[4,3,128]{2,0,1:T(4,128)S(1)}, u32[]{:S(2)}, u32[]{:S(2)}) collective-permute-start(f32[4,3,128]{2,0,1:T(4,128)S(1)} %get-tuple-element.335), channel_id=1, source_target_pairs={{0,8},{8,16},{16,24},{24,0},{1,9},{9,17},{17,25},{25,1},{2,10},{10... | collective-permute-start | bytes 18440 | tf_op jit(solution)/shard_map/ppermute | solution.py:78
  51.3 23.2 %collective-permute-start.3 = (f32[4,3,128]{2,0,1:T(4,128)S(1)}, f32[4,3,128]{2,0,1:T(4,128)S(1)}, u32[]{:S(2)}, u32[]{:S(2)}) collective-permute-start(f32[4,3,128]{2,0,1:T(4,128)S(1)} %get-tuple-element.337), channel_id=1, source_target_pairs={{0,16},{8,24},{16,0},{24,8},{1,17},{9,25},{17,1},{25,9},{2,18},{10... | collective-permute-start | bytes 18440 | tf_op jit(solution)/shard_map/ppermute | solution.py:78
  73.0 1.6 %collective-permute-start.4 = (f32[4,3,128]{2,0,1:T(4,128)S(1)}, f32[4,3,128]{2,0,1:T(4,128)S(1)}, u32[]{:S(2)}, u32[]{:S(2)}) collective-permute-start(f32[4,3,128]{2,0,1:T(4,128)S(1)} %get-tuple-element.336), channel_id=1, source_target_pairs={{0,24},{8,0},{16,8},{24,16},{1,25},{9,1},{17,9},{25,17},{2,26},{10... | collective-permute-start | bytes 18440 | tf_op jit(solution)/shard_map/ppermute | solution.py:78
  77.8 0.8 %copy-start.12 = (f32[19]{0:T(128)S(1)}, f32[19]{0:T(128)}, u32[]{:S(2)}) copy-start(f32[19]{0:T(128)} %constant.208) | copy-start | bytes 232 | tf_op jit(solution)/shard_map/cond
  79.0 0.6 copy-start

commit v12 on v11

--- a/solution.py
+++ b/solution.py
@@ -407,7 +407,7 @@
     def fluid_pack(operands):
         upstream, opened, bounce, reflected = stream_links(operands[0], operands[1])
         force_parts = wall_force(bounce, reflected).reshape(3, cell_count)
-        picked = force_parts[:, wall_index]
+        picked = jnp.stack([jnp.take(force_parts[k], wall_index) for k in range(3)])
         span_pos = wall_index // (across_cells * deep_cells)
         across_pos = wall_index // deep_cells % across_cells + column_index * across_cells
         deep_pos = wall_index % deep_cells

time: 80.9 us -> 91.3 us (1.13)
  local copies, waits for them, and re-layouts: 7.39 us -> 14.4 us
  other arithmetic: 8.32 us -> 11.8 us
    gather x1 -> x3, local copies, waits for them, and re-layouts: 1.64 us -> 9.41 us  [fluid_pack(): picked = jnp.stack([jnp.take(force_parts[k], wall_index) for k in range(3)])]
    cond x0 -> x5, other arithmetic: none -> 2.94 us
    concatenate x1 -> x0, local copies, waits for them, and re-layouts: 1.06 us -> none  [fluid_pack(): packed = jnp.concatenate([picked, positions], axis=0)]
where the time goes in v12:
time: 91.3 us; the launch traced here: 90 us
  blocking collectives  29.2 us (32%)
  starting transfers between devices  26.8 us (29%)
  local copies, waits for them, and re-layouts  14.4 us (16%)
  other arithmetic  11.8 us (13%)
  waiting for transfers between devices  6.27 us (7%)
  between operations  0.95 us (1%)
    ppermute x3, starting transfers between devices, passed_along(): return lax.ppermute(value, axis, pairs)  21.5 us
    all_gather x1, blocking collectives, whole_partition(): return lax.all_gather(every, 'gx', axis=count, tiled=True)  14.1 us
    gather x3, local copies, waits for them, and re-layouts, fluid_pack(): picked = jnp.stack([jnp.take(force_parts[k], wall_index) for k in range(3)])  9.41 us
    all_gather x1, blocking collectives, halo_exchange(): every = lax.all_gather(edges, 'gy', axis=0)  5.35 us
    ppermute x2, starting transfers between devices, shifted(): return lax.ppermute(piece, axes, pairs)  5.33 us
    all_gather x1, blocking collectives, per_device(): received = lax.all_gather(packed, 'group', axis=0, tiled=True)  5.23 us
    ppermute x2, waiting for transfers between devices, shifted(): return lax.ppermute(piece, axes, pairs)  4.67 us
    all_gather x1, blocking collectives, whole_partition(): every = lax.all_gather(block, 'gy', axis=count + 1, tiled=True)  4.59 us
  transfers between devices with their start and end apart: 5, of which 4 were waited for; matrix products, arithmetic and copies ran while one was open for 0% of the time, Pallas kernels for 0%

profile of v12, /device:TPU:0, one launch (start us, length us, event | category | flops | bytes accessed | tf_op | source)
XLA Modules:
  0.0 90.0 jit_solution(14386235875530532443)
XLA Ops:
  0.7 0.7 fusion.59
  1.4 1.0 %fusion.46 = (f32[2,8,128]{2,1,0:T(8,128)S(1)}, f32[2,8,128]{2,1,0:T(8,128)S(1)}, f32[2,8,128]{2,1,0:T(8,128)S(1)}, f32[2,8,128]{2,1,0:T(8,128)S(1)}) fusion(bf16[19,2,8,128]{3,2,1,0:T(8,128)(2,1)} %param.45, f32[19]{0:T(128)} %constant.212, f32[19]{0:T(128)} %constant.213, f32[19]{0:T(128)} %constant.214), kind=kLoop, calls=%fused_computation.133 | loop fusion | flops 303104 | bytes 110820 | tf_op jit(solution)/shard_map/reduce_sum | solution.py:96
  2.4 1.1 %fusion.51 = bf16[19,2,8,128]{3,2,1,0:T(8,128)(2,1)S(1)} fusion(bf16[19,2,8,128]{3,2,1,0:T(8,128)(2,1)} %param.45, f32[2,8,128]{2,1,0:T(8,128)S(1)} %get-tuple-element.286, f32[2,8,128]{2,1,0:T(8,128)S(1)} %get-tuple-element.289, f32[19]{0:T(128)} %constant.214, f32[2,8,128]{2,1,0:T(8,128)S(1)} %get-tuple-element.288, f32[19]{0:T(128)} %constant.213, ...), kind=kLoop, calls=%fused_computation.138 | loop fusion | flops 739328 | bytes 196913 | tf_op jit(solution)/shard_map/convert_element_type | solution.py:395
  3.6 5.3 %all-gather = bf16[40,2,2,128]{3,2,1,0:T(2,128)(2,1)S(1)} all-gather(bf16[20,2,2,128]{3,2,1,0:T(2,128)(2,1)S(1)} %fusion.57), channel_id=2, replica_groups=mesh['group'=4,'gx'=4,'gy'=2] {'gy'}, dimensions={0}, use_global_device_ids=true | all-gather | bytes 61440 | tf_op jit(solution)/shard_map/all_gather | solution.py:58
  9.2 4.0 %collective-permute-start = (bf16[20,1,10,128]{3,2,1,0:T(8,128)(2,1)S(1)}, bf16[20,1,10,128]{3,2,1,0:T(8,128)(2,1)S(1)}, u32[]{:S(2)}, u32[]{:S(2)}) collective-permute-start(bf16[20,1,10,128]{3,2,1,0:T(8,128)(2,1)S(1)} %get-tuple-element.331), channel_id=1, source_target_pairs={{0,2},{1,3},{2,4},{3,5},{4,6},{5,7},{6,8},{7,9},{8,10},{9,11},{10,... | collective-permute-start | bytes 153608 | tf_op jit(solution)/shard_map/ppermute | solution.py:53
  13.2 1.3 %collective-permute-start.1 = (bf16[20,1,10,128]{3,2,1,0:T(8,128)(2,1)S(1)}, bf16[20,1,10,128]{3,2,1,0:T(8,128)(2,1)S(1)}, u32[]{:S(2)}, u32[]{:S(2)}) collective-permute-start(bf16[20,1,10,128]{3,2,1,0:T(8,128)(2,1)S(1)} %get-tuple-element.332), channel_id=1, source_target_pairs={{2,0},{3,1},{4,2},{5,3},{6,4},{7,5},{8,6},{9,7},{10,8},{11,9},{12,... | collective-permute-start | bytes 153608 | tf_op jit(solution)/shard_map/ppermute | solution.py:53
  14.6 0.4 copy.87
  15.0 0.3 collective-permute-done
  15.3 4.4 %collective-permute-done.1 = bf16[20,1,10,128]{3,2,1,0:T(8,128)(2,1)S(1)} collective-permute-done((bf16[20,1,10,128]{3,2,1,0:T(8,128)(2,1)S(1)}, bf16[20,1,10,128]{3,2,1,0:T(8,128)(2,1)S(1)}, u32[]{:S(2)}, u32[]{:S(2)}) %collective-permute-start.1) | collective-permute-done | bytes 51232 | tf_op jit(solution)/shard_map/ppermute | solution.py:53
  19.6 0.5 fusion.33
  20.3 0.5 copy-done.1
  20.8 14.0 %conditional.5 = (f32[4,6,128]{2,0,1:T(4,128)}) conditional(s32[]{:T(128)} %convert_element_type.61, () %tuple.44, (f32[19,1,1,1]{0,3,2,1:T(1,128)S(1)}, f32[19,1,1,1]{0,3,2,1:T(1,128)S(1)}, f32[19,1,1,1]{0,3,2,1:T(1,128)S(1)}, f32[1,4,10,130]{3,2,1,0:T(8,128)S(1)}, f32[19,4,10,130]{3,2,1,0:T(8,128)S(1)}, ...), branch_computations={%region_4.5_spmd, %region_5.10_spmd.clone} | conditional | flops 636197 | bytes 2235472 | solution.py:424
  20.9 0.1 select_select_fusion.2
  21.1 0.1 fusion.21
  21.2 0.1 slice.213
  21.4 0.1 copy-done.13
  21.6 0.2 multiply_reduce_fusion
  21.9 3.1 %gather_fusion = f32[512]{0:T(512)S(1)} fusion(f32[2048]{0:T(1024)S(1)} %bitcast.136, s32[1024]{0:T(1024)S(1)} %pad_clamp_fusion.2), kind=kCustom, calls=%fused_computation.clone | custom fusion | bytes 6144 | tf_op jit(solution)/shard_map/cond/branch_1_fun/jit(_take)/gather | solution.py:410
  25.0 0.6 constant_dynamic-update-slice_fusion.5
  25.6 3.1 %gather_fusion.1 = f32[512]{0:T(512)S(1)} fusion(f32[2048]{0:T(1024)S(1)} %bitcast.135, s32[1024]{0:T(1024)S(1)} %pad_clamp_fusion.2), kind=kCustom, calls=%fused_computation.3.clone | custom fusion | bytes 6144 | tf_op jit(solution)/shard_map/cond/branch_1_fun/jit(_take)/gather | solution.py:410
  28.7 0.6 constant_dynamic-update-slice_fusion.4
  29.3 3.1 %gather_fusion.2 = f32[512]{0:T(512)S(1)} fusion(f32[2048]{0:T(1024)S(1)} %bitcast.134, s32[1024]{0:T(1024)S(1)} %pad_clamp_fusion.2), kind=kCustom, calls=%fused_computation.4.clone | custom fusion | bytes 6144 | tf_op jit(solution)/shard_map/cond/branch_1_fun/jit(_take)/gather | solution.py:410
  32.5 0.6 constant_dynamic-update-slice_fusion.3
  33.1 0.6 constant_dynamic-update-slice_fusion.2
  33.6 0.6 constant_dynamic-update-slice_fusion.1
  34.2 0.6 constant_dynamic-update-slice_fusion
  34.8 0.7 copy.88
  35.5 5.2 %all_gather.17 = f32[16,6,128]{2,1,0:T(8,128)S(1)} all-gather(f32[4,6,128]{2,1,0:T(8,128)S(1)} %copy.88), channel_id=1, replica_groups=mesh['group'=4,'gx'=4,'gy'=2] {'group'}, dimensions={0}, use_global_device_ids=true | all-gather | bytes 61440 | tf_op jit(solution)/shard_map/all_gather | solution.py:430
  40.8 1.1 %conditional.6 = (f32[2,128,8,128]{3,1,2,0:T(8,128)}, f32[3,2048]{0,1:T(8,128)S(1)}) conditional(s32[]{:T(128)} %convert_element_type.67, f32[3,2048]{0,1:T(8,128)S(1)} %bitcast.137, (f32[3,1,1,256]{3,2,1,0:T(1,128)S(1)}, s32[1,1,2,8]{3,2,1,0:T(2,128)S(1)}, f32[16,6,128]{2,1,0:T(8,128)S(1)}, s32[256]{0:T(256)S(1)}, f32[3,2048]{0,1:T(8,128)S(1)}) %tuple.142), branch_computations={%region_9.11_spmd, %region_10.14_spmd} | conditional | flops 15991856 | bytes 2414224 | solution.py:447
  40.8 1.1 %broadcast.217 = f32[2,128,8,128]{3,1,2,0:T(8,128)} broadcast(f32[]{:T(128)} %constant.157.clone), dimensions={} | broadcast | bytes 1048580 | tf_op jit(solution)/shard_map/broadcast.12
  41.9 0.3 copy.100
  42.2 4.6 %all_gather.18 = f32[4,4,8,128]{3,1,0,2:T(4,128)S(1)} all-gather(f32[4,4,4,128]{3,1,0,2:T(4,128)S(1)} %copy.90), channel_id=1, replica_groups=mesh['group'=4,'gx'=4,'gy'=2] {'gy'}, dimensions={2}, use_global_device_ids=true | all-gather | bytes 98304 | tf_op jit(solution)/shard_map/all_gather | solution.py:339
  46.9 14.1 %all_gather.19 = f32[4,16,8,128]{3,2,0,1:T(8,128)S(1)} all-gather(f32[4,4,8,128]{3,2,0,1:T(8,128)S(1)} %copy.91), channel_id=1, replica_groups=mesh['group'=4,'gx'=4,'gy'=2] {'gx'}, dimensions={1}, use_global_device_ids=true | all-gather | bytes 327680 | tf_op jit(solution)/shard_map/all_gather | solution.py:340
  60.9 0.2 conditional.7
  61.1 0.6 dynamic-slice_select_fusion
  61.8 21.4 %collective-permute-start.3 = (f32[4,3,128]{2,0,1:T(4,128)S(1)}, f32[4,3,128]{2,0,1:T(4,128)S(1)}, u32[]{:S(2)}, u32[]{:S(2)}) collective-permute-start(f32[4,3,128]{2,0,1:T(4,128)S(1)} %get-tuple-element.337), channel_id=1, source_target_pairs={{0,16},{8,24},{16,0},{24,8},{1,17},{9,25},{17,1},{25,9},{2,18},{10... | collective-permute-start | bytes 18440 | tf_op jit(solution)/shard_map/ppermute | solution.py:78
  83.3 0.9 %collective-permute-done.2 = f32[4,3,128]{2,0,1:T(4,128)S(1)} collective-permute-done((f32[4,3,128]{2,0,1:T(4,128)S(1)}, f32[4,3,128]{2,0,1:T(4,128)S(1)}, u32[]{:S(2)}, u32[]{:S(2)}) %collective-permute-start.2) | collective-permute-done | bytes 6176 | tf_op jit(solution)/shard_map/ppermute | solution.py:78
  84.2 0.7 collective-permute-done.3
  84.9 0.1 copy.101
  85.0 2.5 %scatter_custom_fusion.1 = f32[3,2048]{0,1:T(8,128)S(1)} fusion(s32[512]{0:T(512)S(1)} %bitcast.177, f32[512,3]{1,0:T(8,128)S(1)} %bitcast.148, f32[]{:T(128)} %constant.176.clone.1), kind=kCustom, calls=%fused_computation.120 | custom fusion | flops 1536 | bytes 24580 | tf_op jit(solution)/shard_map/scatter-add | solution.py:503
  87.6 1.8 %conditional.9 = (bf16[19,2,8,128]{3,2,1,0:T(8,128)(2,1)S(1)}) conditional(s32[]{:T(128)} %convert_element_type.61, () %tuple.41, (f32[1,4,10,130]{3,2,1,0:T(8,128)S(1)}, f32[19,1,1,1]{0,3,2,1:T(1,128)S(1)}, f32[19,1,1,1]{0,3,2,1:T(1,128)S(1)}, f32[19,1,1,1]{0,3,2,1:T(1,128)S(1)}, f32[19,1,1,1]{0,3,2,1:T(1,128)S(1)}, ...), branch_computations={%region_18.20_spmd, %region_19.21_spmd.clone} | conditional | flops 1056324 | bytes 4268820 | solution.py:505
  87.6 0.1 select_select_fusion.1
  87.8 0.1 fusion.1
  87.9 0.2 select_select_fusion
  88.1 0.1 fusion
  88.4 0.3 copy.95
  88.9 0.4 fusion.6
  89.3 0.6 copy-done
  (66 shorter events, 1.1 us)
Async XLA Ops:
  0.6 13.9 %copy-start.6 = (f32[4,4,128]{2,1,0:T(4,128)S(1)}, f32[4,4,128]{2,1,0:T(4,128)}, u32[]{:S(2)}) copy-start(f32[4,4,128]{2,1,0:T(4,128)} %param.49) | copy-start | bytes 24580
  0.6 13.9 %copy-start.7 = (s32[4,4,128]{2,1,0:T(4,128)S(1)}, s32[4,4,128]{2,1,0:T(4,128)}, u32[]{:S(2)}) copy-start(s32[4,4,128]{2,1,0:T(4,128)} %param.50) | copy-start | bytes 24580
  0.7 13.9 %copy-start.2 = (f32[3,4,4,128]{3,2,1,0:T(4,128)S(1)}, f32[3,4,4,128]{3,2,1,0:T(4,128)}, u32[]{:S(2)}) copy-start(f32[3,4,4,128]{3,2,1,0:T(4,128)} %param.48) | copy-start | bytes 73732
  9.2 6.1 %collective-permute-start = (bf16[20,1,10,128]{3,2,1,0:T(8,128)(2,1)S(1)}, bf16[20,1,10,128]{3,2,1,0:T(8,128)(2,1)S(1)}, u32[]{:S(2)}, u32[]{:S(2)}) collective-permute-start(bf16[20,1,10,128]{3,2,1,0:T(8,128)(2,1)S(1)} %get-tuple-element.331), channel_id=1, source_target_pairs={{0,2},{1,3},{2,4},{3,5},{4,6},{5,7},{6,8},{7,9},{8,10},{9,11},{10,... | collective-permute-start | bytes 153608 | tf_op jit(solution)/shard_map/ppermute | solution.py:53
  13.2 6.4 %collective-permute-start.1 = (bf16[20,1,10,128]{3,2,1,0:T(8,128)(2,1)S(1)}, bf16[20,1,10,128]{3,2,1,0:T(8,128)(2,1)S(1)}, u32[]{:S(2)}, u32[]{:S(2)}) collective-permute-start(bf16[20,1,10,128]{3,2,1,0:T(8,128)(2,1)S(1)} %get-tuple-element.332), channel_id=1, source_target_pairs={{2,0},{3,1},{4,2},{5,3},{6,4},{7,5},{8,6},{9,7},{10,8},{11,9},{12,... | collective-permute-start | bytes 153608 | tf_op jit(solution)/shard_map/ppermute | solution.py:53
  20.1 0.7 copy-start.1
  20.1 0.7 copy-start.4
  20.1 0.7 copy-start.5
  20.1 0.7 copy-start.8
  20.8 19.9 %copy-start.9 = (s32[1,1,256]{2,1,0:T(1,128)S(1)}, s32[1,1,256]{2,1,0:T(1,128)}, u32[]{:S(2)}) copy-start(s32[1,1,256]{2,1,0:T(1,128)} %param.52) | copy-start | bytes 3076
  20.8 19.9 %copy-start.10 = (f32[3,1,1,256]{3,2,1,0:T(1,128)S(1)}, f32[3,1,1,256]{3,2,1,0:T(1,128)}, u32[]{:S(2)}) copy-start(f32[3,1,1,256]{3,2,1,0:T(1,128)} %param.53) | copy-start | bytes 9220
  20.8 19.9 %copy-start.11 = (s32[1,1,2,8]{3,2,1,0:T(2,128)S(1)}, s32[1,1,2,8]{3,2,1,0:T(2,128)}, u32[]{:S(2)}) copy-start(s32[1,1,2,8]{3,2,1,0:T(2,128)} %param.54) | copy-start | bytes 196
  20.9 0.7 copy-start.13
  20.9 0.7 copy-start.14
  20.9 0.7 copy-start.15
  41.9 19.1 %copy-start.3 = (f32[24,24]{1,0:T(8,128)S(1)}, f32[24,24]{1,0:T(8,128)}, u32[]{:S(2)}) copy-start(f32[24,24]{1,0:T(8,128)} %param.51) | copy-start | bytes 6916
  61.8 22.4 %collective-permute-start.2 = (f32[4,3,128]{2,0,1:T(4,128)S(1)}, f32[4,3,128]{2,0,1:T(4,128)S(1)}, u32[]{:S(2)}, u32[]{:S(2)}) collective-permute-start(f32[4,3,128]{2,0,1:T(4,128)S(1)} %get-tuple-element.335), channel_id=1, source_target_pairs={{0,8},{8,16},{16,24},{24,0},{1,9},{9,17},{17,25},{25,1},{2,10},{10... | collective-permute-start | bytes 18440 | tf_op jit(solution)/shard_map/ppermute | solution.py:78
  61.8 23.0 %collective-permute-start.3 = (f32[4,3,128]{2,0,1:T(4,128)S(1)}, f32[4,3,128]{2,0,1:T(4,128)S(1)}, u32[]{:S(2)}, u32[]{:S(2)}) collective-permute-start(f32[4,3,128]{2,0,1:T(4,128)S(1)} %get-tuple-element.337), channel_id=1, source_target_pairs={{0,16},{8,24},{16,0},{24,8},{1,17},{9,25},{17,1},{25,9},{2,18},{10... | collective-permute-start | bytes 18440 | tf_op jit(solution)/shard_map/ppermute | solution.py:78
  83.3 1.6 %collective-permute-start.4 = (f32[4,3,128]{2,0,1:T(4,128)S(1)}, f32[4,3,128]{2,0,1:T(4,128)S(1)}, u32[]{:S(2)}, u32[]{:S(2)}) collective-permute-start(f32[4,3,128]{2,0,1:T(4,128)S(1)} %get-tuple-element.336), channel_id=1, source_target_pairs={{0,24},{8,0},{16,8},{24,16},{1,25},{9,1},{17,9},{25,17},{2,26},{10... | collective-permute-start | bytes 18440 | tf_op jit(solution)/shard_map/ppermute | solution.py:78
  88.1 0.8 copy-start.12
  89.3 0.6 copy-start

commit v13 on v11

--- a/solution.py
+++ b/solution.py
@@ -205,7 +205,7 @@
 
 def apply_rows(matrix_ref, values_ref, stiff_ref, out_ref):
     span_cells, across_cells, deep_cells = stiff_ref.shape
-    step = next(size for size in (8, 4, 2, 1) if span_cells % size == 0)
+    step = next(size for size in (16, 8, 4, 2, 1) if span_cells % size == 0)
     shape = (step, across_cells, deep_cells)
     across_at = lax.broadcasted_iota(jnp.int32, shape, 1)
     deep_at = lax.broadcasted_iota(jnp.int32, shape, 2)

time: 80.9 us -> 79.7 us (0.985)
  starting transfers between devices: 27 us -> 25.8 us
    ppermute x3, starting transfers between devices: 21.7 us -> 20.5 us  [passed_along(): return lax.ppermute(value, axis, pairs)]
where the time goes in v13:
time: 79.7 us; the launch traced here: 78.4 us
  blocking collectives  29.3 us (37%)
  starting transfers between devices  25.8 us (32%)
  other arithmetic  8.32 us (10%)
  local copies, waits for them, and re-layouts  7.39 us (9%)
  waiting for transfers between devices  6.25 us (8%)
  between operations  0.97 us (1%)
    ppermute x3, starting transfers between devices, passed_along(): return lax.ppermute(value, axis, pairs)  20.5 us
    all_gather x1, blocking collectives, whole_partition(): return lax.all_gather(every, 'gx', axis=count, tiled=True)  14.1 us
    all_gather x1, blocking collectives, halo_exchange(): every = lax.all_gather(edges, 'gy', axis=0)  5.35 us
    ppermute x2, starting transfers between devices, shifted(): return lax.ppermute(piece, axes, pairs)  5.33 us
    all_gather x1, blocking collectives, per_device(): received = lax.all_gather(packed, 'group', axis=0, tiled=True)  5.25 us
    ppermute x2, waiting for transfers between devices, shifted(): return lax.ppermute(piece, axes, pairs)  4.67 us
    all_gather x1, blocking collectives, whole_partition(): every = lax.all_gather(block, 'gy', axis=count + 1, tiled=True)  4.59 us
    scatter-add x1, other arithmetic, per_device(): jnp.zeros((3, cell_count), jnp.float32).at[:, wall_index].add(speed_parts)  2.51 us
  transfers between devices with their start and end apart: 5, of which 4 were waited for; matrix products, arithmetic and copies ran while one was open for 0% of the time, Pallas kernels for 0%

profile of v13, /device:TPU:0, one launch (start us, length us, event | category | flops | bytes accessed | tf_op | source)
XLA Modules:
  0.0 78.4 jit_solution(15993580242728657310)
XLA Ops:
  0.7 0.7 fusion.59
  1.4 1.0 %fusion.46 = (f32[2,8,128]{2,1,0:T(8,128)S(1)}, f32[2,8,128]{2,1,0:T(8,128)S(1)}, f32[2,8,128]{2,1,0:T(8,128)S(1)}, f32[2,8,128]{2,1,0:T(8,128)S(1)}) fusion(bf16[19,2,8,128]{3,2,1,0:T(8,128)(2,1)} %param.43, f32[19]{0:T(128)} %constant.205, f32[19]{0:T(128)} %constant.206, f32[19]{0:T(128)} %constant.207), kind=kLoop, calls=%fused_computation.126 | loop fusion | flops 303104 | bytes 110820 | tf_op jit(solution)/shard_map/reduce_sum | solution.py:96
  2.4 1.1 %fusion.51 = bf16[19,2,8,128]{3,2,1,0:T(8,128)(2,1)S(1)} fusion(bf16[19,2,8,128]{3,2,1,0:T(8,128)(2,1)} %param.43, f32[2,8,128]{2,1,0:T(8,128)S(1)} %get-tuple-element.283, f32[2,8,128]{2,1,0:T(8,128)S(1)} %get-tuple-element.286, f32[19]{0:T(128)} %constant.207, f32[2,8,128]{2,1,0:T(8,128)S(1)} %get-tuple-element.285, f32[19]{0:T(128)} %constant.206, ...), kind=kLoop, calls=%fused_computation.131 | loop fusion | flops 739328 | bytes 196913 | tf_op jit(solution)/shard_map/convert_element_type | solution.py:395
  3.6 5.3 %all-gather = bf16[40,2,2,128]{3,2,1,0:T(2,128)(2,1)S(1)} all-gather(bf16[20,2,2,128]{3,2,1,0:T(2,128)(2,1)S(1)} %fusion.57), channel_id=2, replica_groups=mesh['group'=4,'gx'=4,'gy'=2] {'gy'}, dimensions={0}, use_global_device_ids=true | all-gather | bytes 61440 | tf_op jit(solution)/shard_map/all_gather | solution.py:58
  9.1 0.1 pad_maximum_fusion.1
  9.2 4.0 %collective-permute-start = (bf16[20,1,10,128]{3,2,1,0:T(8,128)(2,1)S(1)}, bf16[20,1,10,128]{3,2,1,0:T(8,128)(2,1)S(1)}, u32[]{:S(2)}, u32[]{:S(2)}) collective-permute-start(bf16[20,1,10,128]{3,2,1,0:T(8,128)(2,1)S(1)} %get-tuple-element.331), channel_id=1, source_target_pairs={{0,2},{1,3},{2,4},{3,5},{4,6},{5,7},{6,8},{7,9},{8,10},{9,11},{10,... | collective-permute-start | bytes 153608 | tf_op jit(solution)/shard_map/ppermute | solution.py:53
  13.2 1.3 %collective-permute-start.1 = (bf16[20,1,10,128]{3,2,1,0:T(8,128)(2,1)S(1)}, bf16[20,1,10,128]{3,2,1,0:T(8,128)(2,1)S(1)}, u32[]{:S(2)}, u32[]{:S(2)}) collective-permute-start(bf16[20,1,10,128]{3,2,1,0:T(8,128)(2,1)S(1)} %get-tuple-element.332), channel_id=1, source_target_pairs={{2,0},{3,1},{4,2},{5,3},{6,4},{7,5},{8,6},{9,7},{10,8},{11,9},{12,... | collective-permute-start | bytes 153608 | tf_op jit(solution)/shard_map/ppermute | solution.py:53
  14.6 0.4 copy.99
  15.0 0.3 collective-permute-done
  15.3 4.4 %collective-permute-done.1 = bf16[20,1,10,128]{3,2,1,0:T(8,128)(2,1)S(1)} collective-permute-done((bf16[20,1,10,128]{3,2,1,0:T(8,128)(2,1)S(1)}, bf16[20,1,10,128]{3,2,1,0:T(8,128)(2,1)S(1)}, u32[]{:S(2)}, u32[]{:S(2)}) %collective-permute-start.1) | collective-permute-done | bytes 51232 | tf_op jit(solution)/shard_map/ppermute | solution.py:53
  19.6 0.5 fusion.33
  20.2 0.1 slice.272
  20.3 0.5 copy-done.2
  20.8 4.2 %conditional.5 = (f32[4,6,128]{2,0,1:T(4,128)S(1)}) conditional(s32[]{:T(128)} %convert_element_type.61, () %tuple.43, (f32[19,1,1,1]{0,3,2,1:T(1,128)S(1)}, f32[19,1,1,1]{0,3,2,1:T(1,128)S(1)}, f32[19,1,1,1]{0,3,2,1:T(1,128)S(1)}, f32[1,4,10,130]{3,2,1,0:T(8,128)S(1)}, f32[19,4,10,130]{3,2,1,0:T(8,128)S(1)}, ...), branch_computations={%region_4.5_spmd, %region_5.9_spmd.clone} | conditional | flops 646950 | bytes 2346576 | solution.py:424
  20.9 0.1 select_select_fusion.2
  21.1 0.1 fusion.14
  21.2 0.1 slice.207
  21.4 0.1 slice.206
  21.4 0.1 copy-done.13
  21.6 0.2 multiply_reduce_fusion.2
  21.9 0.4 copy.96
  22.3 1.6 %gather_fusion = f32[512,3]{1,0:T(8,128)} fusion(f32[3,2048]{0,1:T(8,128)S(1)} %copy.96, s32[1024]{0:T(1024)S(1)} %pad_clamp_fusion.1), kind=kCustom, calls=%fused_computation.2 | custom fusion | bytes 14336 | tf_op jit(solution)/shard_map/cond/branch_1_fun/gather | solution.py:410
  23.9 1.1 %copy.97 = f32[3,4,128]{2,1,0:T(4,128)S(1)} copy(f32[3,4,128]{0,2,1:T(8,128)} %bitcast.145) | data formatting | bytes 12288 | tf_op jit(solution)/shard_map/cond/branch_1_fun/concatenate | solution.py:421
  25.0 5.2 %all_gather.17 = f32[16,6,128]{2,1,0:T(8,128)S(1)} all-gather(f32[4,6,128]{2,1,0:T(8,128)S(1)} %copy.100), channel_id=1, replica_groups=mesh['group'=4,'gx'=4,'gy'=2] {'group'}, dimensions={0}, use_global_device_ids=true | all-gather | bytes 61440 | tf_op jit(solution)/shard_map/all_gather | solution.py:430
  30.3 1.1 %conditional.6 = (f32[2,128,8,128]{3,1,2,0:T(8,128)}, f32[3,2048]{0,1:T(8,128)S(1)}) conditional(s32[]{:T(128)} %convert_element_type.67, f32[3,2048]{0,1:T(8,128)S(1)} %bitcast.134, (f32[3,1,1,256]{3,2,1,0:T(1,128)S(1)}, s32[1,1,2,8]{3,2,1,0:T(2,128)S(1)}, f32[16,6,128]{2,1,0:T(8,128)S(1)}, s32[256]{0:T(256)S(1)}, f32[3,2048]{0,1:T(8,128)S(1)}) %tuple.142), branch_computations={%region_9.10_spmd, %region_10.13_spmd} | conditional | flops 15991856 | bytes 2414224 | solution.py:447
  30.3 1.1 %broadcast.235 = f32[2,128,8,128]{3,1,2,0:T(8,128)} broadcast(f32[]{:T(128)} %constant.150.clone), dimensions={} | broadcast | bytes 1048580 | tf_op jit(solution)/shard_map/broadcast.18
  31.4 0.3 copy.112
  31.7 4.6 %all_gather.18 = f32[4,4,8,128]{3,1,0,2:T(4,128)S(1)} all-gather(f32[4,4,4,128]{3,1,0,2:T(4,128)S(1)} %copy.102), channel_id=1, replica_groups=mesh['group'=4,'gx'=4,'gy'=2] {'gy'}, dimensions={2}, use_global_device_ids=true | all-gather | bytes 98304 | tf_op jit(solution)/shard_map/all_gather | solution.py:339
  36.4 14.1 %all_gather.19 = f32[4,16,8,128]{3,2,0,1:T(8,128)S(1)} all-gather(f32[4,4,8,128]{3,2,0,1:T(8,128)S(1)} %copy.103), channel_id=1, replica_groups=mesh['group'=4,'gx'=4,'gy'=2] {'gx'}, dimensions={1}, use_global_device_ids=true | all-gather | bytes 327680 | tf_op jit(solution)/shard_map/all_gather | solution.py:340
  50.4 0.2 conditional.7
  50.6 0.6 dynamic-slice_select_fusion
  51.3 0.1 collective-permute-start.2
  51.3 20.4 %collective-permute-start.3 = (f32[4,3,128]{2,0,1:T(4,128)S(1)}, f32[4,3,128]{2,0,1:T(4,128)S(1)}, u32[]{:S(2)}, u32[]{:S(2)}) collective-permute-start(f32[4,3,128]{2,0,1:T(4,128)S(1)} %get-tuple-element.337), channel_id=1, source_target_pairs={{0,16},{8,24},{16,0},{24,8},{1,17},{9,25},{17,1},{25,9},{2,18},{10... | collective-permute-start | bytes 18440 | tf_op jit(solution)/shard_map/ppermute | solution.py:78
  71.8 0.9 %collective-permute-done.2 = f32[4,3,128]{2,0,1:T(4,128)S(1)} collective-permute-done((f32[4,3,128]{2,0,1:T(4,128)S(1)}, f32[4,3,128]{2,0,1:T(4,128)S(1)}, u32[]{:S(2)}, u32[]{:S(2)}) %collective-permute-start.2) | collective-permute-done | bytes 6176 | tf_op jit(solution)/shard_map/ppermute | solution.py:78
  72.7 0.7 collective-permute-done.3
  73.4 0.1 copy.113
  73.5 2.5 %scatter_custom_fusion.1 = f32[3,2048]{0,1:T(8,128)S(1)} fusion(s32[512]{0:T(512)S(1)} %bitcast.175, f32[512,3]{1,0:T(8,128)S(1)} %bitcast.146, f32[]{:T(128)} %constant.169.clone.1), kind=kCustom, calls=%fused_computation.113 | custom fusion | flops 1536 | bytes 24580 | tf_op jit(solution)/shard_map/scatter-add | solution.py:503
  76.0 1.8 %conditional.9 = (bf16[19,2,8,128]{3,2,1,0:T(8,128)(2,1)S(1)}) conditional(s32[]{:T(128)} %convert_element_type.61, () %tuple.40, (f32[1,4,10,130]{3,2,1,0:T(8,128)S(1)}, f32[19,1,1,1]{0,3,2,1:T(1,128)S(1)}, f32[19,1,1,1]{0,3,2,1:T(1,128)S(1)}, f32[19,1,1,1]{0,3,2,1:T(1,128)S(1)}, f32[19,1,1,1]{0,3,2,1:T(1,128)S(1)}, ...), branch_computations={%region_18.19_spmd, %region_19.20_spmd.clone} | conditional | flops 1056324 | bytes 4268820 | solution.py:505
  76.1 0.1 select_select_fusion.1
  76.3 0.1 fusion.1
  76.4 0.2 select_select_fusion
  76.6 0.1 fusion
  76.8 0.1 slice.231
  76.9 0.3 copy.107
  77.3 0.1 slice.230
  77.3 0.1 slice.241
  77.4 0.4 fusion.6
  77.8 0.6 copy-done
  (63 shorter events, 0.6 us)
Async XLA Ops:
  0.6 13.9 %copy-start.6 = (f32[4,4,128]{2,1,0:T(4,128)S(1)}, f32[4,4,128]{2,1,0:T(4,128)}, u32[]{:S(2)}) copy-start(f32[4,4,128]{2,1,0:T(4,128)} %param.47) | copy-start | bytes 24580
  0.6 13.9 %copy-start.7 = (s32[4,4,128]{2,1,0:T(4,128)S(1)}, s32[4,4,128]{2,1,0:T(4,128)}, u32[]{:S(2)}) copy-start(s32[4,4,128]{2,1,0:T(4,128)} %param.48) | copy-start | bytes 24580
  0.7 13.9 %copy-start.1 = (f32[3,4,4,128]{3,2,1,0:T(4,128)S(1)}, f32[3,4,4,128]{3,2,1,0:T(4,128)}, u32[]{:S(2)}) copy-start(f32[3,4,4,128]{3,2,1,0:T(4,128)} %param.46) | copy-start | bytes 73732
  9.2 6.1 %collective-permute-start = (bf16[20,1,10,128]{3,2,1,0:T(8,128)(2,1)S(1)}, bf16[20,1,10,128]{3,2,1,0:T(8,128)(2,1)S(1)}, u32[]{:S(2)}, u32[]{:S(2)}) collective-permute-start(bf16[20,1,10,128]{3,2,1,0:T(8,128)(2,1)S(1)} %get-tuple-element.331), channel_id=1, source_target_pairs={{0,2},{1,3},{2,4},{3,5},{4,6},{5,7},{6,8},{7,9},{8,10},{9,11},{10,... | collective-permute-start | bytes 153608 | tf_op jit(solution)/shard_map/ppermute | solution.py:53
  13.2 6.4 %collective-permute-start.1 = (bf16[20,1,10,128]{3,2,1,0:T(8,128)(2,1)S(1)}, bf16[20,1,10,128]{3,2,1,0:T(8,128)(2,1)S(1)}, u32[]{:S(2)}, u32[]{:S(2)}) collective-permute-start(bf16[20,1,10,128]{3,2,1,0:T(8,128)(2,1)S(1)} %get-tuple-element.332), channel_id=1, source_target_pairs={{2,0},{3,1},{4,2},{5,3},{6,4},{7,5},{8,6},{9,7},{10,8},{11,9},{12,... | collective-permute-start | bytes 153608 | tf_op jit(solution)/shard_map/ppermute | solution.py:53
  20.1 0.7 copy-start.2
  20.1 0.7 copy-start.4
  20.1 0.7 copy-start.5
  20.2 0.7 copy-start.8
  20.8 9.5 %copy-start.9 = (s32[1,1,256]{2,1,0:T(1,128)S(1)}, s32[1,1,256]{2,1,0:T(1,128)}, u32[]{:S(2)}) copy-start(s32[1,1,256]{2,1,0:T(1,128)} %param.50) | copy-start | bytes 3076
  20.8 9.5 %copy-start.10 = (f32[3,1,1,256]{3,2,1,0:T(1,128)S(1)}, f32[3,1,1,256]{3,2,1,0:T(1,128)}, u32[]{:S(2)}) copy-start(f32[3,1,1,256]{3,2,1,0:T(1,128)} %param.51) | copy-start | bytes 9220
  20.8 9.5 %copy-start.11 = (s32[1,1,2,8]{3,2,1,0:T(2,128)S(1)}, s32[1,1,2,8]{3,2,1,0:T(2,128)}, u32[]{:S(2)}) copy-start(s32[1,1,2,8]{3,2,1,0:T(2,128)} %param.52) | copy-start | bytes 196
  20.9 0.7 copy-start.13
  20.9 0.7 copy-start.14
  20.9 0.7 copy-start.15
  31.4 19.1 %copy-start.3 = (f32[24,24]{1,0:T(8,128)S(1)}, f32[24,24]{1,0:T(8,128)}, u32[]{:S(2)}) copy-start(f32[24,24]{1,0:T(8,128)} %param.49) | copy-start | bytes 6916
  51.3 21.4 %collective-permute-start.2 = (f32[4,3,128]{2,0,1:T(4,128)S(1)}, f32[4,3,128]{2,0,1:T(4,128)S(1)}, u32[]{:S(2)}, u32[]{:S(2)}) collective-permute-start(f32[4,3,128]{2,0,1:T(4,128)S(1)} %get-tuple-element.335), channel_id=1, source_target_pairs={{0,8},{8,16},{16,24},{24,0},{1,9},{9,17},{17,25},{25,1},{2,10},{10... | collective-permute-start | bytes 18440 | tf_op jit(solution)/shard_map/ppermute | solution.py:78
  51.3 22.0 %collective-permute-start.3 = (f32[4,3,128]{2,0,1:T(4,128)S(1)}, f32[4,3,128]{2,0,1:T(4,128)S(1)}, u32[]{:S(2)}, u32[]{:S(2)}) collective-permute-start(f32[4,3,128]{2,0,1:T(4,128)S(1)} %get-tuple-element.337), channel_id=1, source_target_pairs={{0,16},{8,24},{16,0},{24,8},{1,17},{9,25},{17,1},{25,9},{2,18},{10... | collective-permute-start | bytes 18440 | tf_op jit(solution)/shard_map/ppermute | solution.py:78
  71.8 1.6 %collective-permute-start.4 = (f32[4,3,128]{2,0,1:T(4,128)S(1)}, f32[4,3,128]{2,0,1:T(4,128)S(1)}, u32[]{:S(2)}, u32[]{:S(2)}) collective-permute-start(f32[4,3,128]{2,0,1:T(4,128)S(1)} %get-tuple-element.336), channel_id=1, source_target_pairs={{0,24},{8,0},{16,8},{24,16},{1,25},{9,1},{17,9},{25,17},{2,26},{10... | collective-permute-start | bytes 18440 | tf_op jit(solution)/shard_map/ppermute | solution.py:78
  76.6 0.8 %copy-start.12 = (f32[19]{0:T(128)S(1)}, f32[19]{0:T(128)}, u32[]{:S(2)}) copy-start(f32[19]{0:T(128)} %constant.208) | copy-start | bytes 232 | tf_op jit(solution)/shard_map/cond
  77.8 0.6 copy-start

commit v14 on v13

--- a/solution.py
+++ b/solution.py
@@ -336,8 +336,8 @@
 def whole_partition(block):
     lead = block.shape[:-3]
     count = len(lead)
-    every = lax.all_gather(block, "gy", axis=count + 1, tiled=True)
-    return lax.all_gather(every, "gx", axis=count, tiled=True)
+    every = lax.all_gather(block, "gx", axis=count, tiled=True)
+    return lax.all_gather(every, "gy", axis=count + 1, tiled=True)
 
 
 def own_part(whole, rows, cols):

time: 79.7 us -> 79.3 us (level)
  starting transfers between devices: 25.8 us -> 24.8 us
    ppermute x3, starting transfers between devices: 20.5 us -> 19.5 us  [passed_along(): return lax.ppermute(value, axis, pairs)]
where the time goes in v14:
time: 79.3 us; the launch traced here: 78 us
  blocking collectives  29.8 us (38%)
  starting transfers between devices  24.8 us (31%)
  other arithmetic  8.32 us (10%)
  local copies, waits for them, and re-layouts  7.37 us (9%)
  waiting for transfers between devices  6.25 us (8%)
  between operations  0.96 us (1%)
    ppermute x3, starting transfers between devices, passed_along(): return lax.ppermute(value, axis, pairs)  19.5 us
    all_gather x1, blocking collectives, whole_partition(): every = lax.all_gather(block, 'gx', axis=count, tiled=True)  13.6 us
    all_gather x1, blocking collectives, whole_partition(): return lax.all_gather(every, 'gy', axis=count + 1, tiled=True)  5.64 us
    all_gather x1, blocking collectives, halo_exchange(): every = lax.all_gather(edges, 'gy', axis=0)  5.35 us
    ppermute x2, starting transfers between devices, shifted(): return lax.ppermute(piece, axes, pairs)  5.33 us
    all_gather x1, blocking collectives, per_device(): received = lax.all_gather(packed, 'group', axis=0, tiled=True)  5.25 us
    ppermute x2, waiting for transfers between devices, shifted(): return lax.ppermute(piece, axes, pairs)  4.67 us
    scatter-add x1, other arithmetic, per_device(): jnp.zeros((3, cell_count), jnp.float32).at[:, wall_index].add(speed_parts)  2.51 us
  transfers between devices with their start and end apart: 5, of which 4 were waited for; matrix products, arithmetic and copies ran while one was open for 0% of the time, Pallas kernels for 0%

profile of v14, /device:TPU:0, one launch (start us, length us, event | category | flops | bytes accessed | tf_op | source)
XLA Modules:
  0.0 78.0 jit_solution(3003537442807521416)
XLA Ops:
  0.7 0.7 fusion.59
  1.4 1.0 %fusion.46 = (f32[2,8,128]{2,1,0:T(8,128)S(1)}, f32[2,8,128]{2,1,0:T(8,128)S(1)}, f32[2,8,128]{2,1,0:T(8,128)S(1)}, f32[2,8,128]{2,1,0:T(8,128)S(1)}) fusion(bf16[19,2,8,128]{3,2,1,0:T(8,128)(2,1)} %param.43, f32[19]{0:T(128)} %constant.205, f32[19]{0:T(128)} %constant.206, f32[19]{0:T(128)} %constant.207), kind=kLoop, calls=%fused_computation.126 | loop fusion | flops 303104 | bytes 110820 | tf_op jit(solution)/shard_map/reduce_sum | solution.py:96
  2.4 1.1 %fusion.51 = bf16[19,2,8,128]{3,2,1,0:T(8,128)(2,1)S(1)} fusion(bf16[19,2,8,128]{3,2,1,0:T(8,128)(2,1)} %param.43, f32[2,8,128]{2,1,0:T(8,128)S(1)} %get-tuple-element.265, f32[2,8,128]{2,1,0:T(8,128)S(1)} %get-tuple-element.268, f32[19]{0:T(128)} %constant.207, f32[2,8,128]{2,1,0:T(8,128)S(1)} %get-tuple-element.267, f32[19]{0:T(128)} %constant.206, ...), kind=kLoop, calls=%fused_computation.131 | loop fusion | flops 739328 | bytes 196913 | tf_op jit(solution)/shard_map/convert_element_type | solution.py:395
  3.6 5.3 %all-gather = bf16[40,2,2,128]{3,2,1,0:T(2,128)(2,1)S(1)} all-gather(bf16[20,2,2,128]{3,2,1,0:T(2,128)(2,1)S(1)} %fusion.57), channel_id=2, replica_groups=mesh['group'=4,'gx'=4,'gy'=2] {'gy'}, dimensions={0}, use_global_device_ids=true | all-gather | bytes 61440 | tf_op jit(solution)/shard_map/all_gather | solution.py:58
  9.1 0.1 pad_maximum_fusion.1
  9.2 4.0 %collective-permute-start = (bf16[20,1,10,128]{3,2,1,0:T(8,128)(2,1)S(1)}, bf16[20,1,10,128]{3,2,1,0:T(8,128)(2,1)S(1)}, u32[]{:S(2)}, u32[]{:S(2)}) collective-permute-start(bf16[20,1,10,128]{3,2,1,0:T(8,128)(2,1)S(1)} %get-tuple-element.313), channel_id=1, source_target_pairs={{0,2},{1,3},{2,4},{3,5},{4,6},{5,7},{6,8},{7,9},{8,10},{9,11},{10,... | collective-permute-start | bytes 153608 | tf_op jit(solution)/shard_map/ppermute | solution.py:53
  13.2 1.3 %collective-permute-start.1 = (bf16[20,1,10,128]{3,2,1,0:T(8,128)(2,1)S(1)}, bf16[20,1,10,128]{3,2,1,0:T(8,128)(2,1)S(1)}, u32[]{:S(2)}, u32[]{:S(2)}) collective-permute-start(bf16[20,1,10,128]{3,2,1,0:T(8,128)(2,1)S(1)} %get-tuple-element.314), channel_id=1, source_target_pairs={{2,0},{3,1},{4,2},{5,3},{6,4},{7,5},{8,6},{9,7},{10,8},{11,9},{12,... | collective-permute-start | bytes 153608 | tf_op jit(solution)/shard_map/ppermute | solution.py:53
  14.6 0.4 copy.86
  15.0 0.3 collective-permute-done
  15.3 4.4 %collective-permute-done.1 = bf16[20,1,10,128]{3,2,1,0:T(8,128)(2,1)S(1)} collective-permute-done((bf16[20,1,10,128]{3,2,1,0:T(8,128)(2,1)S(1)}, bf16[20,1,10,128]{3,2,1,0:T(8,128)(2,1)S(1)}, u32[]{:S(2)}, u32[]{:S(2)}) %collective-permute-start.1) | collective-permute-done | bytes 51232 | tf_op jit(solution)/shard_map/ppermute | solution.py:53
  19.6 0.5 fusion.33
  20.2 0.1 slice.272
  20.3 0.5 copy-done.2
  20.8 4.2 %conditional.5 = (f32[4,6,128]{2,0,1:T(4,128)S(1)}) conditional(s32[]{:T(128)} %convert_element_type.61, () %tuple.43, (f32[19,1,1,1]{0,3,2,1:T(1,128)S(1)}, f32[19,1,1,1]{0,3,2,1:T(1,128)S(1)}, f32[19,1,1,1]{0,3,2,1:T(1,128)S(1)}, f32[1,4,10,130]{3,2,1,0:T(8,128)S(1)}, f32[19,4,10,130]{3,2,1,0:T(8,128)S(1)}, ...), branch_computations={%region_4.5_spmd, %region_5.9_spmd.clone} | conditional | flops 646950 | bytes 2346576 | solution.py:424
  20.9 0.1 select_select_fusion.2
  21.1 0.1 fusion.14
  21.2 0.1 slice.207
  21.4 0.1 slice.206
  21.4 0.1 copy-done.13
  21.6 0.2 multiply_reduce_fusion.2
  21.9 0.4 copy.83
  22.3 1.6 %gather_fusion = f32[512,3]{1,0:T(8,128)} fusion(f32[3,2048]{0,1:T(8,128)S(1)} %copy.83, s32[1024]{0:T(1024)S(1)} %pad_clamp_fusion.1), kind=kCustom, calls=%fused_computation.2 | custom fusion | bytes 14336 | tf_op jit(solution)/shard_map/cond/branch_1_fun/gather | solution.py:410
  23.9 1.1 %copy.84 = f32[3,4,128]{2,1,0:T(4,128)S(1)} copy(f32[3,4,128]{0,2,1:T(8,128)} %bitcast.145) | data formatting | bytes 12288 | tf_op jit(solution)/shard_map/cond/branch_1_fun/concatenate | solution.py:421
  25.0 5.2 %all_gather.17 = f32[16,6,128]{2,1,0:T(8,128)S(1)} all-gather(f32[4,6,128]{2,1,0:T(8,128)S(1)} %copy.87), channel_id=1, replica_groups=mesh['group'=4,'gx'=4,'gy'=2] {'group'}, dimensions={0}, use_global_device_ids=true | all-gather | bytes 61440 | tf_op jit(solution)/shard_map/all_gather | solution.py:430
  30.3 1.1 %conditional.6 = (f32[2,128,8,128]{3,1,2,0:T(8,128)}, f32[3,2048]{0,1:T(8,128)S(1)}) conditional(s32[]{:T(128)} %convert_element_type.67, f32[3,2048]{0,1:T(8,128)S(1)} %bitcast.134, (f32[3,1,1,256]{3,2,1,0:T(1,128)S(1)}, s32[1,1,2,8]{3,2,1,0:T(2,128)S(1)}, f32[16,6,128]{2,1,0:T(8,128)S(1)}, s32[256]{0:T(256)S(1)}, f32[3,2048]{0,1:T(8,128)S(1)}) %tuple.139), branch_computations={%region_9.10_spmd, %region_10.13_spmd} | conditional | flops 15991856 | bytes 2414224 | solution.py:447
  30.3 1.1 %broadcast.235 = f32[2,128,8,128]{3,1,2,0:T(8,128)} broadcast(f32[]{:T(128)} %constant.150.clone), dimensions={} | broadcast | bytes 1048580 | tf_op jit(solution)/shard_map/broadcast.18
  31.4 0.3 copy.98
  31.7 13.6 %all_gather.18 = f32[4,16,4,128]{3,2,1,0:T(4,128)S(1)} all-gather(f32[4,4,4,128]{3,2,1,0:T(4,128)S(1)} %pad_maximum_fusion.2), channel_id=1, replica_groups=mesh['group'=4,'gx'=4,'gy'=2] {'gx'}, dimensions={1}, use_global_device_ids=true | all-gather | bytes 163840 | tf_op jit(solution)/shard_map/all_gather | solution.py:339
  45.3 5.6 %all_gather.19 = f32[4,16,8,128]{3,1,0,2:T(8,128)S(1)} all-gather(f32[4,16,4,128]{3,1,0,2:T(8,128)S(1)} %copy.89), channel_id=1, replica_groups=mesh['group'=4,'gx'=4,'gy'=2] {'gy'}, dimensions={2}, use_global_device_ids=true | all-gather | bytes 393216 | tf_op jit(solution)/shard_map/all_gather | solution.py:340
  51.0 0.2 conditional.7
  51.2 0.6 dynamic-slice_select_fusion
  51.8 0.1 collective-permute-start.2
  51.9 19.4 %collective-permute-start.3 = (f32[4,3,128]{2,0,1:T(4,128)S(1)}, f32[4,3,128]{2,0,1:T(4,128)S(1)}, u32[]{:S(2)}, u32[]{:S(2)}) collective-permute-start(f32[4,3,128]{2,0,1:T(4,128)S(1)} %get-tuple-element.319), channel_id=1, source_target_pairs={{0,16},{8,24},{16,0},{24,8},{1,17},{9,25},{17,1},{25,9},{2,18},{10... | collective-permute-start | bytes 18440 | tf_op jit(solution)/shard_map/ppermute | solution.py:78
  71.3 0.9 %collective-permute-done.2 = f32[4,3,128]{2,0,1:T(4,128)S(1)} collective-permute-done((f32[4,3,128]{2,0,1:T(4,128)S(1)}, f32[4,3,128]{2,0,1:T(4,128)S(1)}, u32[]{:S(2)}, u32[]{:S(2)}) %collective-permute-start.2) | collective-permute-done | bytes 6176 | tf_op jit(solution)/shard_map/ppermute | solution.py:78
  72.2 0.7 collective-permute-done.3
  72.9 0.1 copy.99
  73.1 2.5 %scatter_custom_fusion.1 = f32[3,2048]{0,1:T(8,128)S(1)} fusion(s32[512]{0:T(512)S(1)} %bitcast.175, f32[512,3]{1,0:T(8,128)S(1)} %bitcast.146, f32[]{:T(128)} %constant.169.clone.1), kind=kCustom, calls=%fused_computation.113 | custom fusion | flops 1536 | bytes 24580 | tf_op jit(solution)/shard_map/scatter-add | solution.py:503
  75.6 1.8 %conditional.9 = (bf16[19,2,8,128]{3,2,1,0:T(8,128)(2,1)S(1)}) conditional(s32[]{:T(128)} %convert_element_type.61, () %tuple.40, (f32[1,4,10,130]{3,2,1,0:T(8,128)S(1)}, f32[19,1,1,1]{0,3,2,1:T(1,128)S(1)}, f32[19,1,1,1]{0,3,2,1:T(1,128)S(1)}, f32[19,1,1,1]{0,3,2,1:T(1,128)S(1)}, f32[19,1,1,1]{0,3,2,1:T(1,128)S(1)}, ...), branch_computations={%region_18.19_spmd, %region_19.20_spmd.clone} | conditional | flops 1056324 | bytes 4268820 | solution.py:505
  75.7 0.1 select_select_fusion.1
  75.8 0.1 fusion.1
  76.0 0.2 select_select_fusion
  76.2 0.1 fusion
  76.3 0.1 slice.231
  76.4 0.3 copy.93
  76.8 0.1 slice.230
  76.9 0.1 slice.241
  77.0 0.4 fusion.6
  77.4 0.6 copy-done
  (62 shorter events, 0.5 us)
Async XLA Ops:
  0.6 13.9 %copy-start.6 = (f32[4,4,128]{2,1,0:T(4,128)S(1)}, f32[4,4,128]{2,1,0:T(4,128)}, u32[]{:S(2)}) copy-start(f32[4,4,128]{2,1,0:T(4,128)} %param.47) | copy-start | bytes 24580
  0.6 13.9 %copy-start.7 = (s32[4,4,128]{2,1,0:T(4,128)S(1)}, s32[4,4,128]{2,1,0:T(4,128)}, u32[]{:S(2)}) copy-start(s32[4,4,128]{2,1,0:T(4,128)} %param.48) | copy-start | bytes 24580
  0.7 13.9 %copy-start.1 = (f32[3,4,4,128]{3,2,1,0:T(4,128)S(1)}, f32[3,4,4,128]{3,2,1,0:T(4,128)}, u32[]{:S(2)}) copy-start(f32[3,4,4,128]{3,2,1,0:T(4,128)} %param.46) | copy-start | bytes 73732
  9.2 6.1 %collective-permute-start = (bf16[20,1,10,128]{3,2,1,0:T(8,128)(2,1)S(1)}, bf16[20,1,10,128]{3,2,1,0:T(8,128)(2,1)S(1)}, u32[]{:S(2)}, u32[]{:S(2)}) collective-permute-start(bf16[20,1,10,128]{3,2,1,0:T(8,128)(2,1)S(1)} %get-tuple-element.313), channel_id=1, source_target_pairs={{0,2},{1,3},{2,4},{3,5},{4,6},{5,7},{6,8},{7,9},{8,10},{9,11},{10,... | collective-permute-start | bytes 153608 | tf_op jit(solution)/shard_map/ppermute | solution.py:53
  13.2 6.4 %collective-permute-start.1 = (bf16[20,1,10,128]{3,2,1,0:T(8,128)(2,1)S(1)}, bf16[20,1,10,128]{3,2,1,0:T(8,128)(2,1)S(1)}, u32[]{:S(2)}, u32[]{:S(2)}) collective-permute-start(bf16[20,1,10,128]{3,2,1,0:T(8,128)(2,1)S(1)} %get-tuple-element.314), channel_id=1, source_target_pairs={{2,0},{3,1},{4,2},{5,3},{6,4},{7,5},{8,6},{9,7},{10,8},{11,9},{12,... | collective-permute-start | bytes 153608 | tf_op jit(solution)/shard_map/ppermute | solution.py:53
  20.1 0.7 copy-start.2
  20.1 0.7 copy-start.4
  20.1 0.7 copy-start.5
  20.2 0.7 copy-start.8
  20.8 9.5 %copy-start.9 = (s32[1,1,256]{2,1,0:T(1,128)S(1)}, s32[1,1,256]{2,1,0:T(1,128)}, u32[]{:S(2)}) copy-start(s32[1,1,256]{2,1,0:T(1,128)} %param.50) | copy-start | bytes 3076
  20.8 9.5 %copy-start.10 = (f32[3,1,1,256]{3,2,1,0:T(1,128)S(1)}, f32[3,1,1,256]{3,2,1,0:T(1,128)}, u32[]{:S(2)}) copy-start(f32[3,1,1,256]{3,2,1,0:T(1,128)} %param.51) | copy-start | bytes 9220
  20.8 9.5 %copy-start.11 = (s32[1,1,2,8]{3,2,1,0:T(2,128)S(1)}, s32[1,1,2,8]{3,2,1,0:T(2,128)}, u32[]{:S(2)}) copy-start(s32[1,1,2,8]{3,2,1,0:T(2,128)} %param.52) | copy-start | bytes 196
  20.9 0.7 copy-start.13
  20.9 0.7 copy-start.14
  20.9 0.7 copy-start.15
  31.4 19.6 %copy-start.3 = (f32[24,24]{1,0:T(8,128)S(1)}, f32[24,24]{1,0:T(8,128)}, u32[]{:S(2)}) copy-start(f32[24,24]{1,0:T(8,128)} %param.49) | copy-start | bytes 6916
  51.8 20.4 %collective-permute-start.2 = (f32[4,3,128]{2,0,1:T(4,128)S(1)}, f32[4,3,128]{2,0,1:T(4,128)S(1)}, u32[]{:S(2)}, u32[]{:S(2)}) collective-permute-start(f32[4,3,128]{2,0,1:T(4,128)S(1)} %get-tuple-element.317), channel_id=1, source_target_pairs={{0,8},{8,16},{16,24},{24,0},{1,9},{9,17},{17,25},{25,1},{2,10},{10... | collective-permute-start | bytes 18440 | tf_op jit(solution)/shard_map/ppermute | solution.py:78
  51.9 21.0 %collective-permute-start.3 = (f32[4,3,128]{2,0,1:T(4,128)S(1)}, f32[4,3,128]{2,0,1:T(4,128)S(1)}, u32[]{:S(2)}, u32[]{:S(2)}) collective-permute-start(f32[4,3,128]{2,0,1:T(4,128)S(1)} %get-tuple-element.319), channel_id=1, source_target_pairs={{0,16},{8,24},{16,0},{24,8},{1,17},{9,25},{17,1},{25,9},{2,18},{10... | collective-permute-start | bytes 18440 | tf_op jit(solution)/shard_map/ppermute | solution.py:78
  71.3 1.6 %collective-permute-start.4 = (f32[4,3,128]{2,0,1:T(4,128)S(1)}, f32[4,3,128]{2,0,1:T(4,128)S(1)}, u32[]{:S(2)}, u32[]{:S(2)}) collective-permute-start(f32[4,3,128]{2,0,1:T(4,128)S(1)} %get-tuple-element.318), channel_id=1, source_target_pairs={{0,24},{8,0},{16,8},{24,16},{1,25},{9,1},{17,9},{25,17},{2,26},{10... | collective-permute-start | bytes 18440 | tf_op jit(solution)/shard_map/ppermute | solution.py:78
  76.2 0.8 %copy-start.12 = (f32[19]{0:T(128)S(1)}, f32[19]{0:T(128)}, u32[]{:S(2)}) copy-start(f32[19]{0:T(128)} %constant.208) | copy-start | bytes 232 | tf_op jit(solution)/shard_map/cond
  77.4 0.6 copy-start

commit v15 on v14

--- a/solution.py
+++ b/solution.py
@@ -474,7 +474,9 @@
             lambda operands: jnp.zeros_like(operands[0][0:3]),
             (joined, elem_matrix),
         )
-    solution = jnp.where(is_struct, own_part(whole_solution, rows, cols), 0.0)
+    solution = own_part(whole_solution, rows, cols)
+    if struct_groups > 1:
+        solution = jnp.where(is_struct, solution, 0.0)
     tile_slots = received.shape[0]
 
     def struct_back(operands):

time: 79.3 us -> 79.3 us (level)
  no operation moved by 1% of the time
where the time goes in v15:
time: 79.3 us; the launch traced here: 78 us
  blocking collectives  29.8 us (38%)
  starting transfers between devices  24.8 us (31%)
  local copies, waits for them, and re-layouts  7.99 us (10%)
  other arithmetic  7.69 us (10%)
  waiting for transfers between devices  6.25 us (8%)
  between operations  0.96 us (1%)
    ppermute x3, starting transfers between devices, passed_along(): return lax.ppermute(value, axis, pairs)  19.5 us
    all_gather x1, blocking collectives, whole_partition(): every = lax.all_gather(block, 'gx', axis=count, tiled=True)  13.6 us
    all_gather x1, blocking collectives, whole_partition(): return lax.all_gather(every, 'gy', axis=count + 1, tiled=True)  5.64 us
    all_gather x1, blocking collectives, halo_exchange(): every = lax.all_gather(edges, 'gy', axis=0)  5.35 us
    ppermute x2, starting transfers between devices, shifted(): return lax.ppermute(piece, axes, pairs)  5.33 us
    all_gather x1, blocking collectives, per_device(): received = lax.all_gather(packed, 'group', axis=0, tiled=True)  5.25 us
    ppermute x2, waiting for transfers between devices, shifted(): return lax.ppermute(piece, axes, pairs)  4.67 us
    scatter-add x1, other arithmetic, per_device(): jnp.zeros((3, cell_count), jnp.float32).at[:, wall_index].add(speed_parts)  2.51 us
  transfers between devices with their start and end apart: 5, of which 4 were waited for; matrix products, arithmetic and copies ran while one was open for 0% of the time, Pallas kernels for 0%

profile of v15, /device:TPU:0, one launch (start us, length us, event | category | flops | bytes accessed | tf_op | source)
XLA Modules:
  0.0 78.0 jit_solution(5293299510730560398)
XLA Ops:
  0.7 0.7 fusion.59
  1.4 1.0 %fusion.46 = (f32[2,8,128]{2,1,0:T(8,128)S(1)}, f32[2,8,128]{2,1,0:T(8,128)S(1)}, f32[2,8,128]{2,1,0:T(8,128)S(1)}, f32[2,8,128]{2,1,0:T(8,128)S(1)}) fusion(bf16[19,2,8,128]{3,2,1,0:T(8,128)(2,1)} %param.43, f32[19]{0:T(128)} %constant.205, f32[19]{0:T(128)} %constant.206, f32[19]{0:T(128)} %constant.207), kind=kLoop, calls=%fused_computation.126 | loop fusion | flops 303104 | bytes 110820 | tf_op jit(solution)/shard_map/reduce_sum | solution.py:96
  2.4 1.1 %fusion.51 = bf16[19,2,8,128]{3,2,1,0:T(8,128)(2,1)S(1)} fusion(bf16[19,2,8,128]{3,2,1,0:T(8,128)(2,1)} %param.43, f32[2,8,128]{2,1,0:T(8,128)S(1)} %get-tuple-element.265, f32[2,8,128]{2,1,0:T(8,128)S(1)} %get-tuple-element.268, f32[19]{0:T(128)} %constant.207, f32[2,8,128]{2,1,0:T(8,128)S(1)} %get-tuple-element.267, f32[19]{0:T(128)} %constant.206, ...), kind=kLoop, calls=%fused_computation.131 | loop fusion | flops 739328 | bytes 196913 | tf_op jit(solution)/shard_map/convert_element_type | solution.py:395
  3.6 5.3 %all-gather = bf16[40,2,2,128]{3,2,1,0:T(2,128)(2,1)S(1)} all-gather(bf16[20,2,2,128]{3,2,1,0:T(2,128)(2,1)S(1)} %fusion.57), channel_id=2, replica_groups=mesh['group'=4,'gx'=4,'gy'=2] {'gy'}, dimensions={0}, use_global_device_ids=true | all-gather | bytes 61440 | tf_op jit(solution)/shard_map/all_gather | solution.py:58
  9.1 0.1 pad_maximum_fusion.1
  9.2 4.0 %collective-permute-start = (bf16[20,1,10,128]{3,2,1,0:T(8,128)(2,1)S(1)}, bf16[20,1,10,128]{3,2,1,0:T(8,128)(2,1)S(1)}, u32[]{:S(2)}, u32[]{:S(2)}) collective-permute-start(bf16[20,1,10,128]{3,2,1,0:T(8,128)(2,1)S(1)} %get-tuple-element.313), channel_id=1, source_target_pairs={{0,2},{1,3},{2,4},{3,5},{4,6},{5,7},{6,8},{7,9},{8,10},{9,11},{10,... | collective-permute-start | bytes 153608 | tf_op jit(solution)/shard_map/ppermute | solution.py:53
  13.2 1.3 %collective-permute-start.1 = (bf16[20,1,10,128]{3,2,1,0:T(8,128)(2,1)S(1)}, bf16[20,1,10,128]{3,2,1,0:T(8,128)(2,1)S(1)}, u32[]{:S(2)}, u32[]{:S(2)}) collective-permute-start(bf16[20,1,10,128]{3,2,1,0:T(8,128)(2,1)S(1)} %get-tuple-element.314), channel_id=1, source_target_pairs={{2,0},{3,1},{4,2},{5,3},{6,4},{7,5},{8,6},{9,7},{10,8},{11,9},{12,... | collective-permute-start | bytes 153608 | tf_op jit(solution)/shard_map/ppermute | solution.py:53
  14.6 0.4 copy.86
  15.0 0.3 collective-permute-done
  15.3 4.4 %collective-permute-done.1 = bf16[20,1,10,128]{3,2,1,0:T(8,128)(2,1)S(1)} collective-permute-done((bf16[20,1,10,128]{3,2,1,0:T(8,128)(2,1)S(1)}, bf16[20,1,10,128]{3,2,1,0:T(8,128)(2,1)S(1)}, u32[]{:S(2)}, u32[]{:S(2)}) %collective-permute-start.1) | collective-permute-done | bytes 51232 | tf_op jit(solution)/shard_map/ppermute | solution.py:53
  19.6 0.5 fusion.33
  20.2 0.1 slice.272
  20.3 0.5 copy-done.2
  20.8 4.2 %conditional.5 = (f32[4,6,128]{2,0,1:T(4,128)S(1)}) conditional(s32[]{:T(128)} %convert_element_type.61, () %tuple.43, (f32[19,1,1,1]{0,3,2,1:T(1,128)S(1)}, f32[19,1,1,1]{0,3,2,1:T(1,128)S(1)}, f32[19,1,1,1]{0,3,2,1:T(1,128)S(1)}, f32[1,4,10,130]{3,2,1,0:T(8,128)S(1)}, f32[19,4,10,130]{3,2,1,0:T(8,128)S(1)}, ...), branch_computations={%region_4.5_spmd, %region_5.9_spmd.clone} | conditional | flops 646950 | bytes 2346576 | solution.py:424
  20.9 0.1 select_select_fusion.2
  21.1 0.1 fusion.14
  21.2 0.1 slice.207
  21.4 0.1 slice.206
  21.4 0.1 copy-done.13
  21.6 0.2 multiply_reduce_fusion.2
  21.9 0.4 copy.83
  22.3 1.6 %gather_fusion = f32[512,3]{1,0:T(8,128)} fusion(f32[3,2048]{0,1:T(8,128)S(1)} %copy.83, s32[1024]{0:T(1024)S(1)} %pad_clamp_fusion.1), kind=kCustom, calls=%fused_computation.2 | custom fusion | bytes 14336 | tf_op jit(solution)/shard_map/cond/branch_1_fun/gather | solution.py:410
  23.9 1.1 %copy.84 = f32[3,4,128]{2,1,0:T(4,128)S(1)} copy(f32[3,4,128]{0,2,1:T(8,128)} %bitcast.145) | data formatting | bytes 12288 | tf_op jit(solution)/shard_map/cond/branch_1_fun/concatenate | solution.py:421
  25.0 5.2 %all_gather.17 = f32[16,6,128]{2,1,0:T(8,128)S(1)} all-gather(f32[4,6,128]{2,1,0:T(8,128)S(1)} %copy.87), channel_id=1, replica_groups=mesh['group'=4,'gx'=4,'gy'=2] {'group'}, dimensions={0}, use_global_device_ids=true | all-gather | bytes 61440 | tf_op jit(solution)/shard_map/all_gather | solution.py:430
  30.3 1.1 %conditional.6 = (f32[2,128,8,128]{3,1,2,0:T(8,128)}, f32[3,2048]{0,1:T(8,128)S(1)}) conditional(s32[]{:T(128)} %convert_element_type.67, f32[3,2048]{0,1:T(8,128)S(1)} %bitcast.134, (f32[3,1,1,256]{3,2,1,0:T(1,128)S(1)}, s32[1,1,2,8]{3,2,1,0:T(2,128)S(1)}, f32[16,6,128]{2,1,0:T(8,128)S(1)}, s32[256]{0:T(256)S(1)}, f32[3,2048]{0,1:T(8,128)S(1)}) %tuple.139), branch_computations={%region_9.10_spmd, %region_10.13_spmd} | conditional | flops 15991856 | bytes 2414224 | solution.py:447
  30.3 1.1 %broadcast.235 = f32[2,128,8,128]{3,1,2,0:T(8,128)} broadcast(f32[]{:T(128)} %constant.150.clone), dimensions={} | broadcast | bytes 1048580 | tf_op jit(solution)/shard_map/broadcast.18
  31.4 0.3 copy.98
  31.7 13.6 %all_gather.18 = f32[4,16,4,128]{3,2,1,0:T(4,128)S(1)} all-gather(f32[4,4,4,128]{3,2,1,0:T(4,128)S(1)} %pad_maximum_fusion.2), channel_id=1, replica_groups=mesh['group'=4,'gx'=4,'gy'=2] {'gx'}, dimensions={1}, use_global_device_ids=true | all-gather | bytes 163840 | tf_op jit(solution)/shard_map/all_gather | solution.py:339
  45.3 5.6 %all_gather.19 = f32[4,16,8,128]{3,1,0,2:T(8,128)S(1)} all-gather(f32[4,16,4,128]{3,1,0,2:T(8,128)S(1)} %copy.89), channel_id=1, replica_groups=mesh['group'=4,'gx'=4,'gy'=2] {'gy'}, dimensions={2}, use_global_device_ids=true | all-gather | bytes 393216 | tf_op jit(solution)/shard_map/all_gather | solution.py:340
  51.0 0.2 conditional.7
  51.2 0.6 constant_dynamic-slice_fusion.3
  51.8 0.1 collective-permute-start.2
  51.9 19.4 %collective-permute-start.3 = (f32[4,3,128]{2,0,1:T(4,128)S(1)}, f32[4,3,128]{2,0,1:T(4,128)S(1)}, u32[]{:S(2)}, u32[]{:S(2)}) collective-permute-start(f32[4,3,128]{2,0,1:T(4,128)S(1)} %get-tuple-element.319), channel_id=1, source_target_pairs={{0,16},{8,24},{16,0},{24,8},{1,17},{9,25},{17,1},{25,9},{2,18},{10... | collective-permute-start | bytes 18440 | tf_op jit(solution)/shard_map/ppermute | solution.py:78
  71.3 0.9 %collective-permute-done.2 = f32[4,3,128]{2,0,1:T(4,128)S(1)} collective-permute-done((f32[4,3,128]{2,0,1:T(4,128)S(1)}, f32[4,3,128]{2,0,1:T(4,128)S(1)}, u32[]{:S(2)}, u32[]{:S(2)}) %collective-permute-start.2) | collective-permute-done | bytes 6176 | tf_op jit(solution)/shard_map/ppermute | solution.py:78
  72.2 0.7 collective-permute-done.3
  72.9 0.1 copy.99
  73.1 2.5 %scatter_custom_fusion.1 = f32[3,2048]{0,1:T(8,128)S(1)} fusion(s32[512]{0:T(512)S(1)} %bitcast.175, f32[512,3]{1,0:T(8,128)S(1)} %bitcast.146, f32[]{:T(128)} %constant.169.clone.1), kind=kCustom, calls=%fused_computation.113 | custom fusion | flops 1536 | bytes 24580 | tf_op jit(solution)/shard_map/scatter-add | solution.py:505
  75.6 1.8 %conditional.9 = (bf16[19,2,8,128]{3,2,1,0:T(8,128)(2,1)S(1)}) conditional(s32[]{:T(128)} %convert_element_type.61, () %tuple.40, (f32[1,4,10,130]{3,2,1,0:T(8,128)S(1)}, f32[19,1,1,1]{0,3,2,1:T(1,128)S(1)}, f32[19,1,1,1]{0,3,2,1:T(1,128)S(1)}, f32[19,1,1,1]{0,3,2,1:T(1,128)S(1)}, f32[19,1,1,1]{0,3,2,1:T(1,128)S(1)}, ...), branch_computations={%region_18.19_spmd, %region_19.20_spmd.clone} | conditional | flops 1056324 | bytes 4268820 | solution.py:507
  75.7 0.1 select_select_fusion.1
  75.8 0.1 fusion.1
  76.0 0.2 select_select_fusion
  76.2 0.1 fusion
  76.3 0.1 slice.231
  76.4 0.3 copy.93
  76.8 0.1 slice.230
  76.9 0.1 slice.241
  77.0 0.4 fusion.6
  77.4 0.6 copy-done
  (62 shorter events, 0.5 us)
Async XLA Ops:
  0.6 13.9 %copy-start.6 = (f32[4,4,128]{2,1,0:T(4,128)S(1)}, f32[4,4,128]{2,1,0:T(4,128)}, u32[]{:S(2)}) copy-start(f32[4,4,128]{2,1,0:T(4,128)} %param.47) | copy-start | bytes 24580
  0.6 13.9 %copy-start.7 = (s32[4,4,128]{2,1,0:T(4,128)S(1)}, s32[4,4,128]{2,1,0:T(4,128)}, u32[]{:S(2)}) copy-start(s32[4,4,128]{2,1,0:T(4,128)} %param.48) | copy-start | bytes 24580
  0.7 13.9 %copy-start.1 = (f32[3,4,4,128]{3,2,1,0:T(4,128)S(1)}, f32[3,4,4,128]{3,2,1,0:T(4,128)}, u32[]{:S(2)}) copy-start(f32[3,4,4,128]{3,2,1,0:T(4,128)} %param.46) | copy-start | bytes 73732
  9.2 6.1 %collective-permute-start = (bf16[20,1,10,128]{3,2,1,0:T(8,128)(2,1)S(1)}, bf16[20,1,10,128]{3,2,1,0:T(8,128)(2,1)S(1)}, u32[]{:S(2)}, u32[]{:S(2)}) collective-permute-start(bf16[20,1,10,128]{3,2,1,0:T(8,128)(2,1)S(1)} %get-tuple-element.313), channel_id=1, source_target_pairs={{0,2},{1,3},{2,4},{3,5},{4,6},{5,7},{6,8},{7,9},{8,10},{9,11},{10,... | collective-permute-start | bytes 153608 | tf_op jit(solution)/shard_map/ppermute | solution.py:53
  13.2 6.4 %collective-permute-start.1 = (bf16[20,1,10,128]{3,2,1,0:T(8,128)(2,1)S(1)}, bf16[20,1,10,128]{3,2,1,0:T(8,128)(2,1)S(1)}, u32[]{:S(2)}, u32[]{:S(2)}) collective-permute-start(bf16[20,1,10,128]{3,2,1,0:T(8,128)(2,1)S(1)} %get-tuple-element.314), channel_id=1, source_target_pairs={{2,0},{3,1},{4,2},{5,3},{6,4},{7,5},{8,6},{9,7},{10,8},{11,9},{12,... | collective-permute-start | bytes 153608 | tf_op jit(solution)/shard_map/ppermute | solution.py:53
  20.1 0.7 copy-start.2
  20.1 0.7 copy-start.4
  20.1 0.7 copy-start.5
  20.2 0.7 copy-start.8
  20.8 9.5 %copy-start.9 = (s32[1,1,256]{2,1,0:T(1,128)S(1)}, s32[1,1,256]{2,1,0:T(1,128)}, u32[]{:S(2)}) copy-start(s32[1,1,256]{2,1,0:T(1,128)} %param.50) | copy-start | bytes 3076
  20.8 9.5 %copy-start.10 = (f32[3,1,1,256]{3,2,1,0:T(1,128)S(1)}, f32[3,1,1,256]{3,2,1,0:T(1,128)}, u32[]{:S(2)}) copy-start(f32[3,1,1,256]{3,2,1,0:T(1,128)} %param.51) | copy-start | bytes 9220
  20.8 9.5 %copy-start.11 = (s32[1,1,2,8]{3,2,1,0:T(2,128)S(1)}, s32[1,1,2,8]{3,2,1,0:T(2,128)}, u32[]{:S(2)}) copy-start(s32[1,1,2,8]{3,2,1,0:T(2,128)} %param.52) | copy-start | bytes 196
  20.9 0.7 copy-start.13
  20.9 0.7 copy-start.14
  20.9 0.7 copy-start.15
  31.4 19.6 %copy-start.3 = (f32[24,24]{1,0:T(8,128)S(1)}, f32[24,24]{1,0:T(8,128)}, u32[]{:S(2)}) copy-start(f32[24,24]{1,0:T(8,128)} %param.49) | copy-start | bytes 6916
  51.8 20.4 %collective-permute-start.2 = (f32[4,3,128]{2,0,1:T(4,128)S(1)}, f32[4,3,128]{2,0,1:T(4,128)S(1)}, u32[]{:S(2)}, u32[]{:S(2)}) collective-permute-start(f32[4,3,128]{2,0,1:T(4,128)S(1)} %get-tuple-element.317), channel_id=1, source_target_pairs={{0,8},{8,16},{16,24},{24,0},{1,9},{9,17},{17,25},{25,1},{2,10},{10... | collective-permute-start | bytes 18440 | tf_op jit(solution)/shard_map/ppermute | solution.py:78
  51.9 21.0 %collective-permute-start.3 = (f32[4,3,128]{2,0,1:T(4,128)S(1)}, f32[4,3,128]{2,0,1:T(4,128)S(1)}, u32[]{:S(2)}, u32[]{:S(2)}) collective-permute-start(f32[4,3,128]{2,0,1:T(4,128)S(1)} %get-tuple-element.319), channel_id=1, source_target_pairs={{0,16},{8,24},{16,0},{24,8},{1,17},{9,25},{17,1},{25,9},{2,18},{10... | collective-permute-start | bytes 18440 | tf_op jit(solution)/shard_map/ppermute | solution.py:78
  71.3 1.6 %collective-permute-start.4 = (f32[4,3,128]{2,0,1:T(4,128)S(1)}, f32[4,3,128]{2,0,1:T(4,128)S(1)}, u32[]{:S(2)}, u32[]{:S(2)}) collective-permute-start(f32[4,3,128]{2,0,1:T(4,128)S(1)} %get-tuple-element.318), channel_id=1, source_target_pairs={{0,24},{8,0},{16,8},{24,16},{1,25},{9,1},{17,9},{25,17},{2,26},{10... | collective-permute-start | bytes 18440 | tf_op jit(solution)/shard_map/ppermute | solution.py:78
  76.2 0.8 %copy-start.12 = (f32[19]{0:T(128)S(1)}, f32[19]{0:T(128)}, u32[]{:S(2)}) copy-start(f32[19]{0:T(128)} %constant.208) | copy-start | bytes 232 | tf_op jit(solution)/shard_map/cond
  77.4 0.6 copy-start

commit v16 on v15

--- a/solution.py
+++ b/solution.py
@@ -504,12 +504,15 @@
     speed_parts = wall_gain * own_speeds.transpose(1, 0, 2).reshape(3, point_count)
     wall_speed = jnp.zeros((3, cell_count), jnp.float32).at[:, wall_index].add(speed_parts)
     wall_speed = wall_speed.reshape(3, span_cells, across_cells, deep_cells)
-    new_populations = lax.cond(
-        is_fluid,
-        lambda operands: stream_all(operands[0], operands[1], operands[2]),
-        lambda operands: jnp.zeros(operands[0][:, 1:-1, 1:-1, 1:-1].shape, jnp.bfloat16),
-        (moved, fluid_ext, wall_speed),
-    )
+    upstream, opened, bounce, reflected = stream_links(moved, fluid_ext)
+    inside = fluid_ext[1:-1, 1:-1, 1:-1]
+    settled = inside * (opened * upstream + bounce * reflected)
+    walled = jnp.where(is_fluid, inside * bounce, 0.0)
+    settled = jnp.where(is_fluid, settled, 0.0)
+    correction = per_direction([6.0 * w for w in lattice_weight]) * project_all(
+        [wall_speed[0], wall_speed[1], wall_speed[2]]
+    )
+    new_populations = (settled + walled * correction).astype(jnp.bfloat16)
     return (new_populations, solution)
 
 

time: 79.3 us -> 87 us (1.097)
  other arithmetic: 7.69 us -> 12.7 us
  starting transfers between devices: 24.8 us -> 27.1 us
  local copies, waits for them, and re-layouts: 7.99 us -> 9.77 us
    ppermute x3, starting transfers between devices: 19.5 us -> 21.8 us  [passed_along(): return lax.ppermute(value, axis, pairs)]
    broadcast_in_dim x5 -> x3, other arithmetic: 0.03 us -> 1.98 us  [upstream_of(): jnp.where(shift > 0.5, pick[1], jnp.where(shift < -0.5, pick[-1], pick[0]))]
    slice x3, local copies, waits for them, and re-layouts: 0.22 us -> 1.53 us  [the longest x1 1.44 us: per_device(): wall_speed[0]]
    ppermute x2, waiting for transfers between devices: 4.67 us -> 3.52 us  [shifted(): return lax.ppermute(piece, axes, pairs)]
  transfers between devices with their start and end apart: 5 -> 5, of which waited for: 4 -> 2; matrix products, arithmetic and copies ran while one was open for 0% -> 3% of each run, Pallas kernels for 0% -> 0%
where the time goes in v16:
time: 87 us; the launch traced here: 86.5 us
  blocking collectives  29.8 us (34%)
  starting transfers between devices  27.1 us (31%)
  other arithmetic  12.7 us (15%)
  local copies, waits for them, and re-layouts  9.77 us (11%)
  waiting for transfers between devices  5.73 us (7%)
  between operations  1.08 us (1%)
    ppermute x3, starting transfers between devices, passed_along(): return lax.ppermute(value, axis, pairs)  21.8 us
    all_gather x1, blocking collectives, whole_partition(): every = lax.all_gather(block, 'gx', axis=count, tiled=True)  13.6 us
    all_gather x1, blocking collectives, whole_partition(): return lax.all_gather(every, 'gy', axis=count + 1, tiled=True)  5.64 us
    all_gather x1, blocking collectives, halo_exchange(): every = lax.all_gather(edges, 'gy', axis=0)  5.35 us
    ppermute x2, starting transfers between devices, shifted(): return lax.ppermute(piece, axes, pairs)  5.33 us
    all_gather x1, blocking collectives, per_device(): received = lax.all_gather(packed, 'group', axis=0, tiled=True)  5.25 us
    ppermute x2, waiting for transfers between devices, shifted(): return lax.ppermute(piece, axes, pairs)  3.52 us
    scatter-add x1, other arithmetic, per_device(): jnp.zeros((3, cell_count), jnp.float32).at[:, wall_index].add(speed_parts)  2.63 us
  transfers between devices with their start and end apart: 5, of which 2 were waited for; matrix products, arithmetic and copies ran while one was open for 3% of the time, Pallas kernels for 0%

profile of v16, /device:TPU:0, one launch (start us, length us, event | category | flops | bytes accessed | tf_op | source)
XLA Modules:
  0.0 86.5 jit_solution(10787975511281177845)
XLA Ops:
  0.7 0.7 fusion.61
  1.4 1.0 %fusion.40 = (f32[2,8,128]{2,1,0:T(8,128)S(1)}, f32[2,8,128]{2,1,0:T(8,128)S(1)}, f32[2,8,128]{2,1,0:T(8,128)S(1)}, f32[2,8,128]{2,1,0:T(8,128)S(1)}) fusion(bf16[19,2,8,128]{3,2,1,0:T(8,128)(2,1)} %param.41, f32[19]{0:T(128)} %constant.201, f32[19]{0:T(128)} %constant.202, f32[19]{0:T(128)} %constant.203), kind=kLoop, calls=%fused_computation.105 | loop fusion | flops 303104 | bytes 110820 | tf_op jit(solution)/shard_map/reduce_sum | solution.py:96
  2.5 1.1 %fusion.45 = bf16[19,2,8,128]{3,2,1,0:T(8,128)(2,1)S(1)} fusion(bf16[19,2,8,128]{3,2,1,0:T(8,128)(2,1)} %param.41, f32[2,8,128]{2,1,0:T(8,128)S(1)} %get-tuple-element.179, f32[2,8,128]{2,1,0:T(8,128)S(1)} %get-tuple-element.182, f32[19]{0:T(128)} %constant.203, f32[2,8,128]{2,1,0:T(8,128)S(1)} %get-tuple-element.181, f32[19]{0:T(128)} %constant.202, ...), kind=kLoop, calls=%fused_computation.110 | loop fusion | flops 739328 | bytes 196913 | tf_op jit(solution)/shard_map/convert_element_type | solution.py:395
  3.6 5.3 %all-gather = bf16[40,2,2,128]{3,2,1,0:T(2,128)(2,1)S(1)} all-gather(bf16[20,2,2,128]{3,2,1,0:T(2,128)(2,1)S(1)} %fusion.59), channel_id=2, replica_groups=mesh['group'=4,'gx'=4,'gy'=2] {'gy'}, dimensions={0}, use_global_device_ids=true | all-gather | bytes 61440 | tf_op jit(solution)/shard_map/all_gather | solution.py:58
  9.1 0.1 pad_maximum_fusion.1
  9.2 4.0 %collective-permute-start = (bf16[20,1,10,128]{3,2,1,0:T(8,128)(2,1)S(1)}, bf16[20,1,10,128]{3,2,1,0:T(8,128)(2,1)S(1)}, u32[]{:S(2)}, u32[]{:S(2)}) collective-permute-start(bf16[20,1,10,128]{3,2,1,0:T(8,128)(2,1)S(1)} %get-tuple-element.204), channel_id=1, source_target_pairs={{0,2},{1,3},{2,4},{3,5},{4,6},{5,7},{6,8},{7,9},{8,10},{9,11},{10,... | collective-permute-start | bytes 153608 | tf_op jit(solution)/shard_map/ppermute | solution.py:53
  13.2 1.3 %collective-permute-start.1 = (bf16[20,1,10,128]{3,2,1,0:T(8,128)(2,1)S(1)}, bf16[20,1,10,128]{3,2,1,0:T(8,128)(2,1)S(1)}, u32[]{:S(2)}, u32[]{:S(2)}) collective-permute-start(bf16[20,1,10,128]{3,2,1,0:T(8,128)(2,1)S(1)} %get-tuple-element.205), channel_id=1, source_target_pairs={{2,0},{3,1},{4,2},{5,3},{6,4},{7,5},{8,6},{9,7},{10,8},{11,9},{12,... | collective-permute-start | bytes 153608 | tf_op jit(solution)/shard_map/ppermute | solution.py:53
  14.6 0.6 multiply_bitcast_fusion
  15.2 0.6 compare_select_fusion.4
  15.7 0.4 copy.119
  16.1 3.5 %collective-permute-done.1 = bf16[20,1,10,128]{3,2,1,0:T(8,128)(2,1)S(1)} collective-permute-done((bf16[20,1,10,128]{3,2,1,0:T(8,128)(2,1)S(1)}, bf16[20,1,10,128]{3,2,1,0:T(8,128)(2,1)S(1)}, u32[]{:S(2)}, u32[]{:S(2)}) %collective-permute-start.1) | collective-permute-done | bytes 51232 | tf_op jit(solution)/shard_map/ppermute | solution.py:53
  19.6 0.5 fusion.24
  20.1 0.6 slice_bitcast_fusion.5
  20.8 8.1 %conditional.4 = (f32[4,6,128]{2,0,1:T(4,128)S(1)}) conditional(s32[]{:T(128)} %convert_element_type.66, () %tuple.36, (f32[1,4,10,130]{3,2,1,0:T(8,128)S(1)}, f32[20,4,10,130]{3,2,1,0:T(8,128)S(1)}, s32[1,1,512]{2,1,0:T(1,128)S(1)}, s32[]{:T(128)}, s32[]{:T(128)}, /*index=5*/s32[]{:T(128)}) %tuple.105), branch_computations={%region_4.5_spmd, %region_5.9_spmd.clone.clone} | conditional | flops 646950 | bytes 2354796 | solution.py:424
  20.8 0.7 compare_bitcast_fusion.5
  21.4 0.7 compare_bitcast_fusion.4
  22.1 0.7 compare_bitcast_fusion.3
  22.8 0.6 fusion.18
  23.4 0.1 slice.252
  23.6 0.1 select_select_fusion
  23.7 0.1 fusion.12
  23.9 0.2 copy-done.20
  24.1 0.2 multiply_reduce_fusion.2
  24.4 0.6 pad_maximum_fusion
  25.0 1.1 %copy.135 = f32[3,2048]{0,1:T(8,128)S(1)} copy(f32[3,2048]{1,0:T(4,128)} %pad_maximum_fusion) | data formatting | bytes 49152 | tf_op jit(solution)/shard_map/cond/branch_1_fun/stack | solution.py:144
  26.1 1.6 %gather_fusion = f32[512,3]{1,0:T(8,128)} fusion(f32[3,2048]{0,1:T(8,128)S(1)} %copy.135, s32[1024]{0:T(1024)S(1)} %pad_clamp_fusion.2), kind=kCustom, calls=%fused_computation.2.clone | custom fusion | bytes 14336 | tf_op jit(solution)/shard_map/cond/branch_1_fun/gather | solution.py:410
  27.8 1.1 %copy.136 = f32[3,4,128]{2,1,0:T(4,128)S(1)} copy(f32[3,4,128]{0,2,1:T(8,128)} %bitcast.138) | data formatting | bytes 12288 | tf_op jit(solution)/shard_map/cond/branch_1_fun/concatenate | solution.py:421
  28.9 5.2 %all_gather.17 = f32[16,6,128]{2,1,0:T(8,128)S(1)} all-gather(f32[4,6,128]{2,1,0:T(8,128)S(1)} %copy.120), channel_id=1, replica_groups=mesh['group'=4,'gx'=4,'gy'=2] {'group'}, dimensions={0}, use_global_device_ids=true | all-gather | bytes 61440 | tf_op jit(solution)/shard_map/all_gather | solution.py:430
  34.1 1.1 %conditional.5 = (f32[2,128,8,128]{3,1,2,0:T(8,128)}, f32[3,2048]{0,1:T(8,128)S(1)}) conditional(s32[]{:T(128)} %convert_element_type.65, f32[3,2048]{0,1:T(8,128)S(1)} %bitcast.128, (f32[3,1,1,256]{3,2,1,0:T(1,128)}, s32[1,1,2,8]{3,2,1,0:T(2,128)}, f32[16,6,128]{2,1,0:T(8,128)S(1)}, s32[256]{0:T(256)}, f32[3,2048]{0,1:T(8,128)S(1)}) %tuple.107), branch_computations={%region_9.10_spmd, %region_10.13_spmd} | conditional | flops 15991856 | bytes 2414224 | solution.py:447
  34.1 1.1 %broadcast.231 = f32[2,128,8,128]{3,1,2,0:T(8,128)} broadcast(f32[]{:T(128)} %constant.148.clone), dimensions={} | broadcast | bytes 1048580 | tf_op jit(solution)/shard_map/broadcast.20
  35.2 0.3 copy.133
  35.6 13.6 %all_gather.18 = f32[4,16,4,128]{3,2,1,0:T(4,128)S(1)} all-gather(f32[4,4,4,128]{3,2,1,0:T(4,128)S(1)} %pad_maximum_fusion.2), channel_id=1, replica_groups=mesh['group'=4,'gx'=4,'gy'=2] {'gx'}, dimensions={1}, use_global_device_ids=true | all-gather | bytes 163840 | tf_op jit(solution)/shard_map/all_gather | solution.py:339
  49.2 5.6 %all_gather.19 = f32[4,16,8,128]{3,1,0,2:T(8,128)S(1)} all-gather(f32[4,16,4,128]{3,1,0,2:T(8,128)S(1)} %copy.122), channel_id=1, replica_groups=mesh['group'=4,'gx'=4,'gy'=2] {'gy'}, dimensions={2}, use_global_device_ids=true | all-gather | bytes 393216 | tf_op jit(solution)/shard_map/all_gather | solution.py:340
  54.8 0.2 conditional.6
  55.1 0.6 constant_dynamic-slice_fusion.3
  55.8 21.6 %collective-permute-start.4 = (f32[4,3,128]{2,0,1:T(4,128)S(1)}, f32[4,3,128]{2,0,1:T(4,128)S(1)}, u32[]{:S(2)}, u32[]{:S(2)}) collective-permute-start(f32[4,3,128]{2,0,1:T(4,128)S(1)} %get-tuple-element.209), channel_id=1, source_target_pairs={{0,24},{8,0},{16,8},{24,16},{1,25},{9,1},{17,9},{25,17},{2,26},{10... | collective-permute-start | bytes 18440 | tf_op jit(solution)/shard_map/ppermute | solution.py:78
  77.4 0.1 collective-permute-start.3
  77.6 0.2 select_select_fusion.1
  77.8 0.4 copy-done.16
  78.2 0.3 fusion.36
  78.5 0.1 slice.293
  78.6 0.1 slice.294
  78.7 0.1 slice.274
  78.9 2.2 %collective-permute-done.3 = f32[4,3,128]{2,0,1:T(4,128)S(1)} collective-permute-done((f32[4,3,128]{2,0,1:T(4,128)S(1)}, f32[4,3,128]{2,0,1:T(4,128)S(1)}, u32[]{:S(2)}, u32[]{:S(2)}) %collective-permute-start.3) | collective-permute-done | bytes 6176 | tf_op jit(solution)/shard_map/ppermute | solution.py:78
  81.1 0.1 copy.134
  81.2 2.6 %scatter_custom_fusion.1 = f32[3,2048]{0,1:T(8,128)S(1)} fusion(s32[512]{0:T(512)} %bitcast.166, f32[512,3]{1,0:T(8,128)S(1)} %bitcast.139, f32[]{:T(128)} %constant.163.clone.1), kind=kCustom, calls=%fused_computation.88 | custom fusion | flops 1536 | bytes 25088 | tf_op jit(solution)/shard_map/scatter-add | solution.py:505
  83.9 1.4 %slice_reduce_fusion.2 = (f32[2048]{0:T(1024)S(1)}, f32[2048]{0:T(1024)S(1)}, f32[2048]{0:T(1024)S(1)}) fusion(f32[3,2048]{0,1:T(8,128)S(1)} %scatter_custom_fusion.1), kind=kLoop, calls=%fused_computation.74 | loop fusion | bytes 49152 | tf_op jit(solution)/shard_map/slice | solution.py:513
  85.5 1.0 %fusion.52 = bf16[19,2,8,128]{3,2,1,0:T(8,128)(2,1)} fusion(f32[19,2,8,130]{3,2,1,0:T(8,128)S(1)} %get-tuple-element.212, f32[18,2,8,128]{3,2,1,0:T(8,128)S(1)} %bitcast.132, f32[1,2,8,128]{3,2,1,0:T(8,128)S(1)} %slice.293, f32[19,2,8,130]{3,2,1,0:T(8,128)S(1)} %get-tuple-element.211, f32[2,8,128]{2,1,0:T(8,128)S(1)} %bitcast.145, ...), kind=kLoop, calls=%fused_computation.118 | loop fusion | flops 856064 | bytes 1200471 | tf_op jit(solution)/shard_map/convert_element_type | solution.py:515
  (71 shorter events, 0.6 us)
Async XLA Ops:
  0.6 13.9 %copy-start.6 = (s32[4,4,128]{2,1,0:T(4,128)S(1)}, s32[4,4,128]{2,1,0:T(4,128)}, u32[]{:S(2)}) copy-start(s32[4,4,128]{2,1,0:T(4,128)} %param.46) | copy-start | bytes 24580
  0.6 13.9 %copy-start.5 = (f32[4,4,128]{2,1,0:T(4,128)S(1)}, f32[4,4,128]{2,1,0:T(4,128)}, u32[]{:S(2)}) copy-start(f32[4,4,128]{2,1,0:T(4,128)} %param.45) | copy-start | bytes 24580
  0.7 14.5 %copy-start.3 = (s32[1,1,512]{2,1,0:T(1,128)S(1)}, s32[1,1,512]{2,1,0:T(1,128)}, u32[]{:S(2)}) copy-start(s32[1,1,512]{2,1,0:T(1,128)} %param.43) | copy-start | bytes 6148
  0.7 15.1 %copy-start.2 = (f32[3,4,4,128]{3,2,1,0:T(4,128)S(1)}, f32[3,4,4,128]{3,2,1,0:T(4,128)}, u32[]{:S(2)}) copy-start(f32[3,4,4,128]{3,2,1,0:T(4,128)} %param.44) | copy-start | bytes 73732
  9.2 6.9 %collective-permute-start = (bf16[20,1,10,128]{3,2,1,0:T(8,128)(2,1)S(1)}, bf16[20,1,10,128]{3,2,1,0:T(8,128)(2,1)S(1)}, u32[]{:S(2)}, u32[]{:S(2)}) collective-permute-start(bf16[20,1,10,128]{3,2,1,0:T(8,128)(2,1)S(1)} %get-tuple-element.204), channel_id=1, source_target_pairs={{0,2},{1,3},{2,4},{3,5},{4,6},{5,7},{6,8},{7,9},{8,10},{9,11},{10,... | collective-permute-start | bytes 153608 | tf_op jit(solution)/shard_map/ppermute | solution.py:53
  13.2 6.4 %collective-permute-start.1 = (bf16[20,1,10,128]{3,2,1,0:T(8,128)(2,1)S(1)}, bf16[20,1,10,128]{3,2,1,0:T(8,128)(2,1)S(1)}, u32[]{:S(2)}, u32[]{:S(2)}) collective-permute-start(bf16[20,1,10,128]{3,2,1,0:T(8,128)(2,1)S(1)} %get-tuple-element.205), channel_id=1, source_target_pairs={{2,0},{3,1},{4,2},{5,3},{6,4},{7,5},{8,6},{9,7},{10,8},{11,9},{12,... | collective-permute-start | bytes 153608 | tf_op jit(solution)/shard_map/ppermute | solution.py:53
  23.4 0.7 copy-start.20
  23.4 0.7 copy-start.21
  23.4 0.7 copy-start.22
  24.1 4.7 %copy-start.7 = (f32[1,4,128]{2,1,0:T(4,128)S(1)}, f32[1,4,128]{2,1,0:T(4,128)}, u32[]{:S(2)}) copy-start(f32[1,4,128]{2,1,0:T(4,128)} %get-tuple-element.192) | copy-start | bytes 6148 | tf_op jit(solution)/shard_map/cond
  34.1 1.4 %copy-start.1 = (f32[1,4,4,128]{3,2,1,0:T(4,128)S(1)}, f32[1,4,4,128]{3,2,1,0:T(4,128)}, u32[]{:S(2)}) copy-start(f32[1,4,4,128]{3,2,1,0:T(4,128)} %multiply_bitcast_fusion) | copy-start | bytes 24580
  35.2 19.6 %copy-start.4 = (f32[24,24]{1,0:T(8,128)S(1)}, f32[24,24]{1,0:T(8,128)}, u32[]{:S(2)}) copy-start(f32[24,24]{1,0:T(8,128)} %param.47) | copy-start | bytes 6916
  35.5 20.1 %copy-start.11 = (s32[1,1,256]{2,1,0:T(1,128)S(1)}, s32[1,1,256]{2,1,0:T(1,128)}, u32[]{:S(2)}) copy-start(s32[1,1,256]{2,1,0:T(1,128)} %param.48) | copy-start | bytes 3076
  35.6 20.1 %copy-start.12 = (s32[1,1,2,8]{3,2,1,0:T(2,128)S(1)}, s32[1,1,2,8]{3,2,1,0:T(2,128)}, u32[]{:S(2)}) copy-start(s32[1,1,2,8]{3,2,1,0:T(2,128)} %param.50) | copy-start | bytes 196
  55.0 22.5 %copy-start = (f32[2,10,130]{2,1,0:T(8,128)S(1)}, f32[2,10,130]{2,1,0:T(8,128)}, u32[]{:S(2)}) copy-start(f32[2,10,130]{2,1,0:T(8,128)} %get-tuple-element.203) | copy-start | bytes 31204
  55.0 22.5 %copy-start.18 = (pred[19]{0:T(512)(128)(4,1)S(1)}, pred[19]{0:T(512)(128)(4,1)}, u32[]{:S(2)}) copy-start(pred[19]{0:T(512)(128)(4,1)} %constant.211) | copy-start | bytes 61
  55.1 22.5 %copy-start.19 = (pred[19]{0:T(512)(128)(4,1)S(1)}, pred[19]{0:T(512)(128)(4,1)}, u32[]{:S(2)}) copy-start(pred[19]{0:T(512)(128)(4,1)} %constant.209) | copy-start | bytes 61
  55.7 23.1 %collective-permute-start.2 = (f32[4,3,128]{2,0,1:T(4,128)S(1)}, f32[4,3,128]{2,0,1:T(4,128)S(1)}, u32[]{:S(2)}, u32[]{:S(2)}) collective-permute-start(f32[4,3,128]{2,0,1:T(4,128)S(1)} %get-tuple-element.208), channel_id=1, source_target_pairs={{0,8},{8,16},{16,24},{24,0},{1,9},{9,17},{17,25},{25,1},{2,10},{10... | collective-permute-start | bytes 18440 | tf_op jit(solution)/shard_map/ppermute | solution.py:78
  55.8 23.1 %collective-permute-start.4 = (f32[4,3,128]{2,0,1:T(4,128)S(1)}, f32[4,3,128]{2,0,1:T(4,128)S(1)}, u32[]{:S(2)}, u32[]{:S(2)}) collective-permute-start(f32[4,3,128]{2,0,1:T(4,128)S(1)} %get-tuple-element.209), channel_id=1, source_target_pairs={{0,24},{8,0},{16,8},{24,16},{1,25},{9,1},{17,9},{25,17},{2,26},{10... | collective-permute-start | bytes 18440 | tf_op jit(solution)/shard_map/ppermute | solution.py:78
  77.4 3.6 %collective-permute-start.3 = (f32[4,3,128]{2,0,1:T(4,128)S(1)}, f32[4,3,128]{2,0,1:T(4,128)S(1)}, u32[]{:S(2)}, u32[]{:S(2)}) collective-permute-start(f32[4,3,128]{2,0,1:T(4,128)S(1)} %get-tuple-element.210), channel_id=1, source_target_pairs={{0,16},{8,24},{16,0},{24,8},{1,17},{9,25},{17,1},{25,9},{2,18},{10... | collective-permute-start | bytes 18440 | tf_op jit(solution)/shard_map/ppermute | solution.py:78
  77.6 0.7 copy-start.16
  77.6 0.7 copy-start.17
  83.9 1.5 %copy-start.8 = (f32[19]{0:T(128)S(1)}, f32[19]{0:T(128)}, u32[]{:S(2)}) copy-start(f32[19]{0:T(128)} %constant.203) | copy-start | bytes 232
  83.9 1.5 %copy-start.9 = (f32[19]{0:T(128)S(1)}, f32[19]{0:T(128)}, u32[]{:S(2)}) copy-start(f32[19]{0:T(128)} %constant.202) | copy-start | bytes 232
  83.9 1.5 %copy-start.10 = (f32[19]{0:T(128)S(1)}, f32[19]{0:T(128)}, u32[]{:S(2)}) copy-start(f32[19]{0:T(128)} %constant.201) | copy-start | bytes 232
  83.9 1.5 %copy-start.13 = (f32[19]{0:T(128)S(1)}, f32[19]{0:T(128)}, u32[]{:S(2)}) copy-start(f32[19]{0:T(128)} %constant.216) | copy-start | bytes 232
  83.9 1.5 %copy-start.14 = (pred[19]{0:T(512)(128)(4,1)S(1)}, pred[19]{0:T(512)(128)(4,1)}, u32[]{:S(2)}) copy-start(pred[19]{0:T(512)(128)(4,1)} %constant.215) | copy-start | bytes 61
  83.9 1.5 %copy-start.15 = (pred[19]{0:T(512)(128)(4,1)S(1)}, pred[19]{0:T(512)(128)(4,1)}, u32[]{:S(2)}) copy-start(pred[19]{0:T(512)(128)(4,1)} %constant.205) | copy-start | bytes 61

commit v17 on v15

--- a/solution.py
+++ b/solution.py
@@ -206,7 +206,7 @@
 def apply_rows(matrix_ref, values_ref, stiff_ref, out_ref):
     span_cells, across_cells, deep_cells = stiff_ref.shape
     step = next(size for size in (16, 8, 4, 2, 1) if span_cells % size == 0)
-    shape = (step, across_cells, deep_cells)
+    shape = (step + 1, across_cells, deep_cells)
     across_at = lax.broadcasted_iota(jnp.int32, shape, 1)
     deep_at = lax.broadcasted_iota(jnp.int32, shape, 2)
     corners = [(a, b, c) for a in (0, 1) for b in (0, 1) for c in (0, 1)]
@@ -225,17 +225,23 @@
 
     def behind(value, across, deep):
         if across:
-            value = jnp.where(across_at >= 1, pltpu.roll(value, 1, 1), 0.0)
+            value = jnp.where(across_at[:step] >= 1, pltpu.roll(value, 1, 1), 0.0)
         if deep:
-            value = jnp.where(deep_at >= 1, pltpu.roll(value, 1, 2), 0.0)
+            value = jnp.where(deep_at[:step] >= 1, pltpu.roll(value, 1, 2), 0.0)
         return value
 
     def element_rows(block, carry):
         row = block * step
+        window = [values_ref[component, pl.ds(row, step + 1)] for component in range(3)]
+        shifted = {}
+        for b in (0, 1):
+            for c in (0, 1):
+                for component in range(3):
+                    shifted[(b, c, component)] = ahead(window[component], b, c)
         gathered = []
         for a, b, c in corners:
             for component in range(3):
-                gathered.append(ahead(values_ref[component, pl.ds(row + a, step)], b, c))
+                gathered.append(shifted[(b, c, component)][a : a + step])
         scale = stiff_ref[pl.ds(row, step)]
         for corner_id, (a, b, c) in enumerate(corners):
             for component in range(3):

time: 79.3 us -> 79.1 us (level)
  no operation moved by 1% of the time
where the time goes in v17:
time: 79.1 us; the launch traced here: 77.8 us
  blocking collectives  29.8 us (38%)
  starting transfers between devices  24.7 us (31%)
  local copies, waits for them, and re-layouts  7.99 us (10%)
  other arithmetic  7.69 us (10%)
  waiting for transfers between devices  6.25 us (8%)
  between operations  0.96 us (1%)
    ppermute x3, starting transfers between devices, passed_along(): return lax.ppermute(value, axis, pairs)  19.3 us
    all_gather x1, blocking collectives, whole_partition(): every = lax.all_gather(block, 'gx', axis=count, tiled=True)  13.6 us
    all_gather x1, blocking collectives, whole_partition(): return lax.all_gather(every, 'gy', axis=count + 1, tiled=True)  5.64 us
    all_gather x1, blocking collectives, halo_exchange(): every = lax.all_gather(edges, 'gy', axis=0)  5.35 us
    ppermute x2, starting transfers between devices, shifted(): return lax.ppermute(piece, axes, pairs)  5.33 us
    all_gather x1, blocking collectives, per_device(): received = lax.all_gather(packed, 'group', axis=0, tiled=True)  5.25 us
    ppermute x2, waiting for transfers between devices, shifted(): return lax.ppermute(piece, axes, pairs)  4.67 us
    scatter-add x1, other arithmetic, per_device(): jnp.zeros((3, cell_count), jnp.float32).at[:, wall_index].add(speed_parts)  2.51 us
  transfers between devices with their start and end apart: 5, of which 4 were waited for; matrix products, arithmetic and copies ran while one was open for 0% of the time, Pallas kernels for 0%

profile of v17, /device:TPU:0, one launch (start us, length us, event | category | flops | bytes accessed | tf_op | source)
XLA Modules:
  0.0 77.8 jit_solution(15705220695133710945)
XLA Ops:
  0.7 0.7 fusion.59
  1.4 1.0 %fusion.46 = (f32[2,8,128]{2,1,0:T(8,128)S(1)}, f32[2,8,128]{2,1,0:T(8,128)S(1)}, f32[2,8,128]{2,1,0:T(8,128)S(1)}, f32[2,8,128]{2,1,0:T(8,128)S(1)}) fusion(bf16[19,2,8,128]{3,2,1,0:T(8,128)(2,1)} %param.43, f32[19]{0:T(128)} %constant.205, f32[19]{0:T(128)} %constant.206, f32[19]{0:T(128)} %constant.207), kind=kLoop, calls=%fused_computation.126 | loop fusion | flops 303104 | bytes 110820 | tf_op jit(solution)/shard_map/reduce_sum | solution.py:96
  2.4 1.1 %fusion.51 = bf16[19,2,8,128]{3,2,1,0:T(8,128)(2,1)S(1)} fusion(bf16[19,2,8,128]{3,2,1,0:T(8,128)(2,1)} %param.43, f32[2,8,128]{2,1,0:T(8,128)S(1)} %get-tuple-element.265, f32[2,8,128]{2,1,0:T(8,128)S(1)} %get-tuple-element.268, f32[19]{0:T(128)} %constant.207, f32[2,8,128]{2,1,0:T(8,128)S(1)} %get-tuple-element.267, f32[19]{0:T(128)} %constant.206, ...), kind=kLoop, calls=%fused_computation.131 | loop fusion | flops 739328 | bytes 196913 | tf_op jit(solution)/shard_map/convert_element_type | solution.py:401
  3.6 5.3 %all-gather = bf16[40,2,2,128]{3,2,1,0:T(2,128)(2,1)S(1)} all-gather(bf16[20,2,2,128]{3,2,1,0:T(2,128)(2,1)S(1)} %fusion.57), channel_id=2, replica_groups=mesh['group'=4,'gx'=4,'gy'=2] {'gy'}, dimensions={0}, use_global_device_ids=true | all-gather | bytes 61440 | tf_op jit(solution)/shard_map/all_gather | solution.py:58
  9.1 0.1 pad_maximum_fusion.1
  9.2 4.0 %collective-permute-start = (bf16[20,1,10,128]{3,2,1,0:T(8,128)(2,1)S(1)}, bf16[20,1,10,128]{3,2,1,0:T(8,128)(2,1)S(1)}, u32[]{:S(2)}, u32[]{:S(2)}) collective-permute-start(bf16[20,1,10,128]{3,2,1,0:T(8,128)(2,1)S(1)} %get-tuple-element.313), channel_id=1, source_target_pairs={{0,2},{1,3},{2,4},{3,5},{4,6},{5,7},{6,8},{7,9},{8,10},{9,11},{10,... | collective-permute-start | bytes 153608 | tf_op jit(solution)/shard_map/ppermute | solution.py:53
  13.2 1.3 %collective-permute-start.1 = (bf16[20,1,10,128]{3,2,1,0:T(8,128)(2,1)S(1)}, bf16[20,1,10,128]{3,2,1,0:T(8,128)(2,1)S(1)}, u32[]{:S(2)}, u32[]{:S(2)}) collective-permute-start(bf16[20,1,10,128]{3,2,1,0:T(8,128)(2,1)S(1)} %get-tuple-element.314), channel_id=1, source_target_pairs={{2,0},{3,1},{4,2},{5,3},{6,4},{7,5},{8,6},{9,7},{10,8},{11,9},{12,... | collective-permute-start | bytes 153608 | tf_op jit(solution)/shard_map/ppermute | solution.py:53
  14.6 0.4 copy.86
  15.0 0.3 collective-permute-done
  15.3 4.4 %collective-permute-done.1 = bf16[20,1,10,128]{3,2,1,0:T(8,128)(2,1)S(1)} collective-permute-done((bf16[20,1,10,128]{3,2,1,0:T(8,128)(2,1)S(1)}, bf16[20,1,10,128]{3,2,1,0:T(8,128)(2,1)S(1)}, u32[]{:S(2)}, u32[]{:S(2)}) %collective-permute-start.1) | collective-permute-done | bytes 51232 | tf_op jit(solution)/shard_map/ppermute | solution.py:53
  19.6 0.5 fusion.33
  20.2 0.1 slice.272
  20.3 0.5 copy-done.2
  20.8 4.2 %conditional.5 = (f32[4,6,128]{2,0,1:T(4,128)S(1)}) conditional(s32[]{:T(128)} %convert_element_type.61, () %tuple.43, (f32[19,1,1,1]{0,3,2,1:T(1,128)S(1)}, f32[19,1,1,1]{0,3,2,1:T(1,128)S(1)}, f32[19,1,1,1]{0,3,2,1:T(1,128)S(1)}, f32[1,4,10,130]{3,2,1,0:T(8,128)S(1)}, f32[19,4,10,130]{3,2,1,0:T(8,128)S(1)}, ...), branch_computations={%region_4.5_spmd, %region_5.9_spmd.clone} | conditional | flops 646950 | bytes 2346576 | solution.py:430
  20.9 0.1 select_select_fusion.2
  21.1 0.1 fusion.14
  21.2 0.1 slice.207
  21.4 0.1 slice.206
  21.4 0.1 copy-done.13
  21.6 0.2 multiply_reduce_fusion.2
  21.9 0.4 copy.83
  22.3 1.6 %gather_fusion = f32[512,3]{1,0:T(8,128)} fusion(f32[3,2048]{0,1:T(8,128)S(1)} %copy.83, s32[1024]{0:T(1024)S(1)} %pad_clamp_fusion.1), kind=kCustom, calls=%fused_computation.2 | custom fusion | bytes 14336 | tf_op jit(solution)/shard_map/cond/branch_1_fun/gather | solution.py:416
  23.9 1.1 %copy.84 = f32[3,4,128]{2,1,0:T(4,128)S(1)} copy(f32[3,4,128]{0,2,1:T(8,128)} %bitcast.145) | data formatting | bytes 12288 | tf_op jit(solution)/shard_map/cond/branch_1_fun/concatenate | solution.py:427
  25.0 5.2 %all_gather.17 = f32[16,6,128]{2,1,0:T(8,128)S(1)} all-gather(f32[4,6,128]{2,1,0:T(8,128)S(1)} %copy.87), channel_id=1, replica_groups=mesh['group'=4,'gx'=4,'gy'=2] {'group'}, dimensions={0}, use_global_device_ids=true | all-gather | bytes 61440 | tf_op jit(solution)/shard_map/all_gather | solution.py:436
  30.3 1.1 %conditional.6 = (f32[2,128,8,128]{3,1,2,0:T(8,128)}, f32[3,2048]{0,1:T(8,128)S(1)}) conditional(s32[]{:T(128)} %convert_element_type.67, f32[3,2048]{0,1:T(8,128)S(1)} %bitcast.134, (f32[3,1,1,256]{3,2,1,0:T(1,128)S(1)}, s32[1,1,2,8]{3,2,1,0:T(2,128)S(1)}, f32[16,6,128]{2,1,0:T(8,128)S(1)}, s32[256]{0:T(256)S(1)}, f32[3,2048]{0,1:T(8,128)S(1)}) %tuple.139), branch_computations={%region_9.10_spmd, %region_10.13_spmd} | conditional | flops 15991856 | bytes 2414224 | solution.py:453
  30.3 1.1 %broadcast.235 = f32[2,128,8,128]{3,1,2,0:T(8,128)} broadcast(f32[]{:T(128)} %constant.150.clone), dimensions={} | broadcast | bytes 1048580 | tf_op jit(solution)/shard_map/broadcast.18
  31.4 0.3 copy.98
  31.7 13.6 %all_gather.18 = f32[4,16,4,128]{3,2,1,0:T(4,128)S(1)} all-gather(f32[4,4,4,128]{3,2,1,0:T(4,128)S(1)} %pad_maximum_fusion.2), channel_id=1, replica_groups=mesh['group'=4,'gx'=4,'gy'=2] {'gx'}, dimensions={1}, use_global_device_ids=true | all-gather | bytes 163840 | tf_op jit(solution)/shard_map/all_gather | solution.py:345
  45.3 5.6 %all_gather.19 = f32[4,16,8,128]{3,1,0,2:T(8,128)S(1)} all-gather(f32[4,16,4,128]{3,1,0,2:T(8,128)S(1)} %copy.89), channel_id=1, replica_groups=mesh['group'=4,'gx'=4,'gy'=2] {'gy'}, dimensions={2}, use_global_device_ids=true | all-gather | bytes 393216 | tf_op jit(solution)/shard_map/all_gather | solution.py:346
  51.0 0.2 conditional.7
  51.2 0.6 constant_dynamic-slice_fusion.3
  51.8 0.1 collective-permute-start.2
  51.9 19.3 %collective-permute-start.3 = (f32[4,3,128]{2,0,1:T(4,128)S(1)}, f32[4,3,128]{2,0,1:T(4,128)S(1)}, u32[]{:S(2)}, u32[]{:S(2)}) collective-permute-start(f32[4,3,128]{2,0,1:T(4,128)S(1)} %get-tuple-element.319), channel_id=1, source_target_pairs={{0,16},{8,24},{16,0},{24,8},{1,17},{9,25},{17,1},{25,9},{2,18},{10... | collective-permute-start | bytes 18440 | tf_op jit(solution)/shard_map/ppermute | solution.py:78
  71.2 0.9 %collective-permute-done.2 = f32[4,3,128]{2,0,1:T(4,128)S(1)} collective-permute-done((f32[4,3,128]{2,0,1:T(4,128)S(1)}, f32[4,3,128]{2,0,1:T(4,128)S(1)}, u32[]{:S(2)}, u32[]{:S(2)}) %collective-permute-start.2) | collective-permute-done | bytes 6176 | tf_op jit(solution)/shard_map/ppermute | solution.py:78
  72.1 0.7 collective-permute-done.3
  72.8 0.1 copy.99
  72.9 2.5 %scatter_custom_fusion.1 = f32[3,2048]{0,1:T(8,128)S(1)} fusion(s32[512]{0:T(512)S(1)} %bitcast.175, f32[512,3]{1,0:T(8,128)S(1)} %bitcast.146, f32[]{:T(128)} %constant.169.clone.1), kind=kCustom, calls=%fused_computation.113 | custom fusion | flops 1536 | bytes 24580 | tf_op jit(solution)/shard_map/scatter-add | solution.py:511
  75.4 1.8 %conditional.9 = (bf16[19,2,8,128]{3,2,1,0:T(8,128)(2,1)S(1)}) conditional(s32[]{:T(128)} %convert_element_type.61, () %tuple.40, (f32[1,4,10,130]{3,2,1,0:T(8,128)S(1)}, f32[19,1,1,1]{0,3,2,1:T(1,128)S(1)}, f32[19,1,1,1]{0,3,2,1:T(1,128)S(1)}, f32[19,1,1,1]{0,3,2,1:T(1,128)S(1)}, f32[19,1,1,1]{0,3,2,1:T(1,128)S(1)}, ...), branch_computations={%region_18.19_spmd, %region_19.20_spmd.clone} | conditional | flops 1056324 | bytes 4268820 | solution.py:513
  75.5 0.1 select_select_fusion.1
  75.7 0.1 fusion.1
  75.8 0.2 select_select_fusion
  76.0 0.1 fusion
  76.2 0.1 slice.231
  76.3 0.3 copy.93
  76.6 0.1 slice.230
  76.7 0.1 slice.241
  76.8 0.4 fusion.6
  77.2 0.6 copy-done
  (62 shorter events, 0.5 us)
Async XLA Ops:
  0.6 13.9 %copy-start.6 = (f32[4,4,128]{2,1,0:T(4,128)S(1)}, f32[4,4,128]{2,1,0:T(4,128)}, u32[]{:S(2)}) copy-start(f32[4,4,128]{2,1,0:T(4,128)} %param.47) | copy-start | bytes 24580
  0.6 13.9 %copy-start.7 = (s32[4,4,128]{2,1,0:T(4,128)S(1)}, s32[4,4,128]{2,1,0:T(4,128)}, u32[]{:S(2)}) copy-start(s32[4,4,128]{2,1,0:T(4,128)} %param.48) | copy-start | bytes 24580
  0.7 13.9 %copy-start.1 = (f32[3,4,4,128]{3,2,1,0:T(4,128)S(1)}, f32[3,4,4,128]{3,2,1,0:T(4,128)}, u32[]{:S(2)}) copy-start(f32[3,4,4,128]{3,2,1,0:T(4,128)} %param.46) | copy-start | bytes 73732
  9.2 6.1 %collective-permute-start = (bf16[20,1,10,128]{3,2,1,0:T(8,128)(2,1)S(1)}, bf16[20,1,10,128]{3,2,1,0:T(8,128)(2,1)S(1)}, u32[]{:S(2)}, u32[]{:S(2)}) collective-permute-start(bf16[20,1,10,128]{3,2,1,0:T(8,128)(2,1)S(1)} %get-tuple-element.313), channel_id=1, source_target_pairs={{0,2},{1,3},{2,4},{3,5},{4,6},{5,7},{6,8},{7,9},{8,10},{9,11},{10,... | collective-permute-start | bytes 153608 | tf_op jit(solution)/shard_map/ppermute | solution.py:53
  13.2 6.4 %collective-permute-start.1 = (bf16[20,1,10,128]{3,2,1,0:T(8,128)(2,1)S(1)}, bf16[20,1,10,128]{3,2,1,0:T(8,128)(2,1)S(1)}, u32[]{:S(2)}, u32[]{:S(2)}) collective-permute-start(bf16[20,1,10,128]{3,2,1,0:T(8,128)(2,1)S(1)} %get-tuple-element.314), channel_id=1, source_target_pairs={{2,0},{3,1},{4,2},{5,3},{6,4},{7,5},{8,6},{9,7},{10,8},{11,9},{12,... | collective-permute-start | bytes 153608 | tf_op jit(solution)/shard_map/ppermute | solution.py:53
  20.1 0.7 copy-start.2
  20.1 0.7 copy-start.4
  20.1 0.7 copy-start.5
  20.2 0.7 copy-start.8
  20.8 9.5 %copy-start.9 = (s32[1,1,256]{2,1,0:T(1,128)S(1)}, s32[1,1,256]{2,1,0:T(1,128)}, u32[]{:S(2)}) copy-start(s32[1,1,256]{2,1,0:T(1,128)} %param.50) | copy-start | bytes 3076
  20.8 9.5 %copy-start.10 = (f32[3,1,1,256]{3,2,1,0:T(1,128)S(1)}, f32[3,1,1,256]{3,2,1,0:T(1,128)}, u32[]{:S(2)}) copy-start(f32[3,1,1,256]{3,2,1,0:T(1,128)} %param.51) | copy-start | bytes 9220
  20.8 9.5 %copy-start.11 = (s32[1,1,2,8]{3,2,1,0:T(2,128)S(1)}, s32[1,1,2,8]{3,2,1,0:T(2,128)}, u32[]{:S(2)}) copy-start(s32[1,1,2,8]{3,2,1,0:T(2,128)} %param.52) | copy-start | bytes 196
  20.9 0.7 copy-start.13
  20.9 0.7 copy-start.14
  20.9 0.7 copy-start.15
  31.4 19.6 %copy-start.3 = (f32[24,24]{1,0:T(8,128)S(1)}, f32[24,24]{1,0:T(8,128)}, u32[]{:S(2)}) copy-start(f32[24,24]{1,0:T(8,128)} %param.49) | copy-start | bytes 6916
  51.8 20.2 %collective-permute-start.2 = (f32[4,3,128]{2,0,1:T(4,128)S(1)}, f32[4,3,128]{2,0,1:T(4,128)S(1)}, u32[]{:S(2)}, u32[]{:S(2)}) collective-permute-start(f32[4,3,128]{2,0,1:T(4,128)S(1)} %get-tuple-element.317), channel_id=1, source_target_pairs={{0,8},{8,16},{16,24},{24,0},{1,9},{9,17},{17,25},{25,1},{2,10},{10... | collective-permute-start | bytes 18440 | tf_op jit(solution)/shard_map/ppermute | solution.py:78
  51.9 20.9 %collective-permute-start.3 = (f32[4,3,128]{2,0,1:T(4,128)S(1)}, f32[4,3,128]{2,0,1:T(4,128)S(1)}, u32[]{:S(2)}, u32[]{:S(2)}) collective-permute-start(f32[4,3,128]{2,0,1:T(4,128)S(1)} %get-tuple-element.319), channel_id=1, source_target_pairs={{0,16},{8,24},{16,0},{24,8},{1,17},{9,25},{17,1},{25,9},{2,18},{10... | collective-permute-start | bytes 18440 | tf_op jit(solution)/shard_map/ppermute | solution.py:78
  71.2 1.6 %collective-permute-start.4 = (f32[4,3,128]{2,0,1:T(4,128)S(1)}, f32[4,3,128]{2,0,1:T(4,128)S(1)}, u32[]{:S(2)}, u32[]{:S(2)}) collective-permute-start(f32[4,3,128]{2,0,1:T(4,128)S(1)} %get-tuple-element.318), channel_id=1, source_target_pairs={{0,24},{8,0},{16,8},{24,16},{1,25},{9,1},{17,9},{25,17},{2,26},{10... | collective-permute-start | bytes 18440 | tf_op jit(solution)/shard_map/ppermute | solution.py:78
  76.0 0.8 %copy-start.12 = (f32[19]{0:T(128)S(1)}, f32[19]{0:T(128)}, u32[]{:S(2)}) copy-start(f32[19]{0:T(128)} %constant.208) | copy-start | bytes 232 | tf_op jit(solution)/shard_map/cond
  77.2 0.6 copy-start
